TPU v7x, 32 devices: a whole 2x2x4 slice. The times are simulated.
32 devices in a mesh: dp: 2 (over x), mp: 16 (over z, y, core).
Axes of the slice: x: 2, y: 2, z: 4, core: 2. Of those that a mesh axis runs over, the one named last changes fastest.
Arguments:
- inputs: bfloat16 [256, 8192], P('dp', 'mp'), may hold values from -6 to 6
- out_grad: bfloat16 [256, 8192], P('dp', 'mp'), may hold values from -6 to 6
- w_in: bfloat16 [128, 4, 128, 128], P('mp'), may hold values from -0.25 to 0.25
- in_blocks: int32 [128, 4], P('mp'), may hold values from 0 to 63, as said below
- w_out: bfloat16 [128, 4, 128, 128], P('mp'), may hold values from -0.1875 to 0.1875
- out_blocks: int32 [128, 4], P('mp'), may hold values from 0 to 63, as said below
Outputs:
- outputs: bfloat16 [256, 8192], P('dp', 'mp')
- in_grad: bfloat16 [256, 8192], P('dp', 'mp')
- w_in_grad: bfloat16 [128, 4, 128, 128], P('mp')
- w_out_grad: bfloat16 [128, 4, 128, 128], P('mp')
Inputs may be any that keep to these rules, and one draw needn't show every extreme that they name: `in_blocks`: the 4 input column blocks of one hidden block row are distinct. `out_blocks`: the 4 output column blocks of one hidden block row are distinct.
All inputs are finite; a program needn't handle non-finite values.
Results may differ from a plain program's by a relative error of at most 0.017.
Values may be sent and summed in bfloat16 or wider, within the bound.
No kernel may reach another device: no remote copies, remote signals or barrier semaphores. Data moves between devices by JAX's collectives and lax.ppermute only.
A program may use at most 64 MiB of HBM per device.

v0:
```python
import jax
import jax.numpy as jnp
from jax import lax
from jax.sharding import PartitionSpec as P

root_half = 0.7071067811865476
inv_root_two_pi = 0.3989422804014327


def gelu_value(preact):
    return 0.5 * preact * (1.0 + jax.scipy.special.erf(preact * root_half))


def gelu_slope(preact):
    return (
        0.5 * (1.0 + jax.scipy.special.erf(preact * root_half))
        + preact * jnp.exp(-0.5 * preact * preact) * inv_root_two_pi
    )


def per_device(inputs, out_grad, w_in, in_blocks, w_out, out_blocks):
    tok_rows = inputs.shape[0]
    hid_rows = w_in.shape[0]
    per_row = w_in.shape[1]
    block_size = w_in.shape[2]
    pair_count = hid_rows * per_row
    owners = lax.axis_size("mp")
    in_full, grad_full = (
        lax.all_gather(inputs, "mp", axis=1, tiled=True),
        lax.all_gather(out_grad, "mp", axis=1, tiled=True),
    )
    col_count = in_full.shape[1] // block_size
    in_flat = in_blocks.reshape(pair_count)
    out_flat = out_blocks.reshape(pair_count)
    empty = jnp.zeros((tok_rows, col_count, block_size), jnp.float32)
    in_sel = jnp.take(in_full.reshape(tok_rows, col_count, block_size), in_flat, axis=1)
    in_sel = in_sel.reshape(tok_rows, hid_rows, per_row, block_size)
    preact = jnp.einsum("trki,rkio->tro", in_sel, w_in, preferred_element_type=jnp.float32)
    hidden = gelu_value(preact).astype(jnp.bfloat16)
    out_terms = jnp.einsum("tri,rkio->trko", hidden, w_out, preferred_element_type=jnp.float32)
    out_terms = out_terms.reshape(tok_rows, pair_count, block_size)
    out_local = empty.at[:, out_flat].add(out_terms)
    out_local = out_local.reshape(tok_rows, col_count * block_size)

    def collect(received):
        return received.reshape(owners, tok_rows, -1).sum(axis=0).astype(jnp.bfloat16)

    outputs = collect(lax.all_to_all(out_local, "mp", split_axis=1, concat_axis=0, tiled=True))
    grad_sel = jnp.take(grad_full.reshape(tok_rows, col_count, block_size), out_flat, axis=1)
    grad_sel = grad_sel.reshape(tok_rows, hid_rows, per_row, block_size)
    hid_grad = jnp.einsum("trko,rkio->tri", grad_sel, w_out, preferred_element_type=jnp.float32)
    pre_grad = (hid_grad * gelu_slope(preact)).astype(jnp.bfloat16)
    in_terms = jnp.einsum("tro,rkio->trki", pre_grad, w_in, preferred_element_type=jnp.float32)
    in_terms = in_terms.reshape(tok_rows, pair_count, block_size)
    in_local = empty.at[:, in_flat].add(in_terms)
    in_local = in_local.reshape(tok_rows, col_count * block_size)
    w_in_part = jnp.einsum("trki,tro->rkio", in_sel, pre_grad, preferred_element_type=jnp.float32)
    in_grad = collect(lax.all_to_all(in_local, "mp", split_axis=1, concat_axis=0, tiled=True))
    w_out_part = jnp.einsum("tri,trko->rkio", hidden, grad_sel, preferred_element_type=jnp.float32)
    w_in_total, w_out_total = (
        lax.psum(w_in_part.astype(jnp.bfloat16), "dp").astype(jnp.float32),
        lax.psum(w_out_part.astype(jnp.bfloat16), "dp").astype(jnp.float32),
    )
    w_in_grad = w_in_total.astype(jnp.bfloat16)
    w_out_grad = w_out_total.astype(jnp.bfloat16)
    return (outputs, in_grad, w_in_grad, w_out_grad)


def solution(mesh):
    return jax.shard_map(
        per_device,
        mesh=mesh,
        in_specs=(
            P("dp", "mp"),
            P("dp", "mp"),
            P("mp", None, None, None),
            P("mp", None),
            P("mp", None, None, None),
            P("mp", None),
        ),
        out_specs=(
            P("dp", "mp"),
            P("dp", "mp"),
            P("mp", None, None, None),
            P("mp", None, None, None),
        ),
        check_vma=False,
    )
```

profile of v0, /device:TPU:13, one launch (start us, length us, event | category | flops | bytes accessed | tf_op | source)
XLA Modules:
  0.0 331.5 jit_solution(15757751601421945742)
XLA Ops:
  7.2 1.7 copy.43
  9.0 1.7 copy.48
  11.7 0.8 copy.41
  12.6 39.3 %all-gather.3.cloned.1.call-done = bf16[128,8192]{0,1:T(8,128)(2,1)} async-done(((bf16[128,512]{0,1:T(8,128)(2,1)}), bf16[128,8192]{0,1:T(8,128)(2,1)}) %all-gather.3.cloned.1.call-update) | async-done | bytes 2097168 | tf_op jit(solution)/shard_map/all_gather | solution.py:29
  51.8 3.2 copy.44
  55.1 39.7 %all-gather.5.cloned.1.call-done = bf16[128,8192]{0,1:T(8,128)(2,1)} async-done(((bf16[128,512]{0,1:T(8,128)(2,1)}), bf16[128,8192]{0,1:T(8,128)(2,1)}) %all-gather.5.cloned.1.call-update) | async-done | bytes 2097168 | tf_op jit(solution)/shard_map/all_gather | solution.py:30
  94.8 4.1 %copy.49 = bf16[128,64,128]{2,0,1:T(8,128)(2,1)} copy(bf16[128,64,128]{0,2,1:T(8,128)(2,1)} %bitcast.71) | data formatting | bytes 4194304 | tf_op jit(solution)/shard_map/reshape | solution.py:49
  98.8 1.6 gather_fusion
  100.5 1.4 broadcast_select_fusion.1
  102.3 3.2 gather_fusion.1
  105.6 1.5 broadcast_select_fusion
  107.6 1.8 fusion.14
  109.3 2.4 broadcast_in_dim.14.clone.1
  111.8 7.1 %scatter_fusion.1 = f32[128,64,128]{2,0,1:T(8,128)} fusion(f32[128,64,128]{2,0,1:T(8,128)} %broadcast_in_dim.14.clone.1, s32[32]{0:T(128)S(1)} %fusion.10, f32[32,128,128]{2,1,0:T(8,128)} %bitcast.67), kind=kCustom, calls=%fused_computation.3 | custom fusion | flops 524288 | bytes 6291584 | tf_op jit(solution)/shard_map/scatter-add | solution.py:55
  118.9 5.6 %copy.50 = f32[128,64,128]{0,2,1:T(8,128)} copy(f32[128,64,128]{2,0,1:T(8,128)} %scatter_fusion.1) | data formatting | bytes 8388608 | tf_op jit(solution)/shard_map/scatter-add | solution.py:55
  124.5 6.5 %all-to-all-start.1 = ((f32[128,16,512]{0,2,1:T(8,128)}), f32[128,16,512]{0,2,1:T(8,128)}, u32[]{:S(2)}, u32[]{:S(2)}) async-start(f32[128,16,512]{0,2,1:T(8,128)} %bitcast.63), calls=%async_computation.1 | async-start | bytes 8388608 | tf_op jit(solution)/shard_map/all_to_all | solution.py:58
  131.1 3.0 fusion.12
  134.1 2.5 broadcast_in_dim.14.clone
  136.6 7.1 %scatter_fusion = f32[128,64,128]{2,0,1:T(8,128)} fusion(f32[128,64,128]{2,0,1:T(8,128)} %broadcast_in_dim.14.clone, s32[32]{0:T(128)S(1)} %fusion.9, f32[32,128,128]{2,1,0:T(8,128)} %bitcast.66), kind=kCustom, calls=%fused_computation.2 | custom fusion | flops 524288 | bytes 6291584 | tf_op jit(solution)/shard_map/scatter-add | solution.py:42
  143.7 5.6 %copy.45 = f32[128,64,128]{0,2,1:T(8,128)} copy(f32[128,64,128]{2,0,1:T(8,128)} %scatter_fusion) | data formatting | bytes 8388608 | tf_op jit(solution)/shard_map/scatter-add | solution.py:42
  149.3 74.2 %all-to-all-done.1 = f32[128,16,512]{0,2,1:T(8,128)} async-done(((f32[128,16,512]{0,2,1:T(8,128)}), f32[128,16,512]{0,2,1:T(8,128)}, u32[]{:S(2)}, u32[]{:S(2)}) %all-to-all-start.1) | async-done | bytes 4194336 | tf_op jit(solution)/shard_map/all_to_all | solution.py:58
  223.5 4.9 %all-to-all-start = ((f32[128,16,512]{0,2,1:T(8,128)}), f32[128,16,512]{0,2,1:T(8,128)}, u32[]{:S(2)}, u32[]{:S(2)}) async-start(f32[128,16,512]{0,2,1:T(8,128)} %bitcast.62), calls=%async_computation | async-start | bytes 8388608 | tf_op jit(solution)/shard_map/all_to_all | solution.py:48
  228.5 1.5 convolution_convert_fusion.1
  230.0 1.5 fusion
  231.5 64.4 %all-reduce.3.cloned.1.call-done = (bf16[8,4,128,128]{3,2,1,0:T(8,128)(2,1)}, bf16[8,4,128,128]{2,3,1,0:T(8,128)(2,1)}) async-done(((bf16[8,4,128,128]{3,2,1,0:T(8,128)(2,1)}, bf16[8,4,128,128]{2,3,1,0:T(8,128)(2,1)}), (bf16[8,4,128,128]{3,2,1,0:T(8,128)(2,1)}, bf16[8,4,128,128]{2,3,1,0:T(8,128)(2,1)})) %all-reduce.3.cloned.1.call-update) | async-done | bytes 2097168 | tf_op jit(solution)/shard_map/psum | solution.py:61
  295.9 2.3 copy.55
  298.1 2.4 reduce_sum.19
  300.5 0.8 copy.54
  301.3 19.6 %all-to-all-done = f32[128,16,512]{0,2,1:T(8,128)} async-done(((f32[128,16,512]{0,2,1:T(8,128)}), f32[128,16,512]{0,2,1:T(8,128)}, u32[]{:S(2)}, u32[]{:S(2)}) %all-to-all-start) | async-done | bytes 4194336 | tf_op jit(solution)/shard_map/all_to_all | solution.py:48
  320.9 2.4 reduce_sum.18
  323.3 0.8 copy.53
  324.0 1.0 copy.68
  (31 shorter events, 2.2 us)
Async XLA Ops:
  7.2 94.7 %copy-start = (bf16[8,4,128,128]{3,2,1,0:T(8,128)(2,1)S(1)}, bf16[8,4,128,128]{3,2,1,0:T(8,128)(2,1)}, u32[]{:S(2)}) copy-start(bf16[8,4,128,128]{3,2,1,0:T(8,128)(2,1)} %param.10) | copy-start | bytes 3145732
  7.2 44.7 %all-gather.3.cloned.1.call-start = ((), (), s32[]{:S(2)}) async-start(), calls=%async_computation.2 | async-start | bytes 2228224 | tf_op jit(solution)/shard_map/all_gather | solution.py:29
  9.0 85.8 %all-gather.5.cloned.1.call-start = ((), (), s32[]{:S(2)}) async-start(), calls=%async_computation.3 | async-start | bytes 2228224 | tf_op jit(solution)/shard_map/all_gather | solution.py:30
  105.6 1.5 copy-start.3
  107.0 2.3 copy-start.1
  124.5 99.0 %all-to-all-start.1 = ((f32[128,16,512]{0,2,1:T(8,128)}), f32[128,16,512]{0,2,1:T(8,128)}, u32[]{:S(2)}, u32[]{:S(2)}) async-start(f32[128,16,512]{0,2,1:T(8,128)} %bitcast.63), calls=%async_computation.1 | async-start | bytes 8388608 | tf_op jit(solution)/shard_map/all_to_all | solution.py:58
  223.5 97.4 %all-to-all-start = ((f32[128,16,512]{0,2,1:T(8,128)}), f32[128,16,512]{0,2,1:T(8,128)}, u32[]{:S(2)}, u32[]{:S(2)}) async-start(f32[128,16,512]{0,2,1:T(8,128)} %bitcast.62), calls=%async_computation | async-start | bytes 8388608 | tf_op jit(solution)/shard_map/all_to_all | solution.py:48
  228.4 67.4 %all-reduce.3.cloned.1.call-start = ((), (), s32[]{:S(2)}) async-start(), calls=%async_computation.4 | async-start | bytes 4194304 | tf_op jit(solution)/shard_map/psum | solution.py:61
  228.5 1.5 copy-start.2
  301.3 22.8 %copy-start.4 = (bf16[8,4,128,128]{3,2,1,0:T(8,128)(2,1)S(1)}, bf16[8,4,128,128]{3,2,1,0:T(8,128)(2,1)}, u32[]{:S(2)}) copy-start(bf16[8,4,128,128]{3,2,1,0:T(8,128)(2,1)} %get-tuple-element.25) | copy-start | bytes 3145732
Sparse Core Ops, SparseCore 0:
  10.7 41.0 all-gather.2
  54.6 40.1 all-gather.4
  232.2 63.6 all-reduce.2
where the time goes:
time: 333 us; the launch traced here: 332 us
  waiting for transfers between devices  237 us (71%)
  local copies, waits for them, and re-layouts  38.4 us (12%)
  other arithmetic  21.9 us (7%)
  between operations  13.9 us (4%)
  starting transfers between devices  11.5 us (3%)
  matrix products  8.61 us (3%)
    all_to_all x1, waiting for transfers between devices, per_device(): lax.all_to_all(in_local, 'mp', split_axis=1, concat_axis=0, tiled=True)  74.2 us
    psum x1, waiting for transfers between devices, per_device(): lax.psum(w_in_part.astype(jnp.bfloat16), 'dp').astype(jnp.float32)  64.4 us
    all_gather x1, waiting for transfers between devices, per_device(): lax.all_gather(out_grad, 'mp', axis=1, tiled=True)  39.7 us
    all_gather x1, waiting for transfers between devices, per_device(): lax.all_gather(inputs, 'mp', axis=1, tiled=True)  39.3 us
    all_to_all x1, waiting for transfers between devices, per_device(): lax.all_to_all(out_local, 'mp', split_axis=1, concat_axis=0, tiled=True)  19.6 us
    unnamed x18, local copies, waits for them, and re-layouts  9.78 us
    scatter-add x1, other arithmetic, per_device(): out_local = empty.at[:, out_flat].add(out_terms)  7.12 us
    scatter-add x1, other arithmetic, per_device(): in_local = empty.at[:, in_flat].add(in_terms)  7.1 us
  transfers between devices with their start and end apart: 5, of which 5 were waited for; matrix products, arithmetic and copies ran while one was open for 10% of the time, Pallas kernels for 0%

commit v1 on v0

--- a/solution.py
+++ b/solution.py
@@ -43,9 +43,20 @@
     out_local = out_local.reshape(tok_rows, col_count * block_size)
 
     def collect(received):
-        return received.reshape(owners, tok_rows, -1).sum(axis=0).astype(jnp.bfloat16)
+        received = received.reshape(owners, tok_rows, -1).astype(jnp.float32)
+        return received.sum(axis=0).astype(jnp.bfloat16)
 
-    outputs = collect(lax.all_to_all(out_local, "mp", split_axis=1, concat_axis=0, tiled=True))
+    def send_half(local):
+        return lax.all_to_all(local.astype(jnp.bfloat16), "mp", split_axis=1, concat_axis=0, tiled=True)
+
+    def dp_total(part):
+        part = part.astype(jnp.bfloat16)
+        if lax.axis_size("dp") == 2:
+            other = lax.ppermute(part, "dp", perm=[(0, 1), (1, 0)])
+            return (part.astype(jnp.float32) + other.astype(jnp.float32)).astype(jnp.bfloat16)
+        return lax.psum(part, "dp")
+
+    outputs = collect(send_half(out_local))
     grad_sel = jnp.take(grad_full.reshape(tok_rows, col_count, block_size), out_flat, axis=1)
     grad_sel = grad_sel.reshape(tok_rows, hid_rows, per_row, block_size)
     hid_grad = jnp.einsum("trko,rkio->tri", grad_sel, w_out, preferred_element_type=jnp.float32)
@@ -55,14 +66,10 @@
     in_local = empty.at[:, in_flat].add(in_terms)
     in_local = in_local.reshape(tok_rows, col_count * block_size)
     w_in_part = jnp.einsum("trki,tro->rkio", in_sel, pre_grad, preferred_element_type=jnp.float32)
-    in_grad = collect(lax.all_to_all(in_local, "mp", split_axis=1, concat_axis=0, tiled=True))
+    in_grad = collect(send_half(in_local))
     w_out_part = jnp.einsum("tri,trko->rkio", hidden, grad_sel, preferred_element_type=jnp.float32)
-    w_in_total, w_out_total = (
-        lax.psum(w_in_part.astype(jnp.bfloat16), "dp").astype(jnp.float32),
-        lax.psum(w_out_part.astype(jnp.bfloat16), "dp").astype(jnp.float32),
-    )
-    w_in_grad = w_in_total.astype(jnp.bfloat16)
-    w_out_grad = w_out_total.astype(jnp.bfloat16)
+    w_in_grad = dp_total(w_in_part)
+    w_out_grad = dp_total(w_out_part)
     return (outputs, in_grad, w_in_grad, w_out_grad)
 
 

time: 333 us -> 252 us (0.76)
  the two profiles are of different devices: /device:TPU:13 before, /device:TPU:0 now
where the time goes in v1:
time: 252 us; the launch traced here: 251 us
  waiting for transfers between devices  146 us (58%)
  local copies, waits for them, and re-layouts  33.4 us (13%)
  other arithmetic  31.5 us (12%)
  starting transfers between devices  17.9 us (7%)
  between operations  14.2 us (6%)
  matrix products  7.86 us (3%)
    ppermute x2, waiting for transfers between devices, dp_total(): other = lax.ppermute(part, 'dp', perm=[(0, 1), (1, 0)])  43.6 us
    all_gather x1, waiting for transfers between devices, per_device(): lax.all_gather(inputs, 'mp', axis=1, tiled=True)  42.3 us
    all_gather x1, waiting for transfers between devices, per_device(): lax.all_gather(out_grad, 'mp', axis=1, tiled=True)  39.7 us
    all_to_all x2, waiting for transfers between devices, send_half(): lax.all_to_all(local.astype(jnp.bfloat16), 'mp', split_axis=1, concat_axi...  20.5 us
    all_to_all x2, starting transfers between devices, send_half(): lax.all_to_all(local.astype(jnp.bfloat16), 'mp', split_axis=1, concat_axi...  15.7 us
    convert_element_type x2, local copies, waits for them, and re-layouts, send_half(): local.astype(jnp.bfloat16)  8.17 us
    unnamed x13, local copies, waits for them, and re-layouts  7.85 us
    convert_element_type x2, other arithmetic, send_half(): local.astype(jnp.bfloat16)  7.81 us
  transfers between devices with their start and end apart: 6, of which 5 were waited for; matrix products, arithmetic and copies ran while one was open for 15% of the time, Pallas kernels for 0%

profile of v1, /device:TPU:0, one launch (start us, length us, event | category | flops | bytes accessed | tf_op | source)
XLA Modules:
  0.0 251.1 jit_solution(15929668390697611814)
XLA Ops:
  7.2 1.7 copy.43
  9.0 1.7 copy.48
  12.6 42.3 %all-gather.3.cloned.1.call-done = bf16[128,8192]{0,1:T(8,128)(2,1)} async-done(((bf16[128,512]{0,1:T(8,128)(2,1)}), bf16[128,8192]{0,1:T(8,128)(2,1)}) %all-gather.3.cloned.1.call-update) | async-done | bytes 2097168 | tf_op jit(solution)/shard_map/all_gather | solution.py:29
  54.9 3.2 %copy.44 = bf16[128,64,128]{2,0,1:T(8,128)(2,1)S(1)} copy(bf16[128,64,128]{0,2,1:T(8,128)(2,1)} %bitcast.70) | data formatting | bytes 4194304 | tf_op jit(solution)/shard_map/reshape | solution.py:36
  58.1 39.7 %all-gather.5.cloned.1.call-done = bf16[128,8192]{0,1:T(8,128)(2,1)} async-done(((bf16[128,512]{0,1:T(8,128)(2,1)}), bf16[128,8192]{0,1:T(8,128)(2,1)}) %all-gather.5.cloned.1.call-update) | async-done | bytes 2097168 | tf_op jit(solution)/shard_map/all_gather | solution.py:30
  97.8 4.1 %copy.49 = bf16[128,64,128]{2,0,1:T(8,128)(2,1)} copy(bf16[128,64,128]{0,2,1:T(8,128)(2,1)} %bitcast.71) | data formatting | bytes 4194304 | tf_op jit(solution)/shard_map/reshape | solution.py:60
  101.9 1.6 gather_fusion
  103.5 1.4 broadcast_select_fusion.1
  105.4 3.2 %gather_fusion.1 = bf16[32,128,128]{2,1,0:T(8,128)(2,1)} fusion(bf16[128,64,128]{2,0,1:T(8,128)(2,1)} %copy.49, s32[1024]{0:T(1024)S(1)} %pad_clamp_fusion), kind=kCustom, calls=%fused_computation.1.clone | custom fusion | bytes 2097280 | tf_op jit(solution)/shard_map/jit(_take)/gather | solution.py:60
  108.6 1.5 broadcast_select_fusion
  110.6 1.7 fusion.14
  112.4 2.5 broadcast_in_dim.14.clone.1
  114.8 7.0 %scatter_fusion.1 = f32[128,64,128]{2,0,1:T(8,128)} fusion(f32[128,64,128]{2,0,1:T(8,128)} %broadcast_in_dim.14.clone.1, s32[32]{0:T(128)S(1)} %fusion.10, f32[32,128,128]{2,1,0:T(8,128)} %bitcast.65), kind=kCustom, calls=%fused_computation.3 | custom fusion | flops 524288 | bytes 6291584 | tf_op jit(solution)/shard_map/scatter-add | solution.py:66
  121.8 3.9 %convert_element_type.55 = bf16[128,64,128]{2,0,1:T(8,128)(2,1)} convert(f32[128,64,128]{2,0,1:T(8,128)} %scatter_fusion.1) | non-fusion elementwise | flops 1048576 | bytes 6291456 | tf_op jit(solution)/shard_map/convert_element_type | solution.py:50
  125.7 4.1 %copy.50 = bf16[128,64,128]{0,2,1:T(8,128)(2,1)} copy(bf16[128,64,128]{2,0,1:T(8,128)(2,1)} %convert_element_type.55) | data formatting | bytes 4194304 | tf_op jit(solution)/shard_map/convert_element_type | solution.py:50
  129.8 4.4 %all-to-all-start.1 = ((bf16[128,16,512]{0,2,1:T(8,128)(2,1)}), bf16[128,16,512]{0,2,1:T(8,128)(2,1)}, u32[]{:S(2)}, u32[]{:S(2)}) async-start(bf16[128,16,512]{0,2,1:T(8,128)(2,1)} %bitcast.67), calls=%async_computation.1 | async-start | bytes 4194304 | tf_op jit(solution)/shard_map/all_to_all | solution.py:50
  134.4 3.0 %fusion.12 = f32[8,128,4,128]{3,1,2,0:T(8,128)} fusion(bf16[8,4,128,128]{3,2,1,0:T(8,128)(2,1)} %param.12, f32[128,8,128]{2,0,1:T(8,128)S(1)} %convolution_bitcast_fusion.1), kind=kOutput, calls=%fused_computation.34 | convolution fusion | flops 134873088 | bytes 3670016 | tf_op jit(solution)/shard_map/tri,rkio->trko/dot_general | solution.py:40
  137.4 2.5 broadcast_in_dim.14.clone
  139.8 7.1 %scatter_fusion = f32[128,64,128]{2,0,1:T(8,128)} fusion(f32[128,64,128]{2,0,1:T(8,128)} %broadcast_in_dim.14.clone, s32[32]{0:T(128)S(1)} %fusion.9, f32[32,128,128]{2,1,0:T(8,128)} %bitcast.64), kind=kCustom, calls=%fused_computation.2 | custom fusion | flops 524288 | bytes 6291584 | tf_op jit(solution)/shard_map/scatter-add | solution.py:42
  146.9 3.9 %convert_element_type.52 = bf16[128,64,128]{2,0,1:T(8,128)(2,1)} convert(f32[128,64,128]{2,0,1:T(8,128)} %scatter_fusion) | non-fusion elementwise | flops 1048576 | bytes 6291456 | tf_op jit(solution)/shard_map/convert_element_type | solution.py:50
  150.8 4.1 %copy.45 = bf16[128,64,128]{0,2,1:T(8,128)(2,1)} copy(bf16[128,64,128]{2,0,1:T(8,128)(2,1)} %convert_element_type.52) | data formatting | bytes 4194304 | tf_op jit(solution)/shard_map/convert_element_type | solution.py:50
  154.9 20.5 %all-to-all-done.1 = bf16[128,16,512]{0,2,1:T(8,128)(2,1)} async-done(((bf16[128,16,512]{0,2,1:T(8,128)(2,1)}), bf16[128,16,512]{0,2,1:T(8,128)(2,1)}, u32[]{:S(2)}, u32[]{:S(2)}) %all-to-all-start.1) | async-done | bytes 2097184 | tf_op jit(solution)/shard_map/all_to_all | solution.py:50
  175.4 11.2 %all-to-all-start = ((bf16[128,16,512]{0,2,1:T(8,128)(2,1)}), bf16[128,16,512]{0,2,1:T(8,128)(2,1)}, u32[]{:S(2)}, u32[]{:S(2)}) async-start(bf16[128,16,512]{0,2,1:T(8,128)(2,1)} %bitcast.66), calls=%async_computation | async-start | bytes 4194304 | tf_op jit(solution)/shard_map/all_to_all | solution.py:50
  186.6 1.7 fusion
  188.3 1.5 collective-permute-start.1
  191.0 23.4 %collective-permute-done.1 = bf16[8,4,128,128]{2,3,1,0:T(8,128)(2,1)S(1)} collective-permute-done((bf16[8,4,128,128]{2,3,1,0:T(8,128)(2,1)S(1)}, bf16[8,4,128,128]{2,3,1,0:T(8,128)(2,1)S(1)}, u32[]{:S(2)}, u32[]{:S(2)}) %collective-permute-start.1) | collective-permute-done | bytes 1048608 | tf_op jit(solution)/shard_map/ppermute | solution.py:55
  214.8 1.3 copy.55
  216.1 20.3 %collective-permute-done = bf16[8,4,128,128]{3,2,1,0:T(8,128)(2,1)} collective-permute-done((bf16[8,4,128,128]{3,2,1,0:T(8,128)(2,1)S(1)}, bf16[8,4,128,128]{3,2,1,0:T(8,128)(2,1)}, u32[]{:S(2)}, u32[]{:S(2)}) %collective-permute-start) | collective-permute-done | bytes 1048608 | tf_op jit(solution)/shard_map/ppermute | solution.py:55
  236.4 2.6 %add_convert_fusion.1 = bf16[8,4,128,128]{3,2,1,0:T(8,128)(2,1)} fusion(bf16[8,4,128,128]{3,2,1,0:T(8,128)(2,1)} %collective-permute-done, bf16[8,4,128,128]{3,2,1,0:T(8,128)(2,1)S(1)} %convolution_convert_fusion.1), kind=kLoop, calls=%fused_computation.5 | loop fusion | flops 2097152 | bytes 3145728 | tf_op jit(solution)/shard_map/convert_element_type | solution.py:56
  239.0 1.9 reduce_sum.25
  240.9 0.8 copy.54
  241.6 1.9 reduce_sum.24
  (31 shorter events, 5.3 us)
Async XLA Ops:
  7.2 97.8 %copy-start = (bf16[8,4,128,128]{3,2,1,0:T(8,128)(2,1)S(1)}, bf16[8,4,128,128]{3,2,1,0:T(8,128)(2,1)}, u32[]{:S(2)}) copy-start(bf16[8,4,128,128]{3,2,1,0:T(8,128)(2,1)} %param.10) | copy-start | bytes 3145732
  7.2 47.7 %all-gather.3.cloned.1.call-start = ((), (), s32[]{:S(2)}) async-start(), calls=%async_computation.2 | async-start | bytes 2228224 | tf_op jit(solution)/shard_map/all_gather | solution.py:29
  9.0 88.8 %all-gather.5.cloned.1.call-start = ((), (), s32[]{:S(2)}) async-start(), calls=%async_computation.3 | async-start | bytes 2228224 | tf_op jit(solution)/shard_map/all_gather | solution.py:30
  108.6 1.5 copy-start.2
  110.1 2.3 copy-start.1
  129.8 45.5 %all-to-all-start.1 = ((bf16[128,16,512]{0,2,1:T(8,128)(2,1)}), bf16[128,16,512]{0,2,1:T(8,128)(2,1)}, u32[]{:S(2)}, u32[]{:S(2)}) async-start(bf16[128,16,512]{0,2,1:T(8,128)(2,1)} %bitcast.67), calls=%async_computation.1 | async-start | bytes 4194304 | tf_op jit(solution)/shard_map/all_to_all | solution.py:50
  175.4 66.3 %all-to-all-start = ((bf16[128,16,512]{0,2,1:T(8,128)(2,1)}), bf16[128,16,512]{0,2,1:T(8,128)(2,1)}, u32[]{:S(2)}, u32[]{:S(2)}) async-start(bf16[128,16,512]{0,2,1:T(8,128)(2,1)} %bitcast.66), calls=%async_computation | async-start | bytes 4194304 | tf_op jit(solution)/shard_map/all_to_all | solution.py:50
  188.3 26.0 %collective-permute-start.1 = (bf16[8,4,128,128]{2,3,1,0:T(8,128)(2,1)S(1)}, bf16[8,4,128,128]{2,3,1,0:T(8,128)(2,1)S(1)}, u32[]{:S(2)}, u32[]{:S(2)}) collective-permute-start(bf16[8,4,128,128]{2,3,1,0:T(8,128)(2,1)S(1)} %fusion), channel_id=1, source_target_pairs={{0,16},{16,0},{1,17},{17,1},{2,18},{18,2},{3,19},{19,3},{4,20},{20... | collective-permute-start | bytes 3145736 | tf_op jit(solution)/shard_map/ppermute | solution.py:55
  190.4 46.0 %collective-permute-start = (bf16[8,4,128,128]{3,2,1,0:T(8,128)(2,1)S(1)}, bf16[8,4,128,128]{3,2,1,0:T(8,128)(2,1)}, u32[]{:S(2)}, u32[]{:S(2)}) collective-permute-start(bf16[8,4,128,128]{3,2,1,0:T(8,128)(2,1)S(1)} %convolution_convert_fusion.1), channel_id=1, source_target_pairs={{0,16},{16,0},{1,17},{17,1},{2,18},{18,2},{3,19},{19,3},{4,20},{20... | collective-permute-start | bytes 3145736 | tf_op jit(solution)/shard_map/ppermute | solution.py:55
Sparse Core Ops, SparseCore 0:
  10.7 44.0 all-gather.2
  57.6 40.1 all-gather.4

commit v2 on v0

v2 whole, which is shorter than its diff:
```python
import jax
import jax.numpy as jnp
from jax import lax
from jax.sharding import PartitionSpec as P

root_half = 0.7071067811865476
inv_root_two_pi = 0.3989422804014327


def gelu_value(preact):
    return 0.5 * preact * (1.0 + jax.scipy.special.erf(preact * root_half))


def gelu_slope(preact):
    return (
        0.5 * (1.0 + jax.scipy.special.erf(preact * root_half))
        + preact * jnp.exp(-0.5 * preact * preact) * inv_root_two_pi
    )


def per_device(inputs, out_grad, w_in, in_blocks, w_out, out_blocks):
    tok_rows = inputs.shape[0]
    own_cols = inputs.shape[1]
    hid_rows = w_in.shape[0]
    per_row = w_in.shape[1]
    block_size = w_in.shape[2]
    pair_count = hid_rows * per_row
    owners = lax.axis_size("mp")
    own_blocks = own_cols // block_size
    col_count = owners * own_blocks

    both = jnp.concatenate([inputs, out_grad], axis=1)
    both = jnp.broadcast_to(both[None], (owners, tok_rows, 2 * own_cols))
    got = lax.all_to_all(both, "mp", split_axis=0, concat_axis=0, tiled=True)
    got = got.reshape(owners, tok_rows, 2, own_blocks, block_size)
    got = got.transpose(2, 1, 0, 3, 4).reshape(2, tok_rows, col_count, block_size)
    in_view, grad_view = got[0], got[1]

    in_flat = in_blocks.reshape(pair_count)
    out_flat = out_blocks.reshape(pair_count)
    columns = jnp.arange(col_count, dtype=jnp.int32)
    in_onehot = (in_flat[:, None] == columns[None, :]).astype(jnp.float32)
    out_onehot = (out_flat[:, None] == columns[None, :]).astype(jnp.float32)

    def dp_total(part):
        if lax.axis_size("dp") == 2:
            other = lax.ppermute(part, "dp", perm=[(0, 1), (1, 0)])
            return (part.astype(jnp.float32) + other.astype(jnp.float32)).astype(jnp.bfloat16)
        return lax.psum(part, "dp")

    def column_sums(terms, onehot):
        local = jnp.einsum("tpo,pc->cto", terms, onehot, precision=lax.Precision.HIGHEST,
                           preferred_element_type=jnp.float32)
        local = local.astype(jnp.bfloat16).reshape(owners, own_blocks * tok_rows * block_size)
        got = lax.all_to_all(local, "mp", split_axis=0, concat_axis=0, tiled=True)
        got = got.reshape(owners, own_blocks, tok_rows, block_size).astype(jnp.float32).sum(axis=0)
        return got.transpose(1, 0, 2).reshape(tok_rows, own_cols).astype(jnp.bfloat16)

    in_sel = jnp.take(in_view, in_flat, axis=1)
    in_sel = in_sel.reshape(tok_rows, hid_rows, per_row, block_size)
    grad_sel = jnp.take(grad_view, out_flat, axis=1)
    grad_sel = grad_sel.reshape(tok_rows, hid_rows, per_row, block_size)
    preact = jnp.einsum("trki,rkio->tro", in_sel, w_in, preferred_element_type=jnp.float32)
    hidden = gelu_value(preact).astype(jnp.bfloat16)

    w_out_part = jnp.einsum("tri,trko->rkio", hidden, grad_sel, preferred_element_type=jnp.float32)
    w_out_part = w_out_part.astype(jnp.bfloat16)
    w_out_part, hidden = lax.optimization_barrier((w_out_part, hidden))
    w_out_grad = dp_total(w_out_part)

    out_terms = jnp.einsum("tri,rkio->trko", hidden, w_out, preferred_element_type=jnp.float32)
    out_terms = out_terms.reshape(tok_rows, pair_count, block_size)
    outputs = column_sums(out_terms, out_onehot)

    hid_grad = jnp.einsum("trko,rkio->tri", grad_sel, w_out, preferred_element_type=jnp.float32)
    pre_grad = (hid_grad * gelu_slope(preact)).astype(jnp.bfloat16)

    w_in_part = jnp.einsum("trki,tro->rkio", in_sel, pre_grad, preferred_element_type=jnp.float32)
    w_in_part = w_in_part.astype(jnp.bfloat16)
    w_in_part, pre_grad = lax.optimization_barrier((w_in_part, pre_grad))
    w_in_grad = dp_total(w_in_part)

    in_terms = jnp.einsum("tro,rkio->trki", pre_grad, w_in, preferred_element_type=jnp.float32)
    in_terms = in_terms.reshape(tok_rows, pair_count, block_size)
    in_grad = column_sums(in_terms, in_onehot)
    return (outputs, in_grad, w_in_grad, w_out_grad)


def solution(mesh):
    return jax.shard_map(
        per_device,
        mesh=mesh,
        in_specs=(
            P("dp", "mp"),
            P("dp", "mp"),
            P("mp", None, None, None),
            P("mp", None),
            P("mp", None, None, None),
            P("mp", None),
        ),
        out_specs=(
            P("dp", "mp"),
            P("dp", "mp"),
            P("mp", None, None, None),
            P("mp", None, None, None),
        ),
        check_vma=False,
    )
```

time: 333 us -> 293 us (0.88)
  the two profiles are of different devices: /device:TPU:13 before, /device:TPU:0 now
where the time goes in v2:
time: 293 us; the launch traced here: 292 us
  waiting for transfers between devices  123 us (42%)
  local copies, waits for them, and re-layouts  68.8 us (23%)
  other arithmetic  46 us (16%)
  starting transfers between devices  40.7 us (14%)
  matrix products  12.1 us (4%)
    all_to_all x1, waiting for transfers between devices, per_device(): got = lax.all_to_all(both, 'mp', split_axis=0, concat_axis=0, tiled=True)  77.3 us
    ppermute x2, waiting for transfers between devices, dp_total(): other = lax.ppermute(part, 'dp', perm=[(0, 1), (1, 0)])  41.3 us
    all_to_all x2, starting transfers between devices, column_sums(): got = lax.all_to_all(local, 'mp', split_axis=0, concat_axis=0, tiled=True)  31 us
    unnamed x29, local copies, waits for them, and re-layouts  29.6 us
    all_to_all x2, other arithmetic, column_sums(): got = lax.all_to_all(local, 'mp', split_axis=0, concat_axis=0, tiled=True)  27.4 us
    all_to_all x3, local copies, waits for them, and re-layouts, column_sums(): got = lax.all_to_all(local, 'mp', split_axis=0, concat_axis=0, tiled=True)  16.7 us
    reduce_sum x2, other arithmetic, column_sums(): got.reshape(owners, own_blocks, tok_rows, block_size).astype(jnp.float32)  12 us
    slice x3, local copies, waits for them, and re-layouts, per_device(): in_view, grad_view = (got[0], got[1])  10.5 us
  transfers between devices with their start and end apart: 5, of which 4 were waited for; matrix products, arithmetic and copies ran while one was open for 16% of the time, Pallas kernels for 0%

profile of v2, /device:TPU:0, one launch (start us, length us, event | category | flops | bytes accessed | tf_op | source)
XLA Modules:
  0.0 291.9 jit_solution(11335625745799632335)
XLA Ops:
  1.9 2.8 broadcast_in_dim.8
  4.7 7.6 %all-to-all-start = ((bf16[16,128,1024]{1,2,0:T(8,128)(2,1)}), bf16[16,128,1024]{1,2,0:T(8,128)(2,1)}, u32[]{:S(2)}, u32[]{:S(2)}) async-start(bf16[16,128,1024]{1,2,0:T(8,128)(2,1)} %broadcast_in_dim.8), calls=%async_computation | async-start | bytes 8388608 | tf_op jit(solution)/shard_map/all_to_all | solution.py:34
  12.7 77.3 %all-to-all-done = bf16[16,128,1024]{1,2,0:T(8,128)(2,1)} async-done(((bf16[16,128,1024]{1,2,0:T(8,128)(2,1)}), bf16[16,128,1024]{1,2,0:T(8,128)(2,1)}, u32[]{:S(2)}, u32[]{:S(2)}) %all-to-all-start) | async-done | bytes 4194336 | tf_op jit(solution)/shard_map/all_to_all | solution.py:34
  90.0 4.0 %fusion.29 = (bf16[1,128,16,4,128]{1,4,3,0,2:T(8,128)(2,1)}, bf16[1,128,16,4,128]{1,4,3,0,2:T(8,128)(2,1)S(1)}) fusion(bf16[2,128,16,4,128]{1,4,3,0,2:T(8,128)(2,1)} %bitcast.2), kind=kLoop, calls=%fused_computation.45 | loop fusion | bytes 8388608 | tf_op jit(solution)/shard_map/slice | solution.py:37
  94.0 3.9 %copy.46 = bf16[1,128,16,4,128]{4,1,3,2,0:T(8,128)(2,1)} copy(bf16[1,128,16,4,128]{1,4,3,0,2:T(8,128)(2,1)} %get-tuple-element.29) | data formatting | bytes 4194304 | tf_op jit(solution)/shard_map/slice | solution.py:37
  97.9 2.6 copy.44
  100.4 2.3 gather_fusion.1
  104.2 2.3 gather_fusion
  108.8 1.5 convolution_convert_fusion
  110.7 3.3 %fusion.7 = bf16[64,128,128]{2,0,1:T(8,128)(2,1)S(1)} fusion(f32[128,32,128]{2,0,1:T(8,128)S(1)} %bitcast.77, s32[32]{0:T(128)S(1)} %reshape.62), kind=kOutput, calls=%fused_computation.9 | convolution fusion | flops 403703808 | bytes 4194432 | tf_op jit(solution)/shard_map/tpo,pc->cto/dot_general | solution.py:52
  115.3 6.2 %all_to_all.21 = bf16[16,1,65536]{2,1,0:T(2,128)(2,1)} reshape(bf16[64,128,128]{2,1,0:T(8,128)(2,1)S(1)} %copy.54) | data formatting | bytes 4194304 | tf_op jit(solution)/shard_map/all_to_all | solution.py:55
  122.0 13.0 %reduce.7 = bf16[16,65536]{1,0:T(8,128)(2,1)S(1)} reduce(bf16[16,1,65536]{2,1,0:T(2,128)(2,1)} %all_to_all.21, bf16[]{:T(256)} %broadcast.50), dimensions={1}, to_apply=%all_to_all.21.reduce_sub_computation | reduce | bytes 4194306 | tf_op jit(solution)/shard_map/all_to_all | solution.py:55
  135.0 2.8 reshape.98
  137.8 19.8 %all-to-all-start.2 = ((bf16[16,2,32768]{2,1,0:T(2,128)(2,1)}), bf16[16,2,32768]{2,1,0:T(2,128)(2,1)S(1)}, u32[]{:S(2)}, u32[]{:S(2)}) async-start(bf16[16,2,32768]{2,1,0:T(2,128)(2,1)} %reshape.98), calls=%async_computation.2 | async-start | bytes 4194304 | tf_op jit(solution)/shard_map/all_to_all | solution.py:55
  157.6 1.5 fusion.10
  159.5 3.3 %fusion.4 = bf16[64,128,128]{2,0,1:T(8,128)(2,1)S(1)} fusion(f32[128,32,128]{2,0,1:T(8,128)S(1)} %bitcast.78, s32[32]{0:T(128)S(1)} %eq.28), kind=kOutput, calls=%fused_computation.8 | convolution fusion | flops 403703808 | bytes 4194432 | tf_op jit(solution)/shard_map/tpo,pc->cto/dot_general | solution.py:52
  162.8 2.7 copy.49
  165.5 10.0 %all_to_all.20 = bf16[16,1,65536]{2,1,0:T(2,128)(2,1)} reshape(bf16[64,128,128]{2,1,0:T(8,128)(2,1)} %copy.49) | data formatting | bytes 4194304 | tf_op jit(solution)/shard_map/all_to_all | solution.py:55
  175.5 14.4 %reduce.6 = bf16[16,65536]{1,0:T(8,128)(2,1)} reduce(bf16[16,1,65536]{2,1,0:T(2,128)(2,1)} %all_to_all.20, bf16[]{:T(256)} %broadcast.50), dimensions={1}, to_apply=%all_to_all.20.reduce_sub_computation | reduce | bytes 4194306 | tf_op jit(solution)/shard_map/all_to_all | solution.py:55
  189.9 4.0 %reshape.96 = bf16[16,2,32768]{2,1,0:T(2,128)(2,1)} reshape(bf16[16,65536]{1,0:T(8,128)(2,1)} %reduce.6) | data formatting | bytes 4194304
  193.9 4.8 %all-to-all-done.2 = bf16[16,2,32768]{2,1,0:T(2,128)(2,1)S(1)} async-done(((bf16[16,2,32768]{2,1,0:T(2,128)(2,1)}), bf16[16,2,32768]{2,1,0:T(2,128)(2,1)S(1)}, u32[]{:S(2)}, u32[]{:S(2)}) %all-to-all-start.2) | async-done | bytes 2097184 | tf_op jit(solution)/shard_map/all_to_all | solution.py:55
  198.7 11.3 %all-to-all-start.1 = ((bf16[16,2,32768]{2,1,0:T(2,128)(2,1)}), bf16[16,2,32768]{2,1,0:T(2,128)(2,1)}, u32[]{:S(2)}, u32[]{:S(2)}) async-start(bf16[16,2,32768]{2,1,0:T(2,128)(2,1)} %reshape.96), calls=%async_computation.1 | async-start | bytes 4194304 | tf_op jit(solution)/shard_map/all_to_all | solution.py:55
  210.0 1.6 collective-permute-start.1
  212.1 24.2 %collective-permute-done.1 = bf16[8,4,128,128]{2,3,1,0:T(8,128)(2,1)S(1)} collective-permute-done((bf16[8,4,128,128]{2,3,1,0:T(8,128)(2,1)}, bf16[8,4,128,128]{2,3,1,0:T(8,128)(2,1)S(1)}, u32[]{:S(2)}, u32[]{:S(2)}) %collective-permute-start.1) | collective-permute-done | bytes 1048608 | tf_op jit(solution)/shard_map/ppermute | solution.py:47
  236.2 2.6 add_convert_fusion
  238.8 2.3 copy.59
  241.1 17.2 %collective-permute-done = bf16[8,4,128,128]{3,2,1,0:T(8,128)(2,1)} collective-permute-done((bf16[8,4,128,128]{3,2,1,0:T(8,128)(2,1)S(1)}, bf16[8,4,128,128]{3,2,1,0:T(8,128)(2,1)}, u32[]{:S(2)}, u32[]{:S(2)}) %collective-permute-start) | collective-permute-done | bytes 1048608 | tf_op jit(solution)/shard_map/ppermute | solution.py:47
  258.2 2.7 add_convert_fusion.1
  260.9 6.7 %reshape.99 = bf16[16,1,65536]{2,1,0:T(2,128)(2,1)} reshape(bf16[16,2,32768]{2,1,0:T(2,128)(2,1)S(1)} %all-to-all-done.2) | data formatting | bytes 4194304
  267.6 6.0 %reduce_sum.25 = bf16[65536]{0:T(1024)(128)(2,1)S(1)} reduce(bf16[16,1,65536]{2,1,0:T(2,128)(2,1)} %reshape.99, bf16[]{:T(256)} %constant.9.clone.1), dimensions={0,1}, to_apply=%region_1.3 | reduce | flops 983040 | bytes 2228226 | tf_op jit(solution)/shard_map/reduce_sum | solution.py:56
  274.5 10.5 %reshape.97 = bf16[16,1,65536]{2,1,0:T(2,128)(2,1)} reshape(bf16[16,2,32768]{2,1,0:T(2,128)(2,1)} %all-to-all-done.1) | data formatting | bytes 4194304
  285.0 6.0 %reduce_sum.24 = bf16[65536]{0:T(1024)(128)(2,1)S(1)} reduce(bf16[16,1,65536]{2,1,0:T(2,128)(2,1)} %reshape.97, bf16[]{:T(256)} %constant.9.clone.1), dimensions={0,1}, to_apply=%region_0.0 | reduce | flops 983040 | bytes 2228226 | tf_op jit(solution)/shard_map/reduce_sum | solution.py:56
  (46 shorter events, 10.3 us)
Async XLA Ops:
  0.6 102.3 %copy-start = (bf16[8,4,128,128]{3,2,1,0:T(8,128)(2,1)S(1)}, bf16[8,4,128,128]{3,2,1,0:T(8,128)(2,1)}, u32[]{:S(2)}) copy-start(bf16[8,4,128,128]{3,2,1,0:T(8,128)(2,1)} %param.10) | copy-start | bytes 3145732
  4.7 7.6 %copy-start.8 = (s32[8,4]{0,1:T(4,128)S(1)}, s32[8,4]{0,1:T(4,128)}, u32[]{:S(2)}) copy-start(s32[8,4]{0,1:T(4,128)} %param.11) | copy-start | bytes 388
  4.7 7.8 %copy-start.9 = (s32[8,4]{0,1:T(4,128)S(1)}, s32[8,4]{0,1:T(4,128)}, u32[]{:S(2)}) copy-start(s32[8,4]{0,1:T(4,128)} %param.13) | copy-start | bytes 388
  4.7 85.3 %all-to-all-start = ((bf16[16,128,1024]{1,2,0:T(8,128)(2,1)}), bf16[16,128,1024]{1,2,0:T(8,128)(2,1)}, u32[]{:S(2)}, u32[]{:S(2)}) async-start(bf16[16,128,1024]{1,2,0:T(8,128)(2,1)} %broadcast_in_dim.8), calls=%async_computation | async-start | bytes 8388608 | tf_op jit(solution)/shard_map/all_to_all | solution.py:34
  106.5 1.5 copy-start.5
  106.6 1.7 copy-start.7
  106.7 3.5 %copy-start.3 = (bf16[32,128,128]{2,1,0:T(8,128)(2,1)}, bf16[32,128,128]{2,1,0:T(8,128)(2,1)S(1)}, u32[]{:S(2)}) copy-start(bf16[32,128,128]{2,1,0:T(8,128)(2,1)S(1)} %broadcast_select_fusion.1) | copy-start | bytes 3145732
  137.8 19.8 %copy-start.4 = (bf16[32,128,128]{2,1,0:T(8,128)(2,1)S(1)}, bf16[32,128,128]{2,1,0:T(8,128)(2,1)}, u32[]{:S(2)}) copy-start(bf16[32,128,128]{2,1,0:T(8,128)(2,1)} %copy-done.3) | copy-start | bytes 3145732
  137.8 60.9 %all-to-all-start.2 = ((bf16[16,2,32768]{2,1,0:T(2,128)(2,1)}), bf16[16,2,32768]{2,1,0:T(2,128)(2,1)S(1)}, u32[]{:S(2)}, u32[]{:S(2)}) async-start(bf16[16,2,32768]{2,1,0:T(2,128)(2,1)} %reshape.98), calls=%async_computation.2 | async-start | bytes 4194304 | tf_op jit(solution)/shard_map/all_to_all | solution.py:55
  157.6 1.5 copy-start.6
  193.9 17.7 %copy-start.2 = (bf16[8,4,128,128]{3,2,1,0:T(8,128)(2,1)S(1)}, bf16[8,4,128,128]{3,2,1,0:T(8,128)(2,1)}, u32[]{:S(2)}) copy-start(bf16[8,4,128,128]{3,2,1,0:T(8,128)(2,1)} %convolution_convert_fusion) | copy-start | bytes 3145732
  198.7 75.8 %all-to-all-start.1 = ((bf16[16,2,32768]{2,1,0:T(2,128)(2,1)}), bf16[16,2,32768]{2,1,0:T(2,128)(2,1)}, u32[]{:S(2)}, u32[]{:S(2)}) async-start(bf16[16,2,32768]{2,1,0:T(2,128)(2,1)} %reshape.96), calls=%async_computation.1 | async-start | bytes 4194304 | tf_op jit(solution)/shard_map/all_to_all | solution.py:55
  210.0 26.3 %collective-permute-start.1 = (bf16[8,4,128,128]{2,3,1,0:T(8,128)(2,1)}, bf16[8,4,128,128]{2,3,1,0:T(8,128)(2,1)S(1)}, u32[]{:S(2)}, u32[]{:S(2)}) collective-permute-start(bf16[8,4,128,128]{2,3,1,0:T(8,128)(2,1)} %fusion.10), channel_id=1, source_target_pairs={{0,16},{16,0},{1,17},{17,1},{2,18},{18,2},{3,19},{19,3},{4,20},{20... | collective-permute-start | bytes 3145736 | tf_op jit(solution)/shard_map/ppermute | solution.py:47
  211.6 46.7 %collective-permute-start = (bf16[8,4,128,128]{3,2,1,0:T(8,128)(2,1)S(1)}, bf16[8,4,128,128]{3,2,1,0:T(8,128)(2,1)}, u32[]{:S(2)}, u32[]{:S(2)}) collective-permute-start(bf16[8,4,128,128]{3,2,1,0:T(8,128)(2,1)S(1)} %copy-done.2), channel_id=1, source_target_pairs={{0,16},{16,0},{1,17},{17,1},{2,18},{18,2},{3,19},{19,3},{4,20},{20... | collective-permute-start | bytes 3145736 | tf_op jit(solution)/shard_map/ppermute | solution.py:47
  274.5 17.4 %copy-start.1 = (bf16[8,4,128,128]{3,2,1,0:T(8,128)(2,1)S(1)}, bf16[8,4,128,128]{3,2,1,0:T(8,128)(2,1)}, u32[]{:S(2)}) copy-start(bf16[8,4,128,128]{3,2,1,0:T(8,128)(2,1)} %param.10) | copy-start | bytes 3145732

commit v3 on v0

v3 whole, which is shorter than its diff:
```python
import jax
import jax.numpy as jnp
from jax import lax
from jax.sharding import Mesh, PartitionSpec as P

root_half = 0.7071067811865476
inv_root_two_pi = 0.3989422804014327


def gelu_value(preact):
    return 0.5 * preact * (1.0 + jax.scipy.special.erf(preact * root_half))


def gelu_slope(preact):
    return (
        0.5 * (1.0 + jax.scipy.special.erf(preact * root_half))
        + preact * jnp.exp(-0.5 * preact * preact) * inv_root_two_pi
    )


def swap_core(x):
    return lax.ppermute(x, "core", perm=[(0, 1), (1, 0)])


def per_device(inputs, out_grad, w_in, in_blocks, w_out, out_blocks):
    tok_rows = inputs.shape[0]
    own_cols = inputs.shape[1]
    hid_rows = w_in.shape[0]
    per_row = w_in.shape[1]
    block_size = w_in.shape[2]
    pair_count = hid_rows * per_row
    chips = lax.axis_size("chip")
    pair = lax.axis_size("core")
    own_blocks = own_cols // block_size
    col_count = chips * pair * own_blocks
    core = lax.axis_index("core")

    both = jnp.concatenate([inputs, out_grad], axis=1).reshape(tok_rows, 2, own_blocks, block_size)
    mine = lax.all_gather(both, "chip", axis=0, tiled=False)
    other = swap_core(mine)
    sets = jnp.stack([mine, other], axis=0)

    def select(flat, which):
        owner = flat // own_blocks
        sub = flat % own_blocks
        side = (owner % pair != core).astype(jnp.int32)
        sel = sets[side, owner // pair, :, which, sub, :]
        return sel.reshape(hid_rows, per_row, tok_rows, block_size)

    in_flat = in_blocks.reshape(pair_count)
    out_flat = out_blocks.reshape(pair_count)
    in_sel = select(in_flat, 0)
    grad_sel = select(out_flat, 1)

    def dp_total(part):
        part = part.astype(jnp.bfloat16)
        if lax.axis_size("dp") == 2:
            got = lax.ppermute(part, "dp", perm=[(0, 1), (1, 0)])
            return (part.astype(jnp.float32) + got.astype(jnp.float32)).astype(jnp.bfloat16)
        return lax.psum(part, "dp")

    empty = jnp.zeros((tok_rows, col_count, block_size), jnp.float32)

    def column_sums(terms, flat, tie=None):
        local = empty.at[:, flat].add(terms.reshape(tok_rows, pair_count, block_size))
        local = local.reshape(tok_rows, chips, pair, own_blocks, block_size)
        keep = lax.dynamic_index_in_dim(local, core, axis=2, keepdims=False)
        give = lax.dynamic_index_in_dim(local, 1 - core, axis=2, keepdims=False)
        chip_sum = (keep + swap_core(give)).astype(jnp.bfloat16)
        chip_sum = chip_sum.transpose(1, 0, 2, 3)
        if tie is not None:
            tie, chip_sum = lax.optimization_barrier((tie, chip_sum))
        got = lax.all_to_all(chip_sum, "chip", split_axis=0, concat_axis=0, tiled=True)
        total = got.astype(jnp.float32).sum(axis=0)
        return total.reshape(tok_rows, own_cols).astype(jnp.bfloat16), tie

    preact = jnp.einsum("rkti,rkio->tro", in_sel, w_in, preferred_element_type=jnp.float32)
    hidden = gelu_value(preact).astype(jnp.bfloat16)
    out_terms = jnp.einsum("tri,rkio->trko", hidden, w_out, preferred_element_type=jnp.float32)
    outputs, _ = column_sums(out_terms, out_flat)

    w_out_part = jnp.einsum("tri,rkto->rkio", hidden, grad_sel, preferred_element_type=jnp.float32)
    w_out_grad = dp_total(w_out_part)

    hid_grad = jnp.einsum("rkto,rkio->tri", grad_sel, w_out, preferred_element_type=jnp.float32)
    pre_grad = (hid_grad * gelu_slope(preact)).astype(jnp.bfloat16)
    in_terms = jnp.einsum("tro,rkio->trki", pre_grad, w_in, preferred_element_type=jnp.float32)
    in_grad, w_out_grad = column_sums(in_terms, in_flat, w_out_grad)
    w_in_part = jnp.einsum("rkti,tro->rkio", in_sel, pre_grad, preferred_element_type=jnp.float32)
    w_in_grad = dp_total(w_in_part)
    return (outputs, in_grad, w_in_grad, w_out_grad)


def solution(mesh):
    n_dp, n_mp = mesh.shape["dp"], mesh.shape["mp"]
    pair = 2 if n_mp % 2 == 0 else 1
    split = Mesh(mesh.devices.reshape(n_dp, n_mp // pair, pair), ("dp", "chip", "core"))
    cols = ("chip", "core")
    return jax.shard_map(
        per_device,
        mesh=split,
        in_specs=(
            P("dp", cols),
            P("dp", cols),
            P(cols, None, None, None),
            P(cols, None),
            P(cols, None, None, None),
            P(cols, None),
        ),
        out_specs=(
            P("dp", cols),
            P("dp", cols),
            P(cols, None, None, None),
            P(cols, None, None, None),
        ),
        check_vma=False,
    )
```

time: 333 us -> 200 us (0.60)
  the two profiles are of different devices: /device:TPU:13 before, /device:TPU:0 now
where the time goes in v3:
time: 200 us
  waiting for transfers between devices  108 us (54%)
  other arithmetic  30.7 us (15%)
  local copies, waits for them, and re-layouts  27.2 us (14%)
  between operations  14.2 us (7%)
  starting transfers between devices  11.7 us (6%)
  matrix products  7.64 us (4%)
    all_gather x1, waiting for transfers between devices, per_device(): mine = lax.all_gather(both, 'chip', axis=0, tiled=False)  52.5 us
    ppermute x2, waiting for transfers between devices, dp_total(): got = lax.ppermute(part, 'dp', perm=[(0, 1), (1, 0)])  31 us
    all_to_all x2, waiting for transfers between devices, column_sums(): lax.all_to_all(chip_sum, 'chip', split_axis=0, concat_axis=0, tiled=True)  22.2 us
    scatter-add x2, other arithmetic, column_sums(): empty.at[:, flat].add(terms.reshape(tok_rows, pair_count, block_size))  14.3 us
    all_to_all x2, starting transfers between devices, column_sums(): lax.all_to_all(chip_sum, 'chip', split_axis=0, concat_axis=0, tiled=True)  8.48 us
    unnamed x17, local copies, waits for them, and re-layouts  7.62 us
    gather x2, local copies, waits for them, and re-layouts, select(): sel = sets[side, owner // pair, :, which, sub, :]  6.85 us
    squeeze x2, local copies, waits for them, and re-layouts, column_sums(): give = lax.dynamic_index_in_dim(local, 1 - core, axis=2, keepdims=False)  6.53 us
  transfers between devices with their start and end apart: 8, of which 5 were waited for; matrix products, arithmetic and copies ran while one was open for 16% of the time, Pallas kernels for 0%

profile of v3, /device:TPU:0, one launch (start us, length us, event | category | flops | bytes accessed | tf_op | source)
XLA Modules:
  0.0 199.7 jit_solution(13983211806531929863)
XLA Ops:
  7.2 1.1 copy.39
  8.3 1.0 copy.40
  9.4 0.9 copy.41
  10.3 52.5 %all-gather.2.cloned.1.call-done = bf16[8,128,2,4,128]{4,1,3,2,0:T(8,128)(2,1)} async-done(((bf16[1,128,2,4,128]{4,1,3,2,0:T(8,128)(2,1)}), bf16[8,128,2,4,128]{4,1,3,2,0:T(8,128)(2,1)}) %all-gather.2.cloned.1.call-update) | async-done | bytes 2097168 | tf_op jit(solution)/shard_map/all_gather | solution.py:39
  64.5 2.7 %collective-permute-done = bf16[8,128,2,4,128]{4,1,3,2,0:T(8,128)(2,1)S(1)} collective-permute-done((bf16[8,128,2,4,128]{4,1,3,2,0:T(8,128)(2,1)}, bf16[8,128,2,4,128]{4,1,3,2,0:T(8,128)(2,1)S(1)}, u32[]{:S(2)}, u32[]{:S(2)}) %collective-permute-start) | collective-permute-done | bytes 2097184 | tf_op jit(solution)/shard_map/ppermute | solution.py:22
  67.1 3.9 %pad_maximum_fusion = bf16[2,8,128,2,4,128]{5,2,4,3,1,0:T(8,128)(2,1)} fusion(bf16[1,8,128,2,4,128]{5,2,4,3,1,0:T(8,128)(2,1)S(1)} %bitcast.96, bf16[1,8,128,2,4,128]{5,2,4,3,1,0:T(8,128)(2,1)} %bitcast.95), kind=kLoop, calls=%fused_computation.4 | loop fusion | flops 2097152 | bytes 8388608 | tf_op jit(solution)/shard_map/stack | solution.py:41
  71.0 3.0 %gather_fusion = bf16[32,128,128]{2,1,0:T(8,128)(2,1)S(1)} fusion(bf16[2,8,128,2,4,128]{5,2,4,3,1,0:T(8,128)(2,1)} %pad_maximum_fusion, s32[32]{0:T(128)S(1)} %get-tuple-element.29), kind=kCustom, calls=%fused_computation | custom fusion | bytes 2097664 | tf_op jit(solution)/shard_map/gather | solution.py:47
  74.0 3.9 %gather_fusion.1 = bf16[32,128,128]{2,1,0:T(8,128)(2,1)} fusion(bf16[2,8,128,2,4,128]{5,2,4,3,1,0:T(8,128)(2,1)} %pad_maximum_fusion, s32[32]{0:T(128)S(1)} %get-tuple-element.33), kind=kCustom, calls=%fused_computation.1 | custom fusion | bytes 2097664 | tf_op jit(solution)/shard_map/gather | solution.py:47
  78.3 0.8 copy-done.2
  79.9 1.8 fusion.36
  81.7 2.5 %broadcast_in_dim.2.clone.1 = f32[128,64,128]{2,0,1:T(8,128)} broadcast(f32[]{:T(128)} %constant.94.clone.1), dimensions={} | broadcast | bytes 4194308 | tf_op jit(solution)/shard_map/broadcast_in_dim | solution.py:62
  84.2 7.1 %scatter_fusion.1 = f32[128,64,128]{2,0,1:T(8,128)} fusion(f32[128,64,128]{2,0,1:T(8,128)} %broadcast_in_dim.2.clone.1, s32[32]{0:T(128)S(1)} %get-tuple-element.28, f32[32,128,128]{2,1,0:T(8,128)} %bitcast.92), kind=kCustom, calls=%fused_computation.3 | custom fusion | flops 524288 | bytes 6291584 | tf_op jit(solution)/shard_map/scatter-add | solution.py:65
  91.3 3.2 %dynamic-slice_bitcast_fusion = f32[128,8,4,128]{3,0,2,1:T(8,128)} fusion(f32[128,8,2,4,128]{4,0,3,2,1:T(8,128)} %bitcast.87, s32[]{:T(128)S(6)} %select_n.195), kind=kLoop, calls=%fused_computation.10 | loop fusion | bytes 4194308 | tf_op jit(solution)/shard_map/jit(dynamic_index_in_dim)/squeeze | solution.py:68
  94.7 1.5 fusion.2
  96.2 1.5 collective-permute-start.2
  97.6 3.0 %fusion.34 = f32[8,128,4,128]{3,1,2,0:T(8,128)} fusion(bf16[8,4,128,128]{3,2,1,0:T(8,128)(2,1)} %param.10, f32[128,8,128]{2,0,1:T(8,128)S(1)} %convolution_bitcast_fusion.1), kind=kOutput, calls=%fused_computation.82 | convolution fusion | flops 134873088 | bytes 3670016 | tf_op jit(solution)/shard_map/tri,rkio->trko/dot_general | solution.py:79
  100.6 2.5 %broadcast_in_dim.2.clone = f32[128,64,128]{2,0,1:T(8,128)} broadcast(f32[]{:T(128)} %constant.94.clone.1), dimensions={} | broadcast | bytes 4194308 | tf_op jit(solution)/shard_map/broadcast_in_dim | solution.py:62
  103.1 7.2 %scatter_fusion = f32[128,64,128]{2,0,1:T(8,128)} fusion(f32[128,64,128]{2,0,1:T(8,128)} %broadcast_in_dim.2.clone, s32[32]{0:T(128)S(1)} %get-tuple-element.32, f32[32,128,128]{2,1,0:T(8,128)} %bitcast.91), kind=kCustom, calls=%fused_computation.2 | custom fusion | flops 524288 | bytes 6291584 | tf_op jit(solution)/shard_map/scatter-add | solution.py:65
  110.2 3.3 %dynamic-slice_bitcast_fusion.1 = f32[128,8,4,128]{3,0,2,1:T(8,128)} fusion(f32[128,8,2,4,128]{4,0,3,2,1:T(8,128)} %bitcast.85, s32[]{:T(128)S(6)} %select_n.195), kind=kLoop, calls=%fused_computation.12 | loop fusion | bytes 4194308 | tf_op jit(solution)/shard_map/jit(dynamic_index_in_dim)/squeeze | solution.py:68
  113.5 8.4 %collective-permute-done.2 = bf16[8,4,128,128]{2,3,1,0:T(8,128)(2,1)} collective-permute-done((bf16[8,4,128,128]{2,3,1,0:T(8,128)(2,1)}, bf16[8,4,128,128]{2,3,1,0:T(8,128)(2,1)}, u32[]{:S(2)}, u32[]{:S(2)}) %collective-permute-start.2) | collective-permute-done | bytes 1048608 | tf_op jit(solution)/shard_map/ppermute | solution.py:58
  121.9 1.9 add_convert_fusion.1
  123.8 2.9 %fusion.7 = bf16[8,128,4,128]{3,1,2,0:T(8,128)(2,1)} fusion(f32[128,8,4,128]{3,0,2,1:T(8,128)} %collective-permute-done.3, f32[128,8,2,4,128]{4,0,3,2,1:T(8,128)S(1)} %bitcast.88, s32[]{:T(128)S(6)} %select_n.194), kind=kLoop, calls=%fused_computation.22 | loop fusion | flops 1048576 | bytes 5242884 | tf_op jit(solution)/shard_map/transpose | solution.py:70
  126.7 4.2 %all-to-all-start.1 = ((bf16[8,128,4,128]{3,1,2,0:T(8,128)(2,1)}), bf16[8,128,4,128]{3,1,2,0:T(8,128)(2,1)}, u32[]{:S(2)}, u32[]{:S(2)}) async-start(bf16[8,128,4,128]{3,1,2,0:T(8,128)(2,1)} %fusion.7), calls=%async_computation.1 | async-start | bytes 2097152 | tf_op jit(solution)/shard_map/all_to_all | solution.py:73
  131.0 3.6 %fusion.6 = bf16[8,128,4,128]{3,1,2,0:T(8,128)(2,1)} fusion(f32[128,8,4,128]{3,0,2,1:T(8,128)} %collective-permute-done.1, f32[128,8,2,4,128]{4,0,3,2,1:T(8,128)} %bitcast.86, s32[]{:T(128)S(6)} %select_n.194), kind=kLoop, calls=%fused_computation.21 | loop fusion | flops 1048576 | bytes 5242884 | tf_op jit(solution)/shard_map/transpose | solution.py:70
  134.5 22.2 %all-to-all-done.1 = bf16[8,128,4,128]{3,1,2,0:T(8,128)(2,1)} async-done(((bf16[8,128,4,128]{3,1,2,0:T(8,128)(2,1)}), bf16[8,128,4,128]{3,1,2,0:T(8,128)(2,1)}, u32[]{:S(2)}, u32[]{:S(2)}) %all-to-all-start.1) | async-done | bytes 1048608 | tf_op jit(solution)/shard_map/all_to_all | solution.py:73
  156.7 4.2 %all-to-all-start = ((bf16[8,128,4,128]{3,1,2,0:T(8,128)(2,1)}), bf16[8,128,4,128]{3,1,2,0:T(8,128)(2,1)}, u32[]{:S(2)}, u32[]{:S(2)}) async-start(bf16[8,128,4,128]{3,1,2,0:T(8,128)(2,1)} %fusion.6), calls=%async_computation | async-start | bytes 2097152 | tf_op jit(solution)/shard_map/all_to_all | solution.py:73
  161.5 1.5 collective-permute-start.4
  163.0 22.7 %collective-permute-done.4 = bf16[8,4,128,128]{3,2,1,0:T(8,128)(2,1)S(1)} collective-permute-done((bf16[8,4,128,128]{3,2,1,0:T(8,128)(2,1)S(1)}, bf16[8,4,128,128]{3,2,1,0:T(8,128)(2,1)S(1)}, u32[]{:S(2)}, u32[]{:S(2)}) %collective-permute-start.4) | collective-permute-done | bytes 1048608 | tf_op jit(solution)/shard_map/ppermute | solution.py:58
  185.6 1.3 add_convert_fusion
  187.0 1.3 copy.49
  188.3 1.4 reduce_sum.25
  190.6 1.4 reduce_sum.24
  (30 shorter events, 5.5 us)
Async XLA Ops:
  7.2 70.7 %copy-start = (bf16[8,4,128,128]{3,2,1,0:T(8,128)(2,1)S(1)}, bf16[8,4,128,128]{3,2,1,0:T(8,128)(2,1)}, u32[]{:S(2)}) copy-start(bf16[8,4,128,128]{3,2,1,0:T(8,128)(2,1)} %param.8) | copy-start | bytes 3145732
  7.2 55.6 %all-gather.2.cloned.1.call-start = ((), (), s32[]{:S(2)}) async-start(), calls=%async_computation.2 | async-start | bytes 2359296 | tf_op jit(solution)/shard_map/all_gather | solution.py:39
  62.7 4.4 %collective-permute-start = (bf16[8,128,2,4,128]{4,1,3,2,0:T(8,128)(2,1)}, bf16[8,128,2,4,128]{4,1,3,2,0:T(8,128)(2,1)S(1)}, u32[]{:S(2)}, u32[]{:S(2)}) collective-permute-start(bf16[8,128,2,4,128]{4,1,3,2,0:T(8,128)(2,1)} %all-gather.2.cloned.1.call-done), channel_id=1, source_target_pairs={{0,1},{1,0},{2,3},{3,2},{4,5},{5,4},{6,7},{7,6},{8,9},{9,8},{10,11... | collective-permute-start | bytes 6291464 | tf_op jit(solution)/shard_map/ppermute | solution.py:22
  77.9 1.2 copy-start.2
  77.9 1.5 copy-start.4
  91.3 3.4 %copy-start.3 = (bf16[32,128,128]{2,1,0:T(8,128)(2,1)S(1)}, bf16[32,128,128]{2,1,0:T(8,128)(2,1)}, u32[]{:S(2)}) copy-start(bf16[32,128,128]{2,1,0:T(8,128)(2,1)} %gather_fusion.1) | copy-start | bytes 3145732
  94.5 29.3 %collective-permute-start.3 = (f32[128,8,4,128]{3,0,2,1:T(8,128)}, f32[128,8,4,128]{3,0,2,1:T(8,128)}, u32[]{:S(2)}, u32[]{:S(2)}) collective-permute-start(f32[128,8,4,128]{3,0,2,1:T(8,128)} %dynamic-slice_bitcast_fusion), channel_id=1, source_target_pairs={{0,1},{1,0},{2,3},{3,2},{4,5},{5,4},{6,7},{7,6},{8,9},{9,8},{10,11... | collective-permute-start | bytes 6291464 | tf_op jit(solution)/shard_map/ppermute | solution.py:22
  96.2 25.7 %collective-permute-start.2 = (bf16[8,4,128,128]{2,3,1,0:T(8,128)(2,1)}, bf16[8,4,128,128]{2,3,1,0:T(8,128)(2,1)}, u32[]{:S(2)}, u32[]{:S(2)}) collective-permute-start(bf16[8,4,128,128]{2,3,1,0:T(8,128)(2,1)} %fusion.2), channel_id=1, source_target_pairs={{0,16},{16,0},{1,17},{17,1},{2,18},{18,2},{3,19},{19,3},{4,20},{20... | collective-permute-start | bytes 3145736 | tf_op jit(solution)/shard_map/ppermute | solution.py:58
  110.2 13.6 %copy-start.1 = (f32[128,64,128]{2,0,1:T(8,128)S(1)}, f32[128,64,128]{2,0,1:T(8,128)}, u32[]{:S(2)}) copy-start(f32[128,64,128]{2,0,1:T(8,128)} %scatter_fusion.1) | copy-start | bytes 12582916
  113.5 17.4 %collective-permute-start.1 = (f32[128,8,4,128]{3,0,2,1:T(8,128)}, f32[128,8,4,128]{3,0,2,1:T(8,128)}, u32[]{:S(2)}, u32[]{:S(2)}) collective-permute-start(f32[128,8,4,128]{3,0,2,1:T(8,128)} %dynamic-slice_bitcast_fusion.1), channel_id=1, source_target_pairs={{0,1},{1,0},{2,3},{3,2},{4,5},{5,4},{6,7},{7,6},{8,9},{9,8},{10,11... | collective-permute-start | bytes 6291464 | tf_op jit(solution)/shard_map/ppermute | solution.py:22
  126.7 30.0 %all-to-all-start.1 = ((bf16[8,128,4,128]{3,1,2,0:T(8,128)(2,1)}), bf16[8,128,4,128]{3,1,2,0:T(8,128)(2,1)}, u32[]{:S(2)}, u32[]{:S(2)}) async-start(bf16[8,128,4,128]{3,1,2,0:T(8,128)(2,1)} %fusion.7), calls=%async_computation.1 | async-start | bytes 2097152 | tf_op jit(solution)/shard_map/all_to_all | solution.py:73
  156.7 33.9 %all-to-all-start = ((bf16[8,128,4,128]{3,1,2,0:T(8,128)(2,1)}), bf16[8,128,4,128]{3,1,2,0:T(8,128)(2,1)}, u32[]{:S(2)}, u32[]{:S(2)}) async-start(bf16[8,128,4,128]{3,1,2,0:T(8,128)(2,1)} %fusion.6), calls=%async_computation | async-start | bytes 2097152 | tf_op jit(solution)/shard_map/all_to_all | solution.py:73
  161.5 24.2 %collective-permute-start.4 = (bf16[8,4,128,128]{3,2,1,0:T(8,128)(2,1)S(1)}, bf16[8,4,128,128]{3,2,1,0:T(8,128)(2,1)S(1)}, u32[]{:S(2)}, u32[]{:S(2)}) collective-permute-start(bf16[8,4,128,128]{3,2,1,0:T(8,128)(2,1)S(1)} %convolution_convert_fusion), channel_id=1, source_target_pairs={{0,16},{16,0},{1,17},{17,1},{2,18},{18,2},{3,19},{19,3},{4,20},{20... | collective-permute-start | bytes 3145736 | tf_op jit(solution)/shard_map/ppermute | solution.py:58
Sparse Core Ops, SparseCore 0:
  10.7 51.9 all-gather.1

commit v4 on v3

--- a/solution.py
+++ b/solution.py
@@ -59,25 +59,30 @@
             return (part.astype(jnp.float32) + got.astype(jnp.float32)).astype(jnp.bfloat16)
         return lax.psum(part, "dp")
 
-    empty = jnp.zeros((tok_rows, col_count, block_size), jnp.float32)
+    columns = jnp.arange(col_count, dtype=jnp.int32)
 
     def column_sums(terms, flat, tie=None):
-        local = empty.at[:, flat].add(terms.reshape(tok_rows, pair_count, block_size))
-        local = local.reshape(tok_rows, chips, pair, own_blocks, block_size)
-        keep = lax.dynamic_index_in_dim(local, core, axis=2, keepdims=False)
-        give = lax.dynamic_index_in_dim(local, 1 - core, axis=2, keepdims=False)
+        terms = terms.reshape(tok_rows, pair_count, block_size)
+        hi = terms.astype(jnp.bfloat16)
+        lo = (terms - hi.astype(jnp.float32)).astype(jnp.bfloat16)
+        onehot = (flat[:, None] == columns[None, :]).astype(jnp.bfloat16)
+        parts = jnp.concatenate([hi, lo], axis=1)
+        picks = jnp.concatenate([onehot, onehot], axis=0)
+        local = jnp.einsum("tpo,pc->cto", parts, picks, preferred_element_type=jnp.float32)
+        local = local.reshape(chips, pair, own_blocks, tok_rows, block_size)
+        keep = lax.dynamic_index_in_dim(local, core, axis=1, keepdims=False)
+        give = lax.dynamic_index_in_dim(local, 1 - core, axis=1, keepdims=False)
         chip_sum = (keep + swap_core(give)).astype(jnp.bfloat16)
-        chip_sum = chip_sum.transpose(1, 0, 2, 3)
         if tie is not None:
             tie, chip_sum = lax.optimization_barrier((tie, chip_sum))
         got = lax.all_to_all(chip_sum, "chip", split_axis=0, concat_axis=0, tiled=True)
         total = got.astype(jnp.float32).sum(axis=0)
-        return total.reshape(tok_rows, own_cols).astype(jnp.bfloat16), tie
+        return total.transpose(1, 0, 2).reshape(tok_rows, own_cols).astype(jnp.bfloat16), tie
 
     preact = jnp.einsum("rkti,rkio->tro", in_sel, w_in, preferred_element_type=jnp.float32)
     hidden = gelu_value(preact).astype(jnp.bfloat16)
     out_terms = jnp.einsum("tri,rkio->trko", hidden, w_out, preferred_element_type=jnp.float32)
-    outputs, _ = column_sums(out_terms, out_flat)
+    outputs, grad_sel = column_sums(out_terms, out_flat, grad_sel)
 
     w_out_part = jnp.einsum("tri,rkto->rkio", hidden, grad_sel, preferred_element_type=jnp.float32)
     w_out_grad = dp_total(w_out_part)

time: 200 us -> 181 us (0.905)
  other arithmetic: 30.7 us -> 18.7 us
  waiting for transfers between devices: 108 us -> 102 us
    all_to_all x2, waiting for transfers between devices: 22.2 us -> 0.01 us  [column_sums(): lax.all_to_all(chip_sum, 'chip', split_axis=0, concat_axis=0, tiled=True)]
    ppermute x2, waiting for transfers between devices: 31 us -> 46.5 us  [dp_total(): got = lax.ppermute(part, 'dp', perm=[(0, 1), (1, 0)])]
    scatter-add x2 -> x0, other arithmetic: 14.3 us -> none  [column_sums(): empty.at[:, flat].add(terms.reshape(tok_rows, pair_count, block_size))]
    convert_element_type x0 -> x4, other arithmetic: none -> 9.44 us  [the longest x2 7 us: column_sums(): chip_sum = (keep + swap_core(give)).astype(jnp.bfloat16)]
    dynamic_slice x0 -> x4, local copies, waits for them, and re-layouts: none -> 8.24 us  [the longest x2 4.78 us: column_sums(): keep = lax.dynamic_index_in_dim(local, core, axis=1, keepdims=False)]
    squeeze x2 -> x0, local copies, waits for them, and re-layouts: 6.53 us -> none  [column_sums(): give = lax.dynamic_index_in_dim(local, 1 - core, axis=2, keepdims=False)]
    transpose x2 -> x0, other arithmetic: 6.44 us -> none  [column_sums(): chip_sum = chip_sum.transpose(1, 0, 2, 3)]
    broadcast_in_dim x2 -> x0, local copies, waits for them, and re-layouts: 4.94 us -> none  [per_device(): empty = jnp.zeros((tok_rows, col_count, block_size), jnp.float32)]
  transfers between devices with their start and end apart: 8 -> 8, of which waited for: 5 -> 5; matrix products, arithmetic and copies ran while one was open for 16% -> 9% of each run, Pallas kernels for 0% -> 0%
where the time goes in v4:
time: 181 us
  waiting for transfers between devices  102 us (56%)
  local copies, waits for them, and re-layouts  25.8 us (14%)
  other arithmetic  18.7 us (10%)
  between operations  14.2 us (8%)
  starting transfers between devices  13.3 us (7%)
  matrix products  6.7 us (4%)
    all_gather x1, waiting for transfers between devices, per_device(): mine = lax.all_gather(both, 'chip', axis=0, tiled=False)  52.5 us
    ppermute x2, waiting for transfers between devices, dp_total(): got = lax.ppermute(part, 'dp', perm=[(0, 1), (1, 0)])  46.5 us
    all_to_all x2, starting transfers between devices, column_sums(): lax.all_to_all(chip_sum, 'chip', split_axis=0, concat_axis=0, tiled=True)  9.86 us
    unnamed x15, local copies, waits for them, and re-layouts  7.06 us
    convert_element_type x2, other arithmetic, column_sums(): chip_sum = (keep + swap_core(give)).astype(jnp.bfloat16)  7 us
    gather x2, local copies, waits for them, and re-layouts, select(): sel = sets[side, owner // pair, :, which, sub, :]  6.85 us
    dynamic_slice x2, local copies, waits for them, and re-layouts, column_sums(): keep = lax.dynamic_index_in_dim(local, core, axis=1, keepdims=False)  4.78 us
    another operation x1, other arithmetic, per_device(): sets = jnp.stack([mine, other], axis=0)  3.92 us
  transfers between devices with their start and end apart: 8, of which 5 were waited for; matrix products, arithmetic and copies ran while one was open for 9% of the time, Pallas kernels for 0%

profile of v4, /device:TPU:0, one launch (start us, length us, event | category | flops | bytes accessed | tf_op | source)
XLA Modules:
  0.0 180.5 jit_solution(14825004321587845204)
XLA Ops:
  7.2 1.1 copy.49
  8.3 1.0 copy.48
  9.4 0.9 copy.50
  10.3 52.5 %all-gather.2.cloned.1.call-done = bf16[8,128,2,4,128]{4,1,3,2,0:T(8,128)(2,1)} async-done(((bf16[1,128,2,4,128]{4,1,3,2,0:T(8,128)(2,1)}), bf16[8,128,2,4,128]{4,1,3,2,0:T(8,128)(2,1)}) %all-gather.2.cloned.1.call-update) | async-done | bytes 2097168 | tf_op jit(solution)/shard_map/all_gather | solution.py:39
  62.7 0.8 copy.51
  63.7 0.8 copy.53
  64.6 2.6 %collective-permute-done = bf16[8,128,2,4,128]{4,1,3,2,0:T(8,128)(2,1)S(1)} collective-permute-done((bf16[8,128,2,4,128]{4,1,3,2,0:T(8,128)(2,1)}, bf16[8,128,2,4,128]{4,1,3,2,0:T(8,128)(2,1)S(1)}, u32[]{:S(2)}, u32[]{:S(2)}) %collective-permute-start) | collective-permute-done | bytes 2097184 | tf_op jit(solution)/shard_map/ppermute | solution.py:22
  67.1 3.9 %pad_maximum_fusion = bf16[2,8,128,2,4,128]{5,2,4,3,1,0:T(8,128)(2,1)} fusion(bf16[1,8,128,2,4,128]{5,2,4,3,1,0:T(8,128)(2,1)S(1)} %bitcast.96, bf16[1,8,128,2,4,128]{5,2,4,3,1,0:T(8,128)(2,1)} %bitcast.95), kind=kLoop, calls=%fused_computation.2 | loop fusion | flops 2097152 | bytes 8388608 | tf_op jit(solution)/shard_map/stack | solution.py:41
  71.0 3.0 %gather_fusion.1 = bf16[32,128,128]{2,1,0:T(8,128)(2,1)S(1)} fusion(bf16[2,8,128,2,4,128]{5,2,4,3,1,0:T(8,128)(2,1)} %pad_maximum_fusion, s32[32]{0:T(128)S(1)} %get-tuple-element.32), kind=kCustom, calls=%fused_computation.1 | custom fusion | bytes 2097664 | tf_op jit(solution)/shard_map/gather | solution.py:47
  74.0 1.6 convolution_bitcast_fusion.1
  76.1 1.2 subtract_convert_fusion.1
  77.3 1.2 copy.89
  79.3 2.3 %constant_dynamic-slice_fusion.3 = (f32[8,1,4,128,128]{4,2,1,0,3:T(4,128)}, f32[8,1,4,128,128]{4,2,1,0,3:T(4,128)S(1)}) fusion(f32[8,2,4,128,128]{4,2,1,0,3:T(4,128)S(1)} %bitcast.90, s32[]{:T(128)S(6)} %select_n.180, s32[]{:T(128)S(6)} %select_n.181), kind=kLoop, calls=%fused_computation.81 | loop fusion | bytes 8388616 | tf_op jit(solution)/shard_map/jit(dynamic_index_in_dim)/dynamic_slice | solution.py:73
  81.6 1.7 copy.91
  83.6 3.9 %gather_fusion = bf16[32,128,128]{2,1,0:T(8,128)(2,1)} fusion(bf16[2,8,128,2,4,128]{5,2,4,3,1,0:T(8,128)(2,1)} %pad_maximum_fusion, s32[32]{0:T(128)S(1)} %get-tuple-element.33), kind=kCustom, calls=%fused_computation | custom fusion | bytes 2097664 | tf_op jit(solution)/shard_map/gather | solution.py:47
  87.8 3.8 %fusion.9 = bf16[8,4,128,128]{3,1,2,0:T(4,128)(2,1)} fusion(f32[8,4,128,128]{3,1,2,0:T(4,128)} %collective-permute-done.1, f32[8,1,4,128,128]{4,2,1,0,3:T(4,128)} %get-tuple-element.30), kind=kLoop, calls=%fused_computation.14 | loop fusion | flops 1048576 | bytes 5242880 | tf_op jit(solution)/shard_map/convert_element_type | solution.py:75
  93.3 1.2 subtract_convert_fusion
  94.6 1.2 copy.88
  96.5 2.5 %constant_dynamic-slice_fusion.1 = (f32[8,1,4,128,128]{4,2,1,0,3:T(4,128)}, f32[8,1,4,128,128]{4,2,1,0,3:T(4,128)S(1)}) fusion(f32[8,2,4,128,128]{4,2,1,0,3:T(4,128)S(1)} %bitcast.89, s32[]{:T(128)S(6)} %select_n.180, s32[]{:T(128)S(6)} %select_n.181), kind=kLoop, calls=%fused_computation.79 | loop fusion | bytes 8388616 | tf_op jit(solution)/shard_map/jit(dynamic_index_in_dim)/dynamic_slice | solution.py:73
  99.0 1.7 copy.90
  100.9 4.2 %all-to-all-start = ((bf16[8,4,128,128]{3,1,2,0:T(4,128)(2,1)}), bf16[8,4,128,128]{3,1,2,0:T(4,128)(2,1)}, u32[]{:S(2)}, u32[]{:S(2)}) async-start(bf16[8,4,128,128]{3,1,2,0:T(4,128)(2,1)} %fusion.9), calls=%async_computation | async-start | bytes 2097152 | tf_op jit(solution)/shard_map/all_to_all | solution.py:78
  105.1 1.7 fusion.10
  106.9 1.5 collective-permute-start.2
  108.4 23.9 %collective-permute-done.2 = bf16[8,4,128,128]{2,3,1,0:T(8,128)(2,1)S(1)} collective-permute-done((bf16[8,4,128,128]{2,3,1,0:T(8,128)(2,1)S(1)}, bf16[8,4,128,128]{2,3,1,0:T(8,128)(2,1)S(1)}, u32[]{:S(2)}, u32[]{:S(2)}) %collective-permute-start.2) | collective-permute-done | bytes 1048608 | tf_op jit(solution)/shard_map/ppermute | solution.py:58
  132.8 3.2 %fusion.8 = bf16[8,4,128,128]{3,1,2,0:T(4,128)(2,1)} fusion(f32[8,4,128,128]{3,1,2,0:T(4,128)} %collective-permute-done.3, f32[8,1,4,128,128]{4,2,1,0,3:T(4,128)S(1)} %copy-done.1), kind=kLoop, calls=%fused_computation.12 | loop fusion | flops 1048576 | bytes 5242880 | tf_op jit(solution)/shard_map/convert_element_type | solution.py:75
  136.0 5.6 %all-to-all-start.1 = ((bf16[8,4,128,128]{3,1,2,0:T(4,128)(2,1)}), bf16[8,4,128,128]{3,1,2,0:T(4,128)(2,1)}, u32[]{:S(2)}, u32[]{:S(2)}) async-start(bf16[8,4,128,128]{3,1,2,0:T(4,128)(2,1)} %fusion.8), calls=%async_computation.1 | async-start | bytes 2097152 | tf_op jit(solution)/shard_map/all_to_all | solution.py:78
  142.1 1.5 collective-permute-start.4
  143.7 22.5 %collective-permute-done.4 = bf16[8,4,128,128]{3,2,1,0:T(8,128)(2,1)S(1)} collective-permute-done((bf16[8,4,128,128]{3,2,1,0:T(8,128)(2,1)S(1)}, bf16[8,4,128,128]{3,2,1,0:T(8,128)(2,1)S(1)}, u32[]{:S(2)}, u32[]{:S(2)}) %collective-permute-start.4) | collective-permute-done | bytes 1048608 | tf_op jit(solution)/shard_map/ppermute | solution.py:58
  166.2 1.3 add_convert_fusion
  167.5 1.7 reduce_sum.24
  169.9 1.3 copy.65
  171.3 1.7 reduce_sum.25
  (34 shorter events, 7.0 us)
Async XLA Ops:
  7.2 68.5 %copy-start = (bf16[8,4,128,128]{3,2,1,0:T(8,128)(2,1)S(1)}, bf16[8,4,128,128]{3,2,1,0:T(8,128)(2,1)}, u32[]{:S(2)}) copy-start(bf16[8,4,128,128]{3,2,1,0:T(8,128)(2,1)} %param.10) | copy-start | bytes 3145732
  7.2 55.6 %all-gather.2.cloned.1.call-start = ((), (), s32[]{:S(2)}) async-start(), calls=%async_computation.2 | async-start | bytes 2359296 | tf_op jit(solution)/shard_map/all_gather | solution.py:39
  62.7 4.4 %collective-permute-start = (bf16[8,128,2,4,128]{4,1,3,2,0:T(8,128)(2,1)}, bf16[8,128,2,4,128]{4,1,3,2,0:T(8,128)(2,1)S(1)}, u32[]{:S(2)}, u32[]{:S(2)}) collective-permute-start(bf16[8,128,2,4,128]{4,1,3,2,0:T(8,128)(2,1)} %all-gather.2.cloned.1.call-done), channel_id=1, source_target_pairs={{0,1},{1,0},{2,3},{3,2},{4,5},{5,4},{6,7},{7,6},{8,9},{9,8},{10,11... | collective-permute-start | bytes 6291464 | tf_op jit(solution)/shard_map/ppermute | solution.py:22
  83.3 4.5 %collective-permute-start.1 = (f32[8,4,128,128]{3,1,2,0:T(4,128)}, f32[8,4,128,128]{3,1,2,0:T(4,128)}, u32[]{:S(2)}, u32[]{:S(2)}) collective-permute-start(f32[8,4,128,128]{3,1,2,0:T(4,128)} %bitcast.82), channel_id=1, source_target_pairs={{0,1},{1,0},{2,3},{3,2},{4,5},{5,4},{6,7},{7,6},{8,9},{9,8},{10,11... | collective-permute-start | bytes 6291464 | tf_op jit(solution)/shard_map/ppermute | solution.py:22
  87.8 3.8 %copy-start.3 = (bf16[32,128,128]{2,1,0:T(8,128)(2,1)S(1)}, bf16[32,128,128]{2,1,0:T(8,128)(2,1)}, u32[]{:S(2)}) copy-start(bf16[32,128,128]{2,1,0:T(8,128)(2,1)} %gather_fusion) | copy-start | bytes 3145732
  91.7 1.2 copy-start.2
  100.7 32.1 %collective-permute-start.3 = (f32[8,4,128,128]{3,1,2,0:T(4,128)}, f32[8,4,128,128]{3,1,2,0:T(4,128)}, u32[]{:S(2)}, u32[]{:S(2)}) collective-permute-start(f32[8,4,128,128]{3,1,2,0:T(4,128)} %bitcast.81), channel_id=1, source_target_pairs={{0,1},{1,0},{2,3},{3,2},{4,5},{5,4},{6,7},{7,6},{8,9},{9,8},{10,11... | collective-permute-start | bytes 6291464 | tf_op jit(solution)/shard_map/ppermute | solution.py:22
  100.9 35.1 %all-to-all-start = ((bf16[8,4,128,128]{3,1,2,0:T(4,128)(2,1)}), bf16[8,4,128,128]{3,1,2,0:T(4,128)(2,1)}, u32[]{:S(2)}, u32[]{:S(2)}) async-start(bf16[8,4,128,128]{3,1,2,0:T(4,128)(2,1)} %fusion.9), calls=%async_computation | async-start | bytes 2097152 | tf_op jit(solution)/shard_map/all_to_all | solution.py:78
  106.9 25.9 %copy-start.1 = (f32[8,1,4,128,128]{4,2,1,0,3:T(4,128)S(1)}, f32[8,1,4,128,128]{4,2,1,0,3:T(4,128)}, u32[]{:S(2)}) copy-start(f32[8,1,4,128,128]{4,2,1,0,3:T(4,128)} %get-tuple-element.28) | copy-start | bytes 6291460
  106.9 25.5 %collective-permute-start.2 = (bf16[8,4,128,128]{2,3,1,0:T(8,128)(2,1)S(1)}, bf16[8,4,128,128]{2,3,1,0:T(8,128)(2,1)S(1)}, u32[]{:S(2)}, u32[]{:S(2)}) collective-permute-start(bf16[8,4,128,128]{2,3,1,0:T(8,128)(2,1)S(1)} %fusion.10), channel_id=1, source_target_pairs={{0,16},{16,0},{1,17},{17,1},{2,18},{18,2},{3,19},{19,3},{4,20},{20... | collective-permute-start | bytes 3145736 | tf_op jit(solution)/shard_map/ppermute | solution.py:58
  136.0 35.3 %all-to-all-start.1 = ((bf16[8,4,128,128]{3,1,2,0:T(4,128)(2,1)}), bf16[8,4,128,128]{3,1,2,0:T(4,128)(2,1)}, u32[]{:S(2)}, u32[]{:S(2)}) async-start(bf16[8,4,128,128]{3,1,2,0:T(4,128)(2,1)} %fusion.8), calls=%async_computation.1 | async-start | bytes 2097152 | tf_op jit(solution)/shard_map/all_to_all | solution.py:78
  142.1 24.1 %collective-permute-start.4 = (bf16[8,4,128,128]{3,2,1,0:T(8,128)(2,1)S(1)}, bf16[8,4,128,128]{3,2,1,0:T(8,128)(2,1)S(1)}, u32[]{:S(2)}, u32[]{:S(2)}) collective-permute-start(bf16[8,4,128,128]{3,2,1,0:T(8,128)(2,1)S(1)} %convolution_convert_fusion), channel_id=1, source_target_pairs={{0,16},{16,0},{1,17},{17,1},{2,18},{18,2},{3,19},{19,3},{4,20},{20... | collective-permute-start | bytes 3145736 | tf_op jit(solution)/shard_map/ppermute | solution.py:58
Sparse Core Ops, SparseCore 0:
  10.7 51.9 all-gather.1

commit v5 on v4

--- a/solution.py
+++ b/solution.py
@@ -35,22 +35,22 @@
     col_count = chips * pair * own_blocks
     core = lax.axis_index("core")
 
-    both = jnp.concatenate([inputs, out_grad], axis=1).reshape(tok_rows, 2, own_blocks, block_size)
-    mine = lax.all_gather(both, "chip", axis=0, tiled=False)
-    other = swap_core(mine)
-    sets = jnp.stack([mine, other], axis=0)
+    def gather(x):
+        x = x.reshape(tok_rows, own_blocks, block_size)
+        mine = lax.all_gather(x, "chip", axis=0, tiled=False)
+        return jnp.stack([mine, swap_core(mine)], axis=0)
 
-    def select(flat, which):
+    def select(sets, flat):
         owner = flat // own_blocks
         sub = flat % own_blocks
         side = (owner % pair != core).astype(jnp.int32)
-        sel = sets[side, owner // pair, :, which, sub, :]
+        sel = sets[side, owner // pair, :, sub, :]
         return sel.reshape(hid_rows, per_row, tok_rows, block_size)
 
     in_flat = in_blocks.reshape(pair_count)
     out_flat = out_blocks.reshape(pair_count)
-    in_sel = select(in_flat, 0)
-    grad_sel = select(out_flat, 1)
+    in_sel = select(gather(inputs), in_flat)
+    grad_sel = select(gather(out_grad), out_flat)
 
     def dp_total(part):
         part = part.astype(jnp.bfloat16)

time: 181 us -> 198 us (1.094)
  waiting for transfers between devices: 102 us -> 117 us
    all_gather x1 -> x2, waiting for transfers between devices: 52.5 us -> 67.5 us  [gather(): mine = lax.all_gather(x, 'chip', axis=0, tiled=False)]
    another operation x1 -> x2, other arithmetic: 3.92 us -> 5.84 us  [gather(): return jnp.stack([mine, swap_core(mine)], axis=0)]
  transfers between devices with their start and end apart: 8 -> 10, of which waited for: 5 -> 5; matrix products, arithmetic and copies ran while one was open for 9% -> 18% of each run, Pallas kernels for 0% -> 0%
where the time goes in v5:
time: 198 us; the launch traced here: 197 us
  waiting for transfers between devices  117 us (59%)
  local copies, waits for them, and re-layouts  25.2 us (13%)
  other arithmetic  20.6 us (10%)
  between operations  14.2 us (7%)
  starting transfers between devices  13.7 us (7%)
  matrix products  6.73 us (3%)
    all_gather x2, waiting for transfers between devices, gather(): mine = lax.all_gather(x, 'chip', axis=0, tiled=False)  67.5 us
    ppermute x2, waiting for transfers between devices, dp_total(): got = lax.ppermute(part, 'dp', perm=[(0, 1), (1, 0)])  46.5 us
    all_to_all x2, starting transfers between devices, column_sums(): lax.all_to_all(chip_sum, 'chip', split_axis=0, concat_axis=0, tiled=True)  9.87 us
    unnamed x15, local copies, waits for them, and re-layouts  7.05 us
    convert_element_type x2, other arithmetic, column_sums(): chip_sum = (keep + swap_core(give)).astype(jnp.bfloat16)  7 us
    another operation x2, other arithmetic, gather(): return jnp.stack([mine, swap_core(mine)], axis=0)  5.84 us
    gather x2, local copies, waits for them, and re-layouts, select(): sel = sets[side, owner // pair, :, sub, :]  5.61 us
    dynamic_slice x2, local copies, waits for them, and re-layouts, column_sums(): keep = lax.dynamic_index_in_dim(local, core, axis=1, keepdims=False)  4.78 us
  transfers between devices with their start and end apart: 10, of which 5 were waited for; matrix products, arithmetic and copies ran while one was open for 18% of the time, Pallas kernels for 0%

profile of v5, /device:TPU:0, one launch (start us, length us, event | category | flops | bytes accessed | tf_op | source)
XLA Modules:
  0.0 197.3 jit_solution(3778098690736148061)
XLA Ops:
  7.2 1.1 copy.53
  9.2 44.4 %all-gather.5.cloned.1.call-done = bf16[8,128,4,128]{3,1,2,0:T(8,128)(2,1)} async-done(((bf16[1,128,4,128]{3,1,2,0:T(8,128)(2,1)}), bf16[8,128,4,128]{3,1,2,0:T(8,128)(2,1)}) %all-gather.5.cloned.1.call-update) | async-done | bytes 1048592 | tf_op jit(solution)/shard_map/all_gather | solution.py:40
  53.6 1.0 copy.49
  54.6 0.8 copy.50
  57.2 2.7 %pad_maximum_fusion.1 = bf16[2,8,128,4,128]{4,2,3,1,0:T(8,128)(2,1)} fusion(bf16[1,8,128,4,128]{4,2,3,1,0:T(8,128)(2,1)S(1)} %bitcast.100, bf16[1,8,128,4,128]{4,2,3,1,0:T(8,128)(2,1)} %bitcast.99), kind=kLoop, calls=%fused_computation.3 | loop fusion | flops 1048576 | bytes 4194304 | tf_op jit(solution)/shard_map/stack | solution.py:41
  59.9 2.4 %gather_fusion.1 = bf16[32,128,128]{2,1,0:T(8,128)(2,1)S(1)} fusion(bf16[2,8,128,4,128]{4,2,3,1,0:T(8,128)(2,1)} %pad_maximum_fusion.1, s32[32]{0:T(128)S(1)} %fusion.39), kind=kCustom, calls=%fused_computation.1 | custom fusion | bytes 2097536 | tf_op jit(solution)/shard_map/gather | solution.py:47
  62.3 1.7 convolution_bitcast_fusion.1
  64.4 1.2 copy.91
  65.6 1.2 subtract_convert_fusion.1
  67.6 2.3 %constant_dynamic-slice_fusion.3 = (f32[8,1,4,128,128]{4,2,1,0,3:T(4,128)}, f32[8,1,4,128,128]{4,2,1,0,3:T(4,128)S(1)}) fusion(f32[8,2,4,128,128]{4,2,1,0,3:T(4,128)S(1)} %bitcast.93, s32[]{:T(128)S(6)} %select_n.180, s32[]{:T(128)S(6)} %select_n.181), kind=kLoop, calls=%fused_computation.81 | loop fusion | bytes 8388616 | tf_op jit(solution)/shard_map/jit(dynamic_index_in_dim)/dynamic_slice | solution.py:73
  69.9 1.7 copy.93
  72.1 23.1 %all-gather.3.cloned.1.call-done = bf16[8,128,4,128]{3,1,2,0:T(8,128)(2,1)} async-done(((bf16[1,128,4,128]{3,1,2,0:T(8,128)(2,1)}), bf16[8,128,4,128]{3,1,2,0:T(8,128)(2,1)}) %all-gather.3.cloned.1.call-update) | async-done | bytes 1048592 | tf_op jit(solution)/shard_map/all_gather | solution.py:40
  95.4 2.8 %collective-permute-done = bf16[8,128,4,128]{3,1,2,0:T(8,128)(2,1)} collective-permute-done((bf16[8,128,4,128]{3,1,2,0:T(8,128)(2,1)}, bf16[8,128,4,128]{3,1,2,0:T(8,128)(2,1)}, u32[]{:S(2)}, u32[]{:S(2)}) %collective-permute-start) | collective-permute-done | bytes 1048608 | tf_op jit(solution)/shard_map/ppermute | solution.py:22
  98.2 3.1 %pad_maximum_fusion = bf16[2,8,128,4,128]{4,2,3,1,0:T(8,128)(2,1)} fusion(bf16[1,8,128,4,128]{4,2,3,1,0:T(8,128)(2,1)} %bitcast.2, bf16[1,8,128,4,128]{4,2,3,1,0:T(8,128)(2,1)} %bitcast.98), kind=kLoop, calls=%fused_computation.2 | loop fusion | flops 1048576 | bytes 4194304 | tf_op jit(solution)/shard_map/stack | solution.py:41
  101.3 3.3 %gather_fusion = bf16[32,128,128]{2,1,0:T(8,128)(2,1)} fusion(bf16[2,8,128,4,128]{4,2,3,1,0:T(8,128)(2,1)} %pad_maximum_fusion, s32[32]{0:T(128)S(1)} %fusion.40), kind=kCustom, calls=%fused_computation | custom fusion | bytes 2097536 | tf_op jit(solution)/shard_map/gather | solution.py:47
  104.6 3.8 %fusion.9 = bf16[8,4,128,128]{3,1,2,0:T(4,128)(2,1)} fusion(f32[8,4,128,128]{3,1,2,0:T(4,128)} %collective-permute-done.2, f32[8,1,4,128,128]{4,2,1,0,3:T(4,128)} %get-tuple-element.30), kind=kLoop, calls=%fused_computation.15 | loop fusion | flops 1048576 | bytes 5242880 | tf_op jit(solution)/shard_map/convert_element_type | solution.py:75
  110.1 1.2 subtract_convert_fusion
  111.3 1.2 copy.90
  113.3 2.5 %constant_dynamic-slice_fusion.1 = (f32[8,1,4,128,128]{4,2,1,0,3:T(4,128)}, f32[8,1,4,128,128]{4,2,1,0,3:T(4,128)S(1)}) fusion(f32[8,2,4,128,128]{4,2,1,0,3:T(4,128)S(1)} %bitcast.92, s32[]{:T(128)S(6)} %select_n.180, s32[]{:T(128)S(6)} %select_n.181), kind=kLoop, calls=%fused_computation.79 | loop fusion | bytes 8388616 | tf_op jit(solution)/shard_map/jit(dynamic_index_in_dim)/dynamic_slice | solution.py:73
  115.8 1.7 copy.92
  117.6 4.2 %all-to-all-start = ((bf16[8,4,128,128]{3,1,2,0:T(4,128)(2,1)}), bf16[8,4,128,128]{3,1,2,0:T(4,128)(2,1)}, u32[]{:S(2)}, u32[]{:S(2)}) async-start(bf16[8,4,128,128]{3,1,2,0:T(4,128)(2,1)} %fusion.9), calls=%async_computation | async-start | bytes 2097152 | tf_op jit(solution)/shard_map/all_to_all | solution.py:78
  121.9 1.7 fusion.10
  123.6 1.6 collective-permute-start.3
  125.2 24.0 %collective-permute-done.3 = bf16[8,4,128,128]{2,3,1,0:T(8,128)(2,1)S(1)} collective-permute-done((bf16[8,4,128,128]{2,3,1,0:T(8,128)(2,1)S(1)}, bf16[8,4,128,128]{2,3,1,0:T(8,128)(2,1)S(1)}, u32[]{:S(2)}, u32[]{:S(2)}) %collective-permute-start.3) | collective-permute-done | bytes 1048608 | tf_op jit(solution)/shard_map/ppermute | solution.py:58
  149.6 3.2 %fusion.8 = bf16[8,4,128,128]{3,1,2,0:T(4,128)(2,1)} fusion(f32[8,4,128,128]{3,1,2,0:T(4,128)} %collective-permute-done.4, f32[8,1,4,128,128]{4,2,1,0,3:T(4,128)S(1)} %copy-done.1), kind=kLoop, calls=%fused_computation.13 | loop fusion | flops 1048576 | bytes 5242880 | tf_op jit(solution)/shard_map/convert_element_type | solution.py:75
  152.8 5.6 %all-to-all-start.1 = ((bf16[8,4,128,128]{3,1,2,0:T(4,128)(2,1)}), bf16[8,4,128,128]{3,1,2,0:T(4,128)(2,1)}, u32[]{:S(2)}, u32[]{:S(2)}) async-start(bf16[8,4,128,128]{3,1,2,0:T(4,128)(2,1)} %fusion.8), calls=%async_computation.1 | async-start | bytes 2097152 | tf_op jit(solution)/shard_map/all_to_all | solution.py:78
  158.9 1.5 collective-permute-start.5
  160.4 22.6 %collective-permute-done.5 = bf16[8,4,128,128]{3,2,1,0:T(8,128)(2,1)S(1)} collective-permute-done((bf16[8,4,128,128]{3,2,1,0:T(8,128)(2,1)S(1)}, bf16[8,4,128,128]{3,2,1,0:T(8,128)(2,1)S(1)}, u32[]{:S(2)}, u32[]{:S(2)}) %collective-permute-start.5) | collective-permute-done | bytes 1048608 | tf_op jit(solution)/shard_map/ppermute | solution.py:58
  183.0 1.3 add_convert_fusion
  184.3 1.7 reduce_sum.24
  186.8 1.3 copy.67
  188.1 1.7 reduce_sum.25
  (41 shorter events, 9.3 us)
Async XLA Ops:
  7.2 56.8 %copy-start = (bf16[8,4,128,128]{3,2,1,0:T(8,128)(2,1)S(1)}, bf16[8,4,128,128]{3,2,1,0:T(8,128)(2,1)}, u32[]{:S(2)}) copy-start(bf16[8,4,128,128]{3,2,1,0:T(8,128)(2,1)} %param.10) | copy-start | bytes 3145732
  7.2 46.4 %all-gather.5.cloned.1.call-start = ((), (), s32[]{:S(2)}) async-start(), calls=%async_computation.3 | async-start | bytes 1179648 | tf_op jit(solution)/shard_map/all_gather | solution.py:40
  9.1 86.1 %all-gather.3.cloned.1.call-start = ((), (), s32[]{:S(2)}) async-start(), calls=%async_computation.2 | async-start | bytes 1179648 | tf_op jit(solution)/shard_map/all_gather | solution.py:40
  53.6 3.6 %collective-permute-start.1 = (bf16[8,128,4,128]{3,1,2,0:T(8,128)(2,1)}, bf16[8,128,4,128]{3,1,2,0:T(8,128)(2,1)S(1)}, u32[]{:S(2)}, u32[]{:S(2)}) collective-permute-start(bf16[8,128,4,128]{3,1,2,0:T(8,128)(2,1)} %all-gather.5.cloned.1.call-done), channel_id=1, source_target_pairs={{0,1},{1,0},{2,3},{3,2},{4,5},{5,4},{6,7},{7,6},{8,9},{9,8},{10,11... | collective-permute-start | bytes 3145736 | tf_op jit(solution)/shard_map/ppermute | solution.py:22
  71.6 33.0 %collective-permute-start.2 = (f32[8,4,128,128]{3,1,2,0:T(4,128)}, f32[8,4,128,128]{3,1,2,0:T(4,128)}, u32[]{:S(2)}, u32[]{:S(2)}) collective-permute-start(f32[8,4,128,128]{3,1,2,0:T(4,128)} %bitcast.85), channel_id=1, source_target_pairs={{0,1},{1,0},{2,3},{3,2},{4,5},{5,4},{6,7},{7,6},{8,9},{9,8},{10,11... | collective-permute-start | bytes 6291464 | tf_op jit(solution)/shard_map/ppermute | solution.py:22
  95.2 3.0 %collective-permute-start = (bf16[8,128,4,128]{3,1,2,0:T(8,128)(2,1)}, bf16[8,128,4,128]{3,1,2,0:T(8,128)(2,1)}, u32[]{:S(2)}, u32[]{:S(2)}) collective-permute-start(bf16[8,128,4,128]{3,1,2,0:T(8,128)(2,1)} %all-gather.3.cloned.1.call-done), channel_id=1, source_target_pairs={{0,1},{1,0},{2,3},{3,2},{4,5},{5,4},{6,7},{7,6},{8,9},{9,8},{10,11... | collective-permute-start | bytes 3145736 | tf_op jit(solution)/shard_map/ppermute | solution.py:22
  104.6 3.8 %copy-start.3 = (bf16[32,128,128]{2,1,0:T(8,128)(2,1)S(1)}, bf16[32,128,128]{2,1,0:T(8,128)(2,1)}, u32[]{:S(2)}) copy-start(bf16[32,128,128]{2,1,0:T(8,128)(2,1)} %gather_fusion) | copy-start | bytes 3145732
  108.4 1.2 copy-start.2
  117.5 32.1 %collective-permute-start.4 = (f32[8,4,128,128]{3,1,2,0:T(4,128)}, f32[8,4,128,128]{3,1,2,0:T(4,128)}, u32[]{:S(2)}, u32[]{:S(2)}) collective-permute-start(f32[8,4,128,128]{3,1,2,0:T(4,128)} %bitcast.84), channel_id=1, source_target_pairs={{0,1},{1,0},{2,3},{3,2},{4,5},{5,4},{6,7},{7,6},{8,9},{9,8},{10,11... | collective-permute-start | bytes 6291464 | tf_op jit(solution)/shard_map/ppermute | solution.py:22
  117.6 35.1 %all-to-all-start = ((bf16[8,4,128,128]{3,1,2,0:T(4,128)(2,1)}), bf16[8,4,128,128]{3,1,2,0:T(4,128)(2,1)}, u32[]{:S(2)}, u32[]{:S(2)}) async-start(bf16[8,4,128,128]{3,1,2,0:T(4,128)(2,1)} %fusion.9), calls=%async_computation | async-start | bytes 2097152 | tf_op jit(solution)/shard_map/all_to_all | solution.py:78
  123.6 26.0 %copy-start.1 = (f32[8,1,4,128,128]{4,2,1,0,3:T(4,128)S(1)}, f32[8,1,4,128,128]{4,2,1,0,3:T(4,128)}, u32[]{:S(2)}) copy-start(f32[8,1,4,128,128]{4,2,1,0,3:T(4,128)} %get-tuple-element.28) | copy-start | bytes 6291460
  123.6 25.5 %collective-permute-start.3 = (bf16[8,4,128,128]{2,3,1,0:T(8,128)(2,1)S(1)}, bf16[8,4,128,128]{2,3,1,0:T(8,128)(2,1)S(1)}, u32[]{:S(2)}, u32[]{:S(2)}) collective-permute-start(bf16[8,4,128,128]{2,3,1,0:T(8,128)(2,1)S(1)} %fusion.10), channel_id=1, source_target_pairs={{0,16},{16,0},{1,17},{17,1},{2,18},{18,2},{3,19},{19,3},{4,20},{20... | collective-permute-start | bytes 3145736 | tf_op jit(solution)/shard_map/ppermute | solution.py:58
  152.8 35.3 %all-to-all-start.1 = ((bf16[8,4,128,128]{3,1,2,0:T(4,128)(2,1)}), bf16[8,4,128,128]{3,1,2,0:T(4,128)(2,1)}, u32[]{:S(2)}, u32[]{:S(2)}) async-start(bf16[8,4,128,128]{3,1,2,0:T(4,128)(2,1)} %fusion.8), calls=%async_computation.1 | async-start | bytes 2097152 | tf_op jit(solution)/shard_map/all_to_all | solution.py:78
  158.9 24.1 %collective-permute-start.5 = (bf16[8,4,128,128]{3,2,1,0:T(8,128)(2,1)S(1)}, bf16[8,4,128,128]{3,2,1,0:T(8,128)(2,1)S(1)}, u32[]{:S(2)}, u32[]{:S(2)}) collective-permute-start(bf16[8,4,128,128]{3,2,1,0:T(8,128)(2,1)S(1)} %convolution_convert_fusion), channel_id=1, source_target_pairs={{0,16},{16,0},{1,17},{17,1},{2,18},{18,2},{3,19},{19,3},{4,20},{20... | collective-permute-start | bytes 3145736 | tf_op jit(solution)/shard_map/ppermute | solution.py:58
Sparse Core Ops, SparseCore 0:
  10.7 42.8 all-gather.4
  56.3 38.8 all-gather.2

commit v6 on v4

--- a/solution.py
+++ b/solution.py
@@ -61,7 +61,7 @@
 
     columns = jnp.arange(col_count, dtype=jnp.int32)
 
-    def column_sums(terms, flat, tie=None):
+    def chip_sums(terms, flat):
         terms = terms.reshape(tok_rows, pair_count, block_size)
         hi = terms.astype(jnp.bfloat16)
         lo = (terms - hi.astype(jnp.float32)).astype(jnp.bfloat16)
@@ -72,17 +72,16 @@
         local = local.reshape(chips, pair, own_blocks, tok_rows, block_size)
         keep = lax.dynamic_index_in_dim(local, core, axis=1, keepdims=False)
         give = lax.dynamic_index_in_dim(local, 1 - core, axis=1, keepdims=False)
-        chip_sum = (keep + swap_core(give)).astype(jnp.bfloat16)
-        if tie is not None:
-            tie, chip_sum = lax.optimization_barrier((tie, chip_sum))
-        got = lax.all_to_all(chip_sum, "chip", split_axis=0, concat_axis=0, tiled=True)
+        return (keep + swap_core(give)).astype(jnp.bfloat16)
+
+    def finish(got):
         total = got.astype(jnp.float32).sum(axis=0)
-        return total.transpose(1, 0, 2).reshape(tok_rows, own_cols).astype(jnp.bfloat16), tie
+        return total.transpose(1, 0, 2).reshape(tok_rows, own_cols).astype(jnp.bfloat16)
 
     preact = jnp.einsum("rkti,rkio->tro", in_sel, w_in, preferred_element_type=jnp.float32)
     hidden = gelu_value(preact).astype(jnp.bfloat16)
     out_terms = jnp.einsum("tri,rkio->trko", hidden, w_out, preferred_element_type=jnp.float32)
-    outputs, grad_sel = column_sums(out_terms, out_flat, grad_sel)
+    out_send = chip_sums(out_terms, out_flat)
 
     w_out_part = jnp.einsum("tri,rkto->rkio", hidden, grad_sel, preferred_element_type=jnp.float32)
     w_out_grad = dp_total(w_out_part)
@@ -90,7 +89,10 @@
     hid_grad = jnp.einsum("rkto,rkio->tri", grad_sel, w_out, preferred_element_type=jnp.float32)
     pre_grad = (hid_grad * gelu_slope(preact)).astype(jnp.bfloat16)
     in_terms = jnp.einsum("tro,rkio->trki", pre_grad, w_in, preferred_element_type=jnp.float32)
-    in_grad, w_out_grad = column_sums(in_terms, in_flat, w_out_grad)
+    in_send = chip_sums(in_terms, in_flat)
+    got = lax.all_to_all(jnp.stack([out_send, in_send], axis=1), "chip", split_axis=0, concat_axis=0, tiled=True)
+    outputs = finish(got[:, 0])
+    in_grad = finish(got[:, 1])
     w_in_part = jnp.einsum("rkti,tro->rkio", in_sel, pre_grad, preferred_element_type=jnp.float32)
     w_in_grad = dp_total(w_in_part)
     return (outputs, in_grad, w_in_grad, w_out_grad)

time: 181 us -> 166 us (0.917)
  starting transfers between devices: 13.3 us -> 7.19 us
  local copies, waits for them, and re-layouts: 25.8 us -> 20.8 us
  other arithmetic: 18.7 us -> 15.9 us
    convert_element_type x4 -> x2, other arithmetic: 9.44 us -> 2.44 us  [chip_sums(): lo = (terms - hi.astype(jnp.float32)).astype(jnp.bfloat16)]
    all_to_all x2 -> x1, starting transfers between devices: 9.86 us -> 4.35 us  [per_device(): lax.all_to_all(jnp.stack([out_send, in_send], axis=1), 'chip', split_axis...]
    dynamic_slice x4, local copies, waits for them, and re-layouts: 8.24 us -> 2.98 us  [the longest x2 2.05 us: chip_sums(): keep = lax.dynamic_index_in_dim(local, core, axis=1, keepdims=False)]
    another operation x0 -> x3, other arithmetic: none -> 3.93 us  [per_device(): jnp.stack([out_send, in_send], axis=1)]
    ppermute x3, waiting for transfers between devices: 2.94 us -> 6.13 us  [swap_core(): return lax.ppermute(x, 'core', perm=[(0, 1), (1, 0)])]
    ppermute x2, waiting for transfers between devices: 46.5 us -> 43.4 us  [dp_total(): got = lax.ppermute(part, 'dp', perm=[(0, 1), (1, 0)])]
    unnamed x15 -> x13, local copies, waits for them, and re-layouts: 7.06 us -> 7.41 us
  transfers between devices with their start and end apart: 8 -> 7, of which waited for: 5 -> 6; matrix products, arithmetic and copies ran while one was open for 9% -> 7% of each run, Pallas kernels for 0% -> 0%
where the time goes in v6:
time: 166 us
  waiting for transfers between devices  102 us (61%)
  local copies, waits for them, and re-layouts  20.8 us (13%)
  other arithmetic  15.9 us (10%)
  between operations  14.2 us (9%)
  starting transfers between devices  7.19 us (4%)
  matrix products  5.48 us (3%)
    all_gather x1, waiting for transfers between devices, per_device(): mine = lax.all_gather(both, 'chip', axis=0, tiled=False)  52.5 us
    ppermute x2, waiting for transfers between devices, dp_total(): got = lax.ppermute(part, 'dp', perm=[(0, 1), (1, 0)])  43.4 us
    unnamed x13, local copies, waits for them, and re-layouts  7.41 us
    gather x2, local copies, waits for them, and re-layouts, select(): sel = sets[side, owner // pair, :, which, sub, :]  6.84 us
    ppermute x3, waiting for transfers between devices, swap_core(): return lax.ppermute(x, 'core', perm=[(0, 1), (1, 0)])  6.13 us
    all_to_all x1, starting transfers between devices, per_device(): lax.all_to_all(jnp.stack([out_send, in_send], axis=1), 'chip', split_axis...  4.35 us
    another operation x3, other arithmetic, per_device(): jnp.stack([out_send, in_send], axis=1)  3.93 us
    another operation x1, other arithmetic, per_device(): sets = jnp.stack([mine, other], axis=0)  3.93 us
  transfers between devices with their start and end apart: 7, of which 6 were waited for; matrix products, arithmetic and copies ran while one was open for 7% of the time, Pallas kernels for 0%

profile of v6, /device:TPU:0, one launch (start us, length us, event | category | flops | bytes accessed | tf_op | source)
XLA Modules:
  0.0 165.7 jit_solution(18276809032191915280)
XLA Ops:
  7.2 1.1 copy.50
  8.3 1.0 copy.49
  9.4 0.9 copy.51
  10.3 52.5 %all-gather.2.cloned.1.call-done = bf16[8,128,2,4,128]{4,1,3,2,0:T(8,128)(2,1)} async-done(((bf16[1,128,2,4,128]{4,1,3,2,0:T(8,128)(2,1)}), bf16[8,128,2,4,128]{4,1,3,2,0:T(8,128)(2,1)}) %all-gather.2.cloned.1.call-update) | async-done | bytes 2097168 | tf_op jit(solution)/shard_map/all_gather | solution.py:39
  62.7 0.8 copy.52
  63.7 0.8 copy.48
  64.7 2.5 %collective-permute-done = bf16[8,128,2,4,128]{4,1,3,2,0:T(8,128)(2,1)S(1)} collective-permute-done((bf16[8,128,2,4,128]{4,1,3,2,0:T(8,128)(2,1)}, bf16[8,128,2,4,128]{4,1,3,2,0:T(8,128)(2,1)S(1)}, u32[]{:S(2)}, u32[]{:S(2)}) %collective-permute-start) | collective-permute-done | bytes 2097184 | tf_op jit(solution)/shard_map/ppermute | solution.py:22
  67.1 3.9 %pad_maximum_fusion = bf16[2,8,128,2,4,128]{5,2,4,3,1,0:T(8,128)(2,1)} fusion(bf16[1,8,128,2,4,128]{5,2,4,3,1,0:T(8,128)(2,1)S(1)} %bitcast.106, bf16[1,8,128,2,4,128]{5,2,4,3,1,0:T(8,128)(2,1)} %bitcast.105), kind=kLoop, calls=%fused_computation.2 | loop fusion | flops 2097152 | bytes 8388608 | tf_op jit(solution)/shard_map/stack | solution.py:41
  71.0 3.9 %gather_fusion.1 = bf16[32,128,128]{2,1,0:T(8,128)(2,1)} fusion(bf16[2,8,128,2,4,128]{5,2,4,3,1,0:T(8,128)(2,1)} %pad_maximum_fusion, s32[32]{0:T(128)S(1)} %get-tuple-element.26), kind=kCustom, calls=%fused_computation.1 | custom fusion | bytes 2097664 | tf_op jit(solution)/shard_map/gather | solution.py:47
  74.9 3.0 %gather_fusion = bf16[32,128,128]{2,1,0:T(8,128)(2,1)S(1)} fusion(bf16[2,8,128,2,4,128]{5,2,4,3,1,0:T(8,128)(2,1)} %pad_maximum_fusion, s32[32]{0:T(128)S(1)} %get-tuple-element.27), kind=kCustom, calls=%fused_computation | custom fusion | bytes 2097664 | tf_op jit(solution)/shard_map/gather | solution.py:47
  78.3 0.8 copy-done.1
  80.3 1.2 subtract_convert_fusion
  81.6 1.2 copy.92
  83.2 1.2 subtract_convert_fusion.1
  84.4 1.2 copy.93
  85.7 0.8 fusion.4
  86.4 1.0 constant_dynamic-slice_fusion.1
  88.0 0.7 fusion
  88.8 1.0 constant_dynamic-slice_fusion.3
  90.8 1.2 collective-permute-done.2
  92.6 2.4 %collective-permute-done.1 = f32[8,4,128,128]{3,1,2,0:T(4,128)S(1)} collective-permute-done((f32[8,4,128,128]{3,1,2,0:T(4,128)S(1)}, f32[8,4,128,128]{3,1,2,0:T(4,128)S(1)}, u32[]{:S(2)}, u32[]{:S(2)}) %collective-permute-start.1) | collective-permute-done | bytes 2097184 | tf_op jit(solution)/shard_map/ppermute | solution.py:22
  95.7 2.8 %pad_maximum_fusion.1 = bf16[8,2,4,128,128]{4,2,3,1,0:T(4,128)(2,1)} fusion(bf16[8,1,4,128,128]{4,2,3,1,0:T(4,128)(2,1)S(1)} %fusion.15, bf16[8,1,4,128,128]{4,2,3,1,0:T(4,128)(2,1)S(1)} %fusion.14), kind=kLoop, calls=%fused_computation.11 | loop fusion | flops 1048576 | bytes 4194304 | tf_op jit(solution)/shard_map/stack | solution.py:93
  98.5 4.4 %all-to-all-start = ((bf16[8,2,4,128,128]{4,2,3,1,0:T(4,128)(2,1)}), bf16[8,2,4,128,128]{4,2,3,1,0:T(4,128)(2,1)}, u32[]{:S(2)}, u32[]{:S(2)}) async-start(bf16[8,2,4,128,128]{4,2,3,1,0:T(4,128)(2,1)} %pad_maximum_fusion.1), calls=%async_computation | async-start | bytes 4194304 | tf_op jit(solution)/shard_map/all_to_all | solution.py:93
  102.8 1.7 %fusion.10 = bf16[8,4,128,128]{2,3,1,0:T(8,128)(2,1)S(1)} fusion(bf16[8,4,128,128]{3,2,1,0:T(8,128)(2,1)} %bitcast.101, f32[128,8,128]{2,0,1:T(8,128)S(1)} %convolution_bitcast_fusion.1), kind=kOutput, calls=%fused_computation.26 | convolution fusion | flops 135397376 | bytes 2621440 | tf_op jit(solution)/shard_map/tri,rkto->rkio/dot_general | solution.py:86
  104.6 1.5 collective-permute-start.4
  107.2 23.4 %collective-permute-done.4 = bf16[8,4,128,128]{2,3,1,0:T(8,128)(2,1)S(1)} collective-permute-done((bf16[8,4,128,128]{2,3,1,0:T(8,128)(2,1)S(1)}, bf16[8,4,128,128]{2,3,1,0:T(8,128)(2,1)S(1)}, u32[]{:S(2)}, u32[]{:S(2)}) %collective-permute-start.4) | collective-permute-done | bytes 1048608 | tf_op jit(solution)/shard_map/ppermute | solution.py:58
  131.1 1.3 copy.65
  132.4 20.0 %collective-permute-done.3 = bf16[8,4,128,128]{3,2,1,0:T(8,128)(2,1)} collective-permute-done((bf16[8,4,128,128]{3,2,1,0:T(8,128)(2,1)S(1)}, bf16[8,4,128,128]{3,2,1,0:T(8,128)(2,1)}, u32[]{:S(2)}, u32[]{:S(2)}) %collective-permute-start.3) | collective-permute-done | bytes 1048608 | tf_op jit(solution)/shard_map/ppermute | solution.py:58
  152.4 2.6 %add_convert_fusion.1 = bf16[8,4,128,128]{3,2,1,0:T(8,128)(2,1)} fusion(bf16[8,4,128,128]{3,2,1,0:T(8,128)(2,1)} %collective-permute-done.3, bf16[8,4,128,128]{3,2,1,0:T(8,128)(2,1)S(1)} %convolution_convert_fusion.1), kind=kLoop, calls=%fused_computation.19 | loop fusion | flops 2097152 | bytes 3145728 | tf_op jit(solution)/shard_map/convert_element_type | solution.py:59
  155.0 2.6 %slice_reduce_fusion = (bf16[4,128,128]{2,0,1:T(4,128)(2,1)S(1)}, bf16[4,128,128]{2,0,1:T(4,128)(2,1)S(1)}) fusion(bf16[8,2,4,128,128]{4,2,3,1,0:T(4,128)(2,1)} %all-to-all-done), kind=kLoop, calls=%fused_computation.34 | loop fusion | flops 917504 | bytes 2359296 | tf_op jit(solution)/shard_map/reduce_sum | solution.py:78
  157.5 0.7 copy.97
  158.2 0.7 copy.96
  (30 shorter events, 6.8 us)
Async XLA Ops:
  7.2 70.7 %copy-start = (bf16[8,4,128,128]{3,2,1,0:T(8,128)(2,1)S(1)}, bf16[8,4,128,128]{3,2,1,0:T(8,128)(2,1)}, u32[]{:S(2)}) copy-start(bf16[8,4,128,128]{3,2,1,0:T(8,128)(2,1)} %param.8) | copy-start | bytes 3145732
  7.2 55.6 %all-gather.2.cloned.1.call-start = ((), (), s32[]{:S(2)}) async-start(), calls=%async_computation.1 | async-start | bytes 2359296 | tf_op jit(solution)/shard_map/all_gather | solution.py:39
  62.7 4.4 %collective-permute-start = (bf16[8,128,2,4,128]{4,1,3,2,0:T(8,128)(2,1)}, bf16[8,128,2,4,128]{4,1,3,2,0:T(8,128)(2,1)S(1)}, u32[]{:S(2)}, u32[]{:S(2)}) collective-permute-start(bf16[8,128,2,4,128]{4,1,3,2,0:T(8,128)(2,1)} %all-gather.2.cloned.1.call-done), channel_id=1, source_target_pairs={{0,1},{1,0},{2,3},{3,2},{4,5},{5,4},{6,7},{7,6},{8,9},{9,8},{10,11... | collective-permute-start | bytes 6291464 | tf_op jit(solution)/shard_map/ppermute | solution.py:22
  77.9 1.2 copy-start.1
  77.9 1.5 copy-start.2
  87.8 4.2 %collective-permute-start.2 = (f32[8,4,128,128]{3,1,2,0:T(4,128)S(1)}, f32[8,4,128,128]{3,1,2,0:T(4,128)S(1)}, u32[]{:S(2)}, u32[]{:S(2)}) collective-permute-start(f32[8,4,128,128]{3,1,2,0:T(4,128)S(1)} %bitcast.103), channel_id=1, source_target_pairs={{0,1},{1,0},{2,3},{3,2},{4,5},{5,4},{6,7},{7,6},{8,9},{9,8},{10,11... | collective-permute-start | bytes 6291464 | tf_op jit(solution)/shard_map/ppermute | solution.py:22
  90.4 4.7 %collective-permute-start.1 = (f32[8,4,128,128]{3,1,2,0:T(4,128)S(1)}, f32[8,4,128,128]{3,1,2,0:T(4,128)S(1)}, u32[]{:S(2)}, u32[]{:S(2)}) collective-permute-start(f32[8,4,128,128]{3,1,2,0:T(4,128)S(1)} %bitcast.104), channel_id=1, source_target_pairs={{0,1},{1,0},{2,3},{3,2},{4,5},{5,4},{6,7},{7,6},{8,9},{9,8},{10,11... | collective-permute-start | bytes 6291464 | tf_op jit(solution)/shard_map/ppermute | solution.py:22
  98.5 56.5 %all-to-all-start = ((bf16[8,2,4,128,128]{4,2,3,1,0:T(4,128)(2,1)}), bf16[8,2,4,128,128]{4,2,3,1,0:T(4,128)(2,1)}, u32[]{:S(2)}, u32[]{:S(2)}) async-start(bf16[8,2,4,128,128]{4,2,3,1,0:T(4,128)(2,1)} %pad_maximum_fusion.1), calls=%async_computation | async-start | bytes 4194304 | tf_op jit(solution)/shard_map/all_to_all | solution.py:93
  104.6 26.1 %collective-permute-start.4 = (bf16[8,4,128,128]{2,3,1,0:T(8,128)(2,1)S(1)}, bf16[8,4,128,128]{2,3,1,0:T(8,128)(2,1)S(1)}, u32[]{:S(2)}, u32[]{:S(2)}) collective-permute-start(bf16[8,4,128,128]{2,3,1,0:T(8,128)(2,1)S(1)} %fusion.10), channel_id=1, source_target_pairs={{0,16},{16,0},{1,17},{17,1},{2,18},{18,2},{3,19},{19,3},{4,20},{20... | collective-permute-start | bytes 3145736 | tf_op jit(solution)/shard_map/ppermute | solution.py:58
  106.6 45.8 %collective-permute-start.3 = (bf16[8,4,128,128]{3,2,1,0:T(8,128)(2,1)S(1)}, bf16[8,4,128,128]{3,2,1,0:T(8,128)(2,1)}, u32[]{:S(2)}, u32[]{:S(2)}) collective-permute-start(bf16[8,4,128,128]{3,2,1,0:T(8,128)(2,1)S(1)} %convolution_convert_fusion.1), channel_id=1, source_target_pairs={{0,16},{16,0},{1,17},{17,1},{2,18},{18,2},{3,19},{19,3},{4,20},{20... | collective-permute-start | bytes 3145736 | tf_op jit(solution)/shard_map/ppermute | solution.py:58
Sparse Core Ops, SparseCore 0:
  10.7 51.9 all-gather.1

commit v7 on v6

--- a/solution.py
+++ b/solution.py
@@ -18,10 +18,6 @@
     )
 
 
-def swap_core(x):
-    return lax.ppermute(x, "core", perm=[(0, 1), (1, 0)])
-
-
 def per_device(inputs, out_grad, w_in, in_blocks, w_out, out_blocks):
     tok_rows = inputs.shape[0]
     own_cols = inputs.shape[1]
@@ -29,22 +25,29 @@
     per_row = w_in.shape[1]
     block_size = w_in.shape[2]
     pair_count = hid_rows * per_row
-    chips = lax.axis_size("chip")
+    halves = lax.axis_size("zh")
+    mids = lax.axis_size("mid")
     pair = lax.axis_size("core")
     own_blocks = own_cols // block_size
-    col_count = chips * pair * own_blocks
+    col_count = halves * mids * pair * own_blocks
     core = lax.axis_index("core")
+    half = lax.axis_index("zh")
+
+    def swap(x, axis):
+        return lax.ppermute(x, axis, perm=[(0, 1), (1, 0)])
 
     both = jnp.concatenate([inputs, out_grad], axis=1).reshape(tok_rows, 2, own_blocks, block_size)
-    mine = lax.all_gather(both, "chip", axis=0, tiled=False)
-    other = swap_core(mine)
-    sets = jnp.stack([mine, other], axis=0)
+    near = jnp.stack([both, swap(both, "zh")], axis=0)
+    mine = lax.all_gather(near, "mid", axis=0, tiled=False)
+    sets = jnp.stack([mine, swap(mine, "core")], axis=0)
 
     def select(flat, which):
         owner = flat // own_blocks
         sub = flat % own_blocks
-        side = (owner % pair != core).astype(jnp.int32)
-        sel = sets[side, owner // pair, :, which, sub, :]
+        chip = owner // pair
+        core_side = (owner % pair != core).astype(jnp.int32)
+        half_side = (chip // mids != half).astype(jnp.int32)
+        sel = sets[core_side, chip % mids, half_side, :, which, sub, :]
         return sel.reshape(hid_rows, per_row, tok_rows, block_size)
 
     in_flat = in_blocks.reshape(pair_count)
@@ -69,13 +72,12 @@
         parts = jnp.concatenate([hi, lo], axis=1)
         picks = jnp.concatenate([onehot, onehot], axis=0)
         local = jnp.einsum("tpo,pc->cto", parts, picks, preferred_element_type=jnp.float32)
-        local = local.reshape(chips, pair, own_blocks, tok_rows, block_size)
-        keep = lax.dynamic_index_in_dim(local, core, axis=1, keepdims=False)
-        give = lax.dynamic_index_in_dim(local, 1 - core, axis=1, keepdims=False)
-        return (keep + swap_core(give)).astype(jnp.bfloat16)
+        local = local.reshape(halves, mids, pair, own_blocks, tok_rows, block_size)
+        keep = lax.dynamic_index_in_dim(local, core, axis=2, keepdims=False)
+        give = lax.dynamic_index_in_dim(local, 1 - core, axis=2, keepdims=False)
+        return (keep + swap(give, "core")).astype(jnp.bfloat16)
 
-    def finish(got):
-        total = got.astype(jnp.float32).sum(axis=0)
+    def finish(total):
         return total.transpose(1, 0, 2).reshape(tok_rows, own_cols).astype(jnp.bfloat16)
 
     preact = jnp.einsum("rkti,rkio->tro", in_sel, w_in, preferred_element_type=jnp.float32)
@@ -90,9 +92,14 @@
     pre_grad = (hid_grad * gelu_slope(preact)).astype(jnp.bfloat16)
     in_terms = jnp.einsum("tro,rkio->trki", pre_grad, w_in, preferred_element_type=jnp.float32)
     in_send = chip_sums(in_terms, in_flat)
-    got = lax.all_to_all(jnp.stack([out_send, in_send], axis=1), "chip", split_axis=0, concat_axis=0, tiled=True)
-    outputs = finish(got[:, 0])
-    in_grad = finish(got[:, 1])
+    send = jnp.stack([out_send, in_send], axis=2)
+    got = lax.all_to_all(send, "mid", split_axis=1, concat_axis=1, tiled=True)
+    half_sum = got.astype(jnp.float32).sum(axis=1).astype(jnp.bfloat16)
+    keep = lax.dynamic_index_in_dim(half_sum, half, axis=0, keepdims=False)
+    give = lax.dynamic_index_in_dim(half_sum, 1 - half, axis=0, keepdims=False)
+    total = keep.astype(jnp.float32) + swap(give, "zh").astype(jnp.float32)
+    outputs = finish(total[0])
+    in_grad = finish(total[1])
     w_in_part = jnp.einsum("rkti,tro->rkio", in_sel, pre_grad, preferred_element_type=jnp.float32)
     w_in_grad = dp_total(w_in_part)
     return (outputs, in_grad, w_in_grad, w_out_grad)
@@ -100,9 +107,8 @@
 
 def solution(mesh):
     n_dp, n_mp = mesh.shape["dp"], mesh.shape["mp"]
-    pair = 2 if n_mp % 2 == 0 else 1
-    split = Mesh(mesh.devices.reshape(n_dp, n_mp // pair, pair), ("dp", "chip", "core"))
-    cols = ("chip", "core")
+    split = Mesh(mesh.devices.reshape(n_dp, 2, n_mp // 4, 2), ("dp", "zh", "mid", "core"))
+    cols = ("zh", "mid", "core")
     return jax.shard_map(
         per_device,
         mesh=split,

time: 166 us -> 175 us (1.054)
  starting transfers between devices: 7.19 us -> 13.8 us
  other arithmetic: 15.9 us -> 17.9 us
    ppermute x3 -> x5, waiting for transfers between devices: 6.13 us -> 19.3 us  [swap(): return lax.ppermute(x, axis, perm=[(0, 1), (1, 0)])]
    all_gather x1, waiting for transfers between devices: 52.5 us -> 45.6 us  [per_device(): mine = lax.all_gather(near, 'mid', axis=0, tiled=False)]
    ppermute x2, waiting for transfers between devices: 43.4 us -> 36.7 us  [dp_total(): got = lax.ppermute(part, 'dp', perm=[(0, 1), (1, 0)])]
    ppermute x3 -> x5, starting transfers between devices: 0.65 us -> 7.24 us  [swap(): return lax.ppermute(x, axis, perm=[(0, 1), (1, 0)])]
    unnamed x13 -> x17, local copies, waits for them, and re-layouts: 7.41 us -> 6.05 us
    another operation x4 -> x6, other arithmetic: 7.86 us -> 8.08 us  [the longest x3 3.96 us: per_device(): send = jnp.stack([out_send, in_send], axis=2)]
  transfers between devices with their start and end apart: 7 -> 9, of which waited for: 6 -> 7; matrix products, arithmetic and copies ran while one was open for 7% -> 9% of each run, Pallas kernels for 0% -> 0%
where the time goes in v7:
time: 175 us; the launch traced here: 174 us
  waiting for transfers between devices  102 us (58%)
  local copies, waits for them, and re-layouts  20 us (11%)
  other arithmetic  17.9 us (10%)
  between operations  14.3 us (8%)
  starting transfers between devices  13.8 us (8%)
  matrix products  6.44 us (4%)
    all_gather x1, waiting for transfers between devices, per_device(): mine = lax.all_gather(near, 'mid', axis=0, tiled=False)  45.6 us
    ppermute x2, waiting for transfers between devices, dp_total(): got = lax.ppermute(part, 'dp', perm=[(0, 1), (1, 0)])  36.7 us
    ppermute x5, waiting for transfers between devices, swap(): return lax.ppermute(x, axis, perm=[(0, 1), (1, 0)])  19.3 us
    ppermute x5, starting transfers between devices, swap(): return lax.ppermute(x, axis, perm=[(0, 1), (1, 0)])  7.24 us
    gather x2, local copies, waits for them, and re-layouts, select(): sel = sets[core_side, chip % mids, half_side, :, which, sub, :]  6.92 us
    unnamed x17, local copies, waits for them, and re-layouts  6.05 us
    convert_element_type x2, other arithmetic, dp_total(): (part.astype(jnp.float32) + got.astype(jnp.float32)).astype(jnp.bfloat16)  4.47 us
    all_to_all x1, starting transfers between devices, per_device(): got = lax.all_to_all(send, 'mid', split_axis=1, concat_axis=1, tiled=True)  4.46 us
  transfers between devices with their start and end apart: 9, of which 7 were waited for; matrix products, arithmetic and copies ran while one was open for 9% of the time, Pallas kernels for 0%

profile of v7, /device:TPU:0, one launch (start us, length us, event | category | flops | bytes accessed | tf_op | source)
XLA Modules:
  0.0 174.1 jit_solution(8581625078028833318)
XLA Ops:
  7.2 1.1 copy.52
  8.3 1.0 copy.51
  9.4 4.1 %collective-permute-start = (bf16[128,2,4,128]{0,3,2,1:T(8,128)(2,1)S(1)}, bf16[128,2,4,128]{0,3,2,1:T(8,128)(2,1)S(1)}, u32[]{:S(2)}, u32[]{:S(2)}) collective-permute-start(bf16[128,2,4,128]{0,3,2,1:T(8,128)(2,1)S(1)} %bitcast.120), channel_id=1, source_target_pairs={{0,8},{8,0},{1,9},{9,1},{2,10},{10,2},{3,11},{11,3},{4,12},{12,4},... | collective-permute-start | bytes 786440 | tf_op jit(solution)/shard_map/ppermute | solution.py:37
  13.5 11.9 %collective-permute-done = bf16[128,2,4,128]{0,3,2,1:T(8,128)(2,1)S(1)} collective-permute-done((bf16[128,2,4,128]{0,3,2,1:T(8,128)(2,1)S(1)}, bf16[128,2,4,128]{0,3,2,1:T(8,128)(2,1)S(1)}, u32[]{:S(2)}, u32[]{:S(2)}) %collective-permute-start) | collective-permute-done | bytes 262176 | tf_op jit(solution)/shard_map/ppermute | solution.py:37
  25.5 1.0 copy.53
  26.5 45.6 %all-gather.3.cloned.1.call-done = bf16[8,128,2,4,128]{4,1,3,2,0:T(8,128)(2,1)} async-done(((bf16[2,128,2,4,128]{4,1,3,2,0:T(8,128)(2,1)}), bf16[8,128,2,4,128]{4,1,3,2,0:T(8,128)(2,1)}) %all-gather.3.cloned.1.call-update) | async-done | bytes 2097168 | tf_op jit(solution)/shard_map/all_gather | solution.py:41
  72.7 3.8 %collective-permute-done.1 = bf16[4,2,128,2,4,128]{5,2,4,3,1,0:T(8,128)(2,1)S(1)} collective-permute-done((bf16[4,2,128,2,4,128]{5,2,4,3,1,0:T(8,128)(2,1)}, bf16[4,2,128,2,4,128]{5,2,4,3,1,0:T(8,128)(2,1)S(1)}, u32[]{:S(2)}, u32[]{:S(2)}) %collective-permute-start.1) | collective-permute-done | bytes 2097184 | tf_op jit(solution)/shard_map/ppermute | solution.py:37
  76.5 3.9 %pad_maximum_fusion = bf16[2,4,2,128,2,4,128]{6,3,5,4,2,1,0:T(8,128)(2,1)} fusion(bf16[1,4,2,128,2,4,128]{6,3,5,4,2,1,0:T(8,128)(2,1)S(1)} %bitcast.119, bf16[1,4,2,128,2,4,128]{6,3,5,4,2,1,0:T(8,128)(2,1)} %bitcast.118), kind=kLoop, calls=%fused_computation.2 | loop fusion | flops 2097152 | bytes 8388608 | tf_op jit(solution)/shard_map/stack | solution.py:42
  80.4 3.9 %gather_fusion.1 = bf16[32,128,128]{2,1,0:T(8,128)(2,1)} fusion(bf16[2,4,2,128,2,4,128]{6,3,5,4,2,1,0:T(8,128)(2,1)} %pad_maximum_fusion, s32[32]{0:T(128)S(1)} %get-tuple-element.26), kind=kCustom, calls=%fused_computation.1 | custom fusion | bytes 2097792 | tf_op jit(solution)/shard_map/gather | solution.py:50
  84.3 3.0 %gather_fusion = bf16[32,128,128]{2,1,0:T(8,128)(2,1)S(1)} fusion(bf16[2,4,2,128,2,4,128]{6,3,5,4,2,1,0:T(8,128)(2,1)} %pad_maximum_fusion, s32[32]{0:T(128)S(1)} %get-tuple-element.27), kind=kCustom, calls=%fused_computation | custom fusion | bytes 2097792 | tf_op jit(solution)/shard_map/gather | solution.py:50
  87.8 0.8 copy-done.1
  89.8 1.2 subtract_convert_fusion
  91.0 1.2 copy.98
  92.6 1.2 subtract_convert_fusion.1
  93.9 1.2 copy.99
  95.1 0.7 fusion.4
  95.8 1.1 constant_dynamic-slice_fusion.1
  97.5 0.7 fusion
  98.3 1.3 constant_dynamic-slice_fusion.3
  100.4 1.2 collective-permute-done.3
  102.1 2.5 %collective-permute-done.2 = f32[2,4,4,128,128]{4,2,0,3,1:T(4,128)S(1)} collective-permute-done((f32[2,4,4,128,128]{4,2,0,3,1:T(4,128)S(1)}, f32[2,4,4,128,128]{4,2,0,3,1:T(4,128)S(1)}, u32[]{:S(2)}, u32[]{:S(2)}) %collective-permute-start.2) | collective-permute-done | bytes 2097184 | tf_op jit(solution)/shard_map/ppermute | solution.py:37
  105.1 2.8 %pad_maximum_fusion.1 = bf16[2,4,2,4,128,128]{5,3,0,4,2,1:T(4,128)(2,1)} fusion(bf16[2,4,1,4,128,128]{5,3,0,4,2,1:T(4,128)(2,1)S(1)} %fusion.15, bf16[2,4,1,4,128,128]{5,3,0,4,2,1:T(4,128)(2,1)S(1)} %fusion.14), kind=kLoop, calls=%fused_computation.11 | loop fusion | flops 1048576 | bytes 4194304 | tf_op jit(solution)/shard_map/stack | solution.py:95
  108.0 4.5 %all-to-all-start = ((bf16[2,4,2,4,128,128]{5,3,0,4,2,1:T(4,128)(2,1)}), bf16[2,4,2,4,128,128]{5,3,0,4,2,1:T(4,128)(2,1)}, u32[]{:S(2)}, u32[]{:S(2)}) async-start(bf16[2,4,2,4,128,128]{5,3,0,4,2,1:T(4,128)(2,1)} %pad_maximum_fusion.1), calls=%async_computation | async-start | bytes 4194304 | tf_op jit(solution)/shard_map/all_to_all | solution.py:96
  112.4 2.7 %fusion.10 = bf16[8,4,128,128]{2,3,1,0:T(8,128)(2,1)} fusion(bf16[8,4,128,128]{3,2,1,0:T(8,128)(2,1)} %bitcast.113, f32[128,8,128]{2,0,1:T(8,128)S(1)} %convolution_bitcast_fusion.1), kind=kOutput, calls=%fused_computation.26 | convolution fusion | flops 135397376 | bytes 2621440 | tf_op jit(solution)/shard_map/tri,rkto->rkio/dot_general | solution.py:88
  115.1 1.5 collective-permute-start.6
  117.7 23.7 %collective-permute-done.6 = bf16[8,4,128,128]{2,3,1,0:T(8,128)(2,1)} collective-permute-done((bf16[8,4,128,128]{2,3,1,0:T(8,128)(2,1)}, bf16[8,4,128,128]{2,3,1,0:T(8,128)(2,1)}, u32[]{:S(2)}, u32[]{:S(2)}) %collective-permute-start.6) | collective-permute-done | bytes 1048608 | tf_op jit(solution)/shard_map/ppermute | solution.py:61
  141.4 1.9 %add_convert_fusion = bf16[8,4,128,128]{2,3,1,0:T(8,128)(2,1)S(1)} fusion(bf16[8,4,128,128]{2,3,1,0:T(8,128)(2,1)} %collective-permute-done.6, bf16[8,4,128,128]{2,3,1,0:T(8,128)(2,1)} %fusion.10), kind=kLoop, calls=%fused_computation.18 | loop fusion | flops 2097152 | bytes 3145728 | tf_op jit(solution)/shard_map/convert_element_type | solution.py:62
  143.4 1.3 copy.68
  144.7 2.8 %reduce_sum.12 = bf16[2,2,4,128,128]{4,2,0,3,1:T(4,128)(2,1)S(1)} reduce(bf16[2,4,2,4,128,128]{5,3,0,4,2,1:T(4,128)(2,1)} %all-to-all-done, bf16[]{:T(256)} %constant.137.clone.1), dimensions={1}, to_apply=%region_0.1 | reduce | flops 786432 | bytes 2621442 | tf_op jit(solution)/shard_map/reduce_sum | solution.py:97
  147.6 2.5 %collective-permute-start.4 = (bf16[2,4,128,128]{3,1,2,0:T(4,128)(2,1)S(1)}, bf16[2,4,128,128]{3,1,2,0:T(4,128)(2,1)S(1)}, u32[]{:S(2)}, u32[]{:S(2)}) collective-permute-start(bf16[2,4,128,128]{3,1,2,0:T(4,128)(2,1)S(1)} %dynamic-slice_bitcast_fusion), channel_id=1, source_target_pairs={{0,8},{8,0},{1,9},{9,1},{2,10},{10,2},{3,11},{11,3},{4,12},{12,4},... | collective-permute-start | bytes 786440 | tf_op jit(solution)/shard_map/ppermute | solution.py:37
  150.1 13.0 %collective-permute-done.5 = bf16[8,4,128,128]{3,2,1,0:T(8,128)(2,1)} collective-permute-done((bf16[8,4,128,128]{3,2,1,0:T(8,128)(2,1)S(1)}, bf16[8,4,128,128]{3,2,1,0:T(8,128)(2,1)}, u32[]{:S(2)}, u32[]{:S(2)}) %collective-permute-start.5) | collective-permute-done | bytes 1048608 | tf_op jit(solution)/shard_map/ppermute | solution.py:61
  163.1 2.6 %add_convert_fusion.1 = bf16[8,4,128,128]{3,2,1,0:T(8,128)(2,1)} fusion(bf16[8,4,128,128]{3,2,1,0:T(8,128)(2,1)} %collective-permute-done.5, bf16[8,4,128,128]{3,2,1,0:T(8,128)(2,1)S(1)} %convolution_convert_fusion.1), kind=kLoop, calls=%fused_computation.19 | loop fusion | flops 2097152 | bytes 3145728 | tf_op jit(solution)/shard_map/convert_element_type | solution.py:62
  (42 shorter events, 8.1 us)
Async XLA Ops:
  7.2 80.2 %copy-start = (bf16[8,4,128,128]{3,2,1,0:T(8,128)(2,1)S(1)}, bf16[8,4,128,128]{3,2,1,0:T(8,128)(2,1)}, u32[]{:S(2)}) copy-start(bf16[8,4,128,128]{3,2,1,0:T(8,128)(2,1)} %param.8) | copy-start | bytes 3145732
  7.2 64.9 %copy-start.3 = (s32[8,4]{0,1:T(4,128)S(1)}, s32[8,4]{0,1:T(4,128)}, u32[]{:S(2)}) copy-start(s32[8,4]{0,1:T(4,128)} %param.9) | copy-start | bytes 388
  7.2 65.1 %copy-start.4 = (s32[8,4]{0,1:T(4,128)S(1)}, s32[8,4]{0,1:T(4,128)}, u32[]{:S(2)}) copy-start(s32[8,4]{0,1:T(4,128)} %param.11) | copy-start | bytes 388
  7.2 64.9 %all-gather.3.cloned.1.call-start = ((), (), s32[]{:S(2)}) async-start(), calls=%async_computation.1 | async-start | bytes 2621440 | tf_op jit(solution)/shard_map/all_gather | solution.py:41
  9.4 16.0 %collective-permute-start = (bf16[128,2,4,128]{0,3,2,1:T(8,128)(2,1)S(1)}, bf16[128,2,4,128]{0,3,2,1:T(8,128)(2,1)S(1)}, u32[]{:S(2)}, u32[]{:S(2)}) collective-permute-start(bf16[128,2,4,128]{0,3,2,1:T(8,128)(2,1)S(1)} %bitcast.120), channel_id=1, source_target_pairs={{0,8},{8,0},{1,9},{9,1},{2,10},{10,2},{3,11},{11,3},{4,12},{12,4},... | collective-permute-start | bytes 786440 | tf_op jit(solution)/shard_map/ppermute | solution.py:37
  72.1 4.4 %collective-permute-start.1 = (bf16[4,2,128,2,4,128]{5,2,4,3,1,0:T(8,128)(2,1)}, bf16[4,2,128,2,4,128]{5,2,4,3,1,0:T(8,128)(2,1)S(1)}, u32[]{:S(2)}, u32[]{:S(2)}) collective-permute-start(bf16[4,2,128,2,4,128]{5,2,4,3,1,0:T(8,128)(2,1)} %bitcast.117), channel_id=1, source_target_pairs={{0,1},{1,0},{2,3},{3,2},{4,5},{5,4},{6,7},{7,6},{8,9},{9,8},{10,11... | collective-permute-start | bytes 6291464 | tf_op jit(solution)/shard_map/ppermute | solution.py:37
  87.3 1.2 copy-start.1
  87.3 1.5 copy-start.2
  97.3 4.2 %collective-permute-start.3 = (f32[2,4,4,128,128]{4,2,0,3,1:T(4,128)S(1)}, f32[2,4,4,128,128]{4,2,0,3,1:T(4,128)S(1)}, u32[]{:S(2)}, u32[]{:S(2)}) collective-permute-start(f32[2,4,4,128,128]{4,2,0,3,1:T(4,128)S(1)} %bitcast.115), channel_id=1, source_target_pairs={{0,1},{1,0},{2,3},{3,2},{4,5},{5,4},{6,7},{7,6},{8,9},{9,8},{10,11... | collective-permute-start | bytes 6291464 | tf_op jit(solution)/shard_map/ppermute | solution.py:37
  99.9 4.6 %collective-permute-start.2 = (f32[2,4,4,128,128]{4,2,0,3,1:T(4,128)S(1)}, f32[2,4,4,128,128]{4,2,0,3,1:T(4,128)S(1)}, u32[]{:S(2)}, u32[]{:S(2)}) collective-permute-start(f32[2,4,4,128,128]{4,2,0,3,1:T(4,128)S(1)} %bitcast.116), channel_id=1, source_target_pairs={{0,1},{1,0},{2,3},{3,2},{4,5},{5,4},{6,7},{7,6},{8,9},{9,8},{10,11... | collective-permute-start | bytes 6291464 | tf_op jit(solution)/shard_map/ppermute | solution.py:37
  108.0 36.7 %all-to-all-start = ((bf16[2,4,2,4,128,128]{5,3,0,4,2,1:T(4,128)(2,1)}), bf16[2,4,2,4,128,128]{5,3,0,4,2,1:T(4,128)(2,1)}, u32[]{:S(2)}, u32[]{:S(2)}) async-start(bf16[2,4,2,4,128,128]{5,3,0,4,2,1:T(4,128)(2,1)} %pad_maximum_fusion.1), calls=%async_computation | async-start | bytes 4194304 | tf_op jit(solution)/shard_map/all_to_all | solution.py:96
  115.1 26.3 %collective-permute-start.6 = (bf16[8,4,128,128]{2,3,1,0:T(8,128)(2,1)}, bf16[8,4,128,128]{2,3,1,0:T(8,128)(2,1)}, u32[]{:S(2)}, u32[]{:S(2)}) collective-permute-start(bf16[8,4,128,128]{2,3,1,0:T(8,128)(2,1)} %fusion.10), channel_id=1, source_target_pairs={{0,16},{16,0},{1,17},{17,1},{2,18},{18,2},{3,19},{19,3},{4,20},{20... | collective-permute-start | bytes 3145736 | tf_op jit(solution)/shard_map/ppermute | solution.py:61
  117.1 46.0 %collective-permute-start.5 = (bf16[8,4,128,128]{3,2,1,0:T(8,128)(2,1)S(1)}, bf16[8,4,128,128]{3,2,1,0:T(8,128)(2,1)}, u32[]{:S(2)}, u32[]{:S(2)}) collective-permute-start(bf16[8,4,128,128]{3,2,1,0:T(8,128)(2,1)S(1)} %convolution_convert_fusion.1), channel_id=1, source_target_pairs={{0,16},{16,0},{1,17},{17,1},{2,18},{18,2},{3,19},{19,3},{4,20},{20... | collective-permute-start | bytes 3145736 | tf_op jit(solution)/shard_map/ppermute | solution.py:61
  147.6 18.1 %collective-permute-start.4 = (bf16[2,4,128,128]{3,1,2,0:T(4,128)(2,1)S(1)}, bf16[2,4,128,128]{3,1,2,0:T(4,128)(2,1)S(1)}, u32[]{:S(2)}, u32[]{:S(2)}) collective-permute-start(bf16[2,4,128,128]{3,1,2,0:T(4,128)(2,1)S(1)} %dynamic-slice_bitcast_fusion), channel_id=1, source_target_pairs={{0,8},{8,0},{1,9},{9,1},{2,10},{10,2},{3,11},{11,3},{4,12},{12,4},... | collective-permute-start | bytes 786440 | tf_op jit(solution)/shard_map/ppermute | solution.py:37
Sparse Core Ops, SparseCore 0:
  26.6 45.3 all-gather.2

commit v8 on v6

--- a/solution.py
+++ b/solution.py
@@ -35,22 +35,23 @@
     col_count = chips * pair * own_blocks
     core = lax.axis_index("core")
 
-    both = jnp.concatenate([inputs, out_grad], axis=1).reshape(tok_rows, 2, own_blocks, block_size)
-    mine = lax.all_gather(both, "chip", axis=0, tiled=False)
-    other = swap_core(mine)
-    sets = jnp.stack([mine, other], axis=0)
+    spread = jnp.broadcast_to(inputs.reshape(1, tok_rows, own_blocks, block_size), (chips, tok_rows, own_blocks, block_size))
+    in_mine = lax.all_to_all(spread, "chip", split_axis=0, concat_axis=0, tiled=True)
+    grad_mine = lax.all_gather(out_grad.reshape(tok_rows, own_blocks, block_size), "chip", axis=0, tiled=False)
+    in_sets = jnp.stack([in_mine, swap_core(in_mine)], axis=0)
+    grad_sets = jnp.stack([grad_mine, swap_core(grad_mine)], axis=0)
 
-    def select(flat, which):
+    def select(sets, flat):
         owner = flat // own_blocks
         sub = flat % own_blocks
         side = (owner % pair != core).astype(jnp.int32)
-        sel = sets[side, owner // pair, :, which, sub, :]
+        sel = sets[side, owner // pair, :, sub, :]
         return sel.reshape(hid_rows, per_row, tok_rows, block_size)
 
     in_flat = in_blocks.reshape(pair_count)
     out_flat = out_blocks.reshape(pair_count)
-    in_sel = select(in_flat, 0)
-    grad_sel = select(out_flat, 1)
+    in_sel = select(in_sets, in_flat)
+    grad_sel = select(grad_sets, out_flat)
 
     def dp_total(part):
         part = part.astype(jnp.bfloat16)

time: 166 us -> 174 us (1.048)
  starting transfers between devices: 7.19 us -> 14.5 us
  waiting for transfers between devices: 102 us -> 97.8 us
  matrix products: 5.48 us -> 8.01 us
    all_gather x1, waiting for transfers between devices: 52.5 us -> 19.6 us  [per_device(): lax.all_gather(out_grad.reshape(tok_rows, own_blocks, block_size), 'chip'...]
    all_to_all x0 -> x1, waiting for transfers between devices: none -> 28.9 us  [per_device(): lax.all_to_all(spread, 'chip', split_axis=0, concat_axis=0, tiled=True)]
    all_to_all x0 -> x1, starting transfers between devices: none -> 7.28 us  [per_device(): lax.all_to_all(spread, 'chip', split_axis=0, concat_axis=0, tiled=True)]
    unnamed x13 -> x22, local copies, waits for them, and re-layouts: 7.41 us -> 3.74 us
    broadcast_in_dim x0 -> x2, local copies, waits for them, and re-layouts: none -> 2.22 us  [per_device(): jnp.broadcast_to(inputs.reshape(1, tok_rows, own_blocks, block_size), (ch...]
    ppermute x3 -> x4, waiting for transfers between devices: 6.13 us -> 5.6 us  [swap_core(): return lax.ppermute(x, 'core', perm=[(0, 1), (1, 0)])]
    another operation x1 -> x2, other arithmetic: 3.93 us -> 4.29 us  [the longest x1 2.76 us: per_device(): grad_sets = jnp.stack([grad_mine, swap_core(grad_mine)], axis=0)]
  transfers between devices with their start and end apart: 7 -> 9, of which waited for: 6 -> 6; matrix products, arithmetic and copies ran while one was open for 7% -> 11% of each run, Pallas kernels for 0% -> 0%
where the time goes in v8:
time: 174 us
  waiting for transfers between devices  97.8 us (56%)
  local copies, waits for them, and re-layouts  22 us (13%)
  other arithmetic  17.2 us (10%)
  starting transfers between devices  14.5 us (8%)
  between operations  14.3 us (8%)
  matrix products  8.01 us (5%)
    ppermute x2, waiting for transfers between devices, dp_total(): got = lax.ppermute(part, 'dp', perm=[(0, 1), (1, 0)])  43.7 us
    all_to_all x1, waiting for transfers between devices, per_device(): lax.all_to_all(spread, 'chip', split_axis=0, concat_axis=0, tiled=True)  28.9 us
    all_gather x1, waiting for transfers between devices, per_device(): lax.all_gather(out_grad.reshape(tok_rows, own_blocks, block_size), 'chip'...  19.6 us
    all_to_all x1, starting transfers between devices, per_device(): lax.all_to_all(spread, 'chip', split_axis=0, concat_axis=0, tiled=True)  7.28 us
    gather x2, local copies, waits for them, and re-layouts, select(): sel = sets[side, owner // pair, :, sub, :]  5.61 us
    ppermute x4, waiting for transfers between devices, swap_core(): return lax.ppermute(x, 'core', perm=[(0, 1), (1, 0)])  5.6 us
    all_to_all x1, starting transfers between devices, per_device(): lax.all_to_all(jnp.stack([out_send, in_send], axis=1), 'chip', split_axis...  4.34 us
    another operation x3, other arithmetic, per_device(): jnp.stack([out_send, in_send], axis=1)  3.86 us
  transfers between devices with their start and end apart: 9, of which 6 were waited for; matrix products, arithmetic and copies ran while one was open for 11% of the time, Pallas kernels for 0%

profile of v8, /device:TPU:0, one launch (start us, length us, event | category | flops | bytes accessed | tf_op | source)
XLA Modules:
  0.0 173.8 jit_solution(6910597422397726917)
XLA Ops:
  7.2 1.0 copy_bitcast_fusion.4
  8.2 1.2 broadcast_in_dim.5
  9.4 7.3 %all-to-all-start = ((bf16[8,128,4,128]{3,1,2,0:T(8,128)(2,1)}), bf16[8,128,4,128]{3,1,2,0:T(8,128)(2,1)S(1)}, u32[]{:S(2)}, u32[]{:S(2)}) async-start(bf16[8,128,4,128]{3,1,2,0:T(8,128)(2,1)} %broadcast_in_dim.5), calls=%async_computation | async-start | bytes 2097152 | tf_op jit(solution)/shard_map/all_to_all | solution.py:39
  16.9 0.8 copy.57
  17.7 28.9 %all-to-all-done = bf16[8,128,4,128]{3,1,2,0:T(8,128)(2,1)S(1)} async-done(((bf16[8,128,4,128]{3,1,2,0:T(8,128)(2,1)}), bf16[8,128,4,128]{3,1,2,0:T(8,128)(2,1)S(1)}, u32[]{:S(2)}, u32[]{:S(2)}) %all-to-all-start) | async-done | bytes 1048608 | tf_op jit(solution)/shard_map/all_to_all | solution.py:39
  47.2 19.6 %all-gather.2.cloned.1.call-done = bf16[8,128,4,128]{3,1,2,0:T(8,128)(2,1)} async-done(((bf16[1,128,4,128]{3,1,2,0:T(8,128)(2,1)}), bf16[8,128,4,128]{3,1,2,0:T(8,128)(2,1)}) %all-gather.2.cloned.1.call-update) | async-done | bytes 1048592 | tf_op jit(solution)/shard_map/all_gather | solution.py:40
  66.9 1.5 pad_maximum_fusion
  68.4 2.4 %gather_fusion = bf16[32,128,128]{2,1,0:T(8,128)(2,1)S(1)} fusion(bf16[2,8,128,4,128]{4,2,3,1,0:T(8,128)(2,1)} %pad_maximum_fusion, s32[32]{0:T(128)S(1)} %fusion.42), kind=kCustom, calls=%fused_computation | custom fusion | bytes 2097536 | tf_op jit(solution)/shard_map/gather | solution.py:48
  70.7 1.6 convolution_bitcast_fusion.1
  72.8 2.2 %copy.95 = bf16[128,32,128]{2,1,0:T(8,128)(2,1)} copy(f32[128,32,128]{2,0,1:T(8,128)S(1)} %bitcast.100) | data formatting | bytes 3145728 | tf_op jit(solution)/shard_map/reshape | solution.py:66
  75.0 2.2 %subtract_convert_fusion.1 = bf16[128,32,128]{2,1,0:T(8,128)(2,1)} fusion(f32[128,32,128]{2,0,1:T(8,128)S(1)} %bitcast.101), kind=kLoop, calls=%fused_computation.22 | loop fusion | flops 2097152 | bytes 3145728 | tf_op jit(solution)/shard_map/convert_element_type | solution.py:68
  77.2 2.8 %pad_maximum_fusion.1 = bf16[2,8,128,4,128]{4,2,3,1,0:T(8,128)(2,1)} fusion(bf16[1,8,128,4,128]{4,2,3,1,0:T(8,128)(2,1)} %bitcast.21, bf16[1,8,128,4,128]{4,2,3,1,0:T(8,128)(2,1)S(1)} %bitcast.113), kind=kLoop, calls=%fused_computation.7 | loop fusion | flops 1048576 | bytes 4194304 | tf_op jit(solution)/shard_map/stack | solution.py:42
  80.0 3.3 %gather_fusion.1 = bf16[32,128,128]{2,1,0:T(8,128)(2,1)} fusion(bf16[2,8,128,4,128]{4,2,3,1,0:T(8,128)(2,1)} %pad_maximum_fusion.1, s32[32]{0:T(128)S(1)} %fusion.41), kind=kCustom, calls=%fused_computation.1 | custom fusion | bytes 2097536 | tf_op jit(solution)/shard_map/gather | solution.py:48
  83.2 1.8 %fusion.13 = bf16[128,8,128,1]{2,0,3,1:T(8,128)(2,1)S(1)} fusion(bf16[8,4,128,128]{3,2,1,0:T(8,128)(2,1)} %bitcast.108, bf16[8,4,128,128]{3,2,1,0:T(8,128)(2,1)S(1)} %copy-done, f32[128,8,128]{2,0,1:T(8,128)S(1)} %convolution_bitcast_fusion.1), kind=kOutput, calls=%fused_computation.32 | convolution fusion | flops 135528448 | bytes 2883584 | tf_op jit(solution)/shard_map/rkto,rkio->tri/dot_general | solution.py:90
  85.5 1.2 subtract_convert_fusion
  86.7 1.2 copy.94
  87.9 0.8 fusion.4
  89.5 0.7 fusion
  90.2 3.4 %constant_dynamic-slice_fusion.1 = (f32[8,1,4,128,128]{4,2,1,0,3:T(4,128)S(1)}, f32[8,1,4,128,128]{4,2,1,0,3:T(4,128)S(1)}, f32[8,1,4,128,128]{4,2,1,0,3:T(4,128)}, f32[8,1,4,128,128]{4,2,1,0,3:T(4,128)S(1)}) fusion(f32[8,2,4,128,128]{4,2,1,0,3:T(4,128)S(1)} %bitcast.104, s32[]{:T(128)S(6)} %select_n.173, s32[]{:T(128)S(6)} %select_n.174, ...), kind=kLoop, calls=%fused_computation.85 | loop fusion | bytes 16777224 | tf_op jit(solution)/shard_map/jit(dynamic_index_in_dim)/dynamic_slice | solution.py:74
  93.6 2.0 %copy.97 = f32[8,1,4,128,128]{4,2,3,0,1:T(4,128)S(1)} copy(f32[8,1,4,128,128]{4,2,1,0,3:T(4,128)} %get-tuple-element.26) | data formatting | bytes 4194304 | tf_op jit(solution)/shard_map/jit(dynamic_index_in_dim)/dynamic_slice | solution.py:75
  96.8 3.1 %collective-permute-done.1 = f32[8,4,128,128]{3,1,2,0:T(4,128)S(1)} collective-permute-done((f32[8,4,128,128]{3,1,2,0:T(4,128)S(1)}, f32[8,4,128,128]{3,1,2,0:T(4,128)S(1)}, u32[]{:S(2)}, u32[]{:S(2)}) %collective-permute-start.1) | collective-permute-done | bytes 2097184 | tf_op jit(solution)/shard_map/ppermute | solution.py:22
  100.5 2.4 %collective-permute-done.3 = f32[8,4,128,128]{3,1,2,0:T(4,128)S(1)} collective-permute-done((f32[8,4,128,128]{3,1,2,0:T(4,128)S(1)}, f32[8,4,128,128]{3,1,2,0:T(4,128)S(1)}, u32[]{:S(2)}, u32[]{:S(2)}) %collective-permute-start.3) | collective-permute-done | bytes 2097184 | tf_op jit(solution)/shard_map/ppermute | solution.py:22
  103.5 2.8 %pad_maximum_fusion.2 = bf16[8,2,4,128,128]{4,2,3,1,0:T(4,128)(2,1)} fusion(bf16[8,1,4,128,128]{4,2,3,1,0:T(4,128)(2,1)S(1)} %fusion.15, bf16[8,1,4,128,128]{4,2,3,1,0:T(4,128)(2,1)S(1)} %fusion.14), kind=kLoop, calls=%fused_computation.12 | loop fusion | flops 1048576 | bytes 4194304 | tf_op jit(solution)/shard_map/stack | solution.py:94
  106.3 4.3 %all-to-all-start.1 = ((bf16[8,2,4,128,128]{4,2,3,1,0:T(4,128)(2,1)}), bf16[8,2,4,128,128]{4,2,3,1,0:T(4,128)(2,1)}, u32[]{:S(2)}, u32[]{:S(2)}) async-start(bf16[8,2,4,128,128]{4,2,3,1,0:T(4,128)(2,1)} %pad_maximum_fusion.2), calls=%async_computation.1 | async-start | bytes 4194304 | tf_op jit(solution)/shard_map/all_to_all | solution.py:94
  110.6 1.7 fusion.10
  112.3 1.5 collective-permute-start.5
  115.0 23.4 %collective-permute-done.5 = bf16[8,4,128,128]{2,3,1,0:T(8,128)(2,1)S(1)} collective-permute-done((bf16[8,4,128,128]{2,3,1,0:T(8,128)(2,1)S(1)}, bf16[8,4,128,128]{2,3,1,0:T(8,128)(2,1)S(1)}, u32[]{:S(2)}, u32[]{:S(2)}) %collective-permute-start.5) | collective-permute-done | bytes 1048608 | tf_op jit(solution)/shard_map/ppermute | solution.py:59
  138.8 1.3 copy.65
  140.1 20.3 %collective-permute-done.4 = bf16[8,4,128,128]{3,2,1,0:T(8,128)(2,1)} collective-permute-done((bf16[8,4,128,128]{3,2,1,0:T(8,128)(2,1)S(1)}, bf16[8,4,128,128]{3,2,1,0:T(8,128)(2,1)}, u32[]{:S(2)}, u32[]{:S(2)}) %collective-permute-start.4) | collective-permute-done | bytes 1048608 | tf_op jit(solution)/shard_map/ppermute | solution.py:59
  160.4 2.6 %add_convert_fusion.1 = bf16[8,4,128,128]{3,2,1,0:T(8,128)(2,1)} fusion(bf16[8,4,128,128]{3,2,1,0:T(8,128)(2,1)} %collective-permute-done.4, bf16[8,4,128,128]{3,2,1,0:T(8,128)(2,1)S(1)} %convolution_convert_fusion.1), kind=kLoop, calls=%fused_computation.20 | loop fusion | flops 2097152 | bytes 3145728 | tf_op jit(solution)/shard_map/convert_element_type | solution.py:60
  163.0 2.6 %slice_reduce_fusion = (bf16[4,128,128]{2,0,1:T(4,128)(2,1)S(1)}, bf16[4,128,128]{2,0,1:T(4,128)(2,1)S(1)}) fusion(bf16[8,2,4,128,128]{4,2,3,1,0:T(4,128)(2,1)} %all-to-all-done.1), kind=kLoop, calls=%fused_computation.35 | loop fusion | flops 917504 | bytes 2359296 | tf_op jit(solution)/shard_map/reduce_sum | solution.py:79
  165.6 0.7 copy.98
  (45 shorter events, 6.9 us)
Async XLA Ops:
  7.2 65.2 %copy-start = (bf16[8,4,128,128]{3,2,1,0:T(8,128)(2,1)S(1)}, bf16[8,4,128,128]{3,2,1,0:T(8,128)(2,1)}, u32[]{:S(2)}) copy-start(bf16[8,4,128,128]{3,2,1,0:T(8,128)(2,1)} %param.10) | copy-start | bytes 3145732
  7.2 9.6 %copy-start.5 = (bf16[128,512]{1,0:T(8,128)(2,1)S(1)}, bf16[128,512]{1,0:T(8,128)(2,1)}, u32[]{:S(2)}) copy-start(bf16[128,512]{1,0:T(8,128)(2,1)} %param.7) | copy-start | bytes 393220
  7.2 39.4 %copy-start.6 = (s32[8,4]{0,1:T(4,128)S(1)}, s32[8,4]{0,1:T(4,128)}, u32[]{:S(2)}) copy-start(s32[8,4]{0,1:T(4,128)} %param.9) | copy-start | bytes 388
  7.2 39.7 %copy-start.7 = (s32[8,4]{0,1:T(4,128)S(1)}, s32[8,4]{0,1:T(4,128)}, u32[]{:S(2)}) copy-start(s32[8,4]{0,1:T(4,128)} %param.11) | copy-start | bytes 388
  9.4 37.2 %all-to-all-start = ((bf16[8,128,4,128]{3,1,2,0:T(8,128)(2,1)}), bf16[8,128,4,128]{3,1,2,0:T(8,128)(2,1)S(1)}, u32[]{:S(2)}, u32[]{:S(2)}) async-start(bf16[8,128,4,128]{3,1,2,0:T(8,128)(2,1)} %broadcast_in_dim.5), calls=%async_computation | async-start | bytes 2097152 | tf_op jit(solution)/shard_map/all_to_all | solution.py:39
  16.7 50.1 %all-gather.2.cloned.1.call-start = ((), (), s32[]{:S(2)}) async-start(), calls=%async_computation.2 | async-start | bytes 1179648 | tf_op jit(solution)/shard_map/all_gather | solution.py:40
  46.6 20.2 %collective-permute-start = (bf16[8,128,4,128]{3,1,2,0:T(8,128)(2,1)S(1)}, bf16[8,128,4,128]{3,1,2,0:T(8,128)(2,1)S(1)}, u32[]{:S(2)}, u32[]{:S(2)}) collective-permute-start(bf16[8,128,4,128]{3,1,2,0:T(8,128)(2,1)S(1)} %all-to-all-done), channel_id=1, source_target_pairs={{0,1},{1,0},{2,3},{3,2},{4,5},{5,4},{6,7},{7,6},{8,9},{9,8},{10,11... | collective-permute-start | bytes 3145736 | tf_op jit(solution)/shard_map/ppermute | solution.py:22
  66.8 10.4 %collective-permute-start.2 = (bf16[8,128,4,128]{3,1,2,0:T(8,128)(2,1)}, bf16[8,128,4,128]{3,1,2,0:T(8,128)(2,1)}, u32[]{:S(2)}, u32[]{:S(2)}) collective-permute-start(bf16[8,128,4,128]{3,1,2,0:T(8,128)(2,1)} %all-gather.2.cloned.1.call-done), channel_id=1, source_target_pairs={{0,1},{1,0},{2,3},{3,2},{4,5},{5,4},{6,7},{7,6},{8,9},{9,8},{10,11... | collective-permute-start | bytes 3145736 | tf_op jit(solution)/shard_map/ppermute | solution.py:22
  75.0 2.2 %copy-start.4 = (bf16[8,128,4,128]{3,1,2,0:T(8,128)(2,1)S(1)}, bf16[8,128,4,128]{3,1,2,0:T(8,128)(2,1)}, u32[]{:S(2)}) copy-start(bf16[8,128,4,128]{3,1,2,0:T(8,128)(2,1)} %all-gather.2.cloned.1.call-done) | copy-start | bytes 3145732
  83.2 1.8 %copy-start.1 = (bf16[8,4,128,128]{3,2,1,0:T(8,128)(2,1)S(1)}, bf16[8,4,128,128]{3,2,1,0:T(8,128)(2,1)}, u32[]{:S(2)}) copy-start(bf16[8,4,128,128]{3,2,1,0:T(8,128)(2,1)} %param.8) | copy-start | bytes 3145732
  87.9 1.2 copy-start.2
  87.9 1.5 copy-start.3
  95.6 4.4 %collective-permute-start.1 = (f32[8,4,128,128]{3,1,2,0:T(4,128)S(1)}, f32[8,4,128,128]{3,1,2,0:T(4,128)S(1)}, u32[]{:S(2)}, u32[]{:S(2)}) collective-permute-start(f32[8,4,128,128]{3,1,2,0:T(4,128)S(1)} %bitcast.112), channel_id=1, source_target_pairs={{0,1},{1,0},{2,3},{3,2},{4,5},{5,4},{6,7},{7,6},{8,9},{9,8},{10,11... | collective-permute-start | bytes 6291464 | tf_op jit(solution)/shard_map/ppermute | solution.py:22
  96.7 6.2 %collective-permute-start.3 = (f32[8,4,128,128]{3,1,2,0:T(4,128)S(1)}, f32[8,4,128,128]{3,1,2,0:T(4,128)S(1)}, u32[]{:S(2)}, u32[]{:S(2)}) collective-permute-start(f32[8,4,128,128]{3,1,2,0:T(4,128)S(1)} %bitcast.111), channel_id=1, source_target_pairs={{0,1},{1,0},{2,3},{3,2},{4,5},{5,4},{6,7},{7,6},{8,9},{9,8},{10,11... | collective-permute-start | bytes 6291464 | tf_op jit(solution)/shard_map/ppermute | solution.py:22
  106.3 56.7 %all-to-all-start.1 = ((bf16[8,2,4,128,128]{4,2,3,1,0:T(4,128)(2,1)}), bf16[8,2,4,128,128]{4,2,3,1,0:T(4,128)(2,1)}, u32[]{:S(2)}, u32[]{:S(2)}) async-start(bf16[8,2,4,128,128]{4,2,3,1,0:T(4,128)(2,1)} %pad_maximum_fusion.2), calls=%async_computation.1 | async-start | bytes 4194304 | tf_op jit(solution)/shard_map/all_to_all | solution.py:94
  112.3 26.1 %collective-permute-start.5 = (bf16[8,4,128,128]{2,3,1,0:T(8,128)(2,1)S(1)}, bf16[8,4,128,128]{2,3,1,0:T(8,128)(2,1)S(1)}, u32[]{:S(2)}, u32[]{:S(2)}) collective-permute-start(bf16[8,4,128,128]{2,3,1,0:T(8,128)(2,1)S(1)} %fusion.10), channel_id=1, source_target_pairs={{0,16},{16,0},{1,17},{17,1},{2,18},{18,2},{3,19},{19,3},{4,20},{20... | collective-permute-start | bytes 3145736 | tf_op jit(solution)/shard_map/ppermute | solution.py:59
  114.4 46.0 %collective-permute-start.4 = (bf16[8,4,128,128]{3,2,1,0:T(8,128)(2,1)S(1)}, bf16[8,4,128,128]{3,2,1,0:T(8,128)(2,1)}, u32[]{:S(2)}, u32[]{:S(2)}) collective-permute-start(bf16[8,4,128,128]{3,2,1,0:T(8,128)(2,1)S(1)} %convolution_convert_fusion.1), channel_id=1, source_target_pairs={{0,16},{16,0},{1,17},{17,1},{2,18},{18,2},{3,19},{19,3},{4,20},{20... | collective-permute-start | bytes 3145736 | tf_op jit(solution)/shard_map/ppermute | solution.py:59
Sparse Core Ops, SparseCore 0:
  20.3 46.5 all-gather.1

commit v9 on v6

--- a/solution.py
+++ b/solution.py
@@ -61,27 +61,25 @@
 
     columns = jnp.arange(col_count, dtype=jnp.int32)
 
-    def chip_sums(terms, flat):
-        terms = terms.reshape(tok_rows, pair_count, block_size)
+    def chip_sums(terms, flats):
+        terms = terms.reshape(2, tok_rows, pair_count, block_size)
         hi = terms.astype(jnp.bfloat16)
         lo = (terms - hi.astype(jnp.float32)).astype(jnp.bfloat16)
-        onehot = (flat[:, None] == columns[None, :]).astype(jnp.bfloat16)
-        parts = jnp.concatenate([hi, lo], axis=1)
-        picks = jnp.concatenate([onehot, onehot], axis=0)
-        local = jnp.einsum("tpo,pc->cto", parts, picks, preferred_element_type=jnp.float32)
-        local = local.reshape(chips, pair, own_blocks, tok_rows, block_size)
+        onehot = (flats[:, :, None] == columns[None, None, :]).astype(jnp.bfloat16)
+        parts = jnp.concatenate([hi, lo], axis=2)
+        picks = jnp.concatenate([onehot, onehot], axis=1)
+        local = jnp.einsum("xtpo,xpc->cxto", parts, picks, preferred_element_type=jnp.float32)
+        local = local.reshape(chips, pair, own_blocks, 2, tok_rows, block_size)
         keep = lax.dynamic_index_in_dim(local, core, axis=1, keepdims=False)
         give = lax.dynamic_index_in_dim(local, 1 - core, axis=1, keepdims=False)
         return (keep + swap_core(give)).astype(jnp.bfloat16)
 
-    def finish(got):
-        total = got.astype(jnp.float32).sum(axis=0)
+    def finish(total):
         return total.transpose(1, 0, 2).reshape(tok_rows, own_cols).astype(jnp.bfloat16)
 
     preact = jnp.einsum("rkti,rkio->tro", in_sel, w_in, preferred_element_type=jnp.float32)
     hidden = gelu_value(preact).astype(jnp.bfloat16)
     out_terms = jnp.einsum("tri,rkio->trko", hidden, w_out, preferred_element_type=jnp.float32)
-    out_send = chip_sums(out_terms, out_flat)
 
     w_out_part = jnp.einsum("tri,rkto->rkio", hidden, grad_sel, preferred_element_type=jnp.float32)
     w_out_grad = dp_total(w_out_part)
@@ -89,10 +87,11 @@
     hid_grad = jnp.einsum("rkto,rkio->tri", grad_sel, w_out, preferred_element_type=jnp.float32)
     pre_grad = (hid_grad * gelu_slope(preact)).astype(jnp.bfloat16)
     in_terms = jnp.einsum("tro,rkio->trki", pre_grad, w_in, preferred_element_type=jnp.float32)
-    in_send = chip_sums(in_terms, in_flat)
-    got = lax.all_to_all(jnp.stack([out_send, in_send], axis=1), "chip", split_axis=0, concat_axis=0, tiled=True)
-    outputs = finish(got[:, 0])
-    in_grad = finish(got[:, 1])
+    send = chip_sums(jnp.stack([out_terms, in_terms], axis=0), jnp.stack([out_flat, in_flat], axis=0))
+    got = lax.all_to_all(send, "chip", split_axis=0, concat_axis=0, tiled=True)
+    total = got.astype(jnp.float32).sum(axis=0)
+    outputs = finish(total[:, 0])
+    in_grad = finish(total[:, 1])
     w_in_part = jnp.einsum("rkti,tro->rkio", in_sel, pre_grad, preferred_element_type=jnp.float32)
     w_in_grad = dp_total(w_in_part)
     return (outputs, in_grad, w_in_grad, w_out_grad)

time: 166 us -> 169 us (1.018)
  other arithmetic: 15.9 us -> 12.8 us
  waiting for transfers between devices: 102 us -> 105 us
    another operation x3 -> x1, other arithmetic: 3.93 us -> 0.01 us  [per_device(): jnp.stack([out_flat, in_flat], axis=0)]
    ppermute x3 -> x2, waiting for transfers between devices: 6.13 us -> 9.48 us  [swap_core(): return lax.ppermute(x, 'core', perm=[(0, 1), (1, 0)])]
    convert_element_type x0 -> x1, other arithmetic: none -> 2.46 us  [chip_sums(): return (keep + swap_core(give)).astype(jnp.bfloat16)]
    reshape x2 -> x0, local copies, waits for them, and re-layouts: 2.44 us -> none  [chip_sums(): terms = terms.reshape(tok_rows, pair_count, block_size)]
    dynamic_slice x2 -> x1, local copies, waits for them, and re-layouts: 2.05 us -> 4.15 us  [chip_sums(): keep = lax.dynamic_index_in_dim(local, core, axis=1, keepdims=False)]
    convert_element_type x2 -> x1, other arithmetic: 2.44 us -> 0.69 us  [chip_sums(): lo = (terms - hi.astype(jnp.float32)).astype(jnp.bfloat16)]
    unnamed x13 -> x20, local copies, waits for them, and re-layouts: 7.41 us -> 7.56 us
  transfers between devices with their start and end apart: 7 -> 6, of which waited for: 6 -> 5; matrix products, arithmetic and copies ran while one was open for 7% -> 5% of each run, Pallas kernels for 0% -> 0%
where the time goes in v9:
time: 169 us
  waiting for transfers between devices  105 us (62%)
  local copies, waits for them, and re-layouts  22.1 us (13%)
  between operations  14.2 us (8%)
  other arithmetic  12.8 us (8%)
  matrix products  7.16 us (4%)
  starting transfers between devices  7.05 us (4%)
    all_gather x1, waiting for transfers between devices, per_device(): mine = lax.all_gather(both, 'chip', axis=0, tiled=False)  52.5 us
    ppermute x2, waiting for transfers between devices, dp_total(): got = lax.ppermute(part, 'dp', perm=[(0, 1), (1, 0)])  43.4 us
    ppermute x2, waiting for transfers between devices, swap_core(): return lax.ppermute(x, 'core', perm=[(0, 1), (1, 0)])  9.48 us
    unnamed x20, local copies, waits for them, and re-layouts  7.56 us
    gather x2, local copies, waits for them, and re-layouts, select(): sel = sets[side, owner // pair, :, which, sub, :]  6.84 us
    all_to_all x1, starting transfers between devices, per_device(): got = lax.all_to_all(send, 'chip', split_axis=0, concat_axis=0, tiled=True)  4.65 us
    dynamic_slice x1, local copies, waits for them, and re-layouts, chip_sums(): keep = lax.dynamic_index_in_dim(local, core, axis=1, keepdims=False)  4.15 us
    another operation x1, other arithmetic, per_device(): sets = jnp.stack([mine, other], axis=0)  3.94 us
  transfers between devices with their start and end apart: 6, of which 5 were waited for; matrix products, arithmetic and copies ran while one was open for 5% of the time, Pallas kernels for 0%

profile of v9, /device:TPU:0, one launch (start us, length us, event | category | flops | bytes accessed | tf_op | source)
XLA Modules:
  0.0 168.8 jit_solution(8628915099912297762)
XLA Ops:
  7.2 1.1 copy.44
  8.3 1.0 copy.45
  9.4 0.9 copy.46
  10.3 52.5 %all-gather.2.cloned.1.call-done = bf16[8,128,2,4,128]{4,1,3,2,0:T(8,128)(2,1)} async-done(((bf16[1,128,2,4,128]{4,1,3,2,0:T(8,128)(2,1)}), bf16[8,128,2,4,128]{4,1,3,2,0:T(8,128)(2,1)}) %all-gather.2.cloned.1.call-update) | async-done | bytes 2097168 | tf_op jit(solution)/shard_map/all_gather | solution.py:39
  62.7 0.8 copy.43
  63.7 0.8 copy.42
  64.7 2.5 %collective-permute-done = bf16[8,128,2,4,128]{4,1,3,2,0:T(8,128)(2,1)S(1)} collective-permute-done((bf16[8,128,2,4,128]{4,1,3,2,0:T(8,128)(2,1)}, bf16[8,128,2,4,128]{4,1,3,2,0:T(8,128)(2,1)S(1)}, u32[]{:S(2)}, u32[]{:S(2)}) %collective-permute-start) | collective-permute-done | bytes 2097184 | tf_op jit(solution)/shard_map/ppermute | solution.py:22
  67.1 3.9 %pad_maximum_fusion = bf16[2,8,128,2,4,128]{5,2,4,3,1,0:T(8,128)(2,1)} fusion(bf16[1,8,128,2,4,128]{5,2,4,3,1,0:T(8,128)(2,1)S(1)} %bitcast.91, bf16[1,8,128,2,4,128]{5,2,4,3,1,0:T(8,128)(2,1)} %bitcast.90), kind=kLoop, calls=%fused_computation.2 | loop fusion | flops 2097152 | bytes 8388608 | tf_op jit(solution)/shard_map/stack | solution.py:41
  71.1 3.9 %gather_fusion.1 = bf16[32,128,128]{2,1,0:T(8,128)(2,1)} fusion(bf16[2,8,128,2,4,128]{5,2,4,3,1,0:T(8,128)(2,1)} %pad_maximum_fusion, s32[32]{0:T(128)S(1)} %get-tuple-element.26), kind=kCustom, calls=%fused_computation.1 | custom fusion | bytes 2097664 | tf_op jit(solution)/shard_map/gather | solution.py:47
  74.9 3.0 %gather_fusion = bf16[32,128,128]{2,1,0:T(8,128)(2,1)S(1)} fusion(bf16[2,8,128,2,4,128]{5,2,4,3,1,0:T(8,128)(2,1)} %pad_maximum_fusion, s32[32]{0:T(128)S(1)} %get-tuple-element.27), kind=kCustom, calls=%fused_computation | custom fusion | bytes 2097664 | tf_op jit(solution)/shard_map/gather | solution.py:47
  77.9 2.1 %convolution_bitcast_fusion.1 = f32[128,8,128]{2,0,1:T(8,128)S(1)} fusion(bf16[8,4,128,128]{3,2,1,0:T(8,128)(2,1)S(1)} %bitcast.83, bf16[8,4,128,128]{3,2,1,0:T(8,128)(2,1)} %param.8), kind=kOutput, calls=%fused_computation.19 | convolution fusion | flops 134217728 | bytes 2621440 | tf_op jit(solution)/shard_map/rkti,rkio->tro/dot_general | solution.py:80
  80.4 0.5 fusion.8
  81.4 1.2 copy_dynamic-update-slice_fusion.1
  82.6 1.2 copy_dynamic-update-slice_fusion
  83.8 0.7 subtract_convert_fusion
  84.5 1.5 fusion
  86.1 4.1 %constant_dynamic-slice_fusion.1 = (f32[8,1,4,2,128,128]{5,2,1,0,4,3:T(4,128)}, f32[8,1,4,2,128,128]{5,2,1,0,4,3:T(4,128)S(1)}) fusion(f32[8,2,4,2,128,128]{5,2,1,0,4,3:T(4,128)S(1)} %bitcast.82, s32[]{:T(128)S(6)} %select_n.178, s32[]{:T(128)S(6)} %select_n.179), kind=kLoop, calls=%fused_computation.85 | loop fusion | bytes 16777224 | tf_op jit(solution)/shard_map/jit(dynamic_index_in_dim)/dynamic_slice | solution.py:73
  90.2 1.1 copy.71
  91.5 7.0 %collective-permute-done.1 = f32[8,4,2,128,128]{4,1,3,2,0:T(4,128)S(1)} collective-permute-done((f32[8,4,2,128,128]{4,1,3,2,0:T(4,128)S(1)}, f32[8,4,2,128,128]{4,1,3,2,0:T(4,128)S(1)}, u32[]{:S(2)}, u32[]{:S(2)}) %collective-permute-start.1) | collective-permute-done | bytes 4194336 | tf_op jit(solution)/shard_map/ppermute | solution.py:22
  98.5 2.5 %fusion.4 = bf16[8,4,2,128,128]{4,1,3,2,0:T(4,128)(2,1)} fusion(f32[8,4,2,128,128]{4,1,3,2,0:T(4,128)S(1)} %collective-permute-done.1, f32[8,1,4,2,128,128]{5,2,1,0,4,3:T(4,128)S(1)} %copy-done.1), kind=kLoop, calls=%fused_computation.8 | loop fusion | flops 2097152 | bytes 10485760 | tf_op jit(solution)/shard_map/convert_element_type | solution.py:75
  101.0 4.7 %all-to-all-start = ((bf16[8,4,2,128,128]{4,1,3,2,0:T(4,128)(2,1)}), bf16[8,4,2,128,128]{4,1,3,2,0:T(4,128)(2,1)}, u32[]{:S(2)}, u32[]{:S(2)}) async-start(bf16[8,4,2,128,128]{4,1,3,2,0:T(4,128)(2,1)} %fusion.4), calls=%async_computation | async-start | bytes 4194304 | tf_op jit(solution)/shard_map/all_to_all | solution.py:91
  105.7 1.7 %fusion.5 = bf16[8,4,128,128]{2,3,1,0:T(8,128)(2,1)S(1)} fusion(bf16[8,4,128,128]{3,2,1,0:T(8,128)(2,1)} %bitcast.88, f32[128,8,128]{2,0,1:T(8,128)S(1)} %convolution_bitcast_fusion.1), kind=kOutput, calls=%fused_computation.17 | convolution fusion | flops 135397376 | bytes 2621440 | tf_op jit(solution)/shard_map/tri,rkto->rkio/dot_general | solution.py:84
  107.4 1.5 collective-permute-start.3
  108.9 0.5 convolution_convert_fusion.1
  109.4 0.6 collective-permute-start.2
  110.1 23.4 %collective-permute-done.3 = bf16[8,4,128,128]{2,3,1,0:T(8,128)(2,1)S(1)} collective-permute-done((bf16[8,4,128,128]{2,3,1,0:T(8,128)(2,1)S(1)}, bf16[8,4,128,128]{2,3,1,0:T(8,128)(2,1)S(1)}, u32[]{:S(2)}, u32[]{:S(2)}) %collective-permute-start.3) | collective-permute-done | bytes 1048608 | tf_op jit(solution)/shard_map/ppermute | solution.py:58
  133.9 1.3 copy.55
  135.2 20.0 %collective-permute-done.2 = bf16[8,4,128,128]{3,2,1,0:T(8,128)(2,1)} collective-permute-done((bf16[8,4,128,128]{3,2,1,0:T(8,128)(2,1)S(1)}, bf16[8,4,128,128]{3,2,1,0:T(8,128)(2,1)}, u32[]{:S(2)}, u32[]{:S(2)}) %collective-permute-start.2) | collective-permute-done | bytes 1048608 | tf_op jit(solution)/shard_map/ppermute | solution.py:58
  155.2 2.6 %add_convert_fusion.1 = bf16[8,4,128,128]{3,2,1,0:T(8,128)(2,1)} fusion(bf16[8,4,128,128]{3,2,1,0:T(8,128)(2,1)} %collective-permute-done.2, bf16[8,4,128,128]{3,2,1,0:T(8,128)(2,1)S(1)} %convolution_convert_fusion.1), kind=kLoop, calls=%fused_computation.14 | loop fusion | flops 2097152 | bytes 3145728 | tf_op jit(solution)/shard_map/convert_element_type | solution.py:59
  157.8 2.6 %reduce = bf16[4,2,128,128]{3,0,2,1:T(4,128)(2,1)S(1)} reduce(bf16[8,4,2,128,128]{4,1,3,2,0:T(4,128)(2,1)} %all-to-all-done, bf16[]{:T(256)} %constant.104), dimensions={0}, to_apply=%region_0.1.clone | reduce | flops 917504 | bytes 2359298 | tf_op jit(solution)/shard_map/reduce_sum | solution.py:92
  160.6 0.7 copy.72
  161.2 0.7 copy.73
  (29 shorter events, 2.1 us)
Async XLA Ops:
  7.2 72.8 %copy-start = (bf16[8,4,128,128]{3,2,1,0:T(8,128)(2,1)S(1)}, bf16[8,4,128,128]{3,2,1,0:T(8,128)(2,1)}, u32[]{:S(2)}) copy-start(bf16[8,4,128,128]{3,2,1,0:T(8,128)(2,1)} %param.10) | copy-start | bytes 3145732
  7.2 55.6 %all-gather.2.cloned.1.call-start = ((), (), s32[]{:S(2)}) async-start(), calls=%async_computation.1 | async-start | bytes 2359296 | tf_op jit(solution)/shard_map/all_gather | solution.py:39
  62.7 4.4 %collective-permute-start = (bf16[8,128,2,4,128]{4,1,3,2,0:T(8,128)(2,1)}, bf16[8,128,2,4,128]{4,1,3,2,0:T(8,128)(2,1)S(1)}, u32[]{:S(2)}, u32[]{:S(2)}) collective-permute-start(bf16[8,128,2,4,128]{4,1,3,2,0:T(8,128)(2,1)} %all-gather.2.cloned.1.call-done), channel_id=1, source_target_pairs={{0,1},{1,0},{2,3},{3,2},{4,5},{5,4},{6,7},{7,6},{8,9},{9,8},{10,11... | collective-permute-start | bytes 6291464 | tf_op jit(solution)/shard_map/ppermute | solution.py:22
  77.9 3.0 %copy-start.2 = (bf16[32,128,128]{2,1,0:T(8,128)(2,1)}, bf16[32,128,128]{2,1,0:T(8,128)(2,1)S(1)}, u32[]{:S(2)}) copy-start(bf16[32,128,128]{2,1,0:T(8,128)(2,1)S(1)} %gather_fusion) | copy-start | bytes 3145732
  77.9 2.5 %copy-start.5 = (bf16[32,128,128]{2,1,0:T(8,128)(2,1)S(1)}, bf16[32,128,128]{2,1,0:T(8,128)(2,1)}, u32[]{:S(2)}) copy-start(bf16[32,128,128]{2,1,0:T(8,128)(2,1)} %gather_fusion.1) | copy-start | bytes 3145732
  77.9 3.0 %copy-start.4 = (bf16[8,4,128,128]{3,2,1,0:T(8,128)(2,1)S(1)}, bf16[8,4,128,128]{3,2,1,0:T(8,128)(2,1)}, u32[]{:S(2)}) copy-start(bf16[8,4,128,128]{3,2,1,0:T(8,128)(2,1)} %param.8) | copy-start | bytes 3145732
  90.2 8.3 %copy-start.1 = (f32[8,1,4,2,128,128]{5,2,1,0,4,3:T(4,128)S(1)}, f32[8,1,4,2,128,128]{5,2,1,0,4,3:T(4,128)}, u32[]{:S(2)}) copy-start(f32[8,1,4,2,128,128]{5,2,1,0,4,3:T(4,128)} %get-tuple-element.22) | copy-start | bytes 12582916
  91.3 7.2 %collective-permute-start.1 = (f32[8,4,2,128,128]{4,1,3,2,0:T(4,128)S(1)}, f32[8,4,2,128,128]{4,1,3,2,0:T(4,128)S(1)}, u32[]{:S(2)}, u32[]{:S(2)}) collective-permute-start(f32[8,4,2,128,128]{4,1,3,2,0:T(4,128)S(1)} %bitcast.87), channel_id=1, source_target_pairs={{0,1},{1,0},{2,3},{3,2},{4,5},{5,4},{6,7},{7,6},{8,9},{9,8},{10,11... | collective-permute-start | bytes 12582920 | tf_op jit(solution)/shard_map/ppermute | solution.py:22
  101.0 7.9 %copy-start.3 = (bf16[32,128,128]{2,1,0:T(8,128)(2,1)S(1)}, bf16[32,128,128]{2,1,0:T(8,128)(2,1)}, u32[]{:S(2)}) copy-start(bf16[32,128,128]{2,1,0:T(8,128)(2,1)} %copy-done.2) | copy-start | bytes 3145732
  101.0 56.8 %all-to-all-start = ((bf16[8,4,2,128,128]{4,1,3,2,0:T(4,128)(2,1)}), bf16[8,4,2,128,128]{4,1,3,2,0:T(4,128)(2,1)}, u32[]{:S(2)}, u32[]{:S(2)}) async-start(bf16[8,4,2,128,128]{4,1,3,2,0:T(4,128)(2,1)} %fusion.4), calls=%async_computation | async-start | bytes 4194304 | tf_op jit(solution)/shard_map/all_to_all | solution.py:91
  107.4 26.1 %collective-permute-start.3 = (bf16[8,4,128,128]{2,3,1,0:T(8,128)(2,1)S(1)}, bf16[8,4,128,128]{2,3,1,0:T(8,128)(2,1)S(1)}, u32[]{:S(2)}, u32[]{:S(2)}) collective-permute-start(bf16[8,4,128,128]{2,3,1,0:T(8,128)(2,1)S(1)} %fusion.5), channel_id=1, source_target_pairs={{0,16},{16,0},{1,17},{17,1},{2,18},{18,2},{3,19},{19,3},{4,20},{20... | collective-permute-start | bytes 3145736 | tf_op jit(solution)/shard_map/ppermute | solution.py:58
  109.4 45.8 %collective-permute-start.2 = (bf16[8,4,128,128]{3,2,1,0:T(8,128)(2,1)S(1)}, bf16[8,4,128,128]{3,2,1,0:T(8,128)(2,1)}, u32[]{:S(2)}, u32[]{:S(2)}) collective-permute-start(bf16[8,4,128,128]{3,2,1,0:T(8,128)(2,1)S(1)} %convolution_convert_fusion.1), channel_id=1, source_target_pairs={{0,16},{16,0},{1,17},{17,1},{2,18},{18,2},{3,19},{19,3},{4,20},{20... | collective-permute-start | bytes 3145736 | tf_op jit(solution)/shard_map/ppermute | solution.py:58
Sparse Core Ops, SparseCore 0:
  10.7 51.9 all-gather.1

commit v10 on v6

--- a/solution.py
+++ b/solution.py
@@ -36,6 +36,7 @@
     core = lax.axis_index("core")
 
     both = jnp.concatenate([inputs, out_grad], axis=1).reshape(tok_rows, 2, own_blocks, block_size)
+    both = both.transpose(1, 2, 0, 3)
     mine = lax.all_gather(both, "chip", axis=0, tiled=False)
     other = swap_core(mine)
     sets = jnp.stack([mine, other], axis=0)
@@ -44,7 +45,7 @@
         owner = flat // own_blocks
         sub = flat % own_blocks
         side = (owner % pair != core).astype(jnp.int32)
-        sel = sets[side, owner // pair, :, which, sub, :]
+        sel = sets[side, owner // pair, which, sub]
         return sel.reshape(hid_rows, per_row, tok_rows, block_size)
 
     in_flat = in_blocks.reshape(pair_count)

time: 166 us -> 166 us (level)
  no operation moved by 1% of the time
where the time goes in v10:
time: 166 us
  waiting for transfers between devices  102 us (61%)
  local copies, waits for them, and re-layouts  20.8 us (13%)
  other arithmetic  15.9 us (10%)
  between operations  14.2 us (9%)
  starting transfers between devices  7.2 us (4%)
  matrix products  5.48 us (3%)
    all_gather x1, waiting for transfers between devices, per_device(): mine = lax.all_gather(both, 'chip', axis=0, tiled=False)  52.5 us
    ppermute x2, waiting for transfers between devices, dp_total(): got = lax.ppermute(part, 'dp', perm=[(0, 1), (1, 0)])  43.4 us
    unnamed x13, local copies, waits for them, and re-layouts  7.41 us
    gather x2, local copies, waits for them, and re-layouts, select(): sel = sets[side, owner // pair, which, sub]  6.84 us
    ppermute x3, waiting for transfers between devices, swap_core(): return lax.ppermute(x, 'core', perm=[(0, 1), (1, 0)])  6.13 us
    all_to_all x1, starting transfers between devices, per_device(): lax.all_to_all(jnp.stack([out_send, in_send], axis=1), 'chip', split_axis...  4.35 us
    another operation x1, other arithmetic, per_device(): sets = jnp.stack([mine, other], axis=0)  3.93 us
    another operation x3, other arithmetic, per_device(): jnp.stack([out_send, in_send], axis=1)  3.93 us
  transfers between devices with their start and end apart: 7, of which 6 were waited for; matrix products, arithmetic and copies ran while one was open for 7% of the time, Pallas kernels for 0%

profile of v10, /device:TPU:0, one launch (start us, length us, event | category | flops | bytes accessed | tf_op | source)
XLA Modules:
  0.0 165.7 jit_solution(15124203418932692524)
XLA Ops:
  7.2 1.1 copy.50
  8.3 1.0 copy.49
  9.4 0.9 copy.51
  10.3 52.5 %all-gather.3.cloned.1.call-done = bf16[16,4,128,128]{3,2,1,0:T(8,128)(2,1)} async-done(((bf16[2,4,128,128]{3,2,1,0:T(8,128)(2,1)}), bf16[16,4,128,128]{3,2,1,0:T(8,128)(2,1)}) %all-gather.3.cloned.1.call-update) | async-done | bytes 2097168 | tf_op jit(solution)/shard_map/all_gather | solution.py:40
  62.7 0.8 copy.52
  63.7 0.8 copy.48
  64.7 2.5 %collective-permute-done = bf16[8,2,4,128,128]{4,3,2,1,0:T(8,128)(2,1)S(1)} collective-permute-done((bf16[8,2,4,128,128]{4,3,2,1,0:T(8,128)(2,1)}, bf16[8,2,4,128,128]{4,3,2,1,0:T(8,128)(2,1)S(1)}, u32[]{:S(2)}, u32[]{:S(2)}) %collective-permute-start) | collective-permute-done | bytes 2097184 | tf_op jit(solution)/shard_map/ppermute | solution.py:22
  67.1 3.9 %pad_maximum_fusion = bf16[2,8,2,4,128,128]{5,4,3,2,1,0:T(8,128)(2,1)} fusion(bf16[1,8,2,4,128,128]{5,4,3,2,1,0:T(8,128)(2,1)S(1)} %bitcast.110, bf16[1,8,2,4,128,128]{5,4,3,2,1,0:T(8,128)(2,1)} %bitcast.109), kind=kLoop, calls=%fused_computation.2 | loop fusion | flops 2097152 | bytes 8388608 | tf_op jit(solution)/shard_map/stack | solution.py:42
  71.0 3.9 %gather_fusion.1 = bf16[32,128,128]{2,1,0:T(8,128)(2,1)} fusion(bf16[2,8,2,4,128,128]{5,4,3,2,1,0:T(8,128)(2,1)} %pad_maximum_fusion, s32[32]{0:T(128)S(1)} %get-tuple-element.26), kind=kCustom, calls=%fused_computation.1 | custom fusion | bytes 2097664 | tf_op jit(solution)/shard_map/gather | solution.py:48
  74.9 3.0 %gather_fusion = bf16[32,128,128]{2,1,0:T(8,128)(2,1)S(1)} fusion(bf16[2,8,2,4,128,128]{5,4,3,2,1,0:T(8,128)(2,1)} %pad_maximum_fusion, s32[32]{0:T(128)S(1)} %get-tuple-element.27), kind=kCustom, calls=%fused_computation | custom fusion | bytes 2097664 | tf_op jit(solution)/shard_map/gather | solution.py:48
  78.3 0.8 copy-done.1
  80.3 1.2 subtract_convert_fusion
  81.6 1.2 copy.92
  83.2 1.2 subtract_convert_fusion.1
  84.4 1.2 copy.93
  85.7 0.8 fusion.4
  86.4 1.0 constant_dynamic-slice_fusion.1
  88.0 0.7 fusion
  88.8 1.0 constant_dynamic-slice_fusion.3
  90.8 1.2 collective-permute-done.2
  92.6 2.4 %collective-permute-done.1 = f32[8,4,128,128]{3,1,2,0:T(4,128)S(1)} collective-permute-done((f32[8,4,128,128]{3,1,2,0:T(4,128)S(1)}, f32[8,4,128,128]{3,1,2,0:T(4,128)S(1)}, u32[]{:S(2)}, u32[]{:S(2)}) %collective-permute-start.1) | collective-permute-done | bytes 2097184 | tf_op jit(solution)/shard_map/ppermute | solution.py:22
  95.7 2.8 %pad_maximum_fusion.1 = bf16[8,2,4,128,128]{4,2,3,1,0:T(4,128)(2,1)} fusion(bf16[8,1,4,128,128]{4,2,3,1,0:T(4,128)(2,1)S(1)} %fusion.15, bf16[8,1,4,128,128]{4,2,3,1,0:T(4,128)(2,1)S(1)} %fusion.14), kind=kLoop, calls=%fused_computation.11 | loop fusion | flops 1048576 | bytes 4194304 | tf_op jit(solution)/shard_map/stack | solution.py:94
  98.5 4.4 %all-to-all-start = ((bf16[8,2,4,128,128]{4,2,3,1,0:T(4,128)(2,1)}), bf16[8,2,4,128,128]{4,2,3,1,0:T(4,128)(2,1)}, u32[]{:S(2)}, u32[]{:S(2)}) async-start(bf16[8,2,4,128,128]{4,2,3,1,0:T(4,128)(2,1)} %pad_maximum_fusion.1), calls=%async_computation | async-start | bytes 4194304 | tf_op jit(solution)/shard_map/all_to_all | solution.py:94
  102.8 1.7 %fusion.10 = bf16[8,4,128,128]{2,3,1,0:T(8,128)(2,1)S(1)} fusion(bf16[8,4,128,128]{3,2,1,0:T(8,128)(2,1)} %bitcast.104, f32[128,8,128]{2,0,1:T(8,128)S(1)} %convolution_bitcast_fusion.1), kind=kOutput, calls=%fused_computation.26 | convolution fusion | flops 135397376 | bytes 2621440 | tf_op jit(solution)/shard_map/tri,rkto->rkio/dot_general | solution.py:87
  104.6 1.5 collective-permute-start.4
  107.2 23.4 %collective-permute-done.4 = bf16[8,4,128,128]{2,3,1,0:T(8,128)(2,1)S(1)} collective-permute-done((bf16[8,4,128,128]{2,3,1,0:T(8,128)(2,1)S(1)}, bf16[8,4,128,128]{2,3,1,0:T(8,128)(2,1)S(1)}, u32[]{:S(2)}, u32[]{:S(2)}) %collective-permute-start.4) | collective-permute-done | bytes 1048608 | tf_op jit(solution)/shard_map/ppermute | solution.py:59
  131.1 1.3 copy.65
  132.4 20.0 %collective-permute-done.3 = bf16[8,4,128,128]{3,2,1,0:T(8,128)(2,1)} collective-permute-done((bf16[8,4,128,128]{3,2,1,0:T(8,128)(2,1)S(1)}, bf16[8,4,128,128]{3,2,1,0:T(8,128)(2,1)}, u32[]{:S(2)}, u32[]{:S(2)}) %collective-permute-start.3) | collective-permute-done | bytes 1048608 | tf_op jit(solution)/shard_map/ppermute | solution.py:59
  152.4 2.6 %add_convert_fusion.1 = bf16[8,4,128,128]{3,2,1,0:T(8,128)(2,1)} fusion(bf16[8,4,128,128]{3,2,1,0:T(8,128)(2,1)} %collective-permute-done.3, bf16[8,4,128,128]{3,2,1,0:T(8,128)(2,1)S(1)} %convolution_convert_fusion.1), kind=kLoop, calls=%fused_computation.19 | loop fusion | flops 2097152 | bytes 3145728 | tf_op jit(solution)/shard_map/convert_element_type | solution.py:60
  155.0 2.6 %slice_reduce_fusion = (bf16[4,128,128]{2,0,1:T(4,128)(2,1)S(1)}, bf16[4,128,128]{2,0,1:T(4,128)(2,1)S(1)}) fusion(bf16[8,2,4,128,128]{4,2,3,1,0:T(4,128)(2,1)} %all-to-all-done), kind=kLoop, calls=%fused_computation.34 | loop fusion | flops 917504 | bytes 2359296 | tf_op jit(solution)/shard_map/reduce_sum | solution.py:79
  157.6 0.7 copy.97
  158.2 0.7 copy.96
  (30 shorter events, 6.8 us)
Async XLA Ops:
  7.2 70.7 %copy-start = (bf16[8,4,128,128]{3,2,1,0:T(8,128)(2,1)S(1)}, bf16[8,4,128,128]{3,2,1,0:T(8,128)(2,1)}, u32[]{:S(2)}) copy-start(bf16[8,4,128,128]{3,2,1,0:T(8,128)(2,1)} %param.8) | copy-start | bytes 3145732
  7.2 55.6 %all-gather.3.cloned.1.call-start = ((), (), s32[]{:S(2)}) async-start(), calls=%async_computation.1 | async-start | bytes 2359296 | tf_op jit(solution)/shard_map/all_gather | solution.py:40
  62.7 4.4 %collective-permute-start = (bf16[8,2,4,128,128]{4,3,2,1,0:T(8,128)(2,1)}, bf16[8,2,4,128,128]{4,3,2,1,0:T(8,128)(2,1)S(1)}, u32[]{:S(2)}, u32[]{:S(2)}) collective-permute-start(bf16[8,2,4,128,128]{4,3,2,1,0:T(8,128)(2,1)} %bitcast.108), channel_id=1, source_target_pairs={{0,1},{1,0},{2,3},{3,2},{4,5},{5,4},{6,7},{7,6},{8,9},{9,8},{10,11... | collective-permute-start | bytes 6291464 | tf_op jit(solution)/shard_map/ppermute | solution.py:22
  77.9 1.2 copy-start.1
  77.9 1.5 copy-start.2
  87.8 4.2 %collective-permute-start.2 = (f32[8,4,128,128]{3,1,2,0:T(4,128)S(1)}, f32[8,4,128,128]{3,1,2,0:T(4,128)S(1)}, u32[]{:S(2)}, u32[]{:S(2)}) collective-permute-start(f32[8,4,128,128]{3,1,2,0:T(4,128)S(1)} %bitcast.106), channel_id=1, source_target_pairs={{0,1},{1,0},{2,3},{3,2},{4,5},{5,4},{6,7},{7,6},{8,9},{9,8},{10,11... | collective-permute-start | bytes 6291464 | tf_op jit(solution)/shard_map/ppermute | solution.py:22
  90.4 4.7 %collective-permute-start.1 = (f32[8,4,128,128]{3,1,2,0:T(4,128)S(1)}, f32[8,4,128,128]{3,1,2,0:T(4,128)S(1)}, u32[]{:S(2)}, u32[]{:S(2)}) collective-permute-start(f32[8,4,128,128]{3,1,2,0:T(4,128)S(1)} %bitcast.107), channel_id=1, source_target_pairs={{0,1},{1,0},{2,3},{3,2},{4,5},{5,4},{6,7},{7,6},{8,9},{9,8},{10,11... | collective-permute-start | bytes 6291464 | tf_op jit(solution)/shard_map/ppermute | solution.py:22
  98.5 56.5 %all-to-all-start = ((bf16[8,2,4,128,128]{4,2,3,1,0:T(4,128)(2,1)}), bf16[8,2,4,128,128]{4,2,3,1,0:T(4,128)(2,1)}, u32[]{:S(2)}, u32[]{:S(2)}) async-start(bf16[8,2,4,128,128]{4,2,3,1,0:T(4,128)(2,1)} %pad_maximum_fusion.1), calls=%async_computation | async-start | bytes 4194304 | tf_op jit(solution)/shard_map/all_to_all | solution.py:94
  104.6 26.1 %collective-permute-start.4 = (bf16[8,4,128,128]{2,3,1,0:T(8,128)(2,1)S(1)}, bf16[8,4,128,128]{2,3,1,0:T(8,128)(2,1)S(1)}, u32[]{:S(2)}, u32[]{:S(2)}) collective-permute-start(bf16[8,4,128,128]{2,3,1,0:T(8,128)(2,1)S(1)} %fusion.10), channel_id=1, source_target_pairs={{0,16},{16,0},{1,17},{17,1},{2,18},{18,2},{3,19},{19,3},{4,20},{20... | collective-permute-start | bytes 3145736 | tf_op jit(solution)/shard_map/ppermute | solution.py:59
  106.6 45.8 %collective-permute-start.3 = (bf16[8,4,128,128]{3,2,1,0:T(8,128)(2,1)S(1)}, bf16[8,4,128,128]{3,2,1,0:T(8,128)(2,1)}, u32[]{:S(2)}, u32[]{:S(2)}) collective-permute-start(bf16[8,4,128,128]{3,2,1,0:T(8,128)(2,1)S(1)} %convolution_convert_fusion.1), channel_id=1, source_target_pairs={{0,16},{16,0},{1,17},{17,1},{2,18},{18,2},{3,19},{19,3},{4,20},{20... | collective-permute-start | bytes 3145736 | tf_op jit(solution)/shard_map/ppermute | solution.py:59
Sparse Core Ops, SparseCore 0:
  10.7 51.9 all-gather.2

commit v11 on v10

--- a/solution.py
+++ b/solution.py
@@ -39,14 +39,20 @@
     both = both.transpose(1, 2, 0, 3)
     mine = lax.all_gather(both, "chip", axis=0, tiled=False)
     other = swap_core(mine)
-    sets = jnp.stack([mine, other], axis=0)
+    chip_ids = jnp.arange(chips, dtype=jnp.int32)
+    sub_ids = jnp.arange(own_blocks, dtype=jnp.int32)
 
     def select(flat, which):
         owner = flat // own_blocks
         sub = flat % own_blocks
-        side = (owner % pair != core).astype(jnp.int32)
-        sel = sets[side, owner // pair, which, sub]
-        return sel.reshape(hid_rows, per_row, tok_rows, block_size)
+        hit = (owner // pair)[:, None, None] == chip_ids[None, :, None]
+        hit = hit & (sub[:, None, None] == sub_ids[None, None, :])
+        here = (owner % pair == core)[:, None, None]
+        near = (hit & here).astype(jnp.bfloat16)
+        far = (hit & ~here).astype(jnp.bfloat16)
+        sel = jnp.einsum("pcs,csto->pto", near, mine[:, which], preferred_element_type=jnp.float32)
+        sel = sel + jnp.einsum("pcs,csto->pto", far, other[:, which], preferred_element_type=jnp.float32)
+        return sel.astype(jnp.bfloat16).reshape(hid_rows, per_row, tok_rows, block_size)
 
     in_flat = in_blocks.reshape(pair_count)
     out_flat = out_blocks.reshape(pair_count)

time: 166 us -> 169 us (1.018)
  matrix products: 5.48 us -> 12.2 us
  other arithmetic: 15.9 us -> 13.1 us
  waiting for transfers between devices: 102 us -> 99.9 us
    gather x2 -> x0, local copies, waits for them, and re-layouts: 6.84 us -> none  [select(): sel = sets[side, owner // pair, which, sub]]
    dot_general x0 -> x4, matrix products: none -> 4.26 us  [the longest x2 2.3 us: select(): jnp.einsum('pcs,csto->pto', near, mine[:, which], preferred_element_type=...]
    another operation x1 -> x0, other arithmetic: 3.93 us -> none  [per_device(): sets = jnp.stack([mine, other], axis=0)]
    reshape x1 -> x2, local copies, waits for them, and re-layouts: 0.08 us -> 3.61 us  [select(): sel.astype(jnp.bfloat16).reshape(hid_rows, per_row, tok_rows, block_size)]
    all_gather x0 -> x1, local copies, waits for them, and re-layouts: none -> 2.94 us  [per_device(): mine = lax.all_gather(both, 'chip', axis=0, tiled=False)]
    all_gather x1, waiting for transfers between devices: 52.5 us -> 50.7 us  [per_device(): mine = lax.all_gather(both, 'chip', axis=0, tiled=False)]
    unnamed x13 -> x21, local copies, waits for them, and re-layouts: 7.41 us -> 7.43 us
  transfers between devices with their start and end apart: 7 -> 7, of which waited for: 6 -> 6; matrix products, arithmetic and copies ran while one was open for 7% -> 8% of each run, Pallas kernels for 0% -> 0%
where the time goes in v11:
time: 169 us; the launch traced here: 168 us
  waiting for transfers between devices  99.9 us (59%)
  local copies, waits for them, and re-layouts  21.2 us (13%)
  between operations  14.3 us (8%)
  other arithmetic  13.1 us (8%)
  matrix products  12.2 us (7%)
  starting transfers between devices  7.47 us (4%)
    all_gather x1, waiting for transfers between devices, per_device(): mine = lax.all_gather(both, 'chip', axis=0, tiled=False)  50.7 us
    ppermute x2, waiting for transfers between devices, dp_total(): got = lax.ppermute(part, 'dp', perm=[(0, 1), (1, 0)])  43.5 us
    unnamed x21, local copies, waits for them, and re-layouts  7.43 us
    ppermute x3, waiting for transfers between devices, swap_core(): return lax.ppermute(x, 'core', perm=[(0, 1), (1, 0)])  5.59 us
    all_to_all x1, starting transfers between devices, per_device(): lax.all_to_all(jnp.stack([out_send, in_send], axis=1), 'chip', split_axis...  4.56 us
    another operation x3, other arithmetic, per_device(): jnp.stack([out_send, in_send], axis=1)  3.94 us
    reshape x2, local copies, waits for them, and re-layouts, select(): sel.astype(jnp.bfloat16).reshape(hid_rows, per_row, tok_rows, block_size)  3.61 us
    reshape x2, local copies, waits for them, and re-layouts, chip_sums(): terms = terms.reshape(tok_rows, pair_count, block_size)  3.45 us
  transfers between devices with their start and end apart: 7, of which 6 were waited for; matrix products, arithmetic and copies ran while one was open for 8% of the time, Pallas kernels for 0%

profile of v11, /device:TPU:0, one launch (start us, length us, event | category | flops | bytes accessed | tf_op | source)
XLA Modules:
  0.0 168.2 jit_solution(5231660904949594579)
XLA Ops:
  7.2 1.1 copy.54
  8.3 1.0 copy.55
  9.4 0.9 copy.56
  10.3 0.8 copy.52
  11.1 0.8 copy.53
  12.0 50.7 %all-gather.3.cloned.1.call-done = bf16[16,4,128,128]{3,2,1,0:T(8,128)(2,1)} async-done(((bf16[2,4,128,128]{3,2,1,0:T(8,128)(2,1)}), bf16[16,4,128,128]{3,2,1,0:T(8,128)(2,1)}) %all-gather.3.cloned.1.call-update) | async-done | bytes 2097168 | tf_op jit(solution)/shard_map/all_gather | solution.py:40
  62.7 2.9 %copy.57 = bf16[8,2,4,128,128]{4,0,2,3,1:T(8,128)(2,1)S(1)} copy(bf16[8,2,4,128,128]{4,3,2,1,0:T(8,128)(2,1)} %bitcast.138) | data formatting | bytes 4194304 | tf_op jit(solution)/shard_map/all_gather | solution.py:40
  66.4 1.8 %fusion.18 = f32[32,128,128,1]{2,0,3,1:T(8,128)} fusion(bf16[8,2,4,128,128]{4,0,2,3,1:T(8,128)(2,1)S(1)} %copy.57, pred[32]{0:T(512)(128)(4,1)S(1)} %get-tuple-element.33, pred[32,4]{0,1:T(4,128)(4,1)S(1)} %iota_compare_fusion.4, pred[32,8]{0,1:T(8,128)(4,1)S(1)} %iota_compare_fusion.2), kind=kOutput, calls=%fused_computation.39 | convolution fusion | flops 33556480 | bytes 3147776 | tf_op jit(solution)/shard_map/pcs,csto->pto/dot_general | solution.py:53
  68.2 1.7 %collective-permute-done = bf16[8,2,4,128,128]{4,0,2,3,1:T(8,128)(2,1)S(1)} collective-permute-done((bf16[8,2,4,128,128]{4,0,2,3,1:T(8,128)(2,1)S(1)}, bf16[8,2,4,128,128]{4,0,2,3,1:T(8,128)(2,1)S(1)}, u32[]{:S(2)}, u32[]{:S(2)}) %collective-permute-start) | collective-permute-done | bytes 2097184 | tf_op jit(solution)/shard_map/ppermute | solution.py:22
  70.4 0.8 copy-done.5
  71.2 1.0 copy.70
  72.2 1.7 %convolution_bitcast_fusion.1 = f32[128,8,128]{2,0,1:T(8,128)S(1)} fusion(bf16[8,4,128,128]{2,3,1,0:T(8,128)(2,1)S(1)} %copy.70, bf16[8,4,128,128]{3,2,1,0:T(8,128)(2,1)} %param.8), kind=kOutput, calls=%fused_computation.29 | convolution fusion | flops 134217728 | bytes 2621440 | tf_op jit(solution)/shard_map/rkti,rkio->tro/dot_general | solution.py:88
  74.4 2.2 %copy.102 = bf16[128,32,128]{2,1,0:T(8,128)(2,1)} copy(f32[128,32,128]{2,0,1:T(8,128)S(1)} %bitcast.130) | data formatting | bytes 3145728 | tf_op jit(solution)/shard_map/reshape | solution.py:72
  76.6 2.2 %subtract_convert_fusion.1 = bf16[128,32,128]{2,1,0:T(8,128)(2,1)} fusion(f32[128,32,128]{2,0,1:T(8,128)S(1)} %bitcast.131), kind=kLoop, calls=%fused_computation.22 | loop fusion | flops 2097152 | bytes 3145728 | tf_op jit(solution)/shard_map/convert_element_type | solution.py:74
  78.8 1.5 fusion.9
  80.3 2.6 %copy.71 = bf16[8,4,128,128]{2,3,1,0:T(8,128)(2,1)} copy(bf16[8,4,128,128]{3,1,0,2:T(4,128)(2,1)} %bitcast.136) | data formatting | bytes 2097152 | tf_op jit(solution)/shard_map/reshape | solution.py:55
  82.9 1.8 %fusion.15 = bf16[128,8,128,1]{2,0,3,1:T(8,128)(2,1)S(1)} fusion(bf16[8,4,128,128]{2,3,1,0:T(8,128)(2,1)} %copy.71, bf16[8,4,128,128]{3,2,1,0:T(8,128)(2,1)S(1)} %copy-done, f32[128,8,128]{2,0,1:T(8,128)S(1)} %convolution_bitcast_fusion.1), kind=kOutput, calls=%fused_computation.32 | convolution fusion | flops 135528448 | bytes 2883584 | tf_op jit(solution)/shard_map/rkto,rkio->tri/dot_general | solution.py:96
  85.2 1.2 copy.101
  86.4 1.2 subtract_convert_fusion
  88.7 1.0 constant_dynamic-slice_fusion.3
  91.1 1.0 constant_dynamic-slice_fusion.1
  92.9 1.4 collective-permute-done.1
  94.9 2.4 %collective-permute-done.2 = f32[8,4,128,128]{3,1,2,0:T(4,128)S(1)} collective-permute-done((f32[8,4,128,128]{3,1,2,0:T(4,128)S(1)}, f32[8,4,128,128]{3,1,2,0:T(4,128)S(1)}, u32[]{:S(2)}, u32[]{:S(2)}) %collective-permute-start.2) | collective-permute-done | bytes 2097184 | tf_op jit(solution)/shard_map/ppermute | solution.py:22
  98.0 2.8 %pad_maximum_fusion = bf16[8,2,4,128,128]{4,2,3,1,0:T(4,128)(2,1)} fusion(bf16[8,1,4,128,128]{4,2,3,1,0:T(4,128)(2,1)S(1)} %fusion.17, bf16[8,1,4,128,128]{4,2,3,1,0:T(4,128)(2,1)S(1)} %fusion.16), kind=kLoop, calls=%fused_computation.8 | loop fusion | flops 1048576 | bytes 4194304 | tf_op jit(solution)/shard_map/stack | solution.py:100
  100.7 4.6 %all-to-all-start = ((bf16[8,2,4,128,128]{4,2,3,1,0:T(4,128)(2,1)}), bf16[8,2,4,128,128]{4,2,3,1,0:T(4,128)(2,1)}, u32[]{:S(2)}, u32[]{:S(2)}) async-start(bf16[8,2,4,128,128]{4,2,3,1,0:T(4,128)(2,1)} %pad_maximum_fusion), calls=%async_computation | async-start | bytes 4194304 | tf_op jit(solution)/shard_map/all_to_all | solution.py:100
  105.3 1.7 fusion.12
  107.0 1.5 collective-permute-start.4
  109.6 23.5 %collective-permute-done.4 = bf16[8,4,128,128]{2,3,1,0:T(8,128)(2,1)S(1)} collective-permute-done((bf16[8,4,128,128]{2,3,1,0:T(8,128)(2,1)S(1)}, bf16[8,4,128,128]{2,3,1,0:T(8,128)(2,1)S(1)}, u32[]{:S(2)}, u32[]{:S(2)}) %collective-permute-start.4) | collective-permute-done | bytes 1048608 | tf_op jit(solution)/shard_map/ppermute | solution.py:65
  133.5 1.3 copy.72
  134.8 20.0 %collective-permute-done.3 = bf16[8,4,128,128]{3,2,1,0:T(8,128)(2,1)} collective-permute-done((bf16[8,4,128,128]{3,2,1,0:T(8,128)(2,1)S(1)}, bf16[8,4,128,128]{3,2,1,0:T(8,128)(2,1)}, u32[]{:S(2)}, u32[]{:S(2)}) %collective-permute-start.3) | collective-permute-done | bytes 1048608 | tf_op jit(solution)/shard_map/ppermute | solution.py:65
  154.8 2.6 %add_convert_fusion.1 = bf16[8,4,128,128]{3,2,1,0:T(8,128)(2,1)} fusion(bf16[8,4,128,128]{3,2,1,0:T(8,128)(2,1)} %collective-permute-done.3, bf16[8,4,128,128]{3,2,1,0:T(8,128)(2,1)S(1)} %convolution_convert_fusion.1), kind=kLoop, calls=%fused_computation.20 | loop fusion | flops 2097152 | bytes 3145728 | tf_op jit(solution)/shard_map/convert_element_type | solution.py:66
  157.4 2.6 %slice_reduce_fusion = (bf16[4,128,128]{2,0,1:T(4,128)(2,1)S(1)}, bf16[4,128,128]{2,0,1:T(4,128)(2,1)S(1)}) fusion(bf16[8,2,4,128,128]{4,2,3,1,0:T(4,128)(2,1)} %all-to-all-done), kind=kLoop, calls=%fused_computation.35 | loop fusion | flops 917504 | bytes 2359296 | tf_op jit(solution)/shard_map/reduce_sum | solution.py:85
  (47 shorter events, 9.5 us)
Async XLA Ops:
  7.2 66.8 %copy-start = (bf16[8,4,128,128]{3,2,1,0:T(8,128)(2,1)S(1)}, bf16[8,4,128,128]{3,2,1,0:T(8,128)(2,1)}, u32[]{:S(2)}) copy-start(bf16[8,4,128,128]{3,2,1,0:T(8,128)(2,1)} %param.10) | copy-start | bytes 3145732
  7.2 55.6 %all-gather.3.cloned.1.call-start = ((), (), s32[]{:S(2)}) async-start(), calls=%async_computation.1 | async-start | bytes 2359296 | tf_op jit(solution)/shard_map/all_gather | solution.py:40
  65.7 4.2 %collective-permute-start = (bf16[8,2,4,128,128]{4,0,2,3,1:T(8,128)(2,1)S(1)}, bf16[8,2,4,128,128]{4,0,2,3,1:T(8,128)(2,1)S(1)}, u32[]{:S(2)}, u32[]{:S(2)}) collective-permute-start(bf16[8,2,4,128,128]{4,0,2,3,1:T(8,128)(2,1)S(1)} %copy.57), channel_id=1, source_target_pairs={{0,1},{1,0},{2,3},{3,2},{4,5},{5,4},{6,7},{7,6},{8,9},{9,8},{10,11... | collective-permute-start | bytes 6291464 | tf_op jit(solution)/shard_map/ppermute | solution.py:22
  69.9 1.3 copy-start.5
  74.4 4.4 %copy-start.6 = (bf16[8,2,4,128,128]{4,0,2,3,1:T(8,128)(2,1)S(1)}, bf16[8,2,4,128,128]{4,0,2,3,1:T(8,128)(2,1)}, u32[]{:S(2)}) copy-start(bf16[8,2,4,128,128]{4,0,2,3,1:T(8,128)(2,1)} %copy-done.5) | copy-start | bytes 6291460
  76.6 2.2 %copy-start.1 = (f32[32,128,128,1]{2,0,3,1:T(8,128)S(1)}, f32[32,128,128,1]{2,0,3,1:T(8,128)}, u32[]{:S(2)}) copy-start(f32[32,128,128,1]{2,0,3,1:T(8,128)} %fusion.18) | copy-start | bytes 6291460
  82.9 1.8 %copy-start.2 = (bf16[8,4,128,128]{3,2,1,0:T(8,128)(2,1)S(1)}, bf16[8,4,128,128]{3,2,1,0:T(8,128)(2,1)}, u32[]{:S(2)}) copy-start(bf16[8,4,128,128]{3,2,1,0:T(8,128)(2,1)} %param.8) | copy-start | bytes 3145732
  86.4 1.2 copy-start.3
  86.4 1.5 copy-start.4
  90.1 4.2 %collective-permute-start.1 = (f32[8,4,128,128]{3,1,2,0:T(4,128)S(1)}, f32[8,4,128,128]{3,1,2,0:T(4,128)S(1)}, u32[]{:S(2)}, u32[]{:S(2)}) collective-permute-start(f32[8,4,128,128]{3,1,2,0:T(4,128)S(1)} %bitcast.139), channel_id=1, source_target_pairs={{0,1},{1,0},{2,3},{3,2},{4,5},{5,4},{6,7},{7,6},{8,9},{9,8},{10,11... | collective-permute-start | bytes 6291464 | tf_op jit(solution)/shard_map/ppermute | solution.py:22
  92.5 4.9 %collective-permute-start.2 = (f32[8,4,128,128]{3,1,2,0:T(4,128)S(1)}, f32[8,4,128,128]{3,1,2,0:T(4,128)S(1)}, u32[]{:S(2)}, u32[]{:S(2)}) collective-permute-start(f32[8,4,128,128]{3,1,2,0:T(4,128)S(1)} %bitcast.140), channel_id=1, source_target_pairs={{0,1},{1,0},{2,3},{3,2},{4,5},{5,4},{6,7},{7,6},{8,9},{9,8},{10,11... | collective-permute-start | bytes 6291464 | tf_op jit(solution)/shard_map/ppermute | solution.py:22
  100.7 56.7 %all-to-all-start = ((bf16[8,2,4,128,128]{4,2,3,1,0:T(4,128)(2,1)}), bf16[8,2,4,128,128]{4,2,3,1,0:T(4,128)(2,1)}, u32[]{:S(2)}, u32[]{:S(2)}) async-start(bf16[8,2,4,128,128]{4,2,3,1,0:T(4,128)(2,1)} %pad_maximum_fusion), calls=%async_computation | async-start | bytes 4194304 | tf_op jit(solution)/shard_map/all_to_all | solution.py:100
  107.0 26.1 %collective-permute-start.4 = (bf16[8,4,128,128]{2,3,1,0:T(8,128)(2,1)S(1)}, bf16[8,4,128,128]{2,3,1,0:T(8,128)(2,1)S(1)}, u32[]{:S(2)}, u32[]{:S(2)}) collective-permute-start(bf16[8,4,128,128]{2,3,1,0:T(8,128)(2,1)S(1)} %fusion.12), channel_id=1, source_target_pairs={{0,16},{16,0},{1,17},{17,1},{2,18},{18,2},{3,19},{19,3},{4,20},{20... | collective-permute-start | bytes 3145736 | tf_op jit(solution)/shard_map/ppermute | solution.py:65
  108.9 45.9 %collective-permute-start.3 = (bf16[8,4,128,128]{3,2,1,0:T(8,128)(2,1)S(1)}, bf16[8,4,128,128]{3,2,1,0:T(8,128)(2,1)}, u32[]{:S(2)}, u32[]{:S(2)}) collective-permute-start(bf16[8,4,128,128]{3,2,1,0:T(8,128)(2,1)S(1)} %convolution_convert_fusion.1), channel_id=1, source_target_pairs={{0,16},{16,0},{1,17},{17,1},{2,18},{18,2},{3,19},{19,3},{4,20},{20... | collective-permute-start | bytes 3145736 | tf_op jit(solution)/shard_map/ppermute | solution.py:65
Sparse Core Ops, SparseCore 0:
  10.7 51.9 all-gather.2

commit v12 on v10

--- a/solution.py
+++ b/solution.py
@@ -22,6 +22,20 @@
     return lax.ppermute(x, "core", perm=[(0, 1), (1, 0)])
 
 
+def gather_chips(x, chips):
+    if chips & (chips - 1):
+        return lax.all_gather(x, "chip", axis=0, tiled=False)
+    me = lax.axis_index("chip")
+    held = x[None]
+    step = 1
+    while step < chips:
+        got = lax.ppermute(held, "chip", perm=[(i, i ^ step) for i in range(chips)])
+        upper = (me // step) % 2 == 1
+        held = jnp.where(upper, jnp.concatenate([got, held], axis=0), jnp.concatenate([held, got], axis=0))
+        step *= 2
+    return held
+
+
 def per_device(inputs, out_grad, w_in, in_blocks, w_out, out_blocks):
     tok_rows = inputs.shape[0]
     own_cols = inputs.shape[1]
@@ -37,7 +51,7 @@
 
     both = jnp.concatenate([inputs, out_grad], axis=1).reshape(tok_rows, 2, own_blocks, block_size)
     both = both.transpose(1, 2, 0, 3)
-    mine = lax.all_gather(both, "chip", axis=0, tiled=False)
+    mine = gather_chips(both, chips)
     other = swap_core(mine)
     sets = jnp.stack([mine, other], axis=0)
 

time: 166 us -> 176 us (1.060)
  between operations: 14.2 us -> 0.88 us
  waiting for transfers between devices: 102 us -> 112 us
  starting transfers between devices: 7.2 us -> 15.5 us
  other arithmetic: 15.9 us -> 19.2 us
  matrix products: 5.48 us -> 8.16 us
  local copies, waits for them, and re-layouts: 20.8 us -> 18.8 us
    ppermute x0 -> x3, waiting for transfers between devices: none -> 61.9 us  [gather_chips(): got = lax.ppermute(held, 'chip', perm=[(i, i ^ step) for i in range(chips)])]
    all_gather x1 -> x0, waiting for transfers between devices: 52.5 us -> none  [per_device(): mine = lax.all_gather(both, 'chip', axis=0, tiled=False)]
    ppermute x0 -> x3, starting transfers between devices: none -> 7.45 us  [gather_chips(): got = lax.ppermute(held, 'chip', perm=[(i, i ^ step) for i in range(chips)])]
    select_n x0 -> x4, other arithmetic: none -> 2.22 us  [gather_chips(): jnp.where(upper, jnp.concatenate([got, held], axis=0), jnp.concatenate([h...]
    unnamed x13 -> x21, local copies, waits for them, and re-layouts: 7.41 us -> 5.28 us
  transfers between devices with their start and end apart: 7 -> 9, of which waited for: 6 -> 8; matrix products, arithmetic and copies ran while one was open for 7% -> 6% of each run, Pallas kernels for 0% -> 0%
where the time goes in v12:
time: 176 us; the launch traced here: 175 us
  waiting for transfers between devices  112 us (64%)
  other arithmetic  19.2 us (11%)
  local copies, waits for them, and re-layouts  18.8 us (11%)
  starting transfers between devices  15.5 us (9%)
  matrix products  8.16 us (5%)
    ppermute x3, waiting for transfers between devices, gather_chips(): got = lax.ppermute(held, 'chip', perm=[(i, i ^ step) for i in range(chips)])  61.9 us
    ppermute x2, waiting for transfers between devices, dp_total(): got = lax.ppermute(part, 'dp', perm=[(0, 1), (1, 0)])  43.2 us
    ppermute x3, starting transfers between devices, gather_chips(): got = lax.ppermute(held, 'chip', perm=[(i, i ^ step) for i in range(chips)])  7.45 us
    ppermute x3, waiting for transfers between devices, swap_core(): return lax.ppermute(x, 'core', perm=[(0, 1), (1, 0)])  7.29 us
    gather x2, local copies, waits for them, and re-layouts, select(): sel = sets[side, owner // pair, which, sub]  6.84 us
    all_to_all x1, starting transfers between devices, per_device(): lax.all_to_all(jnp.stack([out_send, in_send], axis=1), 'chip', split_axis...  5.3 us
    unnamed x21, local copies, waits for them, and re-layouts  5.28 us
    another operation x1, other arithmetic, per_device(): sets = jnp.stack([mine, other], axis=0)  3.93 us
  transfers between devices with their start and end apart: 9, of which 8 were waited for; matrix products, arithmetic and copies ran while one was open for 6% of the time, Pallas kernels for 0%

profile of v12, /device:TPU:0, one launch (start us, length us, event | category | flops | bytes accessed | tf_op | source)
XLA Modules:
  0.0 175.0 jit_solution(541502603026679098)
XLA Ops:
  0.6 1.1 copy.49
  1.8 1.0 copy.50
  3.0 3.0 %collective-permute-start = (bf16[1,2,4,128,128]{4,3,2,1,0:T(8,128)(2,1)S(1)}, bf16[1,2,4,128,128]{4,3,2,1,0:T(8,128)(2,1)S(1)}, u32[]{:S(2)}, u32[]{:S(2)}) collective-permute-start(bf16[1,2,4,128,128]{4,3,2,1,0:T(8,128)(2,1)S(1)} %bitcast.112), channel_id=1, source_target_pairs={{0,2},{2,0},{4,6},{6,4},{8,10},{10,8},{12,14},{14,12},{1,3},{3,1},... | collective-permute-start | bytes 786440 | tf_op jit(solution)/shard_map/ppermute | solution.py:32
  6.0 6.3 %collective-permute-done = bf16[1,2,4,128,128]{4,3,2,1,0:T(8,128)(2,1)S(1)} collective-permute-done((bf16[1,2,4,128,128]{4,3,2,1,0:T(8,128)(2,1)S(1)}, bf16[1,2,4,128,128]{4,3,2,1,0:T(8,128)(2,1)S(1)}, u32[]{:S(2)}, u32[]{:S(2)}) %collective-permute-start) | collective-permute-done | bytes 262176 | tf_op jit(solution)/shard_map/ppermute | solution.py:32
  12.4 1.9 %collective-permute-start.1 = (bf16[2,2,4,128,128]{4,3,2,1,0:T(8,128)(2,1)S(1)}, bf16[2,2,4,128,128]{4,3,2,1,0:T(8,128)(2,1)S(1)}, u32[]{:S(2)}, u32[]{:S(2)}) collective-permute-start(bf16[2,2,4,128,128]{4,3,2,1,0:T(8,128)(2,1)S(1)} %maximum_select_fusion.3), channel_id=1, source_target_pairs={{0,4},{2,6},{4,0},{6,2},{8,12},{10,14},{12,8},{14,10},{1,5},{3,7},... | collective-permute-start | bytes 1572872 | tf_op jit(solution)/shard_map/ppermute | solution.py:32
  14.3 11.3 %collective-permute-done.1 = bf16[2,2,4,128,128]{4,3,2,1,0:T(8,128)(2,1)S(1)} collective-permute-done((bf16[2,2,4,128,128]{4,3,2,1,0:T(8,128)(2,1)S(1)}, bf16[2,2,4,128,128]{4,3,2,1,0:T(8,128)(2,1)S(1)}, u32[]{:S(2)}, u32[]{:S(2)}) %collective-permute-start.1) | collective-permute-done | bytes 524320 | tf_op jit(solution)/shard_map/ppermute | solution.py:32
  25.8 2.6 %collective-permute-start.2 = (bf16[4,2,4,128,128]{4,3,2,1,0:T(8,128)(2,1)S(1)}, bf16[4,2,4,128,128]{4,3,2,1,0:T(8,128)(2,1)S(1)}, u32[]{:S(2)}, u32[]{:S(2)}) collective-permute-start(bf16[4,2,4,128,128]{4,3,2,1,0:T(8,128)(2,1)S(1)} %maximum_select_fusion.2), channel_id=1, source_target_pairs={{0,8},{2,10},{4,12},{6,14},{8,0},{10,2},{12,4},{14,6},{1,9},{3,11}... | collective-permute-start | bytes 3145736 | tf_op jit(solution)/shard_map/ppermute | solution.py:32
  28.3 44.3 %collective-permute-done.2 = bf16[4,2,4,128,128]{4,3,2,1,0:T(8,128)(2,1)S(1)} collective-permute-done((bf16[4,2,4,128,128]{4,3,2,1,0:T(8,128)(2,1)S(1)}, bf16[4,2,4,128,128]{4,3,2,1,0:T(8,128)(2,1)S(1)}, u32[]{:S(2)}, u32[]{:S(2)}) %collective-permute-start.2) | collective-permute-done | bytes 1048608 | tf_op jit(solution)/shard_map/ppermute | solution.py:32
  72.6 1.7 maximum_select_fusion.1
  75.2 3.6 %collective-permute-done.3 = bf16[8,2,4,128,128]{4,3,2,1,0:T(8,128)(2,1)} collective-permute-done((bf16[8,2,4,128,128]{4,3,2,1,0:T(8,128)(2,1)}, bf16[8,2,4,128,128]{4,3,2,1,0:T(8,128)(2,1)}, u32[]{:S(2)}, u32[]{:S(2)}) %collective-permute-start.3) | collective-permute-done | bytes 2097184 | tf_op jit(solution)/shard_map/ppermute | solution.py:22
  78.8 3.9 %pad_maximum_fusion = bf16[2,8,2,4,128,128]{5,4,3,2,1,0:T(8,128)(2,1)} fusion(bf16[1,8,2,4,128,128]{5,4,3,2,1,0:T(8,128)(2,1)} %bitcast.7, bf16[1,8,2,4,128,128]{5,4,3,2,1,0:T(8,128)(2,1)S(1)} %maximum_select_fusion), kind=kLoop, calls=%fused_computation.2 | loop fusion | flops 2097152 | bytes 8388608 | tf_op jit(solution)/shard_map/stack | solution.py:56
  82.7 3.0 %gather_fusion = bf16[32,128,128]{2,1,0:T(8,128)(2,1)S(1)} fusion(bf16[2,8,2,4,128,128]{5,4,3,2,1,0:T(8,128)(2,1)} %pad_maximum_fusion, s32[32]{0:T(128)S(1)} %get-tuple-element.27), kind=kCustom, calls=%fused_computation | custom fusion | bytes 2097664 | tf_op jit(solution)/shard_map/gather | solution.py:62
  85.7 1.6 convolution_bitcast_fusion.1
  87.8 2.2 %copy.93 = bf16[128,32,128]{2,1,0:T(8,128)(2,1)} copy(f32[128,32,128]{2,0,1:T(8,128)S(1)} %bitcast.97) | data formatting | bytes 3145728 | tf_op jit(solution)/shard_map/reshape | solution.py:80
  90.0 2.2 %subtract_convert_fusion.1 = bf16[128,32,128]{2,1,0:T(8,128)(2,1)} fusion(f32[128,32,128]{2,0,1:T(8,128)S(1)} %bitcast.98), kind=kLoop, calls=%fused_computation.23 | loop fusion | flops 2097152 | bytes 3145728 | tf_op jit(solution)/shard_map/convert_element_type | solution.py:82
  92.2 3.9 %gather_fusion.1 = bf16[32,128,128]{2,1,0:T(8,128)(2,1)} fusion(bf16[2,8,2,4,128,128]{5,4,3,2,1,0:T(8,128)(2,1)} %pad_maximum_fusion, s32[32]{0:T(128)S(1)} %get-tuple-element.26), kind=kCustom, calls=%fused_computation.1 | custom fusion | bytes 2097664 | tf_op jit(solution)/shard_map/gather | solution.py:62
  96.0 1.8 %fusion.13 = bf16[128,8,128,1]{2,0,3,1:T(8,128)(2,1)S(1)} fusion(bf16[8,4,128,128]{3,2,1,0:T(8,128)(2,1)} %bitcast.107, bf16[8,4,128,128]{3,2,1,0:T(8,128)(2,1)S(1)} %copy-done, f32[128,8,128]{2,0,1:T(8,128)S(1)} %convolution_bitcast_fusion.1), kind=kOutput, calls=%fused_computation.33 | convolution fusion | flops 135528448 | bytes 2883584 | tf_op jit(solution)/shard_map/rkto,rkio->tri/dot_general | solution.py:104
  98.3 1.2 copy.92
  99.5 1.2 subtract_convert_fusion
  101.8 1.0 constant_dynamic-slice_fusion.3
  104.3 1.0 constant_dynamic-slice_fusion.1
  106.2 1.2 collective-permute-done.4
  108.0 2.4 %collective-permute-done.5 = f32[8,4,128,128]{3,1,2,0:T(4,128)S(1)} collective-permute-done((f32[8,4,128,128]{3,1,2,0:T(4,128)S(1)}, f32[8,4,128,128]{3,1,2,0:T(4,128)S(1)}, u32[]{:S(2)}, u32[]{:S(2)}) %collective-permute-start.5) | collective-permute-done | bytes 2097184 | tf_op jit(solution)/shard_map/ppermute | solution.py:22
  111.1 2.8 %pad_maximum_fusion.1 = bf16[8,2,4,128,128]{4,2,3,1,0:T(4,128)(2,1)} fusion(bf16[8,1,4,128,128]{4,2,3,1,0:T(4,128)(2,1)S(1)} %fusion.15, bf16[8,1,4,128,128]{4,2,3,1,0:T(4,128)(2,1)S(1)} %fusion.14), kind=kLoop, calls=%fused_computation.13 | loop fusion | flops 1048576 | bytes 4194304 | tf_op jit(solution)/shard_map/stack | solution.py:108
  113.8 5.3 %all-to-all-start = ((bf16[8,2,4,128,128]{4,2,3,1,0:T(4,128)(2,1)}), bf16[8,2,4,128,128]{4,2,3,1,0:T(4,128)(2,1)}, u32[]{:S(2)}, u32[]{:S(2)}) async-start(bf16[8,2,4,128,128]{4,2,3,1,0:T(4,128)(2,1)} %pad_maximum_fusion.1), calls=%async_computation | async-start | bytes 4194304 | tf_op jit(solution)/shard_map/all_to_all | solution.py:108
  119.1 1.7 fusion.10
  120.8 1.6 collective-permute-start.7
  123.5 23.4 %collective-permute-done.7 = bf16[8,4,128,128]{2,3,1,0:T(8,128)(2,1)S(1)} collective-permute-done((bf16[8,4,128,128]{2,3,1,0:T(8,128)(2,1)S(1)}, bf16[8,4,128,128]{2,3,1,0:T(8,128)(2,1)S(1)}, u32[]{:S(2)}, u32[]{:S(2)}) %collective-permute-start.7) | collective-permute-done | bytes 1048608 | tf_op jit(solution)/shard_map/ppermute | solution.py:73
  147.3 1.3 copy.65
  148.7 19.8 %collective-permute-done.6 = bf16[8,4,128,128]{3,2,1,0:T(8,128)(2,1)} collective-permute-done((bf16[8,4,128,128]{3,2,1,0:T(8,128)(2,1)S(1)}, bf16[8,4,128,128]{3,2,1,0:T(8,128)(2,1)}, u32[]{:S(2)}, u32[]{:S(2)}) %collective-permute-start.6) | collective-permute-done | bytes 1048608 | tf_op jit(solution)/shard_map/ppermute | solution.py:73
  168.4 2.7 %add_convert_fusion.1 = bf16[8,4,128,128]{3,2,1,0:T(8,128)(2,1)} fusion(bf16[8,4,128,128]{3,2,1,0:T(8,128)(2,1)} %collective-permute-done.6, bf16[8,4,128,128]{3,2,1,0:T(8,128)(2,1)S(1)} %convolution_convert_fusion.1), kind=kLoop, calls=%fused_computation.21 | loop fusion | flops 2097152 | bytes 3145728 | tf_op jit(solution)/shard_map/convert_element_type | solution.py:74
  171.1 2.6 %slice_reduce_fusion = (bf16[4,128,128]{2,0,1:T(4,128)(2,1)S(1)}, bf16[4,128,128]{2,0,1:T(4,128)(2,1)S(1)}) fusion(bf16[8,2,4,128,128]{4,2,3,1,0:T(4,128)(2,1)} %all-to-all-done), kind=kLoop, calls=%fused_computation.36 | loop fusion | flops 917504 | bytes 2359296 | tf_op jit(solution)/shard_map/reduce_sum | solution.py:93
  (45 shorter events, 9.5 us)
Async XLA Ops:
  0.6 86.7 %copy-start = (bf16[8,4,128,128]{3,2,1,0:T(8,128)(2,1)S(1)}, bf16[8,4,128,128]{3,2,1,0:T(8,128)(2,1)}, u32[]{:S(2)}) copy-start(bf16[8,4,128,128]{3,2,1,0:T(8,128)(2,1)} %param.10) | copy-start | bytes 3145732
  3.0 9.3 %collective-permute-start = (bf16[1,2,4,128,128]{4,3,2,1,0:T(8,128)(2,1)S(1)}, bf16[1,2,4,128,128]{4,3,2,1,0:T(8,128)(2,1)S(1)}, u32[]{:S(2)}, u32[]{:S(2)}) collective-permute-start(bf16[1,2,4,128,128]{4,3,2,1,0:T(8,128)(2,1)S(1)} %bitcast.112), channel_id=1, source_target_pairs={{0,2},{2,0},{4,6},{6,4},{8,10},{10,8},{12,14},{14,12},{1,3},{3,1},... | collective-permute-start | bytes 786440 | tf_op jit(solution)/shard_map/ppermute | solution.py:32
  12.4 13.2 %collective-permute-start.1 = (bf16[2,2,4,128,128]{4,3,2,1,0:T(8,128)(2,1)S(1)}, bf16[2,2,4,128,128]{4,3,2,1,0:T(8,128)(2,1)S(1)}, u32[]{:S(2)}, u32[]{:S(2)}) collective-permute-start(bf16[2,2,4,128,128]{4,3,2,1,0:T(8,128)(2,1)S(1)} %maximum_select_fusion.3), channel_id=1, source_target_pairs={{0,4},{2,6},{4,0},{6,2},{8,12},{10,14},{12,8},{14,10},{1,5},{3,7},... | collective-permute-start | bytes 1572872 | tf_op jit(solution)/shard_map/ppermute | solution.py:32
  25.8 46.9 %collective-permute-start.2 = (bf16[4,2,4,128,128]{4,3,2,1,0:T(8,128)(2,1)S(1)}, bf16[4,2,4,128,128]{4,3,2,1,0:T(8,128)(2,1)S(1)}, u32[]{:S(2)}, u32[]{:S(2)}) collective-permute-start(bf16[4,2,4,128,128]{4,3,2,1,0:T(8,128)(2,1)S(1)} %maximum_select_fusion.2), channel_id=1, source_target_pairs={{0,8},{2,10},{4,12},{6,14},{8,0},{10,2},{12,4},{14,6},{1,9},{3,11}... | collective-permute-start | bytes 3145736 | tf_op jit(solution)/shard_map/ppermute | solution.py:32
  28.3 46.0 %copy-start.5 = (s32[8,4]{0,1:T(4,128)S(1)}, s32[8,4]{0,1:T(4,128)}, u32[]{:S(2)}) copy-start(s32[8,4]{0,1:T(4,128)} %param.11) | copy-start | bytes 388
  28.3 46.2 %copy-start.6 = (s32[8,4]{0,1:T(4,128)S(1)}, s32[8,4]{0,1:T(4,128)}, u32[]{:S(2)}) copy-start(s32[8,4]{0,1:T(4,128)} %param.9) | copy-start | bytes 388
  74.3 4.5 %collective-permute-start.3 = (bf16[8,2,4,128,128]{4,3,2,1,0:T(8,128)(2,1)}, bf16[8,2,4,128,128]{4,3,2,1,0:T(8,128)(2,1)}, u32[]{:S(2)}, u32[]{:S(2)}) collective-permute-start(bf16[8,2,4,128,128]{4,3,2,1,0:T(8,128)(2,1)} %maximum_select_fusion.1), channel_id=1, source_target_pairs={{0,1},{1,0},{2,3},{3,2},{4,5},{5,4},{6,7},{7,6},{8,9},{9,8},{10,11... | collective-permute-start | bytes 6291464 | tf_op jit(solution)/shard_map/ppermute | solution.py:22
  96.0 1.8 %copy-start.2 = (bf16[8,4,128,128]{3,2,1,0:T(8,128)(2,1)S(1)}, bf16[8,4,128,128]{3,2,1,0:T(8,128)(2,1)}, u32[]{:S(2)}) copy-start(bf16[8,4,128,128]{3,2,1,0:T(8,128)(2,1)} %param.8) | copy-start | bytes 3145732
  99.5 1.2 copy-start.3
  99.5 1.5 copy-start.4
  103.2 4.2 %collective-permute-start.4 = (f32[8,4,128,128]{3,1,2,0:T(4,128)S(1)}, f32[8,4,128,128]{3,1,2,0:T(4,128)S(1)}, u32[]{:S(2)}, u32[]{:S(2)}) collective-permute-start(f32[8,4,128,128]{3,1,2,0:T(4,128)S(1)} %bitcast.109), channel_id=1, source_target_pairs={{0,1},{1,0},{2,3},{3,2},{4,5},{5,4},{6,7},{7,6},{8,9},{9,8},{10,11... | collective-permute-start | bytes 6291464 | tf_op jit(solution)/shard_map/ppermute | solution.py:22
  105.7 4.7 %collective-permute-start.5 = (f32[8,4,128,128]{3,1,2,0:T(4,128)S(1)}, f32[8,4,128,128]{3,1,2,0:T(4,128)S(1)}, u32[]{:S(2)}, u32[]{:S(2)}) collective-permute-start(f32[8,4,128,128]{3,1,2,0:T(4,128)S(1)} %bitcast.110), channel_id=1, source_target_pairs={{0,1},{1,0},{2,3},{3,2},{4,5},{5,4},{6,7},{7,6},{8,9},{9,8},{10,11... | collective-permute-start | bytes 6291464 | tf_op jit(solution)/shard_map/ppermute | solution.py:22
  113.8 57.3 %all-to-all-start = ((bf16[8,2,4,128,128]{4,2,3,1,0:T(4,128)(2,1)}), bf16[8,2,4,128,128]{4,2,3,1,0:T(4,128)(2,1)}, u32[]{:S(2)}, u32[]{:S(2)}) async-start(bf16[8,2,4,128,128]{4,2,3,1,0:T(4,128)(2,1)} %pad_maximum_fusion.1), calls=%async_computation | async-start | bytes 4194304 | tf_op jit(solution)/shard_map/all_to_all | solution.py:108
  120.8 26.1 %collective-permute-start.7 = (bf16[8,4,128,128]{2,3,1,0:T(8,128)(2,1)S(1)}, bf16[8,4,128,128]{2,3,1,0:T(8,128)(2,1)S(1)}, u32[]{:S(2)}, u32[]{:S(2)}) collective-permute-start(bf16[8,4,128,128]{2,3,1,0:T(8,128)(2,1)S(1)} %fusion.10), channel_id=1, source_target_pairs={{0,16},{16,0},{1,17},{17,1},{2,18},{18,2},{3,19},{19,3},{4,20},{20... | collective-permute-start | bytes 3145736 | tf_op jit(solution)/shard_map/ppermute | solution.py:73
  122.9 45.5 %collective-permute-start.6 = (bf16[8,4,128,128]{3,2,1,0:T(8,128)(2,1)S(1)}, bf16[8,4,128,128]{3,2,1,0:T(8,128)(2,1)}, u32[]{:S(2)}, u32[]{:S(2)}) collective-permute-start(bf16[8,4,128,128]{3,2,1,0:T(8,128)(2,1)S(1)} %convolution_convert_fusion.1), channel_id=1, source_target_pairs={{0,16},{16,0},{1,17},{17,1},{2,18},{18,2},{3,19},{19,3},{4,20},{20... | collective-permute-start | bytes 3145736 | tf_op jit(solution)/shard_map/ppermute | solution.py:73
  168.4 6.6 %copy-start.1 = (bf16[8,4,128,128]{3,2,1,0:T(8,128)(2,1)S(1)}, bf16[8,4,128,128]{3,2,1,0:T(8,128)(2,1)}, u32[]{:S(2)}) copy-start(bf16[8,4,128,128]{3,2,1,0:T(8,128)(2,1)} %param.10) | copy-start | bytes 3145732

commit v13 on v12

--- a/solution.py
+++ b/solution.py
@@ -27,13 +27,24 @@
         return lax.all_gather(x, "chip", axis=0, tiled=False)
     me = lax.axis_index("chip")
     held = x[None]
-    step = 1
-    while step < chips:
+    step = chips // 2
+    while step >= 1:
         got = lax.ppermute(held, "chip", perm=[(i, i ^ step) for i in range(chips)])
         upper = (me // step) % 2 == 1
         held = jnp.where(upper, jnp.concatenate([got, held], axis=0), jnp.concatenate([held, got], axis=0))
-        step *= 2
+        step //= 2
     return held
+
+
+def chip_slot(chip, chips):
+    if chips & (chips - 1):
+        return chip
+    slot = jnp.zeros_like(chip)
+    step = chips // 2
+    while step >= 1:
+        slot = slot + ((chip // step) % 2) * (chips // (2 * step))
+        step //= 2
+    return slot
 
 
 def per_device(inputs, out_grad, w_in, in_blocks, w_out, out_blocks):
@@ -59,7 +70,7 @@
         owner = flat // own_blocks
         sub = flat % own_blocks
         side = (owner % pair != core).astype(jnp.int32)
-        sel = sets[side, owner // pair, which, sub]
+        sel = sets[side, chip_slot(owner // pair, chips), which, sub]
         return sel.reshape(hid_rows, per_row, tok_rows, block_size)
 
     in_flat = in_blocks.reshape(pair_count)

time: 176 us -> 161 us (0.915)
  waiting for transfers between devices: 112 us -> 96.9 us
    ppermute x3, waiting for transfers between devices: 61.9 us -> 46.5 us  [gather_chips(): got = lax.ppermute(held, 'chip', perm=[(i, i ^ step) for i in range(chips)])]
    all_to_all x1, starting transfers between devices: 5.3 us -> 7.31 us  [per_device(): lax.all_to_all(jnp.stack([out_send, in_send], axis=1), 'chip', split_axis...]
where the time goes in v13:
time: 161 us; the launch traced here: 160 us
  waiting for transfers between devices  96.9 us (60%)
  other arithmetic  19.2 us (12%)
  local copies, waits for them, and re-layouts  18.8 us (12%)
  starting transfers between devices  16.3 us (10%)
  matrix products  8.15 us (5%)
    ppermute x3, waiting for transfers between devices, gather_chips(): got = lax.ppermute(held, 'chip', perm=[(i, i ^ step) for i in range(chips)])  46.5 us
    ppermute x2, waiting for transfers between devices, dp_total(): got = lax.ppermute(part, 'dp', perm=[(0, 1), (1, 0)])  43.2 us
    all_to_all x1, starting transfers between devices, per_device(): lax.all_to_all(jnp.stack([out_send, in_send], axis=1), 'chip', split_axis...  7.31 us
    ppermute x3, waiting for transfers between devices, swap_core(): return lax.ppermute(x, 'core', perm=[(0, 1), (1, 0)])  7.28 us
    gather x2, local copies, waits for them, and re-layouts, select(): sel = sets[side, chip_slot(owner // pair, chips), which, sub]  6.84 us
    ppermute x3, starting transfers between devices, gather_chips(): got = lax.ppermute(held, 'chip', perm=[(i, i ^ step) for i in range(chips)])  6.23 us
    unnamed x21, local copies, waits for them, and re-layouts  5.28 us
    another operation x1, other arithmetic, per_device(): sets = jnp.stack([mine, other], axis=0)  3.93 us
  transfers between devices with their start and end apart: 9, of which 8 were waited for; matrix products, arithmetic and copies ran while one was open for 6% of the time, Pallas kernels for 0%

profile of v13, /device:TPU:0, one launch (start us, length us, event | category | flops | bytes accessed | tf_op | source)
XLA Modules:
  0.0 160.3 jit_solution(16600146032395036990)
XLA Ops:
  0.6 1.1 copy.49
  1.8 1.0 copy.50
  3.0 4.1 %collective-permute-start = (bf16[1,2,4,128,128]{4,3,2,1,0:T(8,128)(2,1)S(1)}, bf16[1,2,4,128,128]{4,3,2,1,0:T(8,128)(2,1)S(1)}, u32[]{:S(2)}, u32[]{:S(2)}) collective-permute-start(bf16[1,2,4,128,128]{4,3,2,1,0:T(8,128)(2,1)S(1)} %bitcast.112), channel_id=1, source_target_pairs={{0,8},{2,10},{4,12},{6,14},{8,0},{10,2},{12,4},{14,6},{1,9},{3,11}... | collective-permute-start | bytes 786440 | tf_op jit(solution)/shard_map/ppermute | solution.py:32
  7.1 11.9 %collective-permute-done = bf16[1,2,4,128,128]{4,3,2,1,0:T(8,128)(2,1)S(1)} collective-permute-done((bf16[1,2,4,128,128]{4,3,2,1,0:T(8,128)(2,1)S(1)}, bf16[1,2,4,128,128]{4,3,2,1,0:T(8,128)(2,1)S(1)}, u32[]{:S(2)}, u32[]{:S(2)}) %collective-permute-start) | collective-permute-done | bytes 262176 | tf_op jit(solution)/shard_map/ppermute | solution.py:32
  19.9 12.4 %collective-permute-done.1 = bf16[2,2,4,128,128]{4,3,2,1,0:T(8,128)(2,1)S(1)} collective-permute-done((bf16[2,2,4,128,128]{4,3,2,1,0:T(8,128)(2,1)S(1)}, bf16[2,2,4,128,128]{4,3,2,1,0:T(8,128)(2,1)S(1)}, u32[]{:S(2)}, u32[]{:S(2)}) %collective-permute-start.1) | collective-permute-done | bytes 524320 | tf_op jit(solution)/shard_map/ppermute | solution.py:32
  32.5 1.3 collective-permute-start.2
  33.8 22.1 %collective-permute-done.2 = bf16[4,2,4,128,128]{4,3,2,1,0:T(8,128)(2,1)S(1)} collective-permute-done((bf16[4,2,4,128,128]{4,3,2,1,0:T(8,128)(2,1)S(1)}, bf16[4,2,4,128,128]{4,3,2,1,0:T(8,128)(2,1)S(1)}, u32[]{:S(2)}, u32[]{:S(2)}) %collective-permute-start.2) | collective-permute-done | bytes 1048608 | tf_op jit(solution)/shard_map/ppermute | solution.py:32
  55.9 1.7 %maximum_select_fusion.1 = bf16[8,2,4,128,128]{4,3,2,1,0:T(8,128)(2,1)} fusion(bf16[4,2,4,128,128]{4,3,2,1,0:T(8,128)(2,1)S(1)} %maximum_select_fusion.2, bf16[4,2,4,128,128]{4,3,2,1,0:T(8,128)(2,1)S(1)} %collective-permute-done.2, pred[]{:T(512)S(6)} %eq.58), kind=kLoop, calls=%fused_computation.4 | loop fusion | flops 3145728 | bytes 4194305 | tf_op jit(solution)/shard_map/jit(_where)/select_n | solution.py:34
  58.5 3.6 %collective-permute-done.3 = bf16[8,2,4,128,128]{4,3,2,1,0:T(8,128)(2,1)} collective-permute-done((bf16[8,2,4,128,128]{4,3,2,1,0:T(8,128)(2,1)}, bf16[8,2,4,128,128]{4,3,2,1,0:T(8,128)(2,1)}, u32[]{:S(2)}, u32[]{:S(2)}) %collective-permute-start.3) | collective-permute-done | bytes 2097184 | tf_op jit(solution)/shard_map/ppermute | solution.py:22
  62.1 3.9 %pad_maximum_fusion = bf16[2,8,2,4,128,128]{5,4,3,2,1,0:T(8,128)(2,1)} fusion(bf16[1,8,2,4,128,128]{5,4,3,2,1,0:T(8,128)(2,1)} %bitcast.7, bf16[1,8,2,4,128,128]{5,4,3,2,1,0:T(8,128)(2,1)S(1)} %maximum_select_fusion), kind=kLoop, calls=%fused_computation.2 | loop fusion | flops 2097152 | bytes 8388608 | tf_op jit(solution)/shard_map/stack | solution.py:67
  66.0 3.0 %gather_fusion = bf16[32,128,128]{2,1,0:T(8,128)(2,1)S(1)} fusion(bf16[2,8,2,4,128,128]{5,4,3,2,1,0:T(8,128)(2,1)} %pad_maximum_fusion, s32[32]{0:T(128)S(1)} %get-tuple-element.27), kind=kCustom, calls=%fused_computation | custom fusion | bytes 2097664 | tf_op jit(solution)/shard_map/gather | solution.py:73
  69.0 1.6 %convolution_bitcast_fusion.1 = f32[128,8,128]{2,0,1:T(8,128)S(1)} fusion(bf16[8,4,128,128]{3,2,1,0:T(8,128)(2,1)S(1)} %bitcast.104, bf16[8,4,128,128]{3,2,1,0:T(8,128)(2,1)} %param.8), kind=kOutput, calls=%fused_computation.30 | convolution fusion | flops 134217728 | bytes 2621440 | tf_op jit(solution)/shard_map/rkti,rkio->tro/dot_general | solution.py:107
  71.1 2.2 %copy.93 = bf16[128,32,128]{2,1,0:T(8,128)(2,1)} copy(f32[128,32,128]{2,0,1:T(8,128)S(1)} %bitcast.97) | data formatting | bytes 3145728 | tf_op jit(solution)/shard_map/reshape | solution.py:91
  73.3 2.2 %subtract_convert_fusion.1 = bf16[128,32,128]{2,1,0:T(8,128)(2,1)} fusion(f32[128,32,128]{2,0,1:T(8,128)S(1)} %bitcast.98), kind=kLoop, calls=%fused_computation.23 | loop fusion | flops 2097152 | bytes 3145728 | tf_op jit(solution)/shard_map/convert_element_type | solution.py:93
  75.5 3.9 %gather_fusion.1 = bf16[32,128,128]{2,1,0:T(8,128)(2,1)} fusion(bf16[2,8,2,4,128,128]{5,4,3,2,1,0:T(8,128)(2,1)} %pad_maximum_fusion, s32[32]{0:T(128)S(1)} %get-tuple-element.26), kind=kCustom, calls=%fused_computation.1 | custom fusion | bytes 2097664 | tf_op jit(solution)/shard_map/gather | solution.py:73
  79.3 1.8 %fusion.13 = bf16[128,8,128,1]{2,0,3,1:T(8,128)(2,1)S(1)} fusion(bf16[8,4,128,128]{3,2,1,0:T(8,128)(2,1)} %bitcast.107, bf16[8,4,128,128]{3,2,1,0:T(8,128)(2,1)S(1)} %copy-done, f32[128,8,128]{2,0,1:T(8,128)S(1)} %convolution_bitcast_fusion.1), kind=kOutput, calls=%fused_computation.33 | convolution fusion | flops 135528448 | bytes 2883584 | tf_op jit(solution)/shard_map/rkto,rkio->tri/dot_general | solution.py:115
  81.6 1.2 copy.92
  82.8 1.2 subtract_convert_fusion
  85.1 1.0 constant_dynamic-slice_fusion.3
  86.7 0.9 fusion.4
  87.6 1.0 constant_dynamic-slice_fusion.1
  89.5 1.3 collective-permute-done.4
  91.3 2.4 %collective-permute-done.5 = f32[8,4,128,128]{3,1,2,0:T(4,128)S(1)} collective-permute-done((f32[8,4,128,128]{3,1,2,0:T(4,128)S(1)}, f32[8,4,128,128]{3,1,2,0:T(4,128)S(1)}, u32[]{:S(2)}, u32[]{:S(2)}) %collective-permute-start.5) | collective-permute-done | bytes 2097184 | tf_op jit(solution)/shard_map/ppermute | solution.py:22
  94.4 2.8 %pad_maximum_fusion.1 = bf16[8,2,4,128,128]{4,2,3,1,0:T(4,128)(2,1)} fusion(bf16[8,1,4,128,128]{4,2,3,1,0:T(4,128)(2,1)S(1)} %fusion.15, bf16[8,1,4,128,128]{4,2,3,1,0:T(4,128)(2,1)S(1)} %fusion.14), kind=kLoop, calls=%fused_computation.13 | loop fusion | flops 1048576 | bytes 4194304 | tf_op jit(solution)/shard_map/stack | solution.py:119
  97.1 7.3 %all-to-all-start = ((bf16[8,2,4,128,128]{4,2,3,1,0:T(4,128)(2,1)}), bf16[8,2,4,128,128]{4,2,3,1,0:T(4,128)(2,1)}, u32[]{:S(2)}, u32[]{:S(2)}) async-start(bf16[8,2,4,128,128]{4,2,3,1,0:T(4,128)(2,1)} %pad_maximum_fusion.1), calls=%async_computation | async-start | bytes 4194304 | tf_op jit(solution)/shard_map/all_to_all | solution.py:119
  104.4 1.7 %fusion.10 = bf16[8,4,128,128]{2,3,1,0:T(8,128)(2,1)S(1)} fusion(bf16[8,4,128,128]{3,2,1,0:T(8,128)(2,1)} %bitcast.108, f32[128,8,128]{2,0,1:T(8,128)S(1)} %convolution_bitcast_fusion.1), kind=kOutput, calls=%fused_computation.28 | convolution fusion | flops 135397376 | bytes 2621440 | tf_op jit(solution)/shard_map/tri,rkto->rkio/dot_general | solution.py:112
  106.2 1.6 collective-permute-start.7
  108.8 23.4 %collective-permute-done.7 = bf16[8,4,128,128]{2,3,1,0:T(8,128)(2,1)S(1)} collective-permute-done((bf16[8,4,128,128]{2,3,1,0:T(8,128)(2,1)S(1)}, bf16[8,4,128,128]{2,3,1,0:T(8,128)(2,1)S(1)}, u32[]{:S(2)}, u32[]{:S(2)}) %collective-permute-start.7) | collective-permute-done | bytes 1048608 | tf_op jit(solution)/shard_map/ppermute | solution.py:84
  132.7 1.3 copy.65
  134.0 19.8 %collective-permute-done.6 = bf16[8,4,128,128]{3,2,1,0:T(8,128)(2,1)} collective-permute-done((bf16[8,4,128,128]{3,2,1,0:T(8,128)(2,1)S(1)}, bf16[8,4,128,128]{3,2,1,0:T(8,128)(2,1)}, u32[]{:S(2)}, u32[]{:S(2)}) %collective-permute-start.6) | collective-permute-done | bytes 1048608 | tf_op jit(solution)/shard_map/ppermute | solution.py:84
  153.7 2.7 %add_convert_fusion.1 = bf16[8,4,128,128]{3,2,1,0:T(8,128)(2,1)} fusion(bf16[8,4,128,128]{3,2,1,0:T(8,128)(2,1)} %collective-permute-done.6, bf16[8,4,128,128]{3,2,1,0:T(8,128)(2,1)S(1)} %convolution_convert_fusion.1), kind=kLoop, calls=%fused_computation.21 | loop fusion | flops 2097152 | bytes 3145728 | tf_op jit(solution)/shard_map/convert_element_type | solution.py:85
  156.4 2.6 %slice_reduce_fusion = (bf16[4,128,128]{2,0,1:T(4,128)(2,1)S(1)}, bf16[4,128,128]{2,0,1:T(4,128)(2,1)S(1)}) fusion(bf16[8,2,4,128,128]{4,2,3,1,0:T(4,128)(2,1)} %all-to-all-done), kind=kLoop, calls=%fused_computation.36 | loop fusion | flops 917504 | bytes 2359296 | tf_op jit(solution)/shard_map/reduce_sum | solution.py:104
  (45 shorter events, 9.4 us)
Async XLA Ops:
  0.6 70.0 %copy-start = (bf16[8,4,128,128]{3,2,1,0:T(8,128)(2,1)S(1)}, bf16[8,4,128,128]{3,2,1,0:T(8,128)(2,1)}, u32[]{:S(2)}) copy-start(bf16[8,4,128,128]{3,2,1,0:T(8,128)(2,1)} %param.10) | copy-start | bytes 3145732
  3.0 16.0 %collective-permute-start = (bf16[1,2,4,128,128]{4,3,2,1,0:T(8,128)(2,1)S(1)}, bf16[1,2,4,128,128]{4,3,2,1,0:T(8,128)(2,1)S(1)}, u32[]{:S(2)}, u32[]{:S(2)}) collective-permute-start(bf16[1,2,4,128,128]{4,3,2,1,0:T(8,128)(2,1)S(1)} %bitcast.112), channel_id=1, source_target_pairs={{0,8},{2,10},{4,12},{6,14},{8,0},{10,2},{12,4},{14,6},{1,9},{3,11}... | collective-permute-start | bytes 786440 | tf_op jit(solution)/shard_map/ppermute | solution.py:32
  19.1 13.2 %collective-permute-start.1 = (bf16[2,2,4,128,128]{4,3,2,1,0:T(8,128)(2,1)S(1)}, bf16[2,2,4,128,128]{4,3,2,1,0:T(8,128)(2,1)S(1)}, u32[]{:S(2)}, u32[]{:S(2)}) collective-permute-start(bf16[2,2,4,128,128]{4,3,2,1,0:T(8,128)(2,1)S(1)} %maximum_select_fusion.3), channel_id=1, source_target_pairs={{0,4},{2,6},{4,0},{6,2},{8,12},{10,14},{12,8},{14,10},{1,5},{3,7},... | collective-permute-start | bytes 1572872 | tf_op jit(solution)/shard_map/ppermute | solution.py:32
  32.5 23.5 %collective-permute-start.2 = (bf16[4,2,4,128,128]{4,3,2,1,0:T(8,128)(2,1)S(1)}, bf16[4,2,4,128,128]{4,3,2,1,0:T(8,128)(2,1)S(1)}, u32[]{:S(2)}, u32[]{:S(2)}) collective-permute-start(bf16[4,2,4,128,128]{4,3,2,1,0:T(8,128)(2,1)S(1)} %maximum_select_fusion.2), channel_id=1, source_target_pairs={{0,2},{2,0},{4,6},{6,4},{8,10},{10,8},{12,14},{14,12},{1,3},{3,1},... | collective-permute-start | bytes 3145736 | tf_op jit(solution)/shard_map/ppermute | solution.py:32
  33.8 23.8 %copy-start.5 = (s32[8,4]{0,1:T(4,128)S(1)}, s32[8,4]{0,1:T(4,128)}, u32[]{:S(2)}) copy-start(s32[8,4]{0,1:T(4,128)} %param.11) | copy-start | bytes 388
  33.8 24.1 %copy-start.6 = (s32[8,4]{0,1:T(4,128)S(1)}, s32[8,4]{0,1:T(4,128)}, u32[]{:S(2)}) copy-start(s32[8,4]{0,1:T(4,128)} %param.9) | copy-start | bytes 388
  57.6 4.5 %collective-permute-start.3 = (bf16[8,2,4,128,128]{4,3,2,1,0:T(8,128)(2,1)}, bf16[8,2,4,128,128]{4,3,2,1,0:T(8,128)(2,1)}, u32[]{:S(2)}, u32[]{:S(2)}) collective-permute-start(bf16[8,2,4,128,128]{4,3,2,1,0:T(8,128)(2,1)} %maximum_select_fusion.1), channel_id=1, source_target_pairs={{0,1},{1,0},{2,3},{3,2},{4,5},{5,4},{6,7},{7,6},{8,9},{9,8},{10,11... | collective-permute-start | bytes 6291464 | tf_op jit(solution)/shard_map/ppermute | solution.py:22
  79.3 1.8 %copy-start.2 = (bf16[8,4,128,128]{3,2,1,0:T(8,128)(2,1)S(1)}, bf16[8,4,128,128]{3,2,1,0:T(8,128)(2,1)}, u32[]{:S(2)}) copy-start(bf16[8,4,128,128]{3,2,1,0:T(8,128)(2,1)} %param.8) | copy-start | bytes 3145732
  82.8 1.2 copy-start.3
  82.8 1.5 copy-start.4
  86.5 4.2 %collective-permute-start.4 = (f32[8,4,128,128]{3,1,2,0:T(4,128)S(1)}, f32[8,4,128,128]{3,1,2,0:T(4,128)S(1)}, u32[]{:S(2)}, u32[]{:S(2)}) collective-permute-start(f32[8,4,128,128]{3,1,2,0:T(4,128)S(1)} %bitcast.109), channel_id=1, source_target_pairs={{0,1},{1,0},{2,3},{3,2},{4,5},{5,4},{6,7},{7,6},{8,9},{9,8},{10,11... | collective-permute-start | bytes 6291464 | tf_op jit(solution)/shard_map/ppermute | solution.py:22
  89.0 4.7 %collective-permute-start.5 = (f32[8,4,128,128]{3,1,2,0:T(4,128)S(1)}, f32[8,4,128,128]{3,1,2,0:T(4,128)S(1)}, u32[]{:S(2)}, u32[]{:S(2)}) collective-permute-start(f32[8,4,128,128]{3,1,2,0:T(4,128)S(1)} %bitcast.110), channel_id=1, source_target_pairs={{0,1},{1,0},{2,3},{3,2},{4,5},{5,4},{6,7},{7,6},{8,9},{9,8},{10,11... | collective-permute-start | bytes 6291464 | tf_op jit(solution)/shard_map/ppermute | solution.py:22
  97.1 59.3 %all-to-all-start = ((bf16[8,2,4,128,128]{4,2,3,1,0:T(4,128)(2,1)}), bf16[8,2,4,128,128]{4,2,3,1,0:T(4,128)(2,1)}, u32[]{:S(2)}, u32[]{:S(2)}) async-start(bf16[8,2,4,128,128]{4,2,3,1,0:T(4,128)(2,1)} %pad_maximum_fusion.1), calls=%async_computation | async-start | bytes 4194304 | tf_op jit(solution)/shard_map/all_to_all | solution.py:119
  106.2 26.1 %collective-permute-start.7 = (bf16[8,4,128,128]{2,3,1,0:T(8,128)(2,1)S(1)}, bf16[8,4,128,128]{2,3,1,0:T(8,128)(2,1)S(1)}, u32[]{:S(2)}, u32[]{:S(2)}) collective-permute-start(bf16[8,4,128,128]{2,3,1,0:T(8,128)(2,1)S(1)} %fusion.10), channel_id=1, source_target_pairs={{0,16},{16,0},{1,17},{17,1},{2,18},{18,2},{3,19},{19,3},{4,20},{20... | collective-permute-start | bytes 3145736 | tf_op jit(solution)/shard_map/ppermute | solution.py:84
  108.2 45.5 %collective-permute-start.6 = (bf16[8,4,128,128]{3,2,1,0:T(8,128)(2,1)S(1)}, bf16[8,4,128,128]{3,2,1,0:T(8,128)(2,1)}, u32[]{:S(2)}, u32[]{:S(2)}) collective-permute-start(bf16[8,4,128,128]{3,2,1,0:T(8,128)(2,1)S(1)} %convolution_convert_fusion.1), channel_id=1, source_target_pairs={{0,16},{16,0},{1,17},{17,1},{2,18},{18,2},{3,19},{19,3},{4,20},{20... | collective-permute-start | bytes 3145736 | tf_op jit(solution)/shard_map/ppermute | solution.py:84
  153.7 6.6 %copy-start.1 = (bf16[8,4,128,128]{3,2,1,0:T(8,128)(2,1)S(1)}, bf16[8,4,128,128]{3,2,1,0:T(8,128)(2,1)}, u32[]{:S(2)}) copy-start(bf16[8,4,128,128]{3,2,1,0:T(8,128)(2,1)} %param.10) | copy-start | bytes 3145732

commit v14 on v12

--- a/solution.py
+++ b/solution.py
@@ -22,18 +22,36 @@
     return lax.ppermute(x, "core", perm=[(0, 1), (1, 0)])
 
 
-def gather_chips(x, chips):
-    if chips & (chips - 1):
+def chip_orders(chips):
+    if chips & (chips - 1) or chips < 2:
+        return None, None
+    steps = []
+    step = chips // 2
+    while step >= 1:
+        steps.append(step)
+        step //= 2
+    return steps, steps[:1] + steps[1:][::-1]
+
+
+def gather_chips(x, chips, order):
+    if order is None:
         return lax.all_gather(x, "chip", axis=0, tiled=False)
     me = lax.axis_index("chip")
     held = x[None]
-    step = 1
-    while step < chips:
+    for step in order:
         got = lax.ppermute(held, "chip", perm=[(i, i ^ step) for i in range(chips)])
         upper = (me // step) % 2 == 1
         held = jnp.where(upper, jnp.concatenate([got, held], axis=0), jnp.concatenate([held, got], axis=0))
-        step *= 2
     return held
+
+
+def chip_slot(chip, order):
+    if order is None:
+        return chip
+    slot = jnp.zeros_like(chip)
+    for k, step in enumerate(order):
+        slot = slot + ((chip // step) % 2) * (1 << k)
+    return slot
 
 
 def per_device(inputs, out_grad, w_in, in_blocks, w_out, out_blocks):
@@ -49,23 +67,24 @@
     col_count = chips * pair * own_blocks
     core = lax.axis_index("core")
 
-    both = jnp.concatenate([inputs, out_grad], axis=1).reshape(tok_rows, 2, own_blocks, block_size)
-    both = both.transpose(1, 2, 0, 3)
-    mine = gather_chips(both, chips)
-    other = swap_core(mine)
-    sets = jnp.stack([mine, other], axis=0)
+    order_in, order_grad = chip_orders(chips)
 
-    def select(flat, which):
+    def gather(x, order):
+        x = x.reshape(tok_rows, own_blocks, block_size).transpose(1, 0, 2)
+        mine = gather_chips(x, chips, order)
+        return jnp.stack([mine, swap_core(mine)], axis=0)
+
+    def select(sets, flat, order):
         owner = flat // own_blocks
         sub = flat % own_blocks
         side = (owner % pair != core).astype(jnp.int32)
-        sel = sets[side, owner // pair, which, sub]
+        sel = sets[side, chip_slot(owner // pair, order), sub]
         return sel.reshape(hid_rows, per_row, tok_rows, block_size)
 
     in_flat = in_blocks.reshape(pair_count)
     out_flat = out_blocks.reshape(pair_count)
-    in_sel = select(in_flat, 0)
-    grad_sel = select(out_flat, 1)
+    in_sel = select(gather(inputs, order_in), in_flat, order_in)
+    grad_sel = select(gather(out_grad, order_grad), out_flat, order_grad)
 
     def dp_total(part):
         part = part.astype(jnp.bfloat16)

time: 176 us -> 154 us (0.88)
  waiting for transfers between devices: 112 us -> 80.8 us
  starting transfers between devices: 15.5 us -> 25.7 us
  other arithmetic: 19.2 us -> 21.1 us
    ppermute x3 -> x6, waiting for transfers between devices: 61.9 us -> 31.8 us  [gather_chips(): got = lax.ppermute(held, 'chip', perm=[(i, i ^ step) for i in range(chips)])]
    ppermute x3 -> x6, starting transfers between devices: 7.45 us -> 12.8 us  [gather_chips(): got = lax.ppermute(held, 'chip', perm=[(i, i ^ step) for i in range(chips)])]
    all_to_all x1, starting transfers between devices: 5.3 us -> 10.1 us  [per_device(): lax.all_to_all(jnp.stack([out_send, in_send], axis=1), 'chip', split_axis...]
    another operation x1 -> x2, other arithmetic: 3.93 us -> 5.52 us  [gather(): return jnp.stack([mine, swap_core(mine)], axis=0)]
    ppermute x3 -> x4, waiting for transfers between devices: 7.29 us -> 5.71 us  [swap_core(): return lax.ppermute(x, 'core', perm=[(0, 1), (1, 0)])]
    select_n x4 -> x8, other arithmetic: 2.22 us -> 3.79 us  [gather_chips(): jnp.where(upper, jnp.concatenate([got, held], axis=0), jnp.concatenate([h...]
    unnamed x21 -> x25, local copies, waits for them, and re-layouts: 5.28 us -> 5.76 us
  transfers between devices with their start and end apart: 9 -> 13, of which waited for: 8 -> 8; matrix products, arithmetic and copies ran while one was open for 6% -> 14% of each run, Pallas kernels for 0% -> 0%
where the time goes in v14:
time: 154 us
  waiting for transfers between devices  80.8 us (52%)
  starting transfers between devices  25.7 us (17%)
  other arithmetic  21.1 us (14%)
  local copies, waits for them, and re-layouts  18.5 us (12%)
  matrix products  6.77 us (4%)
    ppermute x2, waiting for transfers between devices, dp_total(): got = lax.ppermute(part, 'dp', perm=[(0, 1), (1, 0)])  43.3 us
    ppermute x6, waiting for transfers between devices, gather_chips(): got = lax.ppermute(held, 'chip', perm=[(i, i ^ step) for i in range(chips)])  31.8 us
    ppermute x6, starting transfers between devices, gather_chips(): got = lax.ppermute(held, 'chip', perm=[(i, i ^ step) for i in range(chips)])  12.8 us
    all_to_all x1, starting transfers between devices, per_device(): lax.all_to_all(jnp.stack([out_send, in_send], axis=1), 'chip', split_axis...  10.1 us
    unnamed x25, local copies, waits for them, and re-layouts  5.76 us
    ppermute x4, waiting for transfers between devices, swap_core(): return lax.ppermute(x, 'core', perm=[(0, 1), (1, 0)])  5.71 us
    gather x2, local copies, waits for them, and re-layouts, select(): sel = sets[side, chip_slot(owner // pair, order), sub]  5.61 us
    another operation x2, other arithmetic, gather(): return jnp.stack([mine, swap_core(mine)], axis=0)  5.52 us
  transfers between devices with their start and end apart: 13, of which 8 were waited for; matrix products, arithmetic and copies ran while one was open for 14% of the time, Pallas kernels for 0%

profile of v14, /device:TPU:0, one launch (start us, length us, event | category | flops | bytes accessed | tf_op | source)
XLA Modules:
  0.0 153.7 jit_solution(12352108057994317933)
XLA Ops:
  1.9 4.1 %collective-permute-start = (bf16[1,4,128,128]{3,2,1,0:T(8,128)(2,1)S(1)}, bf16[1,4,128,128]{3,2,1,0:T(8,128)(2,1)S(1)}, u32[]{:S(2)}, u32[]{:S(2)}) collective-permute-start(bf16[1,4,128,128]{3,2,1,0:T(8,128)(2,1)S(1)} %bitcast.120), channel_id=1, source_target_pairs={{0,8},{2,10},{4,12},{6,14},{8,0},{10,2},{12,4},{14,6},{1,9},{3,11}... | collective-permute-start | bytes 393224 | tf_op jit(solution)/shard_map/ppermute | solution.py:42
  6.0 6.3 %collective-permute-done = bf16[1,4,128,128]{3,2,1,0:T(8,128)(2,1)S(1)} collective-permute-done((bf16[1,4,128,128]{3,2,1,0:T(8,128)(2,1)S(1)}, bf16[1,4,128,128]{3,2,1,0:T(8,128)(2,1)S(1)}, u32[]{:S(2)}, u32[]{:S(2)}) %collective-permute-start) | collective-permute-done | bytes 131104 | tf_op jit(solution)/shard_map/ppermute | solution.py:42
  14.3 3.4 %collective-permute-start.5 = (bf16[1,4,128,128]{3,2,1,0:T(8,128)(2,1)S(1)}, bf16[1,4,128,128]{3,2,1,0:T(8,128)(2,1)S(1)}, u32[]{:S(2)}, u32[]{:S(2)}) collective-permute-start(bf16[1,4,128,128]{3,2,1,0:T(8,128)(2,1)S(1)} %bitcast.122), channel_id=1, source_target_pairs={{0,8},{2,10},{4,12},{6,14},{8,0},{10,2},{12,4},{14,6},{1,9},{3,11}... | collective-permute-start | bytes 393224 | tf_op jit(solution)/shard_map/ppermute | solution.py:42
  17.8 5.0 %collective-permute-done.1 = bf16[2,4,128,128]{3,2,1,0:T(8,128)(2,1)S(1)} collective-permute-done((bf16[2,4,128,128]{3,2,1,0:T(8,128)(2,1)S(1)}, bf16[2,4,128,128]{3,2,1,0:T(8,128)(2,1)S(1)}, u32[]{:S(2)}, u32[]{:S(2)}) %collective-permute-start.1) | collective-permute-done | bytes 262176 | tf_op jit(solution)/shard_map/ppermute | solution.py:42
  22.8 1.3 collective-permute-start.2
  25.4 12.5 %collective-permute-done.6 = bf16[2,4,128,128]{3,2,1,0:T(8,128)(2,1)S(1)} collective-permute-done((bf16[2,4,128,128]{3,2,1,0:T(8,128)(2,1)S(1)}, bf16[2,4,128,128]{3,2,1,0:T(8,128)(2,1)S(1)}, u32[]{:S(2)}, u32[]{:S(2)}) %collective-permute-start.6) | collective-permute-done | bytes 262176 | tf_op jit(solution)/shard_map/ppermute | solution.py:42
  38.0 2.3 %collective-permute-start.7 = (bf16[4,4,128,128]{3,2,1,0:T(8,128)(2,1)S(1)}, bf16[4,4,128,128]{3,2,1,0:T(8,128)(2,1)S(1)}, u32[]{:S(2)}, u32[]{:S(2)}) collective-permute-start(bf16[4,4,128,128]{3,2,1,0:T(8,128)(2,1)S(1)} %maximum_select_fusion.5), channel_id=1, source_target_pairs={{0,4},{2,6},{4,0},{6,2},{8,12},{10,14},{12,8},{14,10},{1,5},{3,7},... | collective-permute-start | bytes 1572872 | tf_op jit(solution)/shard_map/ppermute | solution.py:42
  40.3 1.1 maximum_select_fusion.1
  41.7 8.0 %collective-permute-done.7 = bf16[4,4,128,128]{3,2,1,0:T(8,128)(2,1)S(1)} collective-permute-done((bf16[4,4,128,128]{3,2,1,0:T(8,128)(2,1)S(1)}, bf16[4,4,128,128]{3,2,1,0:T(8,128)(2,1)S(1)}, u32[]{:S(2)}, u32[]{:S(2)}) %collective-permute-start.7) | collective-permute-done | bytes 524320 | tf_op jit(solution)/shard_map/ppermute | solution.py:42
  49.7 1.1 maximum_select_fusion.3
  51.0 1.1 maximum_select_fusion.2
  52.1 2.8 %pad_maximum_fusion = bf16[2,8,4,128,128]{4,3,2,1,0:T(8,128)(2,1)} fusion(bf16[1,8,4,128,128]{4,3,2,1,0:T(8,128)(2,1)} %bitcast.7, bf16[1,8,4,128,128]{4,3,2,1,0:T(8,128)(2,1)S(1)} %maximum_select_fusion), kind=kLoop, calls=%fused_computation.2 | loop fusion | flops 1048576 | bytes 4194304 | tf_op jit(solution)/shard_map/stack | solution.py:75
  54.9 2.4 %gather_fusion = bf16[32,128,128]{2,1,0:T(8,128)(2,1)S(1)} fusion(bf16[2,8,4,128,128]{4,3,2,1,0:T(8,128)(2,1)} %pad_maximum_fusion, s32[32]{0:T(128)S(1)} %fusion.54), kind=kCustom, calls=%fused_computation | custom fusion | bytes 2097536 | tf_op jit(solution)/shard_map/gather | solution.py:81
  57.3 1.6 %convolution_bitcast_fusion.1 = f32[128,8,128]{2,0,1:T(8,128)S(1)} fusion(bf16[8,4,128,128]{3,2,1,0:T(8,128)(2,1)S(1)} %bitcast.110, bf16[8,4,128,128]{3,2,1,0:T(8,128)(2,1)} %param.8), kind=kOutput, calls=%fused_computation.29 | convolution fusion | flops 134217728 | bytes 2621440 | tf_op jit(solution)/shard_map/rkti,rkio->tro/dot_general | solution.py:115
  59.3 2.2 %copy.95 = bf16[128,32,128]{2,1,0:T(8,128)(2,1)} copy(f32[128,32,128]{2,0,1:T(8,128)S(1)} %bitcast.104) | data formatting | bytes 3145728 | tf_op jit(solution)/shard_map/reshape | solution.py:99
  61.5 2.2 %subtract_convert_fusion.1 = bf16[128,32,128]{2,1,0:T(8,128)(2,1)} fusion(f32[128,32,128]{2,0,1:T(8,128)S(1)} %bitcast.105), kind=kLoop, calls=%fused_computation.22 | loop fusion | flops 2097152 | bytes 3145728 | tf_op jit(solution)/shard_map/convert_element_type | solution.py:101
  63.8 2.8 %pad_maximum_fusion.1 = bf16[2,8,4,128,128]{4,3,2,1,0:T(8,128)(2,1)} fusion(bf16[1,8,4,128,128]{4,3,2,1,0:T(8,128)(2,1)} %bitcast.30, bf16[1,8,4,128,128]{4,3,2,1,0:T(8,128)(2,1)S(1)} %copy-done.6), kind=kLoop, calls=%fused_computation.7 | loop fusion | flops 1048576 | bytes 4194304 | tf_op jit(solution)/shard_map/stack | solution.py:75
  66.5 3.3 %gather_fusion.1 = bf16[32,128,128]{2,1,0:T(8,128)(2,1)} fusion(bf16[2,8,4,128,128]{4,3,2,1,0:T(8,128)(2,1)} %pad_maximum_fusion.1, s32[32]{0:T(128)S(1)} %fusion.53), kind=kCustom, calls=%fused_computation.1 | custom fusion | bytes 2097536 | tf_op jit(solution)/shard_map/gather | solution.py:81
  69.8 1.8 %fusion.13 = bf16[128,8,128,1]{2,0,3,1:T(8,128)(2,1)S(1)} fusion(bf16[8,4,128,128]{3,2,1,0:T(8,128)(2,1)} %bitcast.114, bf16[8,4,128,128]{3,2,1,0:T(8,128)(2,1)S(1)} %copy-done, f32[128,8,128]{2,0,1:T(8,128)S(1)} %convolution_bitcast_fusion.1), kind=kOutput, calls=%fused_computation.32 | convolution fusion | flops 135528448 | bytes 2883584 | tf_op jit(solution)/shard_map/rkto,rkio->tri/dot_general | solution.py:123
  72.0 1.2 subtract_convert_fusion
  73.2 1.2 copy.94
  76.7 2.3 %constant_dynamic-slice_fusion.1 = (f32[8,1,4,128,128]{4,2,1,0,3:T(4,128)S(1)}, f32[8,1,4,128,128]{4,2,1,0,3:T(4,128)S(1)}, f32[8,1,4,128,128]{4,2,1,0,3:T(4,128)S(1)}, f32[8,1,4,128,128]{4,2,1,0,3:T(4,128)S(1)}) fusion(f32[8,2,4,128,128]{4,2,1,0,3:T(4,128)S(1)} %bitcast.108, s32[]{:T(128)S(6)} %select_n.412, s32[]{:T(128)S(6)} %select_n.413, ...), kind=kLoop, calls=%fused_computation.110 | loop fusion | bytes 16777224 | tf_op jit(solution)/shard_map/jit(dynamic_index_in_dim)/dynamic_slice | solution.py:107
  80.5 3.3 %collective-permute-done.4 = f32[8,4,128,128]{3,1,2,0:T(4,128)S(1)} collective-permute-done((f32[8,4,128,128]{3,1,2,0:T(4,128)S(1)}, f32[8,4,128,128]{3,1,2,0:T(4,128)S(1)}, u32[]{:S(2)}, u32[]{:S(2)}) %collective-permute-start.4) | collective-permute-done | bytes 2097184 | tf_op jit(solution)/shard_map/ppermute | solution.py:22
  84.5 2.4 %collective-permute-done.9 = f32[8,4,128,128]{3,1,2,0:T(4,128)S(1)} collective-permute-done((f32[8,4,128,128]{3,1,2,0:T(4,128)S(1)}, f32[8,4,128,128]{3,1,2,0:T(4,128)S(1)}, u32[]{:S(2)}, u32[]{:S(2)}) %collective-permute-start.9) | collective-permute-done | bytes 2097184 | tf_op jit(solution)/shard_map/ppermute | solution.py:22
  87.4 2.8 %pad_maximum_fusion.2 = bf16[8,2,4,128,128]{4,2,3,1,0:T(4,128)(2,1)} fusion(bf16[8,1,4,128,128]{4,2,3,1,0:T(4,128)(2,1)S(1)} %fusion.15, bf16[8,1,4,128,128]{4,2,3,1,0:T(4,128)(2,1)S(1)} %fusion.14), kind=kLoop, calls=%fused_computation.12 | loop fusion | flops 1048576 | bytes 4194304 | tf_op jit(solution)/shard_map/stack | solution.py:127
  90.2 10.1 %all-to-all-start = ((bf16[8,2,4,128,128]{4,2,3,1,0:T(4,128)(2,1)}), bf16[8,2,4,128,128]{4,2,3,1,0:T(4,128)(2,1)}, u32[]{:S(2)}, u32[]{:S(2)}) async-start(bf16[8,2,4,128,128]{4,2,3,1,0:T(4,128)(2,1)} %pad_maximum_fusion.2), calls=%async_computation | async-start | bytes 4194304 | tf_op jit(solution)/shard_map/all_to_all | solution.py:127
  100.7 1.6 %collective-permute-start.11 = (bf16[8,4,128,128]{2,3,1,0:T(8,128)(2,1)S(1)}, bf16[8,4,128,128]{2,3,1,0:T(8,128)(2,1)S(1)}, u32[]{:S(2)}, u32[]{:S(2)}) collective-permute-start(bf16[8,4,128,128]{2,3,1,0:T(8,128)(2,1)S(1)} %fusion.10), channel_id=1, source_target_pairs={{0,16},{16,0},{1,17},{17,1},{2,18},{18,2},{3,19},{19,3},{4,20},{20... | collective-permute-start | bytes 3145736 | tf_op jit(solution)/shard_map/ppermute | solution.py:92
  103.4 23.4 %collective-permute-done.11 = bf16[8,4,128,128]{2,3,1,0:T(8,128)(2,1)S(1)} collective-permute-done((bf16[8,4,128,128]{2,3,1,0:T(8,128)(2,1)S(1)}, bf16[8,4,128,128]{2,3,1,0:T(8,128)(2,1)S(1)}, u32[]{:S(2)}, u32[]{:S(2)}) %collective-permute-start.11) | collective-permute-done | bytes 1048608 | tf_op jit(solution)/shard_map/ppermute | solution.py:92
  127.3 1.3 copy.67
  128.6 19.9 %collective-permute-done.10 = bf16[8,4,128,128]{3,2,1,0:T(8,128)(2,1)S(1)} collective-permute-done((bf16[8,4,128,128]{3,2,1,0:T(8,128)(2,1)S(1)}, bf16[8,4,128,128]{3,2,1,0:T(8,128)(2,1)S(1)}, u32[]{:S(2)}, u32[]{:S(2)}) %collective-permute-start.10) | collective-permute-done | bytes 1048608 | tf_op jit(solution)/shard_map/ppermute | solution.py:92
  148.4 1.3 add_convert_fusion.1
  149.8 2.6 %slice_reduce_fusion = (bf16[4,128,128]{2,0,1:T(4,128)(2,1)S(1)}, bf16[4,128,128]{2,0,1:T(4,128)(2,1)S(1)}) fusion(bf16[8,2,4,128,128]{4,2,3,1,0:T(4,128)(2,1)} %all-to-all-done), kind=kLoop, calls=%fused_computation.35 | loop fusion | flops 917504 | bytes 2359296 | tf_op jit(solution)/shard_map/reduce_sum | solution.py:112
  (62 shorter events, 14.1 us)
Async XLA Ops:
  0.6 58.3 %copy-start = (bf16[8,4,128,128]{3,2,1,0:T(8,128)(2,1)S(1)}, bf16[8,4,128,128]{3,2,1,0:T(8,128)(2,1)}, u32[]{:S(2)}) copy-start(bf16[8,4,128,128]{3,2,1,0:T(8,128)(2,1)} %param.10) | copy-start | bytes 3145732
  0.6 24.4 %copy-start.7 = (s32[8,4]{0,1:T(4,128)S(1)}, s32[8,4]{0,1:T(4,128)}, u32[]{:S(2)}) copy-start(s32[8,4]{0,1:T(4,128)} %param.9) | copy-start | bytes 388
  0.7 24.5 %copy-start.8 = (s32[8,4]{0,1:T(4,128)S(1)}, s32[8,4]{0,1:T(4,128)}, u32[]{:S(2)}) copy-start(s32[8,4]{0,1:T(4,128)} %param.11) | copy-start | bytes 388
  1.9 10.4 %collective-permute-start = (bf16[1,4,128,128]{3,2,1,0:T(8,128)(2,1)S(1)}, bf16[1,4,128,128]{3,2,1,0:T(8,128)(2,1)S(1)}, u32[]{:S(2)}, u32[]{:S(2)}) collective-permute-start(bf16[1,4,128,128]{3,2,1,0:T(8,128)(2,1)S(1)} %bitcast.120), channel_id=1, source_target_pairs={{0,8},{2,10},{4,12},{6,14},{8,0},{10,2},{12,4},{14,6},{1,9},{3,11}... | collective-permute-start | bytes 393224 | tf_op jit(solution)/shard_map/ppermute | solution.py:42
  12.4 10.4 %collective-permute-start.1 = (bf16[2,4,128,128]{3,2,1,0:T(8,128)(2,1)S(1)}, bf16[2,4,128,128]{3,2,1,0:T(8,128)(2,1)S(1)}, u32[]{:S(2)}, u32[]{:S(2)}) collective-permute-start(bf16[2,4,128,128]{3,2,1,0:T(8,128)(2,1)S(1)} %maximum_select_fusion.6), channel_id=1, source_target_pairs={{0,4},{2,6},{4,0},{6,2},{8,12},{10,14},{12,8},{14,10},{1,5},{3,7},... | collective-permute-start | bytes 786440 | tf_op jit(solution)/shard_map/ppermute | solution.py:42
  14.3 9.8 %collective-permute-start.5 = (bf16[1,4,128,128]{3,2,1,0:T(8,128)(2,1)S(1)}, bf16[1,4,128,128]{3,2,1,0:T(8,128)(2,1)S(1)}, u32[]{:S(2)}, u32[]{:S(2)}) collective-permute-start(bf16[1,4,128,128]{3,2,1,0:T(8,128)(2,1)S(1)} %bitcast.122), channel_id=1, source_target_pairs={{0,8},{2,10},{4,12},{6,14},{8,0},{10,2},{12,4},{14,6},{1,9},{3,11}... | collective-permute-start | bytes 393224 | tf_op jit(solution)/shard_map/ppermute | solution.py:42
  22.8 17.5 %collective-permute-start.2 = (bf16[4,4,128,128]{3,2,1,0:T(8,128)(2,1)S(1)}, bf16[4,4,128,128]{3,2,1,0:T(8,128)(2,1)S(1)}, u32[]{:S(2)}, u32[]{:S(2)}) collective-permute-start(bf16[4,4,128,128]{3,2,1,0:T(8,128)(2,1)S(1)} %maximum_select_fusion.4), channel_id=1, source_target_pairs={{0,2},{2,0},{4,6},{6,4},{8,10},{10,8},{12,14},{14,12},{1,3},{3,1},... | collective-permute-start | bytes 1572872 | tf_op jit(solution)/shard_map/ppermute | solution.py:42
  24.2 13.7 %collective-permute-start.6 = (bf16[2,4,128,128]{3,2,1,0:T(8,128)(2,1)S(1)}, bf16[2,4,128,128]{3,2,1,0:T(8,128)(2,1)S(1)}, u32[]{:S(2)}, u32[]{:S(2)}) collective-permute-start(bf16[2,4,128,128]{3,2,1,0:T(8,128)(2,1)S(1)} %maximum_select_fusion.7), channel_id=1, source_target_pairs={{0,2},{2,0},{4,6},{6,4},{8,10},{10,8},{12,14},{14,12},{1,3},{3,1},... | collective-permute-start | bytes 786440 | tf_op jit(solution)/shard_map/ppermute | solution.py:42
  38.0 11.7 %collective-permute-start.7 = (bf16[4,4,128,128]{3,2,1,0:T(8,128)(2,1)S(1)}, bf16[4,4,128,128]{3,2,1,0:T(8,128)(2,1)S(1)}, u32[]{:S(2)}, u32[]{:S(2)}) collective-permute-start(bf16[4,4,128,128]{3,2,1,0:T(8,128)(2,1)S(1)} %maximum_select_fusion.5), channel_id=1, source_target_pairs={{0,4},{2,6},{4,0},{6,2},{8,12},{10,14},{12,8},{14,10},{1,5},{3,7},... | collective-permute-start | bytes 1572872 | tf_op jit(solution)/shard_map/ppermute | solution.py:42
  41.4 10.7 %collective-permute-start.3 = (bf16[8,4,128,128]{3,2,1,0:T(8,128)(2,1)}, bf16[8,4,128,128]{3,2,1,0:T(8,128)(2,1)}, u32[]{:S(2)}, u32[]{:S(2)}) collective-permute-start(bf16[8,4,128,128]{3,2,1,0:T(8,128)(2,1)} %maximum_select_fusion.1), channel_id=1, source_target_pairs={{0,1},{1,0},{2,3},{3,2},{4,5},{5,4},{6,7},{7,6},{8,9},{9,8},{10,11... | collective-permute-start | bytes 3145736 | tf_op jit(solution)/shard_map/ppermute | solution.py:22
  50.8 12.9 %collective-permute-start.8 = (bf16[8,4,128,128]{3,2,1,0:T(8,128)(2,1)}, bf16[8,4,128,128]{3,2,1,0:T(8,128)(2,1)}, u32[]{:S(2)}, u32[]{:S(2)}) collective-permute-start(bf16[8,4,128,128]{3,2,1,0:T(8,128)(2,1)} %maximum_select_fusion.3), channel_id=1, source_target_pairs={{0,1},{1,0},{2,3},{3,2},{4,5},{5,4},{6,7},{7,6},{8,9},{9,8},{10,11... | collective-permute-start | bytes 3145736 | tf_op jit(solution)/shard_map/ppermute | solution.py:22
  61.5 2.2 %copy-start.6 = (bf16[1,8,4,128,128]{4,3,2,1,0:T(8,128)(2,1)S(1)}, bf16[1,8,4,128,128]{4,3,2,1,0:T(8,128)(2,1)}, u32[]{:S(2)}) copy-start(bf16[1,8,4,128,128]{4,3,2,1,0:T(8,128)(2,1)} %maximum_select_fusion.2) | copy-start | bytes 3145732
  69.8 1.8 %copy-start.2 = (bf16[8,4,128,128]{3,2,1,0:T(8,128)(2,1)S(1)}, bf16[8,4,128,128]{3,2,1,0:T(8,128)(2,1)}, u32[]{:S(2)}) copy-start(bf16[8,4,128,128]{3,2,1,0:T(8,128)(2,1)} %param.8) | copy-start | bytes 3145732
  74.4 1.2 copy-start.4
  74.4 1.5 copy-start.5
  79.5 4.4 %collective-permute-start.4 = (f32[8,4,128,128]{3,1,2,0:T(4,128)S(1)}, f32[8,4,128,128]{3,1,2,0:T(4,128)S(1)}, u32[]{:S(2)}, u32[]{:S(2)}) collective-permute-start(f32[8,4,128,128]{3,1,2,0:T(4,128)S(1)} %bitcast.119), channel_id=1, source_target_pairs={{0,1},{1,0},{2,3},{3,2},{4,5},{5,4},{6,7},{7,6},{8,9},{9,8},{10,11... | collective-permute-start | bytes 6291464 | tf_op jit(solution)/shard_map/ppermute | solution.py:22
  80.4 6.4 %collective-permute-start.9 = (f32[8,4,128,128]{3,1,2,0:T(4,128)S(1)}, f32[8,4,128,128]{3,1,2,0:T(4,128)S(1)}, u32[]{:S(2)}, u32[]{:S(2)}) collective-permute-start(f32[8,4,128,128]{3,1,2,0:T(4,128)S(1)} %bitcast.118), channel_id=1, source_target_pairs={{0,1},{1,0},{2,3},{3,2},{4,5},{5,4},{6,7},{7,6},{8,9},{9,8},{10,11... | collective-permute-start | bytes 6291464 | tf_op jit(solution)/shard_map/ppermute | solution.py:22
  90.2 10.1 %copy-start.3 = (bf16[32,128,128]{2,1,0:T(8,128)(2,1)S(1)}, bf16[32,128,128]{2,1,0:T(8,128)(2,1)}, u32[]{:S(2)}) copy-start(bf16[32,128,128]{2,1,0:T(8,128)(2,1)} %gather_fusion.1) | copy-start | bytes 3145732
  90.2 59.6 %all-to-all-start = ((bf16[8,2,4,128,128]{4,2,3,1,0:T(4,128)(2,1)}), bf16[8,2,4,128,128]{4,2,3,1,0:T(4,128)(2,1)}, u32[]{:S(2)}, u32[]{:S(2)}) async-start(bf16[8,2,4,128,128]{4,2,3,1,0:T(4,128)(2,1)} %pad_maximum_fusion.2), calls=%async_computation | async-start | bytes 4194304 | tf_op jit(solution)/shard_map/all_to_all | solution.py:127
  100.7 26.1 %collective-permute-start.11 = (bf16[8,4,128,128]{2,3,1,0:T(8,128)(2,1)S(1)}, bf16[8,4,128,128]{2,3,1,0:T(8,128)(2,1)S(1)}, u32[]{:S(2)}, u32[]{:S(2)}) collective-permute-start(bf16[8,4,128,128]{2,3,1,0:T(8,128)(2,1)S(1)} %fusion.10), channel_id=1, source_target_pairs={{0,16},{16,0},{1,17},{17,1},{2,18},{18,2},{3,19},{19,3},{4,20},{20... | collective-permute-start | bytes 3145736 | tf_op jit(solution)/shard_map/ppermute | solution.py:92
  102.8 45.6 %collective-permute-start.10 = (bf16[8,4,128,128]{3,2,1,0:T(8,128)(2,1)S(1)}, bf16[8,4,128,128]{3,2,1,0:T(8,128)(2,1)S(1)}, u32[]{:S(2)}, u32[]{:S(2)}) collective-permute-start(bf16[8,4,128,128]{3,2,1,0:T(8,128)(2,1)S(1)} %convolution_convert_fusion.1), channel_id=1, source_target_pairs={{0,16},{16,0},{1,17},{17,1},{2,18},{18,2},{3,19},{19,3},{4,20},{20... | collective-permute-start | bytes 3145736 | tf_op jit(solution)/shard_map/ppermute | solution.py:92
  148.4 5.3 %copy-start.1 = (bf16[8,4,128,128]{3,2,1,0:T(8,128)(2,1)S(1)}, bf16[8,4,128,128]{3,2,1,0:T(8,128)(2,1)}, u32[]{:S(2)}) copy-start(bf16[8,4,128,128]{3,2,1,0:T(8,128)(2,1)} %param.10) | copy-start | bytes 3145732

commit v15 on v14

--- a/solution.py
+++ b/solution.py
@@ -54,6 +54,27 @@
     return slot
 
 
+def reduce_chips(buf, chips, order):
+    if order is None:
+        got = lax.all_to_all(buf.astype(jnp.bfloat16), "chip", split_axis=0, concat_axis=0, tiled=True)
+        return got.astype(jnp.float32).sum(axis=0)
+    me = lax.axis_index("chip")
+    nbits = chips.bit_length() - 1
+    rest = buf.shape[1:]
+    buf = buf.reshape((2,) * nbits + rest)
+    bits = list(range(nbits - 1, -1, -1))
+    for step in order:
+        bit = step.bit_length() - 1
+        axis = bits.index(bit)
+        mine = (me // step) % 2
+        keep = lax.dynamic_index_in_dim(buf, mine, axis=axis, keepdims=False)
+        give = lax.dynamic_index_in_dim(buf, 1 - mine, axis=axis, keepdims=False)
+        got = lax.ppermute(give.astype(jnp.bfloat16), "chip", perm=[(i, i ^ step) for i in range(chips)])
+        buf = keep + got.astype(jnp.float32)
+        bits.pop(axis)
+    return buf
+
+
 def per_device(inputs, out_grad, w_in, in_blocks, w_out, out_blocks):
     tok_rows = inputs.shape[0]
     own_cols = inputs.shape[1]
@@ -106,10 +127,9 @@
         local = local.reshape(chips, pair, own_blocks, tok_rows, block_size)
         keep = lax.dynamic_index_in_dim(local, core, axis=1, keepdims=False)
         give = lax.dynamic_index_in_dim(local, 1 - core, axis=1, keepdims=False)
-        return (keep + swap_core(give)).astype(jnp.bfloat16)
+        return keep + swap_core(give)
 
-    def finish(got):
-        total = got.astype(jnp.float32).sum(axis=0)
+    def finish(total):
         return total.transpose(1, 0, 2).reshape(tok_rows, own_cols).astype(jnp.bfloat16)
 
     preact = jnp.einsum("rkti,rkio->tro", in_sel, w_in, preferred_element_type=jnp.float32)
@@ -124,9 +144,8 @@
     pre_grad = (hid_grad * gelu_slope(preact)).astype(jnp.bfloat16)
     in_terms = jnp.einsum("tro,rkio->trki", pre_grad, w_in, preferred_element_type=jnp.float32)
     in_send = chip_sums(in_terms, in_flat)
-    got = lax.all_to_all(jnp.stack([out_send, in_send], axis=1), "chip", split_axis=0, concat_axis=0, tiled=True)
-    outputs = finish(got[:, 0])
-    in_grad = finish(got[:, 1])
+    outputs = finish(reduce_chips(out_send, chips, order_in[::-1] if order_in else None))
+    in_grad = finish(reduce_chips(in_send, chips, order_grad[::-1] if order_grad else None))
     w_in_part = jnp.einsum("rkti,tro->rkio", in_sel, pre_grad, preferred_element_type=jnp.float32)
     w_in_grad = dp_total(w_in_part)
     return (outputs, in_grad, w_in_grad, w_out_grad)

time: 154 us -> 166 us (1.078)
  local copies, waits for them, and re-layouts: 18.5 us -> 28.6 us
  waiting for transfers between devices: 80.8 us -> 73.1 us
  starting transfers between devices: 25.7 us -> 31.4 us
  other arithmetic: 21.1 us -> 23.2 us
    ppermute x0 -> x6, starting transfers between devices: none -> 15.9 us  [reduce_chips(): lax.ppermute(give.astype(jnp.bfloat16), 'chip', perm=[(i, i ^ step) for i...]
    ppermute x2, waiting for transfers between devices: 43.3 us -> 30.4 us  [dp_total(): got = lax.ppermute(part, 'dp', perm=[(0, 1), (1, 0)])]
    ppermute x0 -> x6, waiting for transfers between devices: none -> 10.9 us  [reduce_chips(): lax.ppermute(give.astype(jnp.bfloat16), 'chip', perm=[(i, i ^ step) for i...]
    all_to_all x1 -> x0, starting transfers between devices: 10.1 us -> none  [per_device(): lax.all_to_all(jnp.stack([out_send, in_send], axis=1), 'chip', split_axis...]
    add x0 -> x6, other arithmetic: none -> 8.54 us  [the longest x2 5.98 us: chip_sums(): return keep + swap_core(give)]
    ppermute x4, waiting for transfers between devices: 5.71 us -> 0.01 us  [swap_core(): return lax.ppermute(x, 'core', perm=[(0, 1), (1, 0)])]
    dynamic_slice x2, local copies, waits for them, and re-layouts: 0.76 us -> 5.19 us  [chip_sums(): give = lax.dynamic_index_in_dim(local, 1 - core, axis=1, keepdims=False)]
    another operation x3 -> x0, other arithmetic: 3.93 us -> none  [per_device(): jnp.stack([out_send, in_send], axis=1)]
  transfers between devices with their start and end apart: 13 -> 18, of which waited for: 8 -> 9; matrix products, arithmetic and copies ran while one was open for 14% -> 22% of each run, Pallas kernels for 0% -> 0%
where the time goes in v15:
time: 166 us; the launch traced here: 165 us
  waiting for transfers between devices  73.1 us (44%)
  starting transfers between devices  31.4 us (19%)
  local copies, waits for them, and re-layouts  28.6 us (17%)
  other arithmetic  23.2 us (14%)
  matrix products  8.01 us (5%)
    ppermute x6, waiting for transfers between devices, gather_chips(): got = lax.ppermute(held, 'chip', perm=[(i, i ^ step) for i in range(chips)])  31.8 us
    ppermute x2, waiting for transfers between devices, dp_total(): got = lax.ppermute(part, 'dp', perm=[(0, 1), (1, 0)])  30.4 us
    ppermute x6, starting transfers between devices, reduce_chips(): lax.ppermute(give.astype(jnp.bfloat16), 'chip', perm=[(i, i ^ step) for i...  15.9 us
    ppermute x6, starting transfers between devices, gather_chips(): got = lax.ppermute(held, 'chip', perm=[(i, i ^ step) for i in range(chips)])  12.8 us
    ppermute x6, waiting for transfers between devices, reduce_chips(): lax.ppermute(give.astype(jnp.bfloat16), 'chip', perm=[(i, i ^ step) for i...  10.9 us
    unnamed x31, local copies, waits for them, and re-layouts  7.3 us
    add x2, other arithmetic, chip_sums(): return keep + swap_core(give)  5.98 us
    gather x2, local copies, waits for them, and re-layouts, select(): sel = sets[side, chip_slot(owner // pair, order), sub]  5.61 us
  transfers between devices with their start and end apart: 18, of which 9 were waited for; matrix products, arithmetic and copies ran while one was open for 22% of the time, Pallas kernels for 0%

profile of v15, /device:TPU:0, one launch (start us, length us, event | category | flops | bytes accessed | tf_op | source)
XLA Modules:
  0.0 165.1 jit_solution(18110337658471395629)
XLA Ops:
  1.9 4.1 %collective-permute-start = (bf16[1,4,128,128]{3,2,1,0:T(8,128)(2,1)S(1)}, bf16[1,4,128,128]{3,2,1,0:T(8,128)(2,1)S(1)}, u32[]{:S(2)}, u32[]{:S(2)}) collective-permute-start(bf16[1,4,128,128]{3,2,1,0:T(8,128)(2,1)S(1)} %bitcast.140), channel_id=1, source_target_pairs={{0,8},{2,10},{4,12},{6,14},{8,0},{10,2},{12,4},{14,6},{1,9},{3,11}... | collective-permute-start | bytes 393224 | tf_op jit(solution)/shard_map/ppermute | solution.py:42
  6.0 6.3 %collective-permute-done = bf16[1,4,128,128]{3,2,1,0:T(8,128)(2,1)S(1)} collective-permute-done((bf16[1,4,128,128]{3,2,1,0:T(8,128)(2,1)S(1)}, bf16[1,4,128,128]{3,2,1,0:T(8,128)(2,1)S(1)}, u32[]{:S(2)}, u32[]{:S(2)}) %collective-permute-start) | collective-permute-done | bytes 131104 | tf_op jit(solution)/shard_map/ppermute | solution.py:42
  14.3 3.4 %collective-permute-start.8 = (bf16[1,4,128,128]{3,2,1,0:T(8,128)(2,1)S(1)}, bf16[1,4,128,128]{3,2,1,0:T(8,128)(2,1)S(1)}, u32[]{:S(2)}, u32[]{:S(2)}) collective-permute-start(bf16[1,4,128,128]{3,2,1,0:T(8,128)(2,1)S(1)} %bitcast.142), channel_id=1, source_target_pairs={{0,8},{2,10},{4,12},{6,14},{8,0},{10,2},{12,4},{14,6},{1,9},{3,11}... | collective-permute-start | bytes 393224 | tf_op jit(solution)/shard_map/ppermute | solution.py:42
  17.8 5.0 %collective-permute-done.1 = bf16[2,4,128,128]{3,2,1,0:T(8,128)(2,1)S(1)} collective-permute-done((bf16[2,4,128,128]{3,2,1,0:T(8,128)(2,1)S(1)}, bf16[2,4,128,128]{3,2,1,0:T(8,128)(2,1)S(1)}, u32[]{:S(2)}, u32[]{:S(2)}) %collective-permute-start.1) | collective-permute-done | bytes 262176 | tf_op jit(solution)/shard_map/ppermute | solution.py:42
  25.4 12.5 %collective-permute-done.9 = bf16[2,4,128,128]{3,2,1,0:T(8,128)(2,1)S(1)} collective-permute-done((bf16[2,4,128,128]{3,2,1,0:T(8,128)(2,1)S(1)}, bf16[2,4,128,128]{3,2,1,0:T(8,128)(2,1)S(1)}, u32[]{:S(2)}, u32[]{:S(2)}) %collective-permute-start.9) | collective-permute-done | bytes 262176 | tf_op jit(solution)/shard_map/ppermute | solution.py:42
  38.0 2.3 %collective-permute-start.10 = (bf16[4,4,128,128]{3,2,1,0:T(8,128)(2,1)S(1)}, bf16[4,4,128,128]{3,2,1,0:T(8,128)(2,1)S(1)}, u32[]{:S(2)}, u32[]{:S(2)}) collective-permute-start(bf16[4,4,128,128]{3,2,1,0:T(8,128)(2,1)S(1)} %maximum_select_fusion.5), channel_id=1, source_target_pairs={{0,4},{2,6},{4,0},{6,2},{8,12},{10,14},{12,8},{14,10},{1,5},{3,7},... | collective-permute-start | bytes 1572872 | tf_op jit(solution)/shard_map/ppermute | solution.py:42
  41.7 8.0 %collective-permute-done.10 = bf16[4,4,128,128]{3,2,1,0:T(8,128)(2,1)S(1)} collective-permute-done((bf16[4,4,128,128]{3,2,1,0:T(8,128)(2,1)S(1)}, bf16[4,4,128,128]{3,2,1,0:T(8,128)(2,1)S(1)}, u32[]{:S(2)}, u32[]{:S(2)}) %collective-permute-start.10) | collective-permute-done | bytes 524320 | tf_op jit(solution)/shard_map/ppermute | solution.py:42
  52.1 2.8 %pad_maximum_fusion = bf16[2,8,4,128,128]{4,3,2,1,0:T(8,128)(2,1)} fusion(bf16[1,8,4,128,128]{4,3,2,1,0:T(8,128)(2,1)} %bitcast.7, bf16[1,8,4,128,128]{4,3,2,1,0:T(8,128)(2,1)S(1)} %maximum_select_fusion), kind=kLoop, calls=%fused_computation.2 | loop fusion | flops 1048576 | bytes 4194304 | tf_op jit(solution)/shard_map/stack | solution.py:96
  54.9 2.4 %gather_fusion = bf16[32,128,128]{2,1,0:T(8,128)(2,1)S(1)} fusion(bf16[2,8,4,128,128]{4,3,2,1,0:T(8,128)(2,1)} %pad_maximum_fusion, s32[32]{0:T(128)S(1)} %fusion.60), kind=kCustom, calls=%fused_computation | custom fusion | bytes 2097536 | tf_op jit(solution)/shard_map/gather | solution.py:102
  57.3 1.6 convolution_bitcast_fusion.1
  59.4 2.2 %copy.80 = bf16[128,32,128]{2,1,0:T(8,128)(2,1)} copy(f32[128,32,128]{2,0,1:T(8,128)S(1)} %bitcast.122) | data formatting | bytes 3145728 | tf_op jit(solution)/shard_map/reshape | solution.py:120
  61.6 2.2 %subtract_convert_fusion.1 = bf16[128,32,128]{2,1,0:T(8,128)(2,1)} fusion(f32[128,32,128]{2,0,1:T(8,128)S(1)} %bitcast.123), kind=kLoop, calls=%fused_computation.19 | loop fusion | flops 2097152 | bytes 3145728 | tf_op jit(solution)/shard_map/convert_element_type | solution.py:122
  63.8 2.8 %pad_maximum_fusion.1 = bf16[2,8,4,128,128]{4,3,2,1,0:T(8,128)(2,1)} fusion(bf16[1,8,4,128,128]{4,3,2,1,0:T(8,128)(2,1)} %bitcast.38, bf16[1,8,4,128,128]{4,3,2,1,0:T(8,128)(2,1)S(1)} %copy-done.9), kind=kLoop, calls=%fused_computation.7 | loop fusion | flops 1048576 | bytes 4194304 | tf_op jit(solution)/shard_map/stack | solution.py:96
  66.5 3.3 %gather_fusion.1 = bf16[32,128,128]{2,1,0:T(8,128)(2,1)} fusion(bf16[2,8,4,128,128]{4,3,2,1,0:T(8,128)(2,1)} %pad_maximum_fusion.1, s32[32]{0:T(128)S(1)} %fusion.59), kind=kCustom, calls=%fused_computation.1 | custom fusion | bytes 2097536 | tf_op jit(solution)/shard_map/gather | solution.py:102
  69.8 1.8 %fusion.11 = bf16[128,8,128,1]{2,0,3,1:T(8,128)(2,1)S(1)} fusion(bf16[8,4,128,128]{3,2,1,0:T(8,128)(2,1)} %bitcast.136, bf16[8,4,128,128]{3,2,1,0:T(8,128)(2,1)S(1)} %copy-done, f32[128,8,128]{2,0,1:T(8,128)S(1)} %convolution_bitcast_fusion.1), kind=kOutput, calls=%fused_computation.29 | convolution fusion | flops 135528448 | bytes 2883584 | tf_op jit(solution)/shard_map/rkto,rkio->tri/dot_general | solution.py:143
  76.8 4.2 %constant_dynamic-slice_fusion.1 = (f32[8,1,4,128,128]{4,2,1,0,3:T(4,128)}, f32[8,1,4,128,128]{4,2,1,0,3:T(4,128)S(1)}, f32[8,1,4,128,128]{4,2,1,0,3:T(4,128)S(1)}, f32[8,1,4,128,128]{4,2,1,0,3:T(4,128)}) fusion(f32[8,2,4,128,128]{4,2,1,0,3:T(4,128)S(1)} %bitcast.126, s32[]{:T(128)S(6)} %select_n.458, s32[]{:T(128)S(6)} %select_n.459, ...), kind=kLoop, calls=%fused_computation.77 | loop fusion | bytes 16777224 | tf_op jit(solution)/shard_map/jit(dynamic_index_in_dim)/dynamic_slice | solution.py:128
  81.0 2.6 %copy.82 = f32[8,1,4,128,128]{4,3,2,0,1:T(8,128)} copy(f32[8,1,4,128,128]{4,2,1,0,3:T(4,128)S(1)} %get-tuple-element.20) | data formatting | bytes 4194304 | tf_op jit(solution)/shard_map/jit(dynamic_index_in_dim)/dynamic_slice | solution.py:129
  84.1 2.6 %copy.81 = f32[8,1,4,128,128]{4,3,2,0,1:T(8,128)} copy(f32[8,1,4,128,128]{4,2,1,0,3:T(4,128)S(1)} %get-tuple-element.17) | data formatting | bytes 4194304 | tf_op jit(solution)/shard_map/jit(dynamic_index_in_dim)/dynamic_slice | solution.py:129
  87.2 1.6 collective-permute-start.16
  88.8 1.7 %fusion.8 = bf16[8,4,128,128]{2,3,1,0:T(8,128)(2,1)S(1)} fusion(bf16[8,4,128,128]{3,2,1,0:T(8,128)(2,1)} %bitcast.137, f32[128,8,128]{2,0,1:T(8,128)S(1)} %convolution_bitcast_fusion.1), kind=kOutput, calls=%fused_computation.24 | convolution fusion | flops 135397376 | bytes 2621440 | tf_op jit(solution)/shard_map/tri,rkto->rkio/dot_general | solution.py:140
  91.1 22.1 %collective-permute-done.16 = bf16[8,4,128,128]{3,2,1,0:T(8,128)(2,1)S(1)} collective-permute-done((bf16[8,4,128,128]{3,2,1,0:T(8,128)(2,1)S(1)}, bf16[8,4,128,128]{3,2,1,0:T(8,128)(2,1)S(1)}, u32[]{:S(2)}, u32[]{:S(2)}) %collective-permute-start.16) | collective-permute-done | bytes 1048608 | tf_op jit(solution)/shard_map/ppermute | solution.py:113
  114.6 3.1 %bitcast_add_fusion.1 = f32[8,4,128,128]{3,2,1,0:T(8,128)S(1)} fusion(f32[8,4,128,128]{3,2,1,0:T(8,128)} %collective-permute-done.4, f32[8,1,4,128,128]{4,2,1,0,3:T(4,128)S(1)} %copy-done.3), kind=kLoop, calls=%fused_computation.13 | loop fusion | flops 524288 | bytes 6291456 | tf_op jit(solution)/shard_map/add | solution.py:130
  118.5 1.5 collective-permute-start.5
  120.1 2.9 %bitcast_add_fusion = f32[8,4,128,128]{3,2,1,0:T(8,128)S(1)} fusion(f32[8,4,128,128]{3,2,1,0:T(8,128)} %collective-permute-done.12, f32[8,1,4,128,128]{4,2,1,0,3:T(4,128)S(1)} %copy-done.2), kind=kLoop, calls=%fused_computation.12 | loop fusion | flops 524288 | bytes 6291456 | tf_op jit(solution)/shard_map/add | solution.py:130
  125.2 1.7 %collective-permute-start.13 = (bf16[2,2,4,128,128]{4,3,2,1,0:T(8,128)(2,1)}, bf16[2,2,4,128,128]{4,3,2,1,0:T(8,128)(2,1)}, u32[]{:S(2)}, u32[]{:S(2)}) collective-permute-start(bf16[2,2,4,128,128]{4,3,2,1,0:T(8,128)(2,1)} %fusion.17), channel_id=1, source_target_pairs={{0,4},{2,6},{4,0},{6,2},{8,12},{10,14},{12,8},{14,10},{1,5},{3,7},... | collective-permute-start | bytes 1572872 | tf_op jit(solution)/shard_map/ppermute | solution.py:72
  127.0 8.3 %collective-permute-done.17 = bf16[8,4,128,128]{2,3,1,0:T(8,128)(2,1)S(1)} collective-permute-done((bf16[8,4,128,128]{2,3,1,0:T(8,128)(2,1)S(1)}, bf16[8,4,128,128]{2,3,1,0:T(8,128)(2,1)S(1)}, u32[]{:S(2)}, u32[]{:S(2)}) %collective-permute-start.17) | collective-permute-done | bytes 1048608 | tf_op jit(solution)/shard_map/ppermute | solution.py:113
  138.3 1.8 %collective-permute-start.6 = (bf16[2,4,128,128]{3,2,1,0:T(8,128)(2,1)S(1)}, bf16[2,4,128,128]{3,2,1,0:T(8,128)(2,1)S(1)}, u32[]{:S(2)}, u32[]{:S(2)}) collective-permute-start(bf16[2,4,128,128]{3,2,1,0:T(8,128)(2,1)S(1)} %fusion.19), channel_id=1, source_target_pairs={{0,4},{2,6},{4,0},{6,2},{8,12},{10,14},{12,8},{14,10},{1,5},{3,7},... | collective-permute-start | bytes 786440 | tf_op jit(solution)/shard_map/ppermute | solution.py:72
  141.4 1.6 collective-permute-start.14
  143.0 3.5 %collective-permute-done.6 = bf16[2,4,128,128]{3,2,1,0:T(8,128)(2,1)S(1)} collective-permute-done((bf16[2,4,128,128]{3,2,1,0:T(8,128)(2,1)S(1)}, bf16[2,4,128,128]{3,2,1,0:T(8,128)(2,1)S(1)}, u32[]{:S(2)}, u32[]{:S(2)}) %collective-permute-start.6) | collective-permute-done | bytes 262176 | tf_op jit(solution)/shard_map/ppermute | solution.py:72
  146.5 6.6 %collective-permute-start.7 = (bf16[4,128,128]{2,1,0:T(8,128)(2,1)S(1)}, bf16[4,128,128]{2,1,0:T(8,128)(2,1)S(1)}, u32[]{:S(2)}, u32[]{:S(2)}) collective-permute-start(bf16[4,128,128]{2,1,0:T(8,128)(2,1)S(1)} %fusion.23), channel_id=1, source_target_pairs={{0,8},{2,10},{4,12},{6,14},{8,0},{10,2},{12,4},{14,6},{1,9},{3,11}... | collective-permute-start | bytes 393224 | tf_op jit(solution)/shard_map/ppermute | solution.py:72
  153.2 2.6 %collective-permute-start.15 = (bf16[4,128,128]{2,1,0:T(8,128)(2,1)S(1)}, bf16[4,128,128]{2,1,0:T(8,128)(2,1)S(1)}, u32[]{:S(2)}, u32[]{:S(2)}) collective-permute-start(bf16[4,128,128]{2,1,0:T(8,128)(2,1)S(1)} %fusion.24), channel_id=1, source_target_pairs={{0,8},{2,10},{4,12},{6,14},{8,0},{10,2},{12,4},{14,6},{1,9},{3,11}... | collective-permute-start | bytes 393224 | tf_op jit(solution)/shard_map/ppermute | solution.py:72
  155.9 6.8 %collective-permute-done.7 = bf16[4,128,128]{2,1,0:T(8,128)(2,1)S(1)} collective-permute-done((bf16[4,128,128]{2,1,0:T(8,128)(2,1)S(1)}, bf16[4,128,128]{2,1,0:T(8,128)(2,1)S(1)}, u32[]{:S(2)}, u32[]{:S(2)}) %collective-permute-start.7) | collective-permute-done | bytes 131104 | tf_op jit(solution)/shard_map/ppermute | solution.py:72
  (90 shorter events, 28.3 us)
Async XLA Ops:
  0.6 58.3 %copy-start = (bf16[8,4,128,128]{3,2,1,0:T(8,128)(2,1)S(1)}, bf16[8,4,128,128]{3,2,1,0:T(8,128)(2,1)}, u32[]{:S(2)}) copy-start(bf16[8,4,128,128]{3,2,1,0:T(8,128)(2,1)} %param.10) | copy-start | bytes 3145732
  0.6 24.4 %copy-start.10 = (s32[8,4]{0,1:T(4,128)S(1)}, s32[8,4]{0,1:T(4,128)}, u32[]{:S(2)}) copy-start(s32[8,4]{0,1:T(4,128)} %param.9) | copy-start | bytes 388
  0.7 24.5 %copy-start.11 = (s32[8,4]{0,1:T(4,128)S(1)}, s32[8,4]{0,1:T(4,128)}, u32[]{:S(2)}) copy-start(s32[8,4]{0,1:T(4,128)} %param.11) | copy-start | bytes 388
  1.9 10.4 %collective-permute-start = (bf16[1,4,128,128]{3,2,1,0:T(8,128)(2,1)S(1)}, bf16[1,4,128,128]{3,2,1,0:T(8,128)(2,1)S(1)}, u32[]{:S(2)}, u32[]{:S(2)}) collective-permute-start(bf16[1,4,128,128]{3,2,1,0:T(8,128)(2,1)S(1)} %bitcast.140), channel_id=1, source_target_pairs={{0,8},{2,10},{4,12},{6,14},{8,0},{10,2},{12,4},{14,6},{1,9},{3,11}... | collective-permute-start | bytes 393224 | tf_op jit(solution)/shard_map/ppermute | solution.py:42
  12.4 10.4 %collective-permute-start.1 = (bf16[2,4,128,128]{3,2,1,0:T(8,128)(2,1)S(1)}, bf16[2,4,128,128]{3,2,1,0:T(8,128)(2,1)S(1)}, u32[]{:S(2)}, u32[]{:S(2)}) collective-permute-start(bf16[2,4,128,128]{3,2,1,0:T(8,128)(2,1)S(1)} %maximum_select_fusion.6), channel_id=1, source_target_pairs={{0,4},{2,6},{4,0},{6,2},{8,12},{10,14},{12,8},{14,10},{1,5},{3,7},... | collective-permute-start | bytes 786440 | tf_op jit(solution)/shard_map/ppermute | solution.py:42
  14.3 9.8 %collective-permute-start.8 = (bf16[1,4,128,128]{3,2,1,0:T(8,128)(2,1)S(1)}, bf16[1,4,128,128]{3,2,1,0:T(8,128)(2,1)S(1)}, u32[]{:S(2)}, u32[]{:S(2)}) collective-permute-start(bf16[1,4,128,128]{3,2,1,0:T(8,128)(2,1)S(1)} %bitcast.142), channel_id=1, source_target_pairs={{0,8},{2,10},{4,12},{6,14},{8,0},{10,2},{12,4},{14,6},{1,9},{3,11}... | collective-permute-start | bytes 393224 | tf_op jit(solution)/shard_map/ppermute | solution.py:42
  22.8 17.5 %collective-permute-start.2 = (bf16[4,4,128,128]{3,2,1,0:T(8,128)(2,1)S(1)}, bf16[4,4,128,128]{3,2,1,0:T(8,128)(2,1)S(1)}, u32[]{:S(2)}, u32[]{:S(2)}) collective-permute-start(bf16[4,4,128,128]{3,2,1,0:T(8,128)(2,1)S(1)} %maximum_select_fusion.4), channel_id=1, source_target_pairs={{0,2},{2,0},{4,6},{6,4},{8,10},{10,8},{12,14},{14,12},{1,3},{3,1},... | collective-permute-start | bytes 1572872 | tf_op jit(solution)/shard_map/ppermute | solution.py:42
  24.2 13.7 %collective-permute-start.9 = (bf16[2,4,128,128]{3,2,1,0:T(8,128)(2,1)S(1)}, bf16[2,4,128,128]{3,2,1,0:T(8,128)(2,1)S(1)}, u32[]{:S(2)}, u32[]{:S(2)}) collective-permute-start(bf16[2,4,128,128]{3,2,1,0:T(8,128)(2,1)S(1)} %maximum_select_fusion.7), channel_id=1, source_target_pairs={{0,2},{2,0},{4,6},{6,4},{8,10},{10,8},{12,14},{14,12},{1,3},{3,1},... | collective-permute-start | bytes 786440 | tf_op jit(solution)/shard_map/ppermute | solution.py:42
  38.0 11.7 %collective-permute-start.10 = (bf16[4,4,128,128]{3,2,1,0:T(8,128)(2,1)S(1)}, bf16[4,4,128,128]{3,2,1,0:T(8,128)(2,1)S(1)}, u32[]{:S(2)}, u32[]{:S(2)}) collective-permute-start(bf16[4,4,128,128]{3,2,1,0:T(8,128)(2,1)S(1)} %maximum_select_fusion.5), channel_id=1, source_target_pairs={{0,4},{2,6},{4,0},{6,2},{8,12},{10,14},{12,8},{14,10},{1,5},{3,7},... | collective-permute-start | bytes 1572872 | tf_op jit(solution)/shard_map/ppermute | solution.py:42
  41.4 10.7 %collective-permute-start.3 = (bf16[8,4,128,128]{3,2,1,0:T(8,128)(2,1)}, bf16[8,4,128,128]{3,2,1,0:T(8,128)(2,1)}, u32[]{:S(2)}, u32[]{:S(2)}) collective-permute-start(bf16[8,4,128,128]{3,2,1,0:T(8,128)(2,1)} %maximum_select_fusion.1), channel_id=1, source_target_pairs={{0,1},{1,0},{2,3},{3,2},{4,5},{5,4},{6,7},{7,6},{8,9},{9,8},{10,11... | collective-permute-start | bytes 3145736 | tf_op jit(solution)/shard_map/ppermute | solution.py:22
  50.8 12.9 %collective-permute-start.11 = (bf16[8,4,128,128]{3,2,1,0:T(8,128)(2,1)}, bf16[8,4,128,128]{3,2,1,0:T(8,128)(2,1)}, u32[]{:S(2)}, u32[]{:S(2)}) collective-permute-start(bf16[8,4,128,128]{3,2,1,0:T(8,128)(2,1)} %maximum_select_fusion.3), channel_id=1, source_target_pairs={{0,1},{1,0},{2,3},{3,2},{4,5},{5,4},{6,7},{7,6},{8,9},{9,8},{10,11... | collective-permute-start | bytes 3145736 | tf_op jit(solution)/shard_map/ppermute | solution.py:22
  61.6 2.2 %copy-start.9 = (bf16[1,8,4,128,128]{4,3,2,1,0:T(8,128)(2,1)S(1)}, bf16[1,8,4,128,128]{4,3,2,1,0:T(8,128)(2,1)}, u32[]{:S(2)}) copy-start(bf16[1,8,4,128,128]{4,3,2,1,0:T(8,128)(2,1)} %maximum_select_fusion.2) | copy-start | bytes 3145732
  69.8 1.8 %copy-start.6 = (bf16[8,4,128,128]{3,2,1,0:T(8,128)(2,1)S(1)}, bf16[8,4,128,128]{3,2,1,0:T(8,128)(2,1)}, u32[]{:S(2)}) copy-start(bf16[8,4,128,128]{3,2,1,0:T(8,128)(2,1)} %param.8) | copy-start | bytes 3145732
  74.5 1.2 copy-start.7
  74.5 1.5 copy-start.8
  83.5 31.0 %collective-permute-start.4 = (f32[8,4,128,128]{3,2,1,0:T(8,128)}, f32[8,4,128,128]{3,2,1,0:T(8,128)}, u32[]{:S(2)}, u32[]{:S(2)}) collective-permute-start(f32[8,4,128,128]{3,2,1,0:T(8,128)} %bitcast.121), channel_id=1, source_target_pairs={{0,1},{1,0},{2,3},{3,2},{4,5},{5,4},{6,7},{7,6},{8,9},{9,8},{10,11... | collective-permute-start | bytes 6291464 | tf_op jit(solution)/shard_map/ppermute | solution.py:22
  86.7 33.4 %collective-permute-start.12 = (f32[8,4,128,128]{3,2,1,0:T(8,128)}, f32[8,4,128,128]{3,2,1,0:T(8,128)}, u32[]{:S(2)}, u32[]{:S(2)}) collective-permute-start(f32[8,4,128,128]{3,2,1,0:T(8,128)} %bitcast.120), channel_id=1, source_target_pairs={{0,1},{1,0},{2,3},{3,2},{4,5},{5,4},{6,7},{7,6},{8,9},{9,8},{10,11... | collective-permute-start | bytes 6291464 | tf_op jit(solution)/shard_map/ppermute | solution.py:22
  87.2 26.0 %collective-permute-start.16 = (bf16[8,4,128,128]{3,2,1,0:T(8,128)(2,1)S(1)}, bf16[8,4,128,128]{3,2,1,0:T(8,128)(2,1)S(1)}, u32[]{:S(2)}, u32[]{:S(2)}) collective-permute-start(bf16[8,4,128,128]{3,2,1,0:T(8,128)(2,1)S(1)} %convolution_convert_fusion.1), channel_id=1, source_target_pairs={{0,16},{16,0},{1,17},{17,1},{2,18},{18,2},{3,19},{19,3},{4,20},{20... | collective-permute-start | bytes 3145736 | tf_op jit(solution)/shard_map/ppermute | solution.py:113
  90.5 24.1 %copy-start.3 = (f32[8,1,4,128,128]{4,2,1,0,3:T(4,128)S(1)}, f32[8,1,4,128,128]{4,2,1,0,3:T(4,128)}, u32[]{:S(2)}) copy-start(f32[8,1,4,128,128]{4,2,1,0,3:T(4,128)} %get-tuple-element.21) | copy-start | bytes 6291460
  90.5 44.8 %collective-permute-start.17 = (bf16[8,4,128,128]{2,3,1,0:T(8,128)(2,1)S(1)}, bf16[8,4,128,128]{2,3,1,0:T(8,128)(2,1)S(1)}, u32[]{:S(2)}, u32[]{:S(2)}) collective-permute-start(bf16[8,4,128,128]{2,3,1,0:T(8,128)(2,1)S(1)} %fusion.8), channel_id=1, source_target_pairs={{0,16},{16,0},{1,17},{17,1},{2,18},{18,2},{3,19},{19,3},{4,20},{20... | collective-permute-start | bytes 3145736 | tf_op jit(solution)/shard_map/ppermute | solution.py:113
  114.6 5.5 %copy-start.2 = (f32[8,1,4,128,128]{4,2,1,0,3:T(4,128)S(1)}, f32[8,1,4,128,128]{4,2,1,0,3:T(4,128)}, u32[]{:S(2)}) copy-start(f32[8,1,4,128,128]{4,2,1,0,3:T(4,128)} %get-tuple-element.16) | copy-start | bytes 6291460
  118.5 18.4 %collective-permute-start.5 = (bf16[2,2,4,128,128]{4,3,2,1,0:T(8,128)(2,1)}, bf16[2,2,4,128,128]{4,3,2,1,0:T(8,128)(2,1)}, u32[]{:S(2)}, u32[]{:S(2)}) collective-permute-start(bf16[2,2,4,128,128]{4,3,2,1,0:T(8,128)(2,1)} %fusion.16), channel_id=1, source_target_pairs={{0,2},{2,0},{4,6},{6,4},{8,10},{10,8},{12,14},{14,12},{1,3},{3,1},... | collective-permute-start | bytes 1572872 | tf_op jit(solution)/shard_map/ppermute | solution.py:72
  123.0 1.4 copy-start.4
  125.2 14.9 %collective-permute-start.13 = (bf16[2,2,4,128,128]{4,3,2,1,0:T(8,128)(2,1)}, bf16[2,2,4,128,128]{4,3,2,1,0:T(8,128)(2,1)}, u32[]{:S(2)}, u32[]{:S(2)}) collective-permute-start(bf16[2,2,4,128,128]{4,3,2,1,0:T(8,128)(2,1)} %fusion.17), channel_id=1, source_target_pairs={{0,4},{2,6},{4,0},{6,2},{8,12},{10,14},{12,8},{14,10},{1,5},{3,7},... | collective-permute-start | bytes 1572872 | tf_op jit(solution)/shard_map/ppermute | solution.py:72
  137.0 3.2 %copy-start.5 = (f32[8,4,128,128]{3,2,1,0:T(8,128)S(1)}, f32[8,4,128,128]{3,2,1,0:T(8,128)}, u32[]{:S(2)}) copy-start(f32[8,4,128,128]{3,2,1,0:T(8,128)} %copy-done.4) | copy-start | bytes 6291460
  138.3 8.1 %collective-permute-start.6 = (bf16[2,4,128,128]{3,2,1,0:T(8,128)(2,1)S(1)}, bf16[2,4,128,128]{3,2,1,0:T(8,128)(2,1)S(1)}, u32[]{:S(2)}, u32[]{:S(2)}) collective-permute-start(bf16[2,4,128,128]{3,2,1,0:T(8,128)(2,1)S(1)} %fusion.19), channel_id=1, source_target_pairs={{0,4},{2,6},{4,0},{6,2},{8,12},{10,14},{12,8},{14,10},{1,5},{3,7},... | collective-permute-start | bytes 786440 | tf_op jit(solution)/shard_map/ppermute | solution.py:72
  141.4 11.8 %collective-permute-start.14 = (bf16[2,4,128,128]{3,2,1,0:T(8,128)(2,1)S(1)}, bf16[2,4,128,128]{3,2,1,0:T(8,128)(2,1)S(1)}, u32[]{:S(2)}, u32[]{:S(2)}) collective-permute-start(bf16[2,4,128,128]{3,2,1,0:T(8,128)(2,1)S(1)} %fusion.20), channel_id=1, source_target_pairs={{0,2},{2,0},{4,6},{6,4},{8,10},{10,8},{12,14},{14,12},{1,3},{3,1},... | collective-permute-start | bytes 786440 | tf_op jit(solution)/shard_map/ppermute | solution.py:72
  146.4 18.7 %copy-start.1 = (bf16[8,4,128,128]{3,2,1,0:T(8,128)(2,1)S(1)}, bf16[8,4,128,128]{3,2,1,0:T(8,128)(2,1)}, u32[]{:S(2)}) copy-start(bf16[8,4,128,128]{3,2,1,0:T(8,128)(2,1)} %param.10) | copy-start | bytes 3145732
  146.5 16.2 %collective-permute-start.7 = (bf16[4,128,128]{2,1,0:T(8,128)(2,1)S(1)}, bf16[4,128,128]{2,1,0:T(8,128)(2,1)S(1)}, u32[]{:S(2)}, u32[]{:S(2)}) collective-permute-start(bf16[4,128,128]{2,1,0:T(8,128)(2,1)S(1)} %fusion.23), channel_id=1, source_target_pairs={{0,8},{2,10},{4,12},{6,14},{8,0},{10,2},{12,4},{14,6},{1,9},{3,11}... | collective-permute-start | bytes 393224 | tf_op jit(solution)/shard_map/ppermute | solution.py:72
  153.2 10.9 %collective-permute-start.15 = (bf16[4,128,128]{2,1,0:T(8,128)(2,1)S(1)}, bf16[4,128,128]{2,1,0:T(8,128)(2,1)S(1)}, u32[]{:S(2)}, u32[]{:S(2)}) collective-permute-start(bf16[4,128,128]{2,1,0:T(8,128)(2,1)S(1)} %fusion.24), channel_id=1, source_target_pairs={{0,8},{2,10},{4,12},{6,14},{8,0},{10,2},{12,4},{14,6},{1,9},{3,11}... | collective-permute-start | bytes 393224 | tf_op jit(solution)/shard_map/ppermute | solution.py:72

commit v16 on v14

--- a/solution.py
+++ b/solution.py
@@ -97,12 +97,8 @@
 
     def chip_sums(terms, flat):
         terms = terms.reshape(tok_rows, pair_count, block_size)
-        hi = terms.astype(jnp.bfloat16)
-        lo = (terms - hi.astype(jnp.float32)).astype(jnp.bfloat16)
         onehot = (flat[:, None] == columns[None, :]).astype(jnp.bfloat16)
-        parts = jnp.concatenate([hi, lo], axis=1)
-        picks = jnp.concatenate([onehot, onehot], axis=0)
-        local = jnp.einsum("tpo,pc->cto", parts, picks, preferred_element_type=jnp.float32)
+        local = jnp.einsum("tpo,pc->cto", terms.astype(jnp.bfloat16), onehot, preferred_element_type=jnp.float32)
         local = local.reshape(chips, pair, own_blocks, tok_rows, block_size)
         keep = lax.dynamic_index_in_dim(local, core, axis=1, keepdims=False)
         give = lax.dynamic_index_in_dim(local, 1 - core, axis=1, keepdims=False)

time: 154 us -> 129 us (0.84)
  waiting for transfers between devices: 80.8 us -> 72.9 us
  other arithmetic: 21.1 us -> 14.5 us
  starting transfers between devices: 25.7 us -> 19.8 us
  local copies, waits for them, and re-layouts: 18.5 us -> 13.8 us
    ppermute x6, waiting for transfers between devices: 31.8 us -> 23.9 us  [gather_chips(): got = lax.ppermute(held, 'chip', perm=[(i, i ^ step) for i in range(chips)])]
    convert_element_type x2 -> x0, other arithmetic: 3.43 us -> none  [chip_sums(): lo = (terms - hi.astype(jnp.float32)).astype(jnp.bfloat16)]
    reshape x2 -> x0, local copies, waits for them, and re-layouts: 3.41 us -> none  [chip_sums(): terms = terms.reshape(tok_rows, pair_count, block_size)]
    ppermute x6, starting transfers between devices: 12.8 us -> 9.51 us  [gather_chips(): got = lax.ppermute(held, 'chip', perm=[(i, i ^ step) for i in range(chips)])]
    all_to_all x1, starting transfers between devices: 10.1 us -> 6.95 us  [per_device(): lax.all_to_all(jnp.stack([out_send, in_send], axis=1), 'chip', split_axis...]
    another operation x3, other arithmetic: 3.93 us -> 1.22 us  [per_device(): jnp.stack([out_send, in_send], axis=1)]
    gather x2, local copies, waits for them, and re-layouts: 5.61 us -> 4.02 us  [select(): sel = sets[side, chip_slot(owner // pair, order), sub]]
    dynamic_slice x1, local copies, waits for them, and re-layouts: 2.35 us -> 0.78 us  [chip_sums(): keep = lax.dynamic_index_in_dim(local, core, axis=1, keepdims=False)]
  transfers between devices with their start and end apart: 13 -> 13, of which waited for: 8 -> 8; matrix products, arithmetic and copies ran while one was open for 14% -> 12% of each run, Pallas kernels for 0% -> 0%
where the time goes in v16:
time: 129 us
  waiting for transfers between devices  72.9 us (57%)
  starting transfers between devices  19.8 us (15%)
  other arithmetic  14.5 us (11%)
  local copies, waits for them, and re-layouts  13.8 us (11%)
  matrix products  6.98 us (5%)
    ppermute x2, waiting for transfers between devices, dp_total(): got = lax.ppermute(part, 'dp', perm=[(0, 1), (1, 0)])  43.4 us
    ppermute x6, waiting for transfers between devices, gather_chips(): got = lax.ppermute(held, 'chip', perm=[(i, i ^ step) for i in range(chips)])  23.9 us
    ppermute x6, starting transfers between devices, gather_chips(): got = lax.ppermute(held, 'chip', perm=[(i, i ^ step) for i in range(chips)])  9.51 us
    all_to_all x1, starting transfers between devices, per_device(): lax.all_to_all(jnp.stack([out_send, in_send], axis=1), 'chip', split_axis...  6.95 us
    unnamed x17, local copies, waits for them, and re-layouts  5.9 us
    ppermute x4, waiting for transfers between devices, swap_core(): return lax.ppermute(x, 'core', perm=[(0, 1), (1, 0)])  5.66 us
    another operation x2, other arithmetic, gather(): return jnp.stack([mine, swap_core(mine)], axis=0)  4.49 us
    gather x2, local copies, waits for them, and re-layouts, select(): sel = sets[side, chip_slot(owner // pair, order), sub]  4.02 us
  transfers between devices with their start and end apart: 13, of which 8 were waited for; matrix products, arithmetic and copies ran while one was open for 12% of the time, Pallas kernels for 0%

profile of v16, /device:TPU:0, one launch (start us, length us, event | category | flops | bytes accessed | tf_op | source)
XLA Modules:
  0.0 128.9 jit_solution(3336926098502389629)
XLA Ops:
  0.6 1.1 copy.66
  1.9 4.1 %collective-permute-start.5 = (bf16[1,4,128,128]{3,2,1,0:T(8,128)(2,1)S(1)}, bf16[1,4,128,128]{3,2,1,0:T(8,128)(2,1)S(1)}, u32[]{:S(2)}, u32[]{:S(2)}) collective-permute-start(bf16[1,4,128,128]{3,2,1,0:T(8,128)(2,1)S(1)} %bitcast.118), channel_id=1, source_target_pairs={{0,8},{2,10},{4,12},{6,14},{8,0},{10,2},{12,4},{14,6},{1,9},{3,11}... | collective-permute-start | bytes 393224 | tf_op jit(solution)/shard_map/ppermute | solution.py:42
  6.0 1.0 copy.59
  7.3 8.7 %collective-permute-done.5 = bf16[1,4,128,128]{3,2,1,0:T(8,128)(2,1)S(1)} collective-permute-done((bf16[1,4,128,128]{3,2,1,0:T(8,128)(2,1)S(1)}, bf16[1,4,128,128]{3,2,1,0:T(8,128)(2,1)S(1)}, u32[]{:S(2)}, u32[]{:S(2)}) %collective-permute-start.5) | collective-permute-done | bytes 131104 | tf_op jit(solution)/shard_map/ppermute | solution.py:42
  16.0 1.9 %collective-permute-start.6 = (bf16[2,4,128,128]{3,2,1,0:T(8,128)(2,1)S(1)}, bf16[2,4,128,128]{3,2,1,0:T(8,128)(2,1)S(1)}, u32[]{:S(2)}, u32[]{:S(2)}) collective-permute-start(bf16[2,4,128,128]{3,2,1,0:T(8,128)(2,1)S(1)} %maximum_select_fusion.7), channel_id=1, source_target_pairs={{0,2},{2,0},{4,6},{6,4},{8,10},{10,8},{12,14},{14,12},{1,3},{3,1},... | collective-permute-start | bytes 786440 | tf_op jit(solution)/shard_map/ppermute | solution.py:42
  18.0 0.8 collective-permute-start.1
  18.7 4.0 %collective-permute-done.6 = bf16[2,4,128,128]{3,2,1,0:T(8,128)(2,1)S(1)} collective-permute-done((bf16[2,4,128,128]{3,2,1,0:T(8,128)(2,1)S(1)}, bf16[2,4,128,128]{3,2,1,0:T(8,128)(2,1)S(1)}, u32[]{:S(2)}, u32[]{:S(2)}) %collective-permute-start.6) | collective-permute-done | bytes 262176 | tf_op jit(solution)/shard_map/ppermute | solution.py:42
  22.8 1.5 %collective-permute-start.7 = (bf16[4,4,128,128]{3,2,1,0:T(8,128)(2,1)S(1)}, bf16[4,4,128,128]{3,2,1,0:T(8,128)(2,1)S(1)}, u32[]{:S(2)}, u32[]{:S(2)}) collective-permute-start(bf16[4,4,128,128]{3,2,1,0:T(8,128)(2,1)S(1)} %maximum_select_fusion.5), channel_id=1, source_target_pairs={{0,4},{2,6},{4,0},{6,2},{8,12},{10,14},{12,8},{14,10},{1,5},{3,7},... | collective-permute-start | bytes 1572872 | tf_op jit(solution)/shard_map/ppermute | solution.py:42
  24.3 2.4 %collective-permute-done.1 = bf16[2,4,128,128]{3,2,1,0:T(8,128)(2,1)S(1)} collective-permute-done((bf16[2,4,128,128]{3,2,1,0:T(8,128)(2,1)S(1)}, bf16[2,4,128,128]{3,2,1,0:T(8,128)(2,1)S(1)}, u32[]{:S(2)}, u32[]{:S(2)}) %collective-permute-start.1) | collective-permute-done | bytes 262176 | tf_op jit(solution)/shard_map/ppermute | solution.py:42
  26.8 1.1 collective-permute-start.2
  27.9 8.8 %collective-permute-done.7 = bf16[4,4,128,128]{3,2,1,0:T(8,128)(2,1)S(1)} collective-permute-done((bf16[4,4,128,128]{3,2,1,0:T(8,128)(2,1)S(1)}, bf16[4,4,128,128]{3,2,1,0:T(8,128)(2,1)S(1)}, u32[]{:S(2)}, u32[]{:S(2)}) %collective-permute-start.7) | collective-permute-done | bytes 524320 | tf_op jit(solution)/shard_map/ppermute | solution.py:42
  36.7 1.1 maximum_select_fusion.3
  37.9 1.1 maximum_select_fusion.1
  40.1 1.2 maximum_select_fusion
  41.5 1.4 %pad_maximum_fusion.1 = bf16[2,8,4,128,128]{4,3,2,1,0:T(8,128)(2,1)S(1)} fusion(bf16[1,8,4,128,128]{4,3,2,1,0:T(8,128)(2,1)} %bitcast.31, bf16[1,8,4,128,128]{4,3,2,1,0:T(8,128)(2,1)S(1)} %maximum_select_fusion.2), kind=kLoop, calls=%fused_computation.3 | loop fusion | flops 1048576 | bytes 4194304 | tf_op jit(solution)/shard_map/stack | solution.py:75
  42.9 1.7 %gather_fusion.1 = bf16[32,128,128]{2,1,0:T(8,128)(2,1)} fusion(bf16[2,8,4,128,128]{4,3,2,1,0:T(8,128)(2,1)S(1)} %pad_maximum_fusion.1, s32[32]{0:T(128)S(1)} %fusion.53), kind=kCustom, calls=%fused_computation.1 | custom fusion | bytes 2097536 | tf_op jit(solution)/shard_map/gather | solution.py:81
  44.6 3.1 %pad_maximum_fusion = bf16[2,8,4,128,128]{4,3,2,1,0:T(8,128)(2,1)} fusion(bf16[1,8,4,128,128]{4,3,2,1,0:T(8,128)(2,1)} %bitcast.8, bf16[1,8,4,128,128]{4,3,2,1,0:T(8,128)(2,1)} %maximum_select_fusion), kind=kLoop, calls=%fused_computation.2 | loop fusion | flops 1048576 | bytes 4194304 | tf_op jit(solution)/shard_map/stack | solution.py:75
  47.6 2.4 %gather_fusion = bf16[32,128,128]{2,1,0:T(8,128)(2,1)S(1)} fusion(bf16[2,8,4,128,128]{4,3,2,1,0:T(8,128)(2,1)} %pad_maximum_fusion, s32[32]{0:T(128)S(1)} %fusion.54), kind=kCustom, calls=%fused_computation | custom fusion | bytes 2097536 | tf_op jit(solution)/shard_map/gather | solution.py:81
  50.0 1.7 %convolution_bitcast_fusion.1 = f32[128,8,128]{2,0,1:T(8,128)S(1)} fusion(bf16[8,4,128,128]{3,2,1,0:T(8,128)(2,1)S(1)} %bitcast.104, bf16[8,4,128,128]{3,2,1,0:T(8,128)(2,1)} %param.8), kind=kOutput, calls=%fused_computation.19 | convolution fusion | flops 134217728 | bytes 2621440 | tf_op jit(solution)/shard_map/rkti,rkio->tro/dot_general | solution.py:111
  53.8 0.8 fusion.8
  54.7 0.8 fusion.10
  57.8 3.2 %collective-permute-done.4 = f32[8,4,128,128]{3,2,1,0:T(8,128)S(1)} collective-permute-done((f32[8,4,128,128]{3,2,1,0:T(8,128)S(1)}, f32[8,4,128,128]{3,2,1,0:T(8,128)S(1)}, u32[]{:S(2)}, u32[]{:S(2)}) %collective-permute-start.4) | collective-permute-done | bytes 2097184 | tf_op jit(solution)/shard_map/ppermute | solution.py:22
  61.5 2.5 %collective-permute-done.9 = f32[8,4,128,128]{3,2,1,0:T(8,128)S(1)} collective-permute-done((f32[8,4,128,128]{3,2,1,0:T(8,128)S(1)}, f32[8,4,128,128]{3,2,1,0:T(8,128)S(1)}, u32[]{:S(2)}, u32[]{:S(2)}) %collective-permute-start.9) | collective-permute-done | bytes 2097184 | tf_op jit(solution)/shard_map/ppermute | solution.py:22
  64.7 1.5 %copy.72 = bf16[8,2,4,128,128]{4,3,2,1,0:T(8,128)(2,1)} copy(bf16[8,2,4,128,128]{4,3,2,0,1:T(8,128)(2,1)S(1)} %pad_maximum_fusion.2) | data formatting | bytes 4194304 | tf_op jit(solution)/shard_map/stack | solution.py:123
  66.1 7.0 %all-to-all-start = ((bf16[8,2,4,128,128]{4,3,2,1,0:T(8,128)(2,1)}), bf16[8,2,4,128,128]{4,3,2,1,0:T(8,128)(2,1)}, u32[]{:S(2)}, u32[]{:S(2)}) async-start(bf16[8,2,4,128,128]{4,3,2,1,0:T(8,128)(2,1)} %copy.72), calls=%async_computation | async-start | bytes 4194304 | tf_op jit(solution)/shard_map/all_to_all | solution.py:123
  73.1 1.7 %fusion.2 = bf16[8,4,128,128]{2,3,1,0:T(8,128)(2,1)S(1)} fusion(bf16[8,4,128,128]{3,2,1,0:T(8,128)(2,1)} %bitcast.110, f32[128,8,128]{2,0,1:T(8,128)S(1)} %convolution_bitcast_fusion.1), kind=kOutput, calls=%fused_computation.17 | convolution fusion | flops 135397376 | bytes 2621440 | tf_op jit(solution)/shard_map/tri,rkto->rkio/dot_general | solution.py:116
  74.8 1.6 %collective-permute-start.11 = (bf16[8,4,128,128]{2,3,1,0:T(8,128)(2,1)S(1)}, bf16[8,4,128,128]{2,3,1,0:T(8,128)(2,1)S(1)}, u32[]{:S(2)}, u32[]{:S(2)}) collective-permute-start(bf16[8,4,128,128]{2,3,1,0:T(8,128)(2,1)S(1)} %fusion.2), channel_id=1, source_target_pairs={{0,16},{16,0},{1,17},{17,1},{2,18},{18,2},{3,19},{19,3},{4,20},{20... | collective-permute-start | bytes 3145736 | tf_op jit(solution)/shard_map/ppermute | solution.py:92
  77.5 23.4 %collective-permute-done.11 = bf16[8,4,128,128]{2,3,1,0:T(8,128)(2,1)S(1)} collective-permute-done((bf16[8,4,128,128]{2,3,1,0:T(8,128)(2,1)S(1)}, bf16[8,4,128,128]{2,3,1,0:T(8,128)(2,1)S(1)}, u32[]{:S(2)}, u32[]{:S(2)}) %collective-permute-start.11) | collective-permute-done | bytes 1048608 | tf_op jit(solution)/shard_map/ppermute | solution.py:92
  101.3 1.3 %copy.81 = bf16[8,4,128,128]{3,2,1,0:T(8,128)(2,1)} copy(bf16[8,4,128,128]{2,3,1,0:T(8,128)(2,1)S(1)} %add_convert_fusion) | data formatting | bytes 2097152
  102.6 20.0 %collective-permute-done.10 = bf16[8,4,128,128]{3,2,1,0:T(8,128)(2,1)} collective-permute-done((bf16[8,4,128,128]{3,2,1,0:T(8,128)(2,1)S(1)}, bf16[8,4,128,128]{3,2,1,0:T(8,128)(2,1)}, u32[]{:S(2)}, u32[]{:S(2)}) %collective-permute-start.10) | collective-permute-done | bytes 1048608 | tf_op jit(solution)/shard_map/ppermute | solution.py:92
  122.6 2.6 %add_convert_fusion.1 = bf16[8,4,128,128]{3,2,1,0:T(8,128)(2,1)} fusion(bf16[8,4,128,128]{3,2,1,0:T(8,128)(2,1)} %collective-permute-done.10, bf16[8,4,128,128]{3,2,1,0:T(8,128)(2,1)S(1)} %convolution_convert_fusion.1), kind=kLoop, calls=%fused_computation.12 | loop fusion | flops 2097152 | bytes 3145728 | tf_op jit(solution)/shard_map/convert_element_type | solution.py:93
  125.2 1.9 %slice_reduce_fusion = (bf16[4,128,128]{2,1,0:T(8,128)(2,1)S(1)}, bf16[4,128,128]{2,1,0:T(8,128)(2,1)S(1)}) fusion(bf16[8,2,4,128,128]{4,3,2,1,0:T(8,128)(2,1)} %all-to-all-done), kind=kLoop, calls=%fused_computation.25 | loop fusion | flops 917504 | bytes 2359296 | tf_op jit(solution)/shard_map/reduce_sum | solution.py:108
  (52 shorter events, 10.7 us)
Async XLA Ops:
  0.6 51.1 %copy-start = (bf16[8,4,128,128]{3,2,1,0:T(8,128)(2,1)S(1)}, bf16[8,4,128,128]{3,2,1,0:T(8,128)(2,1)}, u32[]{:S(2)}) copy-start(bf16[8,4,128,128]{3,2,1,0:T(8,128)(2,1)} %param.10) | copy-start | bytes 3145732
  1.9 14.0 %collective-permute-start.5 = (bf16[1,4,128,128]{3,2,1,0:T(8,128)(2,1)S(1)}, bf16[1,4,128,128]{3,2,1,0:T(8,128)(2,1)S(1)}, u32[]{:S(2)}, u32[]{:S(2)}) collective-permute-start(bf16[1,4,128,128]{3,2,1,0:T(8,128)(2,1)S(1)} %bitcast.118), channel_id=1, source_target_pairs={{0,8},{2,10},{4,12},{6,14},{8,0},{10,2},{12,4},{14,6},{1,9},{3,11}... | collective-permute-start | bytes 393224 | tf_op jit(solution)/shard_map/ppermute | solution.py:42
  7.2 10.8 %collective-permute-start = (bf16[1,4,128,128]{3,2,1,0:T(8,128)(2,1)S(1)}, bf16[1,4,128,128]{3,2,1,0:T(8,128)(2,1)S(1)}, u32[]{:S(2)}, u32[]{:S(2)}) collective-permute-start(bf16[1,4,128,128]{3,2,1,0:T(8,128)(2,1)S(1)} %bitcast.116), channel_id=1, source_target_pairs={{0,8},{2,10},{4,12},{6,14},{8,0},{10,2},{12,4},{14,6},{1,9},{3,11}... | collective-permute-start | bytes 393224 | tf_op jit(solution)/shard_map/ppermute | solution.py:42
  16.0 6.7 %collective-permute-start.6 = (bf16[2,4,128,128]{3,2,1,0:T(8,128)(2,1)S(1)}, bf16[2,4,128,128]{3,2,1,0:T(8,128)(2,1)S(1)}, u32[]{:S(2)}, u32[]{:S(2)}) collective-permute-start(bf16[2,4,128,128]{3,2,1,0:T(8,128)(2,1)S(1)} %maximum_select_fusion.7), channel_id=1, source_target_pairs={{0,2},{2,0},{4,6},{6,4},{8,10},{10,8},{12,14},{14,12},{1,3},{3,1},... | collective-permute-start | bytes 786440 | tf_op jit(solution)/shard_map/ppermute | solution.py:42
  18.0 8.8 %collective-permute-start.1 = (bf16[2,4,128,128]{3,2,1,0:T(8,128)(2,1)S(1)}, bf16[2,4,128,128]{3,2,1,0:T(8,128)(2,1)S(1)}, u32[]{:S(2)}, u32[]{:S(2)}) collective-permute-start(bf16[2,4,128,128]{3,2,1,0:T(8,128)(2,1)S(1)} %maximum_select_fusion.6), channel_id=1, source_target_pairs={{0,4},{2,6},{4,0},{6,2},{8,12},{10,14},{12,8},{14,10},{1,5},{3,7},... | collective-permute-start | bytes 786440 | tf_op jit(solution)/shard_map/ppermute | solution.py:42
  22.8 14.0 %collective-permute-start.7 = (bf16[4,4,128,128]{3,2,1,0:T(8,128)(2,1)S(1)}, bf16[4,4,128,128]{3,2,1,0:T(8,128)(2,1)S(1)}, u32[]{:S(2)}, u32[]{:S(2)}) collective-permute-start(bf16[4,4,128,128]{3,2,1,0:T(8,128)(2,1)S(1)} %maximum_select_fusion.5), channel_id=1, source_target_pairs={{0,4},{2,6},{4,0},{6,2},{8,12},{10,14},{12,8},{14,10},{1,5},{3,7},... | collective-permute-start | bytes 1572872 | tf_op jit(solution)/shard_map/ppermute | solution.py:42
  26.8 12.7 %copy-start.3 = (s32[8,4]{0,1:T(4,128)S(1)}, s32[8,4]{0,1:T(4,128)}, u32[]{:S(2)}) copy-start(s32[8,4]{0,1:T(4,128)} %param.9) | copy-start | bytes 388
  26.8 12.9 %copy-start.4 = (s32[8,4]{0,1:T(4,128)S(1)}, s32[8,4]{0,1:T(4,128)}, u32[]{:S(2)}) copy-start(s32[8,4]{0,1:T(4,128)} %param.11) | copy-start | bytes 388
  26.8 11.0 %collective-permute-start.2 = (bf16[4,4,128,128]{3,2,1,0:T(8,128)(2,1)S(1)}, bf16[4,4,128,128]{3,2,1,0:T(8,128)(2,1)S(1)}, u32[]{:S(2)}, u32[]{:S(2)}) collective-permute-start(bf16[4,4,128,128]{3,2,1,0:T(8,128)(2,1)S(1)} %maximum_select_fusion.4), channel_id=1, source_target_pairs={{0,2},{2,0},{4,6},{6,4},{8,10},{10,8},{12,14},{14,12},{1,3},{3,1},... | collective-permute-start | bytes 1572872 | tf_op jit(solution)/shard_map/ppermute | solution.py:42
  37.9 3.6 %collective-permute-start.8 = (bf16[8,4,128,128]{3,2,1,0:T(8,128)(2,1)}, bf16[8,4,128,128]{3,2,1,0:T(8,128)(2,1)}, u32[]{:S(2)}, u32[]{:S(2)}) collective-permute-start(bf16[8,4,128,128]{3,2,1,0:T(8,128)(2,1)} %maximum_select_fusion.3), channel_id=1, source_target_pairs={{0,1},{1,0},{2,3},{3,2},{4,5},{5,4},{6,7},{7,6},{8,9},{9,8},{10,11... | collective-permute-start | bytes 3145736 | tf_op jit(solution)/shard_map/ppermute | solution.py:22
  39.0 5.5 %collective-permute-start.3 = (bf16[8,4,128,128]{3,2,1,0:T(8,128)(2,1)}, bf16[8,4,128,128]{3,2,1,0:T(8,128)(2,1)}, u32[]{:S(2)}, u32[]{:S(2)}) collective-permute-start(bf16[8,4,128,128]{3,2,1,0:T(8,128)(2,1)} %maximum_select_fusion.1), channel_id=1, source_target_pairs={{0,1},{1,0},{2,3},{3,2},{4,5},{5,4},{6,7},{7,6},{8,9},{9,8},{10,11... | collective-permute-start | bytes 3145736 | tf_op jit(solution)/shard_map/ppermute | solution.py:22
  50.0 2.2 %copy-start.2 = (bf16[32,128,128]{2,1,0:T(8,128)(2,1)S(1)}, bf16[32,128,128]{2,1,0:T(8,128)(2,1)}, u32[]{:S(2)}) copy-start(bf16[32,128,128]{2,1,0:T(8,128)(2,1)} %gather_fusion.1) | copy-start | bytes 3145732
  52.2 1.2 copy-start.1
  56.7 4.2 %collective-permute-start.4 = (f32[8,4,128,128]{3,2,1,0:T(8,128)S(1)}, f32[8,4,128,128]{3,2,1,0:T(8,128)S(1)}, u32[]{:S(2)}, u32[]{:S(2)}) collective-permute-start(f32[8,4,128,128]{3,2,1,0:T(8,128)S(1)} %bitcast.115), channel_id=1, source_target_pairs={{0,1},{1,0},{2,3},{3,2},{4,5},{5,4},{6,7},{7,6},{8,9},{9,8},{10,11... | collective-permute-start | bytes 6291464 | tf_op jit(solution)/shard_map/ppermute | solution.py:22
  57.2 6.7 %collective-permute-start.9 = (f32[8,4,128,128]{3,2,1,0:T(8,128)S(1)}, f32[8,4,128,128]{3,2,1,0:T(8,128)S(1)}, u32[]{:S(2)}, u32[]{:S(2)}) collective-permute-start(f32[8,4,128,128]{3,2,1,0:T(8,128)S(1)} %bitcast.114), channel_id=1, source_target_pairs={{0,1},{1,0},{2,3},{3,2},{4,5},{5,4},{6,7},{7,6},{8,9},{9,8},{10,11... | collective-permute-start | bytes 6291464 | tf_op jit(solution)/shard_map/ppermute | solution.py:22
  66.1 59.0 %all-to-all-start = ((bf16[8,2,4,128,128]{4,3,2,1,0:T(8,128)(2,1)}), bf16[8,2,4,128,128]{4,3,2,1,0:T(8,128)(2,1)}, u32[]{:S(2)}, u32[]{:S(2)}) async-start(bf16[8,2,4,128,128]{4,3,2,1,0:T(8,128)(2,1)} %copy.72), calls=%async_computation | async-start | bytes 4194304 | tf_op jit(solution)/shard_map/all_to_all | solution.py:123
  74.8 26.1 %collective-permute-start.11 = (bf16[8,4,128,128]{2,3,1,0:T(8,128)(2,1)S(1)}, bf16[8,4,128,128]{2,3,1,0:T(8,128)(2,1)S(1)}, u32[]{:S(2)}, u32[]{:S(2)}) collective-permute-start(bf16[8,4,128,128]{2,3,1,0:T(8,128)(2,1)S(1)} %fusion.2), channel_id=1, source_target_pairs={{0,16},{16,0},{1,17},{17,1},{2,18},{18,2},{3,19},{19,3},{4,20},{20... | collective-permute-start | bytes 3145736 | tf_op jit(solution)/shard_map/ppermute | solution.py:92
  76.9 45.7 %collective-permute-start.10 = (bf16[8,4,128,128]{3,2,1,0:T(8,128)(2,1)S(1)}, bf16[8,4,128,128]{3,2,1,0:T(8,128)(2,1)}, u32[]{:S(2)}, u32[]{:S(2)}) collective-permute-start(bf16[8,4,128,128]{3,2,1,0:T(8,128)(2,1)S(1)} %convolution_convert_fusion.1), channel_id=1, source_target_pairs={{0,16},{16,0},{1,17},{17,1},{2,18},{18,2},{3,19},{19,3},{4,20},{20... | collective-permute-start | bytes 3145736 | tf_op jit(solution)/shard_map/ppermute | solution.py:92

commit v17 on v16

--- a/solution.py
+++ b/solution.py
@@ -102,7 +102,7 @@
         local = local.reshape(chips, pair, own_blocks, tok_rows, block_size)
         keep = lax.dynamic_index_in_dim(local, core, axis=1, keepdims=False)
         give = lax.dynamic_index_in_dim(local, 1 - core, axis=1, keepdims=False)
-        return (keep + swap_core(give)).astype(jnp.bfloat16)
+        return (keep + swap_core(give.astype(jnp.bfloat16)).astype(jnp.float32)).astype(jnp.bfloat16)
 
     def finish(got):
         total = got.astype(jnp.float32).sum(axis=0)

time: 129 us -> 133 us (1.031)
  local copies, waits for them, and re-layouts: 13.8 us -> 19.5 us
  waiting for transfers between devices: 72.9 us -> 67.9 us
  other arithmetic: 14.5 us -> 18.2 us
    ppermute x4, waiting for transfers between devices: 5.66 us -> 0.41 us  [swap_core(): return lax.ppermute(x, 'core', perm=[(0, 1), (1, 0)])]
    unnamed x17 -> x25, local copies, waits for them, and re-layouts: 5.9 us -> 8.94 us
    another operation x3, other arithmetic: 1.22 us -> 3.93 us  [per_device(): jnp.stack([out_send, in_send], axis=1)]
    convert_element_type x0 -> x2, local copies, waits for them, and re-layouts: none -> 2.23 us  [chip_sums(): give.astype(jnp.bfloat16)]
    dynamic_slice x3 -> x0, local copies, waits for them, and re-layouts: 1.59 us -> none  [the longest x2 0.81 us: chip_sums(): give = lax.dynamic_index_in_dim(local, 1 - core, axis=1, keepdims=False)]
    gather x2, local copies, waits for them, and re-layouts: 4.02 us -> 5.61 us  [select(): sel = sets[side, chip_slot(owner // pair, order), sub]]
  transfers between devices with their start and end apart: 13 -> 13, of which waited for: 8 -> 9; matrix products, arithmetic and copies ran while one was open for 12% -> 18% of each run, Pallas kernels for 0% -> 0%
where the time goes in v17:
time: 133 us
  waiting for transfers between devices  67.9 us (51%)
  local copies, waits for them, and re-layouts  19.5 us (15%)
  starting transfers between devices  19 us (14%)
  other arithmetic  18.2 us (14%)
  matrix products  6.99 us (5%)
    ppermute x2, waiting for transfers between devices, dp_total(): got = lax.ppermute(part, 'dp', perm=[(0, 1), (1, 0)])  43 us
    ppermute x6, waiting for transfers between devices, gather_chips(): got = lax.ppermute(held, 'chip', perm=[(i, i ^ step) for i in range(chips)])  24.5 us
    ppermute x6, starting transfers between devices, gather_chips(): got = lax.ppermute(held, 'chip', perm=[(i, i ^ step) for i in range(chips)])  9.22 us
    unnamed x25, local copies, waits for them, and re-layouts  8.94 us
    all_to_all x1, starting transfers between devices, per_device(): lax.all_to_all(jnp.stack([out_send, in_send], axis=1), 'chip', split_axis...  6.78 us
    gather x2, local copies, waits for them, and re-layouts, select(): sel = sets[side, chip_slot(owner // pair, order), sub]  5.61 us
    another operation x2, other arithmetic, gather(): return jnp.stack([mine, swap_core(mine)], axis=0)  5.51 us
    another operation x3, other arithmetic, per_device(): jnp.stack([out_send, in_send], axis=1)  3.93 us
  transfers between devices with their start and end apart: 13, of which 9 were waited for; matrix products, arithmetic and copies ran while one was open for 18% of the time, Pallas kernels for 0%

profile of v17, /device:TPU:0, one launch (start us, length us, event | category | flops | bytes accessed | tf_op | source)
XLA Modules:
  0.0 132.5 jit_solution(1952297808109202387)
XLA Ops:
  0.6 1.1 copy.60
  1.9 4.1 %collective-permute-start = (bf16[1,4,128,128]{3,2,1,0:T(8,128)(2,1)S(1)}, bf16[1,4,128,128]{3,2,1,0:T(8,128)(2,1)S(1)}, u32[]{:S(2)}, u32[]{:S(2)}) collective-permute-start(bf16[1,4,128,128]{3,2,1,0:T(8,128)(2,1)S(1)} %bitcast.114), channel_id=1, source_target_pairs={{0,8},{2,10},{4,12},{6,14},{8,0},{10,2},{12,4},{14,6},{1,9},{3,11}... | collective-permute-start | bytes 393224 | tf_op jit(solution)/shard_map/ppermute | solution.py:42
  7.3 8.7 %collective-permute-done = bf16[1,4,128,128]{3,2,1,0:T(8,128)(2,1)S(1)} collective-permute-done((bf16[1,4,128,128]{3,2,1,0:T(8,128)(2,1)S(1)}, bf16[1,4,128,128]{3,2,1,0:T(8,128)(2,1)S(1)}, u32[]{:S(2)}, u32[]{:S(2)}) %collective-permute-start) | collective-permute-done | bytes 131104 | tf_op jit(solution)/shard_map/ppermute | solution.py:42
  16.1 2.0 %collective-permute-done.5 = bf16[1,4,128,128]{3,2,1,0:T(8,128)(2,1)S(1)} collective-permute-done((bf16[1,4,128,128]{3,2,1,0:T(8,128)(2,1)S(1)}, bf16[1,4,128,128]{3,2,1,0:T(8,128)(2,1)S(1)}, u32[]{:S(2)}, u32[]{:S(2)}) %collective-permute-start.5) | collective-permute-done | bytes 131104 | tf_op jit(solution)/shard_map/ppermute | solution.py:42
  18.0 1.7 %collective-permute-start.6 = (bf16[2,4,128,128]{3,2,1,0:T(8,128)(2,1)S(1)}, bf16[2,4,128,128]{3,2,1,0:T(8,128)(2,1)S(1)}, u32[]{:S(2)}, u32[]{:S(2)}) collective-permute-start(bf16[2,4,128,128]{3,2,1,0:T(8,128)(2,1)S(1)} %maximum_select_fusion.7), channel_id=1, source_target_pairs={{0,2},{2,0},{4,6},{6,4},{8,10},{10,8},{12,14},{14,12},{1,3},{3,1},... | collective-permute-start | bytes 786440 | tf_op jit(solution)/shard_map/ppermute | solution.py:42
  19.7 3.8 %collective-permute-done.1 = bf16[2,4,128,128]{3,2,1,0:T(8,128)(2,1)S(1)} collective-permute-done((bf16[2,4,128,128]{3,2,1,0:T(8,128)(2,1)S(1)}, bf16[2,4,128,128]{3,2,1,0:T(8,128)(2,1)S(1)}, u32[]{:S(2)}, u32[]{:S(2)}) %collective-permute-start.1) | collective-permute-done | bytes 262176 | tf_op jit(solution)/shard_map/ppermute | solution.py:42
  23.6 1.6 %collective-permute-start.2 = (bf16[4,4,128,128]{3,2,1,0:T(8,128)(2,1)S(1)}, bf16[4,4,128,128]{3,2,1,0:T(8,128)(2,1)S(1)}, u32[]{:S(2)}, u32[]{:S(2)}) collective-permute-start(bf16[4,4,128,128]{3,2,1,0:T(8,128)(2,1)S(1)} %maximum_select_fusion.4), channel_id=1, source_target_pairs={{0,2},{2,0},{4,6},{6,4},{8,10},{10,8},{12,14},{14,12},{1,3},{3,1},... | collective-permute-start | bytes 1572872 | tf_op jit(solution)/shard_map/ppermute | solution.py:42
  25.3 1.0 collective-permute-done.6
  26.4 1.7 %collective-permute-start.7 = (bf16[4,4,128,128]{3,2,1,0:T(8,128)(2,1)S(1)}, bf16[4,4,128,128]{3,2,1,0:T(8,128)(2,1)S(1)}, u32[]{:S(2)}, u32[]{:S(2)}) collective-permute-start(bf16[4,4,128,128]{3,2,1,0:T(8,128)(2,1)S(1)} %maximum_select_fusion.5), channel_id=1, source_target_pairs={{0,4},{2,6},{4,0},{6,2},{8,12},{10,14},{12,8},{14,10},{1,5},{3,7},... | collective-permute-start | bytes 1572872 | tf_op jit(solution)/shard_map/ppermute | solution.py:42
  28.1 8.7 %collective-permute-done.2 = bf16[4,4,128,128]{3,2,1,0:T(8,128)(2,1)S(1)} collective-permute-done((bf16[4,4,128,128]{3,2,1,0:T(8,128)(2,1)S(1)}, bf16[4,4,128,128]{3,2,1,0:T(8,128)(2,1)S(1)}, u32[]{:S(2)}, u32[]{:S(2)}) %collective-permute-start.2) | collective-permute-done | bytes 524320 | tf_op jit(solution)/shard_map/ppermute | solution.py:42
  36.7 1.1 maximum_select_fusion.1
  38.4 1.1 maximum_select_fusion.3
  40.3 1.1 maximum_select_fusion.2
  41.5 2.8 %pad_maximum_fusion = bf16[2,8,4,128,128]{4,3,2,1,0:T(8,128)(2,1)} fusion(bf16[1,8,4,128,128]{4,3,2,1,0:T(8,128)(2,1)} %bitcast.8, bf16[1,8,4,128,128]{4,3,2,1,0:T(8,128)(2,1)S(1)} %maximum_select_fusion), kind=kLoop, calls=%fused_computation.2 | loop fusion | flops 1048576 | bytes 4194304 | tf_op jit(solution)/shard_map/stack | solution.py:75
  44.2 2.4 %gather_fusion = bf16[32,128,128]{2,1,0:T(8,128)(2,1)S(1)} fusion(bf16[2,8,4,128,128]{4,3,2,1,0:T(8,128)(2,1)} %pad_maximum_fusion, s32[32]{0:T(128)S(1)} %fusion.56), kind=kCustom, calls=%fused_computation | custom fusion | bytes 2097536 | tf_op jit(solution)/shard_map/gather | solution.py:81
  46.6 1.7 %convolution_bitcast_fusion.1 = f32[128,8,128]{2,0,1:T(8,128)S(1)} fusion(bf16[8,4,128,128]{3,2,1,0:T(8,128)(2,1)S(1)} %bitcast.102, bf16[8,4,128,128]{3,2,1,0:T(8,128)(2,1)} %param.8), kind=kOutput, calls=%fused_computation.19 | convolution fusion | flops 134217728 | bytes 2621440 | tf_op jit(solution)/shard_map/rkti,rkio->tro/dot_general | solution.py:111
  48.3 2.8 %pad_maximum_fusion.1 = bf16[2,8,4,128,128]{4,3,2,1,0:T(8,128)(2,1)} fusion(bf16[1,8,4,128,128]{4,3,2,1,0:T(8,128)(2,1)} %bitcast.31, bf16[1,8,4,128,128]{4,3,2,1,0:T(8,128)(2,1)S(1)} %copy-done.6), kind=kLoop, calls=%fused_computation.3 | loop fusion | flops 1048576 | bytes 4194304 | tf_op jit(solution)/shard_map/stack | solution.py:75
  51.1 3.3 %gather_fusion.1 = bf16[32,128,128]{2,1,0:T(8,128)(2,1)} fusion(bf16[2,8,4,128,128]{4,3,2,1,0:T(8,128)(2,1)} %pad_maximum_fusion.1, s32[32]{0:T(128)S(1)} %fusion.55), kind=kCustom, calls=%fused_computation.1 | custom fusion | bytes 2097536 | tf_op jit(solution)/shard_map/gather | solution.py:81
  56.9 1.1 fusion.6
  60.2 2.0 %copy-done.2 = f32[8,2,4,128,128]{4,0,3,2,1:T(8,128)} copy-done((f32[8,2,4,128,128]{4,0,3,2,1:T(8,128)}, f32[8,2,4,128,128]{4,0,3,2,1:T(8,128)S(1)}, u32[]{:S(2)}) %copy-start.2) | copy-done | bytes 4194328
  62.2 1.1 fusion.7
  63.6 2.3 %fusion.8 = bf16[8,1,4,128,128]{4,0,3,2,1:T(8,128)(2,1)S(1)} fusion(bf16[8,4,128,128]{3,0,2,1:T(8,128)(2,1)} %collective-permute-done.4, f32[8,2,4,128,128]{4,0,3,2,1:T(8,128)} %copy-done.1, s32[]{:T(128)S(6)} %select_n.412), kind=kLoop, calls=%fused_computation.25 | loop fusion | flops 1572864 | bytes 4194308 | tf_op jit(solution)/shard_map/stack | solution.py:123
  66.8 1.5 %fusion.9 = bf16[8,1,4,128,128]{4,0,3,2,1:T(8,128)(2,1)S(1)} fusion(bf16[8,4,128,128]{3,0,2,1:T(8,128)(2,1)} %collective-permute-done.9, f32[8,2,4,128,128]{4,0,3,2,1:T(8,128)S(1)} %copy-done.3, s32[]{:T(128)S(6)} %select_n.412), kind=kLoop, calls=%fused_computation.26 | loop fusion | flops 1572864 | bytes 4194308 | tf_op jit(solution)/shard_map/stack | solution.py:123
  68.4 1.9 %copy.69 = bf16[8,2,4,128,128]{4,3,2,1,0:T(8,128)(2,1)} copy(bf16[8,2,4,128,128]{4,0,3,2,1:T(8,128)(2,1)S(1)} %pad_maximum_fusion.2) | data formatting | bytes 4194304 | tf_op jit(solution)/shard_map/stack | solution.py:123
  70.3 6.8 %all-to-all-start = ((bf16[8,2,4,128,128]{4,3,2,1,0:T(8,128)(2,1)}), bf16[8,2,4,128,128]{4,3,2,1,0:T(8,128)(2,1)}, u32[]{:S(2)}, u32[]{:S(2)}) async-start(bf16[8,2,4,128,128]{4,3,2,1,0:T(8,128)(2,1)} %copy.69), calls=%async_computation | async-start | bytes 4194304 | tf_op jit(solution)/shard_map/all_to_all | solution.py:123
  77.1 1.7 %fusion.2 = bf16[8,4,128,128]{2,3,1,0:T(8,128)(2,1)S(1)} fusion(bf16[8,4,128,128]{3,2,1,0:T(8,128)(2,1)} %bitcast.108, f32[128,8,128]{2,0,1:T(8,128)S(1)} %convolution_bitcast_fusion.1), kind=kOutput, calls=%fused_computation.17 | convolution fusion | flops 135397376 | bytes 2621440 | tf_op jit(solution)/shard_map/tri,rkto->rkio/dot_general | solution.py:116
  78.8 1.6 %collective-permute-start.11 = (bf16[8,4,128,128]{2,3,1,0:T(8,128)(2,1)S(1)}, bf16[8,4,128,128]{2,3,1,0:T(8,128)(2,1)S(1)}, u32[]{:S(2)}, u32[]{:S(2)}) collective-permute-start(bf16[8,4,128,128]{2,3,1,0:T(8,128)(2,1)S(1)} %fusion.2), channel_id=1, source_target_pairs={{0,16},{16,0},{1,17},{17,1},{2,18},{18,2},{3,19},{19,3},{4,20},{20... | collective-permute-start | bytes 3145736 | tf_op jit(solution)/shard_map/ppermute | solution.py:92
  81.5 23.5 %collective-permute-done.11 = bf16[8,4,128,128]{2,3,1,0:T(8,128)(2,1)S(1)} collective-permute-done((bf16[8,4,128,128]{2,3,1,0:T(8,128)(2,1)S(1)}, bf16[8,4,128,128]{2,3,1,0:T(8,128)(2,1)S(1)}, u32[]{:S(2)}, u32[]{:S(2)}) %collective-permute-start.11) | collective-permute-done | bytes 1048608 | tf_op jit(solution)/shard_map/ppermute | solution.py:92
  105.4 1.3 copy.78
  106.7 19.6 %collective-permute-done.10 = bf16[8,4,128,128]{3,2,1,0:T(8,128)(2,1)} collective-permute-done((bf16[8,4,128,128]{3,2,1,0:T(8,128)(2,1)S(1)}, bf16[8,4,128,128]{3,2,1,0:T(8,128)(2,1)}, u32[]{:S(2)}, u32[]{:S(2)}) %collective-permute-start.10) | collective-permute-done | bytes 1048608 | tf_op jit(solution)/shard_map/ppermute | solution.py:92
  126.2 2.6 %add_convert_fusion.1 = bf16[8,4,128,128]{3,2,1,0:T(8,128)(2,1)} fusion(bf16[8,4,128,128]{3,2,1,0:T(8,128)(2,1)} %collective-permute-done.10, bf16[8,4,128,128]{3,2,1,0:T(8,128)(2,1)S(1)} %convolution_convert_fusion.1), kind=kLoop, calls=%fused_computation.10 | loop fusion | flops 2097152 | bytes 3145728 | tf_op jit(solution)/shard_map/convert_element_type | solution.py:93
  128.8 1.9 %slice_reduce_fusion = (bf16[4,128,128]{2,1,0:T(8,128)(2,1)S(1)}, bf16[4,128,128]{2,1,0:T(8,128)(2,1)S(1)}) fusion(bf16[8,2,4,128,128]{4,3,2,1,0:T(8,128)(2,1)} %all-to-all-done), kind=kLoop, calls=%fused_computation.27 | loop fusion | flops 917504 | bytes 2359296 | tf_op jit(solution)/shard_map/reduce_sum | solution.py:108
  (59 shorter events, 12.3 us)
Async XLA Ops:
  0.6 53.7 %copy-start = (bf16[8,4,128,128]{3,2,1,0:T(8,128)(2,1)S(1)}, bf16[8,4,128,128]{3,2,1,0:T(8,128)(2,1)}, u32[]{:S(2)}) copy-start(bf16[8,4,128,128]{3,2,1,0:T(8,128)(2,1)} %param.10) | copy-start | bytes 3145732
  1.9 14.0 %collective-permute-start = (bf16[1,4,128,128]{3,2,1,0:T(8,128)(2,1)S(1)}, bf16[1,4,128,128]{3,2,1,0:T(8,128)(2,1)S(1)}, u32[]{:S(2)}, u32[]{:S(2)}) collective-permute-start(bf16[1,4,128,128]{3,2,1,0:T(8,128)(2,1)S(1)} %bitcast.114), channel_id=1, source_target_pairs={{0,8},{2,10},{4,12},{6,14},{8,0},{10,2},{12,4},{14,6},{1,9},{3,11}... | collective-permute-start | bytes 393224 | tf_op jit(solution)/shard_map/ppermute | solution.py:42
  7.2 10.8 %collective-permute-start.5 = (bf16[1,4,128,128]{3,2,1,0:T(8,128)(2,1)S(1)}, bf16[1,4,128,128]{3,2,1,0:T(8,128)(2,1)S(1)}, u32[]{:S(2)}, u32[]{:S(2)}) collective-permute-start(bf16[1,4,128,128]{3,2,1,0:T(8,128)(2,1)S(1)} %bitcast.112), channel_id=1, source_target_pairs={{0,8},{2,10},{4,12},{6,14},{8,0},{10,2},{12,4},{14,6},{1,9},{3,11}... | collective-permute-start | bytes 393224 | tf_op jit(solution)/shard_map/ppermute | solution.py:42
  16.0 7.6 %collective-permute-start.1 = (bf16[2,4,128,128]{3,2,1,0:T(8,128)(2,1)S(1)}, bf16[2,4,128,128]{3,2,1,0:T(8,128)(2,1)S(1)}, u32[]{:S(2)}, u32[]{:S(2)}) collective-permute-start(bf16[2,4,128,128]{3,2,1,0:T(8,128)(2,1)S(1)} %maximum_select_fusion.6), channel_id=1, source_target_pairs={{0,4},{2,6},{4,0},{6,2},{8,12},{10,14},{12,8},{14,10},{1,5},{3,7},... | collective-permute-start | bytes 786440 | tf_op jit(solution)/shard_map/ppermute | solution.py:42
  18.0 8.3 %collective-permute-start.6 = (bf16[2,4,128,128]{3,2,1,0:T(8,128)(2,1)S(1)}, bf16[2,4,128,128]{3,2,1,0:T(8,128)(2,1)S(1)}, u32[]{:S(2)}, u32[]{:S(2)}) collective-permute-start(bf16[2,4,128,128]{3,2,1,0:T(8,128)(2,1)S(1)} %maximum_select_fusion.7), channel_id=1, source_target_pairs={{0,2},{2,0},{4,6},{6,4},{8,10},{10,8},{12,14},{14,12},{1,3},{3,1},... | collective-permute-start | bytes 786440 | tf_op jit(solution)/shard_map/ppermute | solution.py:42
  19.7 18.2 %copy-start.7 = (s32[8,4]{0,1:T(4,128)S(1)}, s32[8,4]{0,1:T(4,128)}, u32[]{:S(2)}) copy-start(s32[8,4]{0,1:T(4,128)} %param.9) | copy-start | bytes 388
  23.6 13.1 %collective-permute-start.2 = (bf16[4,4,128,128]{3,2,1,0:T(8,128)(2,1)S(1)}, bf16[4,4,128,128]{3,2,1,0:T(8,128)(2,1)S(1)}, u32[]{:S(2)}, u32[]{:S(2)}) collective-permute-start(bf16[4,4,128,128]{3,2,1,0:T(8,128)(2,1)S(1)} %maximum_select_fusion.4), channel_id=1, source_target_pairs={{0,2},{2,0},{4,6},{6,4},{8,10},{10,8},{12,14},{14,12},{1,3},{3,1},... | collective-permute-start | bytes 1572872 | tf_op jit(solution)/shard_map/ppermute | solution.py:42
  26.4 13.4 %copy-start.8 = (s32[8,4]{0,1:T(4,128)S(1)}, s32[8,4]{0,1:T(4,128)}, u32[]{:S(2)}) copy-start(s32[8,4]{0,1:T(4,128)} %param.11) | copy-start | bytes 388
  26.4 12.0 %collective-permute-start.7 = (bf16[4,4,128,128]{3,2,1,0:T(8,128)(2,1)S(1)}, bf16[4,4,128,128]{3,2,1,0:T(8,128)(2,1)S(1)}, u32[]{:S(2)}, u32[]{:S(2)}) collective-permute-start(bf16[4,4,128,128]{3,2,1,0:T(8,128)(2,1)S(1)} %maximum_select_fusion.5), channel_id=1, source_target_pairs={{0,4},{2,6},{4,0},{6,2},{8,12},{10,14},{12,8},{14,10},{1,5},{3,7},... | collective-permute-start | bytes 1572872 | tf_op jit(solution)/shard_map/ppermute | solution.py:42
  37.9 3.6 %collective-permute-start.3 = (bf16[8,4,128,128]{3,2,1,0:T(8,128)(2,1)}, bf16[8,4,128,128]{3,2,1,0:T(8,128)(2,1)}, u32[]{:S(2)}, u32[]{:S(2)}) collective-permute-start(bf16[8,4,128,128]{3,2,1,0:T(8,128)(2,1)} %maximum_select_fusion.1), channel_id=1, source_target_pairs={{0,1},{1,0},{2,3},{3,2},{4,5},{5,4},{6,7},{7,6},{8,9},{9,8},{10,11... | collective-permute-start | bytes 3145736 | tf_op jit(solution)/shard_map/ppermute | solution.py:22
  39.5 8.8 %collective-permute-start.8 = (bf16[8,4,128,128]{3,2,1,0:T(8,128)(2,1)}, bf16[8,4,128,128]{3,2,1,0:T(8,128)(2,1)}, u32[]{:S(2)}, u32[]{:S(2)}) collective-permute-start(bf16[8,4,128,128]{3,2,1,0:T(8,128)(2,1)} %maximum_select_fusion.3), channel_id=1, source_target_pairs={{0,1},{1,0},{2,3},{3,2},{4,5},{5,4},{6,7},{7,6},{8,9},{9,8},{10,11... | collective-permute-start | bytes 3145736 | tf_op jit(solution)/shard_map/ppermute | solution.py:22
  46.6 1.8 %copy-start.6 = (bf16[1,8,4,128,128]{4,3,2,1,0:T(8,128)(2,1)S(1)}, bf16[1,8,4,128,128]{4,3,2,1,0:T(8,128)(2,1)}, u32[]{:S(2)}) copy-start(bf16[1,8,4,128,128]{4,3,2,1,0:T(8,128)(2,1)} %maximum_select_fusion.2) | copy-start | bytes 3145732
  54.4 1.2 copy-start.5
  56.9 2.4 %copy-start.1 = (f32[8,2,4,128,128]{4,0,3,2,1:T(8,128)}, f32[8,2,4,128,128]{4,0,3,2,1:T(8,128)S(1)}, u32[]{:S(2)}) copy-start(f32[8,2,4,128,128]{4,0,3,2,1:T(8,128)S(1)} %fusion.12) | copy-start | bytes 12582916
  56.9 2.0 %copy-start.4 = (bf16[8,4,128,128]{3,2,1,0:T(8,128)(2,1)S(1)}, bf16[8,4,128,128]{3,2,1,0:T(8,128)(2,1)}, u32[]{:S(2)}) copy-start(bf16[8,4,128,128]{3,2,1,0:T(8,128)(2,1)} %param.8) | copy-start | bytes 3145732
  58.1 5.6 %collective-permute-start.4 = (bf16[8,4,128,128]{3,0,2,1:T(8,128)(2,1)}, bf16[8,4,128,128]{3,0,2,1:T(8,128)(2,1)}, u32[]{:S(2)}, u32[]{:S(2)}) collective-permute-start(bf16[8,4,128,128]{3,0,2,1:T(8,128)(2,1)} %fusion.6), channel_id=1, source_target_pairs={{0,1},{1,0},{2,3},{3,2},{4,5},{5,4},{6,7},{7,6},{8,9},{9,8},{10,11... | collective-permute-start | bytes 3145736 | tf_op jit(solution)/shard_map/ppermute | solution.py:22
  60.2 2.0 %copy-start.2 = (f32[8,2,4,128,128]{4,0,3,2,1:T(8,128)}, f32[8,2,4,128,128]{4,0,3,2,1:T(8,128)S(1)}, u32[]{:S(2)}) copy-start(f32[8,2,4,128,128]{4,0,3,2,1:T(8,128)S(1)} %fusion.10) | copy-start | bytes 12582916
  63.3 3.0 %collective-permute-start.9 = (bf16[8,4,128,128]{3,0,2,1:T(8,128)(2,1)}, bf16[8,4,128,128]{3,0,2,1:T(8,128)(2,1)}, u32[]{:S(2)}, u32[]{:S(2)}) collective-permute-start(bf16[8,4,128,128]{3,0,2,1:T(8,128)(2,1)} %fusion.7), channel_id=1, source_target_pairs={{0,1},{1,0},{2,3},{3,2},{4,5},{5,4},{6,7},{7,6},{8,9},{9,8},{10,11... | collective-permute-start | bytes 3145736 | tf_op jit(solution)/shard_map/ppermute | solution.py:22
  63.6 3.1 %copy-start.3 = (f32[8,2,4,128,128]{4,0,3,2,1:T(8,128)S(1)}, f32[8,2,4,128,128]{4,0,3,2,1:T(8,128)}, u32[]{:S(2)}) copy-start(f32[8,2,4,128,128]{4,0,3,2,1:T(8,128)} %copy-done.2) | copy-start | bytes 12582916
  70.3 58.5 %all-to-all-start = ((bf16[8,2,4,128,128]{4,3,2,1,0:T(8,128)(2,1)}), bf16[8,2,4,128,128]{4,3,2,1,0:T(8,128)(2,1)}, u32[]{:S(2)}, u32[]{:S(2)}) async-start(bf16[8,2,4,128,128]{4,3,2,1,0:T(8,128)(2,1)} %copy.69), calls=%async_computation | async-start | bytes 4194304 | tf_op jit(solution)/shard_map/all_to_all | solution.py:123
  78.8 26.1 %collective-permute-start.11 = (bf16[8,4,128,128]{2,3,1,0:T(8,128)(2,1)S(1)}, bf16[8,4,128,128]{2,3,1,0:T(8,128)(2,1)S(1)}, u32[]{:S(2)}, u32[]{:S(2)}) collective-permute-start(bf16[8,4,128,128]{2,3,1,0:T(8,128)(2,1)S(1)} %fusion.2), channel_id=1, source_target_pairs={{0,16},{16,0},{1,17},{17,1},{2,18},{18,2},{3,19},{19,3},{4,20},{20... | collective-permute-start | bytes 3145736 | tf_op jit(solution)/shard_map/ppermute | solution.py:92
  80.9 45.4 %collective-permute-start.10 = (bf16[8,4,128,128]{3,2,1,0:T(8,128)(2,1)S(1)}, bf16[8,4,128,128]{3,2,1,0:T(8,128)(2,1)}, u32[]{:S(2)}, u32[]{:S(2)}) collective-permute-start(bf16[8,4,128,128]{3,2,1,0:T(8,128)(2,1)S(1)} %convolution_convert_fusion.1), channel_id=1, source_target_pairs={{0,16},{16,0},{1,17},{17,1},{2,18},{18,2},{3,19},{19,3},{4,20},{20... | collective-permute-start | bytes 3145736 | tf_op jit(solution)/shard_map/ppermute | solution.py:92

commit v18 on v16

--- a/solution.py
+++ b/solution.py
@@ -36,21 +36,20 @@
 def gather_chips(x, chips, order):
     if order is None:
         return lax.all_gather(x, "chip", axis=0, tiled=False)
-    me = lax.axis_index("chip")
     held = x[None]
     for step in order:
         got = lax.ppermute(held, "chip", perm=[(i, i ^ step) for i in range(chips)])
-        upper = (me // step) % 2 == 1
-        held = jnp.where(upper, jnp.concatenate([got, held], axis=0), jnp.concatenate([held, got], axis=0))
+        held = jnp.concatenate([held, got], axis=0)
     return held
 
 
 def chip_slot(chip, order):
     if order is None:
         return chip
+    me = lax.axis_index("chip")
     slot = jnp.zeros_like(chip)
     for k, step in enumerate(order):
-        slot = slot + ((chip // step) % 2) * (1 << k)
+        slot = slot + ((chip // step) % 2 != (me // step) % 2).astype(chip.dtype) * (1 << k)
     return slot
 
 

time: 129 us -> 130 us (level)
  local copies, waits for them, and re-layouts: 13.8 us -> 15.3 us
    select_n x8 -> x0, other arithmetic: 3.81 us -> none  [gather_chips(): jnp.where(upper, jnp.concatenate([got, held], axis=0), jnp.concatenate([h...]
    another operation x2 -> x4, other arithmetic: 4.49 us -> 7.41 us  [gather(): return jnp.stack([mine, swap_core(mine)], axis=0)]
    unnamed x17 -> x21, local copies, waits for them, and re-layouts: 5.9 us -> 6.86 us
where the time goes in v18:
time: 130 us
  waiting for transfers between devices  73 us (56%)
  starting transfers between devices  19.7 us (15%)
  local copies, waits for them, and re-layouts  15.3 us (12%)
  other arithmetic  13.8 us (11%)
  matrix products  6.98 us (5%)
    ppermute x2, waiting for transfers between devices, dp_total(): got = lax.ppermute(part, 'dp', perm=[(0, 1), (1, 0)])  43.4 us
    ppermute x6, waiting for transfers between devices, gather_chips(): got = lax.ppermute(held, 'chip', perm=[(i, i ^ step) for i in range(chips)])  24 us
    ppermute x6, starting transfers between devices, gather_chips(): got = lax.ppermute(held, 'chip', perm=[(i, i ^ step) for i in range(chips)])  9.51 us
    another operation x4, other arithmetic, gather(): return jnp.stack([mine, swap_core(mine)], axis=0)  7.41 us
    all_to_all x1, starting transfers between devices, per_device(): lax.all_to_all(jnp.stack([out_send, in_send], axis=1), 'chip', split_axis...  6.9 us
    unnamed x21, local copies, waits for them, and re-layouts  6.86 us
    ppermute x4, waiting for transfers between devices, swap_core(): return lax.ppermute(x, 'core', perm=[(0, 1), (1, 0)])  5.66 us
    gather x2, local copies, waits for them, and re-layouts, select(): sel = sets[side, chip_slot(owner // pair, order), sub]  4.02 us
  transfers between devices with their start and end apart: 13, of which 8 were waited for; matrix products, arithmetic and copies ran while one was open for 12% of the time, Pallas kernels for 0%

profile of v18, /device:TPU:0, one launch (start us, length us, event | category | flops | bytes accessed | tf_op | source)
XLA Modules:
  0.0 129.7 jit_solution(12525558986153517060)
XLA Ops:
  0.6 1.1 copy.66
  1.9 4.1 %collective-permute-start.5 = (bf16[1,4,128,128]{3,2,1,0:T(8,128)(2,1)S(1)}, bf16[1,4,128,128]{3,2,1,0:T(8,128)(2,1)S(1)}, u32[]{:S(2)}, u32[]{:S(2)}) collective-permute-start(bf16[1,4,128,128]{3,2,1,0:T(8,128)(2,1)S(1)} %bitcast.116), channel_id=1, source_target_pairs={{0,8},{2,10},{4,12},{6,14},{8,0},{10,2},{12,4},{14,6},{1,9},{3,11}... | collective-permute-start | bytes 393224 | tf_op jit(solution)/shard_map/ppermute | solution.py:41
  6.0 1.0 copy.59
  7.3 8.7 %collective-permute-done.5 = bf16[1,4,128,128]{3,2,1,0:T(8,128)(2,1)S(1)} collective-permute-done((bf16[1,4,128,128]{3,2,1,0:T(8,128)(2,1)S(1)}, bf16[1,4,128,128]{3,2,1,0:T(8,128)(2,1)S(1)}, u32[]{:S(2)}, u32[]{:S(2)}) %collective-permute-start.5) | collective-permute-done | bytes 131104 | tf_op jit(solution)/shard_map/ppermute | solution.py:41
  16.0 1.9 %collective-permute-start.6 = (bf16[2,4,128,128]{3,2,1,0:T(8,128)(2,1)S(1)}, bf16[2,4,128,128]{3,2,1,0:T(8,128)(2,1)S(1)}, u32[]{:S(2)}, u32[]{:S(2)}) collective-permute-start(bf16[2,4,128,128]{3,2,1,0:T(8,128)(2,1)S(1)} %pad_maximum_fusion.8), channel_id=1, source_target_pairs={{0,2},{2,0},{4,6},{6,4},{8,10},{10,8},{12,14},{14,12},{1,3},{3,1},... | collective-permute-start | bytes 786440 | tf_op jit(solution)/shard_map/ppermute | solution.py:41
  18.0 0.8 collective-permute-start.1
  18.7 4.0 %collective-permute-done.6 = bf16[2,4,128,128]{3,2,1,0:T(8,128)(2,1)S(1)} collective-permute-done((bf16[2,4,128,128]{3,2,1,0:T(8,128)(2,1)S(1)}, bf16[2,4,128,128]{3,2,1,0:T(8,128)(2,1)S(1)}, u32[]{:S(2)}, u32[]{:S(2)}) %collective-permute-start.6) | collective-permute-done | bytes 262176 | tf_op jit(solution)/shard_map/ppermute | solution.py:41
  22.8 1.5 %collective-permute-start.7 = (bf16[4,4,128,128]{3,2,1,0:T(8,128)(2,1)S(1)}, bf16[4,4,128,128]{3,2,1,0:T(8,128)(2,1)S(1)}, u32[]{:S(2)}, u32[]{:S(2)}) collective-permute-start(bf16[4,4,128,128]{3,2,1,0:T(8,128)(2,1)S(1)} %pad_maximum_fusion.6), channel_id=1, source_target_pairs={{0,4},{2,6},{4,0},{6,2},{8,12},{10,14},{12,8},{14,10},{1,5},{3,7},... | collective-permute-start | bytes 1572872 | tf_op jit(solution)/shard_map/ppermute | solution.py:41
  24.3 2.5 %collective-permute-done.1 = bf16[2,4,128,128]{3,2,1,0:T(8,128)(2,1)S(1)} collective-permute-done((bf16[2,4,128,128]{3,2,1,0:T(8,128)(2,1)S(1)}, bf16[2,4,128,128]{3,2,1,0:T(8,128)(2,1)S(1)}, u32[]{:S(2)}, u32[]{:S(2)}) %collective-permute-start.1) | collective-permute-done | bytes 262176 | tf_op jit(solution)/shard_map/ppermute | solution.py:41
  26.8 1.1 collective-permute-start.2
  27.9 8.8 %collective-permute-done.7 = bf16[4,4,128,128]{3,2,1,0:T(8,128)(2,1)S(1)} collective-permute-done((bf16[4,4,128,128]{3,2,1,0:T(8,128)(2,1)S(1)}, bf16[4,4,128,128]{3,2,1,0:T(8,128)(2,1)S(1)}, u32[]{:S(2)}, u32[]{:S(2)}) %collective-permute-start.7) | collective-permute-done | bytes 524320 | tf_op jit(solution)/shard_map/ppermute | solution.py:41
  36.8 1.1 fusion.53
  37.9 1.5 %fusion.54 = (bf16[1,8,4,128,128]{4,3,2,1,0:T(8,128)(2,1)}, bf16[8,4,128,128]{3,2,1,0:T(8,128)(2,1)}) fusion(bf16[4,4,128,128]{3,2,1,0:T(8,128)(2,1)S(1)} %collective-permute-done.2, bf16[2,4,128,128]{3,2,1,0:T(8,128)(2,1)S(1)} %collective-permute-done.1, bf16[1,4,128,128]{3,2,1,0:T(8,128)(2,1)S(1)} %collective-permute-done, ...), kind=kLoop, calls=%fused_computation.147 | loop fusion | flops 1572864 | bytes 3145728 | tf_op jit(solution)/shard_map/stack | solution.py:74
  41.0 1.0 copy-done.3
  42.0 1.7 %pad_maximum_fusion.1 = bf16[2,8,4,128,128]{4,3,2,1,0:T(8,128)(2,1)S(1)} fusion(bf16[1,8,4,128,128]{4,3,2,1,0:T(8,128)(2,1)} %bitcast.120, bf16[1,8,4,128,128]{4,3,2,1,0:T(8,128)(2,1)} %get-tuple-element.32), kind=kLoop, calls=%fused_computation.3 | loop fusion | flops 1048576 | bytes 4194304 | tf_op jit(solution)/shard_map/stack | solution.py:74
  43.7 1.7 %gather_fusion.1 = bf16[32,128,128]{2,1,0:T(8,128)(2,1)} fusion(bf16[2,8,4,128,128]{4,3,2,1,0:T(8,128)(2,1)S(1)} %pad_maximum_fusion.1, s32[32]{0:T(128)S(1)} %fusion.49), kind=kCustom, calls=%fused_computation.1 | custom fusion | bytes 2097536 | tf_op jit(solution)/shard_map/gather | solution.py:80
  45.4 3.1 %pad_maximum_fusion = bf16[2,8,4,128,128]{4,3,2,1,0:T(8,128)(2,1)} fusion(bf16[1,8,4,128,128]{4,3,2,1,0:T(8,128)(2,1)} %bitcast.7, bf16[1,8,4,128,128]{4,3,2,1,0:T(8,128)(2,1)} %get-tuple-element.30), kind=kLoop, calls=%fused_computation.2 | loop fusion | flops 1048576 | bytes 4194304 | tf_op jit(solution)/shard_map/stack | solution.py:74
  48.4 2.4 %gather_fusion = bf16[32,128,128]{2,1,0:T(8,128)(2,1)S(1)} fusion(bf16[2,8,4,128,128]{4,3,2,1,0:T(8,128)(2,1)} %pad_maximum_fusion, s32[32]{0:T(128)S(1)} %fusion.50), kind=kCustom, calls=%fused_computation | custom fusion | bytes 2097536 | tf_op jit(solution)/shard_map/gather | solution.py:80
  50.8 1.7 %convolution_bitcast_fusion.1 = f32[128,8,128]{2,0,1:T(8,128)S(1)} fusion(bf16[8,4,128,128]{3,2,1,0:T(8,128)(2,1)S(1)} %bitcast.104, bf16[8,4,128,128]{3,2,1,0:T(8,128)(2,1)} %param.8), kind=kOutput, calls=%fused_computation.19 | convolution fusion | flops 134217728 | bytes 2621440 | tf_op jit(solution)/shard_map/rkti,rkio->tro/dot_general | solution.py:110
  54.7 0.8 fusion.8
  55.5 0.8 fusion.10
  58.6 3.2 %collective-permute-done.4 = f32[8,4,128,128]{3,2,1,0:T(8,128)S(1)} collective-permute-done((f32[8,4,128,128]{3,2,1,0:T(8,128)S(1)}, f32[8,4,128,128]{3,2,1,0:T(8,128)S(1)}, u32[]{:S(2)}, u32[]{:S(2)}) %collective-permute-start.4) | collective-permute-done | bytes 2097184 | tf_op jit(solution)/shard_map/ppermute | solution.py:22
  62.3 2.5 %collective-permute-done.9 = f32[8,4,128,128]{3,2,1,0:T(8,128)S(1)} collective-permute-done((f32[8,4,128,128]{3,2,1,0:T(8,128)S(1)}, f32[8,4,128,128]{3,2,1,0:T(8,128)S(1)}, u32[]{:S(2)}, u32[]{:S(2)}) %collective-permute-start.9) | collective-permute-done | bytes 2097184 | tf_op jit(solution)/shard_map/ppermute | solution.py:22
  65.5 1.5 %copy.72 = bf16[8,2,4,128,128]{4,3,2,1,0:T(8,128)(2,1)} copy(bf16[8,2,4,128,128]{4,3,2,0,1:T(8,128)(2,1)S(1)} %pad_maximum_fusion.2) | data formatting | bytes 4194304 | tf_op jit(solution)/shard_map/stack | solution.py:122
  67.0 6.9 %all-to-all-start = ((bf16[8,2,4,128,128]{4,3,2,1,0:T(8,128)(2,1)}), bf16[8,2,4,128,128]{4,3,2,1,0:T(8,128)(2,1)}, u32[]{:S(2)}, u32[]{:S(2)}) async-start(bf16[8,2,4,128,128]{4,3,2,1,0:T(8,128)(2,1)} %copy.72), calls=%async_computation | async-start | bytes 4194304 | tf_op jit(solution)/shard_map/all_to_all | solution.py:122
  73.9 1.7 %fusion.2 = bf16[8,4,128,128]{2,3,1,0:T(8,128)(2,1)S(1)} fusion(bf16[8,4,128,128]{3,2,1,0:T(8,128)(2,1)} %bitcast.108, f32[128,8,128]{2,0,1:T(8,128)S(1)} %convolution_bitcast_fusion.1), kind=kOutput, calls=%fused_computation.17 | convolution fusion | flops 135397376 | bytes 2621440 | tf_op jit(solution)/shard_map/tri,rkto->rkio/dot_general | solution.py:115
  75.6 1.6 %collective-permute-start.11 = (bf16[8,4,128,128]{2,3,1,0:T(8,128)(2,1)S(1)}, bf16[8,4,128,128]{2,3,1,0:T(8,128)(2,1)S(1)}, u32[]{:S(2)}, u32[]{:S(2)}) collective-permute-start(bf16[8,4,128,128]{2,3,1,0:T(8,128)(2,1)S(1)} %fusion.2), channel_id=1, source_target_pairs={{0,16},{16,0},{1,17},{17,1},{2,18},{18,2},{3,19},{19,3},{4,20},{20... | collective-permute-start | bytes 3145736 | tf_op jit(solution)/shard_map/ppermute | solution.py:91
  78.3 23.4 %collective-permute-done.11 = bf16[8,4,128,128]{2,3,1,0:T(8,128)(2,1)S(1)} collective-permute-done((bf16[8,4,128,128]{2,3,1,0:T(8,128)(2,1)S(1)}, bf16[8,4,128,128]{2,3,1,0:T(8,128)(2,1)S(1)}, u32[]{:S(2)}, u32[]{:S(2)}) %collective-permute-start.11) | collective-permute-done | bytes 1048608 | tf_op jit(solution)/shard_map/ppermute | solution.py:91
  102.1 1.3 %copy.81 = bf16[8,4,128,128]{3,2,1,0:T(8,128)(2,1)} copy(bf16[8,4,128,128]{2,3,1,0:T(8,128)(2,1)S(1)} %add_convert_fusion) | data formatting | bytes 2097152
  103.4 20.0 %collective-permute-done.10 = bf16[8,4,128,128]{3,2,1,0:T(8,128)(2,1)} collective-permute-done((bf16[8,4,128,128]{3,2,1,0:T(8,128)(2,1)S(1)}, bf16[8,4,128,128]{3,2,1,0:T(8,128)(2,1)}, u32[]{:S(2)}, u32[]{:S(2)}) %collective-permute-start.10) | collective-permute-done | bytes 1048608 | tf_op jit(solution)/shard_map/ppermute | solution.py:91
  123.4 2.6 %add_convert_fusion.1 = bf16[8,4,128,128]{3,2,1,0:T(8,128)(2,1)} fusion(bf16[8,4,128,128]{3,2,1,0:T(8,128)(2,1)} %collective-permute-done.10, bf16[8,4,128,128]{3,2,1,0:T(8,128)(2,1)S(1)} %convolution_convert_fusion.1), kind=kLoop, calls=%fused_computation.12 | loop fusion | flops 2097152 | bytes 3145728 | tf_op jit(solution)/shard_map/convert_element_type | solution.py:92
  126.0 1.9 %slice_reduce_fusion = (bf16[4,128,128]{2,1,0:T(8,128)(2,1)S(1)}, bf16[4,128,128]{2,1,0:T(8,128)(2,1)S(1)}) fusion(bf16[8,2,4,128,128]{4,3,2,1,0:T(8,128)(2,1)} %all-to-all-done), kind=kLoop, calls=%fused_computation.25 | loop fusion | flops 917504 | bytes 2359296 | tf_op jit(solution)/shard_map/reduce_sum | solution.py:107
  (54 shorter events, 11.0 us)
Async XLA Ops:
  0.6 51.9 %copy-start = (bf16[8,4,128,128]{3,2,1,0:T(8,128)(2,1)S(1)}, bf16[8,4,128,128]{3,2,1,0:T(8,128)(2,1)}, u32[]{:S(2)}) copy-start(bf16[8,4,128,128]{3,2,1,0:T(8,128)(2,1)} %param.10) | copy-start | bytes 3145732
  1.9 14.0 %collective-permute-start.5 = (bf16[1,4,128,128]{3,2,1,0:T(8,128)(2,1)S(1)}, bf16[1,4,128,128]{3,2,1,0:T(8,128)(2,1)S(1)}, u32[]{:S(2)}, u32[]{:S(2)}) collective-permute-start(bf16[1,4,128,128]{3,2,1,0:T(8,128)(2,1)S(1)} %bitcast.116), channel_id=1, source_target_pairs={{0,8},{2,10},{4,12},{6,14},{8,0},{10,2},{12,4},{14,6},{1,9},{3,11}... | collective-permute-start | bytes 393224 | tf_op jit(solution)/shard_map/ppermute | solution.py:41
  7.2 10.8 %collective-permute-start = (bf16[1,4,128,128]{3,2,1,0:T(8,128)(2,1)S(1)}, bf16[1,4,128,128]{3,2,1,0:T(8,128)(2,1)S(1)}, u32[]{:S(2)}, u32[]{:S(2)}) collective-permute-start(bf16[1,4,128,128]{3,2,1,0:T(8,128)(2,1)S(1)} %bitcast.112), channel_id=1, source_target_pairs={{0,8},{2,10},{4,12},{6,14},{8,0},{10,2},{12,4},{14,6},{1,9},{3,11}... | collective-permute-start | bytes 393224 | tf_op jit(solution)/shard_map/ppermute | solution.py:41
  16.0 6.7 %collective-permute-start.6 = (bf16[2,4,128,128]{3,2,1,0:T(8,128)(2,1)S(1)}, bf16[2,4,128,128]{3,2,1,0:T(8,128)(2,1)S(1)}, u32[]{:S(2)}, u32[]{:S(2)}) collective-permute-start(bf16[2,4,128,128]{3,2,1,0:T(8,128)(2,1)S(1)} %pad_maximum_fusion.8), channel_id=1, source_target_pairs={{0,2},{2,0},{4,6},{6,4},{8,10},{10,8},{12,14},{14,12},{1,3},{3,1},... | collective-permute-start | bytes 786440 | tf_op jit(solution)/shard_map/ppermute | solution.py:41
  18.0 8.8 %collective-permute-start.1 = (bf16[2,4,128,128]{3,2,1,0:T(8,128)(2,1)S(1)}, bf16[2,4,128,128]{3,2,1,0:T(8,128)(2,1)S(1)}, u32[]{:S(2)}, u32[]{:S(2)}) collective-permute-start(bf16[2,4,128,128]{3,2,1,0:T(8,128)(2,1)S(1)} %pad_maximum_fusion.7), channel_id=1, source_target_pairs={{0,4},{2,6},{4,0},{6,2},{8,12},{10,14},{12,8},{14,10},{1,5},{3,7},... | collective-permute-start | bytes 786440 | tf_op jit(solution)/shard_map/ppermute | solution.py:41
  22.8 14.0 %collective-permute-start.7 = (bf16[4,4,128,128]{3,2,1,0:T(8,128)(2,1)S(1)}, bf16[4,4,128,128]{3,2,1,0:T(8,128)(2,1)S(1)}, u32[]{:S(2)}, u32[]{:S(2)}) collective-permute-start(bf16[4,4,128,128]{3,2,1,0:T(8,128)(2,1)S(1)} %pad_maximum_fusion.6), channel_id=1, source_target_pairs={{0,4},{2,6},{4,0},{6,2},{8,12},{10,14},{12,8},{14,10},{1,5},{3,7},... | collective-permute-start | bytes 1572872 | tf_op jit(solution)/shard_map/ppermute | solution.py:41
  26.8 11.1 %collective-permute-start.2 = (bf16[4,4,128,128]{3,2,1,0:T(8,128)(2,1)S(1)}, bf16[4,4,128,128]{3,2,1,0:T(8,128)(2,1)S(1)}, u32[]{:S(2)}, u32[]{:S(2)}) collective-permute-start(bf16[4,4,128,128]{3,2,1,0:T(8,128)(2,1)S(1)} %pad_maximum_fusion.5), channel_id=1, source_target_pairs={{0,2},{2,0},{4,6},{6,4},{8,10},{10,8},{12,14},{14,12},{1,3},{3,1},... | collective-permute-start | bytes 1572872 | tf_op jit(solution)/shard_map/ppermute | solution.py:41
  37.9 2.0 %copy-start.5 = (s32[8,4]{0,1:T(4,128)S(1)}, s32[8,4]{0,1:T(4,128)}, u32[]{:S(2)}) copy-start(s32[8,4]{0,1:T(4,128)} %param.9) | copy-start | bytes 388
  37.9 2.2 %copy-start.6 = (s32[8,4]{0,1:T(4,128)S(1)}, s32[8,4]{0,1:T(4,128)}, u32[]{:S(2)}) copy-start(s32[8,4]{0,1:T(4,128)} %param.11) | copy-start | bytes 388
  37.9 3.1 %collective-permute-start.8 = (bf16[8,4,128,128]{3,2,1,0:T(8,128)(2,1)S(1)}, bf16[8,4,128,128]{3,2,1,0:T(8,128)(2,1)S(1)}, u32[]{:S(2)}, u32[]{:S(2)}) collective-permute-start(bf16[8,4,128,128]{3,2,1,0:T(8,128)(2,1)S(1)} %get-tuple-element.33), channel_id=1, source_target_pairs={{0,1},{1,0},{2,3},{3,2},{4,5},{5,4},{6,7},{7,6},{8,9},{9,8},{10,11... | collective-permute-start | bytes 3145736 | tf_op jit(solution)/shard_map/ppermute | solution.py:22
  39.4 6.0 %collective-permute-start.3 = (bf16[8,4,128,128]{3,2,1,0:T(8,128)(2,1)}, bf16[8,4,128,128]{3,2,1,0:T(8,128)(2,1)}, u32[]{:S(2)}, u32[]{:S(2)}) collective-permute-start(bf16[8,4,128,128]{3,2,1,0:T(8,128)(2,1)} %get-tuple-element.31), channel_id=1, source_target_pairs={{0,1},{1,0},{2,3},{3,2},{4,5},{5,4},{6,7},{7,6},{8,9},{9,8},{10,11... | collective-permute-start | bytes 3145736 | tf_op jit(solution)/shard_map/ppermute | solution.py:22
  41.0 1.0 copy-start.3
  50.8 2.2 %copy-start.2 = (bf16[32,128,128]{2,1,0:T(8,128)(2,1)S(1)}, bf16[32,128,128]{2,1,0:T(8,128)(2,1)}, u32[]{:S(2)}) copy-start(bf16[32,128,128]{2,1,0:T(8,128)(2,1)} %gather_fusion.1) | copy-start | bytes 3145732
  53.0 1.2 copy-start.1
  54.7 0.9 copy-start.4
  57.6 4.2 %collective-permute-start.4 = (f32[8,4,128,128]{3,2,1,0:T(8,128)S(1)}, f32[8,4,128,128]{3,2,1,0:T(8,128)S(1)}, u32[]{:S(2)}, u32[]{:S(2)}) collective-permute-start(f32[8,4,128,128]{3,2,1,0:T(8,128)S(1)} %bitcast.111), channel_id=1, source_target_pairs={{0,1},{1,0},{2,3},{3,2},{4,5},{5,4},{6,7},{7,6},{8,9},{9,8},{10,11... | collective-permute-start | bytes 6291464 | tf_op jit(solution)/shard_map/ppermute | solution.py:22
  58.1 6.7 %collective-permute-start.9 = (f32[8,4,128,128]{3,2,1,0:T(8,128)S(1)}, f32[8,4,128,128]{3,2,1,0:T(8,128)S(1)}, u32[]{:S(2)}, u32[]{:S(2)}) collective-permute-start(f32[8,4,128,128]{3,2,1,0:T(8,128)S(1)} %bitcast.110), channel_id=1, source_target_pairs={{0,1},{1,0},{2,3},{3,2},{4,5},{5,4},{6,7},{7,6},{8,9},{9,8},{10,11... | collective-permute-start | bytes 6291464 | tf_op jit(solution)/shard_map/ppermute | solution.py:22
  67.0 59.0 %all-to-all-start = ((bf16[8,2,4,128,128]{4,3,2,1,0:T(8,128)(2,1)}), bf16[8,2,4,128,128]{4,3,2,1,0:T(8,128)(2,1)}, u32[]{:S(2)}, u32[]{:S(2)}) async-start(bf16[8,2,4,128,128]{4,3,2,1,0:T(8,128)(2,1)} %copy.72), calls=%async_computation | async-start | bytes 4194304 | tf_op jit(solution)/shard_map/all_to_all | solution.py:122
  75.6 26.1 %collective-permute-start.11 = (bf16[8,4,128,128]{2,3,1,0:T(8,128)(2,1)S(1)}, bf16[8,4,128,128]{2,3,1,0:T(8,128)(2,1)S(1)}, u32[]{:S(2)}, u32[]{:S(2)}) collective-permute-start(bf16[8,4,128,128]{2,3,1,0:T(8,128)(2,1)S(1)} %fusion.2), channel_id=1, source_target_pairs={{0,16},{16,0},{1,17},{17,1},{2,18},{18,2},{3,19},{19,3},{4,20},{20... | collective-permute-start | bytes 3145736 | tf_op jit(solution)/shard_map/ppermute | solution.py:91
  77.7 45.7 %collective-permute-start.10 = (bf16[8,4,128,128]{3,2,1,0:T(8,128)(2,1)S(1)}, bf16[8,4,128,128]{3,2,1,0:T(8,128)(2,1)}, u32[]{:S(2)}, u32[]{:S(2)}) collective-permute-start(bf16[8,4,128,128]{3,2,1,0:T(8,128)(2,1)S(1)} %convolution_convert_fusion.1), channel_id=1, source_target_pairs={{0,16},{16,0},{1,17},{17,1},{2,18},{18,2},{3,19},{19,3},{4,20},{20... | collective-permute-start | bytes 3145736 | tf_op jit(solution)/shard_map/ppermute | solution.py:91

commit v19 on v16

--- a/solution.py
+++ b/solution.py
@@ -67,7 +67,7 @@
     col_count = chips * pair * own_blocks
     core = lax.axis_index("core")
 
-    order_in, order_grad = chip_orders(chips)
+    order_grad, order_in = chip_orders(chips)
 
     def gather(x, order):
         x = x.reshape(tok_rows, own_blocks, block_size).transpose(1, 0, 2)

time: 129 us -> 129 us (level)
  transfers between devices with their start and end apart: 13 -> 13, of which waited for: 8 -> 10; matrix products, arithmetic and copies ran while one was open for 12% -> 12% of each run, Pallas kernels for 0% -> 0%
where the time goes in v19:
time: 129 us
  waiting for transfers between devices  73.8 us (57%)
  starting transfers between devices  18.8 us (15%)
  other arithmetic  14.5 us (11%)
  local copies, waits for them, and re-layouts  13.8 us (11%)
  matrix products  6.99 us (5%)
    ppermute x2, waiting for transfers between devices, dp_total(): got = lax.ppermute(part, 'dp', perm=[(0, 1), (1, 0)])  43.4 us
    ppermute x6, waiting for transfers between devices, gather_chips(): got = lax.ppermute(held, 'chip', perm=[(i, i ^ step) for i in range(chips)])  24.7 us
    ppermute x6, starting transfers between devices, gather_chips(): got = lax.ppermute(held, 'chip', perm=[(i, i ^ step) for i in range(chips)])  9.22 us
    all_to_all x1, starting transfers between devices, per_device(): lax.all_to_all(jnp.stack([out_send, in_send], axis=1), 'chip', split_axis...  6.79 us
    unnamed x17, local copies, waits for them, and re-layouts  5.89 us
    ppermute x4, waiting for transfers between devices, swap_core(): return lax.ppermute(x, 'core', perm=[(0, 1), (1, 0)])  5.78 us
    another operation x2, other arithmetic, gather(): return jnp.stack([mine, swap_core(mine)], axis=0)  4.49 us
    gather x2, local copies, waits for them, and re-layouts, select(): sel = sets[side, chip_slot(owner // pair, order), sub]  4.02 us
  transfers between devices with their start and end apart: 13, of which 10 were waited for; matrix products, arithmetic and copies ran while one was open for 12% of the time, Pallas kernels for 0%

profile of v19, /device:TPU:0, one launch (start us, length us, event | category | flops | bytes accessed | tf_op | source)
XLA Modules:
  0.0 128.9 jit_solution(13082013485007497472)
XLA Ops:
  0.6 1.1 copy.66
  1.9 4.1 %collective-permute-start.5 = (bf16[1,4,128,128]{3,2,1,0:T(8,128)(2,1)S(1)}, bf16[1,4,128,128]{3,2,1,0:T(8,128)(2,1)S(1)}, u32[]{:S(2)}, u32[]{:S(2)}) collective-permute-start(bf16[1,4,128,128]{3,2,1,0:T(8,128)(2,1)S(1)} %bitcast.118), channel_id=1, source_target_pairs={{0,8},{2,10},{4,12},{6,14},{8,0},{10,2},{12,4},{14,6},{1,9},{3,11}... | collective-permute-start | bytes 393224 | tf_op jit(solution)/shard_map/ppermute | solution.py:42
  6.0 1.0 copy.59
  7.3 8.7 %collective-permute-done.5 = bf16[1,4,128,128]{3,2,1,0:T(8,128)(2,1)S(1)} collective-permute-done((bf16[1,4,128,128]{3,2,1,0:T(8,128)(2,1)S(1)}, bf16[1,4,128,128]{3,2,1,0:T(8,128)(2,1)S(1)}, u32[]{:S(2)}, u32[]{:S(2)}) %collective-permute-start.5) | collective-permute-done | bytes 131104 | tf_op jit(solution)/shard_map/ppermute | solution.py:42
  16.1 2.0 %collective-permute-done = bf16[1,4,128,128]{3,2,1,0:T(8,128)(2,1)S(1)} collective-permute-done((bf16[1,4,128,128]{3,2,1,0:T(8,128)(2,1)S(1)}, bf16[1,4,128,128]{3,2,1,0:T(8,128)(2,1)S(1)}, u32[]{:S(2)}, u32[]{:S(2)}) %collective-permute-start) | collective-permute-done | bytes 131104 | tf_op jit(solution)/shard_map/ppermute | solution.py:42
  18.0 1.7 %collective-permute-start.1 = (bf16[2,4,128,128]{3,2,1,0:T(8,128)(2,1)S(1)}, bf16[2,4,128,128]{3,2,1,0:T(8,128)(2,1)S(1)}, u32[]{:S(2)}, u32[]{:S(2)}) collective-permute-start(bf16[2,4,128,128]{3,2,1,0:T(8,128)(2,1)S(1)} %maximum_select_fusion.6), channel_id=1, source_target_pairs={{0,2},{2,0},{4,6},{6,4},{8,10},{10,8},{12,14},{14,12},{1,3},{3,1},... | collective-permute-start | bytes 786440 | tf_op jit(solution)/shard_map/ppermute | solution.py:42
  19.7 3.8 %collective-permute-done.6 = bf16[2,4,128,128]{3,2,1,0:T(8,128)(2,1)S(1)} collective-permute-done((bf16[2,4,128,128]{3,2,1,0:T(8,128)(2,1)S(1)}, bf16[2,4,128,128]{3,2,1,0:T(8,128)(2,1)S(1)}, u32[]{:S(2)}, u32[]{:S(2)}) %collective-permute-start.6) | collective-permute-done | bytes 262176 | tf_op jit(solution)/shard_map/ppermute | solution.py:42
  23.6 1.6 %collective-permute-start.7 = (bf16[4,4,128,128]{3,2,1,0:T(8,128)(2,1)S(1)}, bf16[4,4,128,128]{3,2,1,0:T(8,128)(2,1)S(1)}, u32[]{:S(2)}, u32[]{:S(2)}) collective-permute-start(bf16[4,4,128,128]{3,2,1,0:T(8,128)(2,1)S(1)} %maximum_select_fusion.5), channel_id=1, source_target_pairs={{0,2},{2,0},{4,6},{6,4},{8,10},{10,8},{12,14},{14,12},{1,3},{3,1},... | collective-permute-start | bytes 1572872 | tf_op jit(solution)/shard_map/ppermute | solution.py:42
  25.3 1.0 collective-permute-done.1
  26.4 1.7 %collective-permute-start.2 = (bf16[4,4,128,128]{3,2,1,0:T(8,128)(2,1)S(1)}, bf16[4,4,128,128]{3,2,1,0:T(8,128)(2,1)S(1)}, u32[]{:S(2)}, u32[]{:S(2)}) collective-permute-start(bf16[4,4,128,128]{3,2,1,0:T(8,128)(2,1)S(1)} %maximum_select_fusion.4), channel_id=1, source_target_pairs={{0,4},{2,6},{4,0},{6,2},{8,12},{10,14},{12,8},{14,10},{1,5},{3,7},... | collective-permute-start | bytes 1572872 | tf_op jit(solution)/shard_map/ppermute | solution.py:42
  28.1 8.7 %collective-permute-done.7 = bf16[4,4,128,128]{3,2,1,0:T(8,128)(2,1)S(1)} collective-permute-done((bf16[4,4,128,128]{3,2,1,0:T(8,128)(2,1)S(1)}, bf16[4,4,128,128]{3,2,1,0:T(8,128)(2,1)S(1)}, u32[]{:S(2)}, u32[]{:S(2)}) %collective-permute-start.7) | collective-permute-done | bytes 524320 | tf_op jit(solution)/shard_map/ppermute | solution.py:42
  36.7 1.1 maximum_select_fusion.3
  38.4 1.1 maximum_select_fusion.1
  40.1 1.2 maximum_select_fusion
  41.5 1.4 %pad_maximum_fusion.1 = bf16[2,8,4,128,128]{4,3,2,1,0:T(8,128)(2,1)S(1)} fusion(bf16[1,8,4,128,128]{4,3,2,1,0:T(8,128)(2,1)} %bitcast.31, bf16[1,8,4,128,128]{4,3,2,1,0:T(8,128)(2,1)S(1)} %maximum_select_fusion.2), kind=kLoop, calls=%fused_computation.3 | loop fusion | flops 1048576 | bytes 4194304 | tf_op jit(solution)/shard_map/stack | solution.py:75
  42.9 1.7 %gather_fusion.1 = bf16[32,128,128]{2,1,0:T(8,128)(2,1)} fusion(bf16[2,8,4,128,128]{4,3,2,1,0:T(8,128)(2,1)S(1)} %pad_maximum_fusion.1, s32[32]{0:T(128)S(1)} %fusion.53), kind=kCustom, calls=%fused_computation.1 | custom fusion | bytes 2097536 | tf_op jit(solution)/shard_map/gather | solution.py:81
  44.6 3.1 %pad_maximum_fusion = bf16[2,8,4,128,128]{4,3,2,1,0:T(8,128)(2,1)} fusion(bf16[1,8,4,128,128]{4,3,2,1,0:T(8,128)(2,1)} %bitcast.8, bf16[1,8,4,128,128]{4,3,2,1,0:T(8,128)(2,1)} %maximum_select_fusion), kind=kLoop, calls=%fused_computation.2 | loop fusion | flops 1048576 | bytes 4194304 | tf_op jit(solution)/shard_map/stack | solution.py:75
  47.6 2.4 %gather_fusion = bf16[32,128,128]{2,1,0:T(8,128)(2,1)S(1)} fusion(bf16[2,8,4,128,128]{4,3,2,1,0:T(8,128)(2,1)} %pad_maximum_fusion, s32[32]{0:T(128)S(1)} %fusion.54), kind=kCustom, calls=%fused_computation | custom fusion | bytes 2097536 | tf_op jit(solution)/shard_map/gather | solution.py:81
  50.0 1.7 %convolution_bitcast_fusion.1 = f32[128,8,128]{2,0,1:T(8,128)S(1)} fusion(bf16[8,4,128,128]{3,2,1,0:T(8,128)(2,1)S(1)} %bitcast.104, bf16[8,4,128,128]{3,2,1,0:T(8,128)(2,1)} %param.8), kind=kOutput, calls=%fused_computation.19 | convolution fusion | flops 134217728 | bytes 2621440 | tf_op jit(solution)/shard_map/rkti,rkio->tro/dot_general | solution.py:111
  53.9 0.8 fusion.8
  54.7 0.8 fusion.10
  57.8 3.3 %collective-permute-done.4 = f32[8,4,128,128]{3,2,1,0:T(8,128)S(1)} collective-permute-done((f32[8,4,128,128]{3,2,1,0:T(8,128)S(1)}, f32[8,4,128,128]{3,2,1,0:T(8,128)S(1)}, u32[]{:S(2)}, u32[]{:S(2)}) %collective-permute-start.4) | collective-permute-done | bytes 2097184 | tf_op jit(solution)/shard_map/ppermute | solution.py:22
  61.6 2.5 %collective-permute-done.9 = f32[8,4,128,128]{3,2,1,0:T(8,128)S(1)} collective-permute-done((f32[8,4,128,128]{3,2,1,0:T(8,128)S(1)}, f32[8,4,128,128]{3,2,1,0:T(8,128)S(1)}, u32[]{:S(2)}, u32[]{:S(2)}) %collective-permute-start.9) | collective-permute-done | bytes 2097184 | tf_op jit(solution)/shard_map/ppermute | solution.py:22
  64.8 1.5 %copy.72 = bf16[8,2,4,128,128]{4,3,2,1,0:T(8,128)(2,1)} copy(bf16[8,2,4,128,128]{4,3,2,0,1:T(8,128)(2,1)S(1)} %pad_maximum_fusion.2) | data formatting | bytes 4194304 | tf_op jit(solution)/shard_map/stack | solution.py:123
  66.3 6.8 %all-to-all-start = ((bf16[8,2,4,128,128]{4,3,2,1,0:T(8,128)(2,1)}), bf16[8,2,4,128,128]{4,3,2,1,0:T(8,128)(2,1)}, u32[]{:S(2)}, u32[]{:S(2)}) async-start(bf16[8,2,4,128,128]{4,3,2,1,0:T(8,128)(2,1)} %copy.72), calls=%async_computation | async-start | bytes 4194304 | tf_op jit(solution)/shard_map/all_to_all | solution.py:123
  73.1 1.7 %fusion.2 = bf16[8,4,128,128]{2,3,1,0:T(8,128)(2,1)S(1)} fusion(bf16[8,4,128,128]{3,2,1,0:T(8,128)(2,1)} %bitcast.110, f32[128,8,128]{2,0,1:T(8,128)S(1)} %convolution_bitcast_fusion.1), kind=kOutput, calls=%fused_computation.17 | convolution fusion | flops 135397376 | bytes 2621440 | tf_op jit(solution)/shard_map/tri,rkto->rkio/dot_general | solution.py:116
  74.8 1.6 %collective-permute-start.11 = (bf16[8,4,128,128]{2,3,1,0:T(8,128)(2,1)S(1)}, bf16[8,4,128,128]{2,3,1,0:T(8,128)(2,1)S(1)}, u32[]{:S(2)}, u32[]{:S(2)}) collective-permute-start(bf16[8,4,128,128]{2,3,1,0:T(8,128)(2,1)S(1)} %fusion.2), channel_id=1, source_target_pairs={{0,16},{16,0},{1,17},{17,1},{2,18},{18,2},{3,19},{19,3},{4,20},{20... | collective-permute-start | bytes 3145736 | tf_op jit(solution)/shard_map/ppermute | solution.py:92
  77.5 23.4 %collective-permute-done.11 = bf16[8,4,128,128]{2,3,1,0:T(8,128)(2,1)S(1)} collective-permute-done((bf16[8,4,128,128]{2,3,1,0:T(8,128)(2,1)S(1)}, bf16[8,4,128,128]{2,3,1,0:T(8,128)(2,1)S(1)}, u32[]{:S(2)}, u32[]{:S(2)}) %collective-permute-start.11) | collective-permute-done | bytes 1048608 | tf_op jit(solution)/shard_map/ppermute | solution.py:92
  101.3 1.3 %copy.81 = bf16[8,4,128,128]{3,2,1,0:T(8,128)(2,1)} copy(bf16[8,4,128,128]{2,3,1,0:T(8,128)(2,1)S(1)} %add_convert_fusion) | data formatting | bytes 2097152
  102.6 20.0 %collective-permute-done.10 = bf16[8,4,128,128]{3,2,1,0:T(8,128)(2,1)} collective-permute-done((bf16[8,4,128,128]{3,2,1,0:T(8,128)(2,1)S(1)}, bf16[8,4,128,128]{3,2,1,0:T(8,128)(2,1)}, u32[]{:S(2)}, u32[]{:S(2)}) %collective-permute-start.10) | collective-permute-done | bytes 1048608 | tf_op jit(solution)/shard_map/ppermute | solution.py:92
  122.6 2.6 %add_convert_fusion.1 = bf16[8,4,128,128]{3,2,1,0:T(8,128)(2,1)} fusion(bf16[8,4,128,128]{3,2,1,0:T(8,128)(2,1)} %collective-permute-done.10, bf16[8,4,128,128]{3,2,1,0:T(8,128)(2,1)S(1)} %convolution_convert_fusion.1), kind=kLoop, calls=%fused_computation.12 | loop fusion | flops 2097152 | bytes 3145728 | tf_op jit(solution)/shard_map/convert_element_type | solution.py:93
  125.2 1.9 %slice_reduce_fusion = (bf16[4,128,128]{2,1,0:T(8,128)(2,1)S(1)}, bf16[4,128,128]{2,1,0:T(8,128)(2,1)S(1)}) fusion(bf16[8,2,4,128,128]{4,3,2,1,0:T(8,128)(2,1)} %all-to-all-done), kind=kLoop, calls=%fused_computation.25 | loop fusion | flops 917504 | bytes 2359296 | tf_op jit(solution)/shard_map/reduce_sum | solution.py:108
  (52 shorter events, 10.8 us)
Async XLA Ops:
  0.6 51.1 %copy-start = (bf16[8,4,128,128]{3,2,1,0:T(8,128)(2,1)S(1)}, bf16[8,4,128,128]{3,2,1,0:T(8,128)(2,1)}, u32[]{:S(2)}) copy-start(bf16[8,4,128,128]{3,2,1,0:T(8,128)(2,1)} %param.10) | copy-start | bytes 3145732
  1.9 14.0 %collective-permute-start.5 = (bf16[1,4,128,128]{3,2,1,0:T(8,128)(2,1)S(1)}, bf16[1,4,128,128]{3,2,1,0:T(8,128)(2,1)S(1)}, u32[]{:S(2)}, u32[]{:S(2)}) collective-permute-start(bf16[1,4,128,128]{3,2,1,0:T(8,128)(2,1)S(1)} %bitcast.118), channel_id=1, source_target_pairs={{0,8},{2,10},{4,12},{6,14},{8,0},{10,2},{12,4},{14,6},{1,9},{3,11}... | collective-permute-start | bytes 393224 | tf_op jit(solution)/shard_map/ppermute | solution.py:42
  7.2 10.8 %collective-permute-start = (bf16[1,4,128,128]{3,2,1,0:T(8,128)(2,1)S(1)}, bf16[1,4,128,128]{3,2,1,0:T(8,128)(2,1)S(1)}, u32[]{:S(2)}, u32[]{:S(2)}) collective-permute-start(bf16[1,4,128,128]{3,2,1,0:T(8,128)(2,1)S(1)} %bitcast.116), channel_id=1, source_target_pairs={{0,8},{2,10},{4,12},{6,14},{8,0},{10,2},{12,4},{14,6},{1,9},{3,11}... | collective-permute-start | bytes 393224 | tf_op jit(solution)/shard_map/ppermute | solution.py:42
  16.0 7.6 %collective-permute-start.6 = (bf16[2,4,128,128]{3,2,1,0:T(8,128)(2,1)S(1)}, bf16[2,4,128,128]{3,2,1,0:T(8,128)(2,1)S(1)}, u32[]{:S(2)}, u32[]{:S(2)}) collective-permute-start(bf16[2,4,128,128]{3,2,1,0:T(8,128)(2,1)S(1)} %maximum_select_fusion.7), channel_id=1, source_target_pairs={{0,4},{2,6},{4,0},{6,2},{8,12},{10,14},{12,8},{14,10},{1,5},{3,7},... | collective-permute-start | bytes 786440 | tf_op jit(solution)/shard_map/ppermute | solution.py:42
  18.0 8.3 %collective-permute-start.1 = (bf16[2,4,128,128]{3,2,1,0:T(8,128)(2,1)S(1)}, bf16[2,4,128,128]{3,2,1,0:T(8,128)(2,1)S(1)}, u32[]{:S(2)}, u32[]{:S(2)}) collective-permute-start(bf16[2,4,128,128]{3,2,1,0:T(8,128)(2,1)S(1)} %maximum_select_fusion.6), channel_id=1, source_target_pairs={{0,2},{2,0},{4,6},{6,4},{8,10},{10,8},{12,14},{14,12},{1,3},{3,1},... | collective-permute-start | bytes 786440 | tf_op jit(solution)/shard_map/ppermute | solution.py:42
  23.6 13.1 %collective-permute-start.7 = (bf16[4,4,128,128]{3,2,1,0:T(8,128)(2,1)S(1)}, bf16[4,4,128,128]{3,2,1,0:T(8,128)(2,1)S(1)}, u32[]{:S(2)}, u32[]{:S(2)}) collective-permute-start(bf16[4,4,128,128]{3,2,1,0:T(8,128)(2,1)S(1)} %maximum_select_fusion.5), channel_id=1, source_target_pairs={{0,2},{2,0},{4,6},{6,4},{8,10},{10,8},{12,14},{14,12},{1,3},{3,1},... | collective-permute-start | bytes 1572872 | tf_op jit(solution)/shard_map/ppermute | solution.py:42
  26.4 13.2 %copy-start.3 = (s32[8,4]{0,1:T(4,128)S(1)}, s32[8,4]{0,1:T(4,128)}, u32[]{:S(2)}) copy-start(s32[8,4]{0,1:T(4,128)} %param.9) | copy-start | bytes 388
  26.4 13.4 %copy-start.4 = (s32[8,4]{0,1:T(4,128)S(1)}, s32[8,4]{0,1:T(4,128)}, u32[]{:S(2)}) copy-start(s32[8,4]{0,1:T(4,128)} %param.11) | copy-start | bytes 388
  26.4 12.0 %collective-permute-start.2 = (bf16[4,4,128,128]{3,2,1,0:T(8,128)(2,1)S(1)}, bf16[4,4,128,128]{3,2,1,0:T(8,128)(2,1)S(1)}, u32[]{:S(2)}, u32[]{:S(2)}) collective-permute-start(bf16[4,4,128,128]{3,2,1,0:T(8,128)(2,1)S(1)} %maximum_select_fusion.4), channel_id=1, source_target_pairs={{0,4},{2,6},{4,0},{6,2},{8,12},{10,14},{12,8},{14,10},{1,5},{3,7},... | collective-permute-start | bytes 1572872 | tf_op jit(solution)/shard_map/ppermute | solution.py:42
  37.9 3.6 %collective-permute-start.8 = (bf16[8,4,128,128]{3,2,1,0:T(8,128)(2,1)}, bf16[8,4,128,128]{3,2,1,0:T(8,128)(2,1)}, u32[]{:S(2)}, u32[]{:S(2)}) collective-permute-start(bf16[8,4,128,128]{3,2,1,0:T(8,128)(2,1)} %maximum_select_fusion.3), channel_id=1, source_target_pairs={{0,1},{1,0},{2,3},{3,2},{4,5},{5,4},{6,7},{7,6},{8,9},{9,8},{10,11... | collective-permute-start | bytes 3145736 | tf_op jit(solution)/shard_map/ppermute | solution.py:22
  39.5 5.0 %collective-permute-start.3 = (bf16[8,4,128,128]{3,2,1,0:T(8,128)(2,1)}, bf16[8,4,128,128]{3,2,1,0:T(8,128)(2,1)}, u32[]{:S(2)}, u32[]{:S(2)}) collective-permute-start(bf16[8,4,128,128]{3,2,1,0:T(8,128)(2,1)} %maximum_select_fusion.1), channel_id=1, source_target_pairs={{0,1},{1,0},{2,3},{3,2},{4,5},{5,4},{6,7},{7,6},{8,9},{9,8},{10,11... | collective-permute-start | bytes 3145736 | tf_op jit(solution)/shard_map/ppermute | solution.py:22
  50.0 2.2 %copy-start.2 = (bf16[32,128,128]{2,1,0:T(8,128)(2,1)S(1)}, bf16[32,128,128]{2,1,0:T(8,128)(2,1)}, u32[]{:S(2)}) copy-start(bf16[32,128,128]{2,1,0:T(8,128)(2,1)} %gather_fusion.1) | copy-start | bytes 3145732
  52.2 1.2 copy-start.1
  56.8 4.4 %collective-permute-start.4 = (f32[8,4,128,128]{3,2,1,0:T(8,128)S(1)}, f32[8,4,128,128]{3,2,1,0:T(8,128)S(1)}, u32[]{:S(2)}, u32[]{:S(2)}) collective-permute-start(f32[8,4,128,128]{3,2,1,0:T(8,128)S(1)} %bitcast.115), channel_id=1, source_target_pairs={{0,1},{1,0},{2,3},{3,2},{4,5},{5,4},{6,7},{7,6},{8,9},{9,8},{10,11... | collective-permute-start | bytes 6291464 | tf_op jit(solution)/shard_map/ppermute | solution.py:22
  57.7 6.4 %collective-permute-start.9 = (f32[8,4,128,128]{3,2,1,0:T(8,128)S(1)}, f32[8,4,128,128]{3,2,1,0:T(8,128)S(1)}, u32[]{:S(2)}, u32[]{:S(2)}) collective-permute-start(f32[8,4,128,128]{3,2,1,0:T(8,128)S(1)} %bitcast.114), channel_id=1, source_target_pairs={{0,1},{1,0},{2,3},{3,2},{4,5},{5,4},{6,7},{7,6},{8,9},{9,8},{10,11... | collective-permute-start | bytes 6291464 | tf_op jit(solution)/shard_map/ppermute | solution.py:22
  66.3 58.9 %all-to-all-start = ((bf16[8,2,4,128,128]{4,3,2,1,0:T(8,128)(2,1)}), bf16[8,2,4,128,128]{4,3,2,1,0:T(8,128)(2,1)}, u32[]{:S(2)}, u32[]{:S(2)}) async-start(bf16[8,2,4,128,128]{4,3,2,1,0:T(8,128)(2,1)} %copy.72), calls=%async_computation | async-start | bytes 4194304 | tf_op jit(solution)/shard_map/all_to_all | solution.py:123
  74.8 26.1 %collective-permute-start.11 = (bf16[8,4,128,128]{2,3,1,0:T(8,128)(2,1)S(1)}, bf16[8,4,128,128]{2,3,1,0:T(8,128)(2,1)S(1)}, u32[]{:S(2)}, u32[]{:S(2)}) collective-permute-start(bf16[8,4,128,128]{2,3,1,0:T(8,128)(2,1)S(1)} %fusion.2), channel_id=1, source_target_pairs={{0,16},{16,0},{1,17},{17,1},{2,18},{18,2},{3,19},{19,3},{4,20},{20... | collective-permute-start | bytes 3145736 | tf_op jit(solution)/shard_map/ppermute | solution.py:92
  76.9 45.7 %collective-permute-start.10 = (bf16[8,4,128,128]{3,2,1,0:T(8,128)(2,1)S(1)}, bf16[8,4,128,128]{3,2,1,0:T(8,128)(2,1)}, u32[]{:S(2)}, u32[]{:S(2)}) collective-permute-start(bf16[8,4,128,128]{3,2,1,0:T(8,128)(2,1)S(1)} %convolution_convert_fusion.1), channel_id=1, source_target_pairs={{0,16},{16,0},{1,17},{17,1},{2,18},{18,2},{3,19},{19,3},{4,20},{20... | collective-permute-start | bytes 3145736 | tf_op jit(solution)/shard_map/ppermute | solution.py:92

commit v20 on v19

--- a/solution.py
+++ b/solution.py
@@ -114,7 +114,6 @@
     out_send = chip_sums(out_terms, out_flat)
 
     w_out_part = jnp.einsum("tri,rkto->rkio", hidden, grad_sel, preferred_element_type=jnp.float32)
-    w_out_grad = dp_total(w_out_part)
 
     hid_grad = jnp.einsum("rkto,rkio->tri", grad_sel, w_out, preferred_element_type=jnp.float32)
     pre_grad = (hid_grad * gelu_slope(preact)).astype(jnp.bfloat16)
@@ -124,7 +123,8 @@
     outputs = finish(got[:, 0])
     in_grad = finish(got[:, 1])
     w_in_part = jnp.einsum("rkti,tro->rkio", in_sel, pre_grad, preferred_element_type=jnp.float32)
-    w_in_grad = dp_total(w_in_part)
+    w_both = dp_total(jnp.stack([w_in_part, w_out_part], axis=0))
+    w_in_grad, w_out_grad = w_both[0], w_both[1]
     return (outputs, in_grad, w_in_grad, w_out_grad)
 
 

time: 129 us -> 129 us (level)
  waiting for transfers between devices: 73.8 us -> 76.6 us
  other arithmetic: 14.5 us -> 12.8 us
    ppermute x2 -> x1, waiting for transfers between devices: 43.4 us -> 46.1 us  [dp_total(): got = lax.ppermute(part, 'dp', perm=[(0, 1), (1, 0)])]
    convert_element_type x2 -> x1, other arithmetic: 2.99 us -> 1.08 us  [dp_total(): (part.astype(jnp.float32) + got.astype(jnp.float32)).astype(jnp.bfloat16)]
    squeeze x0 -> x1, local copies, waits for them, and re-layouts: none -> 1.45 us  [per_device(): w_in_grad, w_out_grad = (w_both[0], w_both[1])]
    unnamed x17 -> x18, local copies, waits for them, and re-layouts: 5.89 us -> 5.29 us
  transfers between devices with their start and end apart: 13 -> 12, of which waited for: 10 -> 9; matrix products, arithmetic and copies ran while one was open for 12% -> 10% of each run, Pallas kernels for 0% -> 0%
where the time goes in v20:
time: 129 us
  waiting for transfers between devices  76.6 us (59%)
  starting transfers between devices  18.2 us (14%)
  local copies, waits for them, and re-layouts  14.7 us (11%)
  other arithmetic  12.8 us (10%)
  matrix products  5.74 us (4%)
    ppermute x1, waiting for transfers between devices, dp_total(): got = lax.ppermute(part, 'dp', perm=[(0, 1), (1, 0)])  46.1 us
    ppermute x6, waiting for transfers between devices, gather_chips(): got = lax.ppermute(held, 'chip', perm=[(i, i ^ step) for i in range(chips)])  24.7 us
    ppermute x6, starting transfers between devices, gather_chips(): got = lax.ppermute(held, 'chip', perm=[(i, i ^ step) for i in range(chips)])  9.22 us
    all_to_all x1, starting transfers between devices, per_device(): lax.all_to_all(jnp.stack([out_send, in_send], axis=1), 'chip', split_axis...  6.79 us
    ppermute x4, waiting for transfers between devices, swap_core(): return lax.ppermute(x, 'core', perm=[(0, 1), (1, 0)])  5.78 us
    unnamed x18, local copies, waits for them, and re-layouts  5.29 us
    another operation x2, other arithmetic, gather(): return jnp.stack([mine, swap_core(mine)], axis=0)  4.48 us
    gather x2, local copies, waits for them, and re-layouts, select(): sel = sets[side, chip_slot(owner // pair, order), sub]  4.02 us
  transfers between devices with their start and end apart: 12, of which 9 were waited for; matrix products, arithmetic and copies ran while one was open for 10% of the time, Pallas kernels for 0%

profile of v20, /device:TPU:0, one launch (start us, length us, event | category | flops | bytes accessed | tf_op | source)
XLA Modules:
  0.0 129.0 jit_solution(14904747419529779753)
XLA Ops:
  0.6 1.1 copy.66
  1.9 4.1 %collective-permute-start.5 = (bf16[1,4,128,128]{3,2,1,0:T(8,128)(2,1)S(1)}, bf16[1,4,128,128]{3,2,1,0:T(8,128)(2,1)S(1)}, u32[]{:S(2)}, u32[]{:S(2)}) collective-permute-start(bf16[1,4,128,128]{3,2,1,0:T(8,128)(2,1)S(1)} %bitcast.126), channel_id=1, source_target_pairs={{0,8},{2,10},{4,12},{6,14},{8,0},{10,2},{12,4},{14,6},{1,9},{3,11}... | collective-permute-start | bytes 393224 | tf_op jit(solution)/shard_map/ppermute | solution.py:42
  6.0 1.0 copy.59
  7.3 8.7 %collective-permute-done.5 = bf16[1,4,128,128]{3,2,1,0:T(8,128)(2,1)S(1)} collective-permute-done((bf16[1,4,128,128]{3,2,1,0:T(8,128)(2,1)S(1)}, bf16[1,4,128,128]{3,2,1,0:T(8,128)(2,1)S(1)}, u32[]{:S(2)}, u32[]{:S(2)}) %collective-permute-start.5) | collective-permute-done | bytes 131104 | tf_op jit(solution)/shard_map/ppermute | solution.py:42
  16.1 2.0 %collective-permute-done = bf16[1,4,128,128]{3,2,1,0:T(8,128)(2,1)S(1)} collective-permute-done((bf16[1,4,128,128]{3,2,1,0:T(8,128)(2,1)S(1)}, bf16[1,4,128,128]{3,2,1,0:T(8,128)(2,1)S(1)}, u32[]{:S(2)}, u32[]{:S(2)}) %collective-permute-start) | collective-permute-done | bytes 131104 | tf_op jit(solution)/shard_map/ppermute | solution.py:42
  18.0 1.7 %collective-permute-start.1 = (bf16[2,4,128,128]{3,2,1,0:T(8,128)(2,1)S(1)}, bf16[2,4,128,128]{3,2,1,0:T(8,128)(2,1)S(1)}, u32[]{:S(2)}, u32[]{:S(2)}) collective-permute-start(bf16[2,4,128,128]{3,2,1,0:T(8,128)(2,1)S(1)} %maximum_select_fusion.6), channel_id=1, source_target_pairs={{0,2},{2,0},{4,6},{6,4},{8,10},{10,8},{12,14},{14,12},{1,3},{3,1},... | collective-permute-start | bytes 786440 | tf_op jit(solution)/shard_map/ppermute | solution.py:42
  19.7 3.8 %collective-permute-done.6 = bf16[2,4,128,128]{3,2,1,0:T(8,128)(2,1)S(1)} collective-permute-done((bf16[2,4,128,128]{3,2,1,0:T(8,128)(2,1)S(1)}, bf16[2,4,128,128]{3,2,1,0:T(8,128)(2,1)S(1)}, u32[]{:S(2)}, u32[]{:S(2)}) %collective-permute-start.6) | collective-permute-done | bytes 262176 | tf_op jit(solution)/shard_map/ppermute | solution.py:42
  23.6 1.6 %collective-permute-start.7 = (bf16[4,4,128,128]{3,2,1,0:T(8,128)(2,1)S(1)}, bf16[4,4,128,128]{3,2,1,0:T(8,128)(2,1)S(1)}, u32[]{:S(2)}, u32[]{:S(2)}) collective-permute-start(bf16[4,4,128,128]{3,2,1,0:T(8,128)(2,1)S(1)} %maximum_select_fusion.5), channel_id=1, source_target_pairs={{0,2},{2,0},{4,6},{6,4},{8,10},{10,8},{12,14},{14,12},{1,3},{3,1},... | collective-permute-start | bytes 1572872 | tf_op jit(solution)/shard_map/ppermute | solution.py:42
  25.3 1.0 collective-permute-done.1
  26.4 1.7 %collective-permute-start.2 = (bf16[4,4,128,128]{3,2,1,0:T(8,128)(2,1)S(1)}, bf16[4,4,128,128]{3,2,1,0:T(8,128)(2,1)S(1)}, u32[]{:S(2)}, u32[]{:S(2)}) collective-permute-start(bf16[4,4,128,128]{3,2,1,0:T(8,128)(2,1)S(1)} %maximum_select_fusion.4), channel_id=1, source_target_pairs={{0,4},{2,6},{4,0},{6,2},{8,12},{10,14},{12,8},{14,10},{1,5},{3,7},... | collective-permute-start | bytes 1572872 | tf_op jit(solution)/shard_map/ppermute | solution.py:42
  28.1 8.7 %collective-permute-done.7 = bf16[4,4,128,128]{3,2,1,0:T(8,128)(2,1)S(1)} collective-permute-done((bf16[4,4,128,128]{3,2,1,0:T(8,128)(2,1)S(1)}, bf16[4,4,128,128]{3,2,1,0:T(8,128)(2,1)S(1)}, u32[]{:S(2)}, u32[]{:S(2)}) %collective-permute-start.7) | collective-permute-done | bytes 524320 | tf_op jit(solution)/shard_map/ppermute | solution.py:42
  36.7 1.1 maximum_select_fusion.3
  38.4 1.1 maximum_select_fusion.1
  40.1 1.2 maximum_select_fusion
  41.5 1.4 %pad_maximum_fusion.1 = bf16[2,8,4,128,128]{4,3,2,1,0:T(8,128)(2,1)S(1)} fusion(bf16[1,8,4,128,128]{4,3,2,1,0:T(8,128)(2,1)} %bitcast.31, bf16[1,8,4,128,128]{4,3,2,1,0:T(8,128)(2,1)S(1)} %maximum_select_fusion.2), kind=kLoop, calls=%fused_computation.4 | loop fusion | flops 1048576 | bytes 4194304 | tf_op jit(solution)/shard_map/stack | solution.py:75
  42.9 1.7 %gather_fusion.1 = bf16[32,128,128]{2,1,0:T(8,128)(2,1)} fusion(bf16[2,8,4,128,128]{4,3,2,1,0:T(8,128)(2,1)S(1)} %pad_maximum_fusion.1, s32[32]{0:T(128)S(1)} %fusion.54), kind=kCustom, calls=%fused_computation.1 | custom fusion | bytes 2097536 | tf_op jit(solution)/shard_map/gather | solution.py:81
  44.6 3.1 %pad_maximum_fusion = bf16[2,8,4,128,128]{4,3,2,1,0:T(8,128)(2,1)} fusion(bf16[1,8,4,128,128]{4,3,2,1,0:T(8,128)(2,1)} %bitcast.8, bf16[1,8,4,128,128]{4,3,2,1,0:T(8,128)(2,1)} %maximum_select_fusion), kind=kLoop, calls=%fused_computation.3 | loop fusion | flops 1048576 | bytes 4194304 | tf_op jit(solution)/shard_map/stack | solution.py:75
  47.7 2.4 %gather_fusion = bf16[32,128,128]{2,1,0:T(8,128)(2,1)S(1)} fusion(bf16[2,8,4,128,128]{4,3,2,1,0:T(8,128)(2,1)} %pad_maximum_fusion, s32[32]{0:T(128)S(1)} %fusion.55), kind=kCustom, calls=%fused_computation | custom fusion | bytes 2097536 | tf_op jit(solution)/shard_map/gather | solution.py:81
  50.0 1.7 %convolution_bitcast_fusion.1 = f32[128,8,128]{2,0,1:T(8,128)S(1)} fusion(bf16[8,4,128,128]{3,2,1,0:T(8,128)(2,1)S(1)} %bitcast.112, bf16[8,4,128,128]{3,2,1,0:T(8,128)(2,1)} %param.8), kind=kOutput, calls=%fused_computation.20 | convolution fusion | flops 134217728 | bytes 2621440 | tf_op jit(solution)/shard_map/rkti,rkio->tro/dot_general | solution.py:111
  53.9 0.8 fusion.9
  54.7 0.8 fusion.11
  55.6 0.8 constant_dynamic-slice_fusion.1
  57.8 3.3 %collective-permute-done.4 = f32[8,4,128,128]{3,2,1,0:T(8,128)S(1)} collective-permute-done((f32[8,4,128,128]{3,2,1,0:T(8,128)S(1)}, f32[8,4,128,128]{3,2,1,0:T(8,128)S(1)}, u32[]{:S(2)}, u32[]{:S(2)}) %collective-permute-start.4) | collective-permute-done | bytes 2097184 | tf_op jit(solution)/shard_map/ppermute | solution.py:22
  61.6 2.5 %collective-permute-done.9 = f32[8,4,128,128]{3,2,1,0:T(8,128)S(1)} collective-permute-done((f32[8,4,128,128]{3,2,1,0:T(8,128)S(1)}, f32[8,4,128,128]{3,2,1,0:T(8,128)S(1)}, u32[]{:S(2)}, u32[]{:S(2)}) %collective-permute-start.9) | collective-permute-done | bytes 2097184 | tf_op jit(solution)/shard_map/ppermute | solution.py:22
  64.8 1.5 %copy.72 = bf16[8,2,4,128,128]{4,3,2,1,0:T(8,128)(2,1)} copy(bf16[8,2,4,128,128]{4,3,2,0,1:T(8,128)(2,1)S(1)} %pad_maximum_fusion.2) | data formatting | bytes 4194304 | tf_op jit(solution)/shard_map/stack | solution.py:122
  66.3 6.8 %all-to-all-start = ((bf16[8,2,4,128,128]{4,3,2,1,0:T(8,128)(2,1)}), bf16[8,2,4,128,128]{4,3,2,1,0:T(8,128)(2,1)}, u32[]{:S(2)}, u32[]{:S(2)}) async-start(bf16[8,2,4,128,128]{4,3,2,1,0:T(8,128)(2,1)} %copy.72), calls=%async_computation | async-start | bytes 4194304 | tf_op jit(solution)/shard_map/all_to_all | solution.py:122
  75.0 1.6 %collective-permute-start.10 = (bf16[2,8,4,128,128]{4,3,2,1,0:T(8,128)(2,1)S(1)}, bf16[2,8,4,128,128]{4,3,2,1,0:T(8,128)(2,1)S(1)}, u32[]{:S(2)}, u32[]{:S(2)}) collective-permute-start(bf16[2,8,4,128,128]{4,3,2,1,0:T(8,128)(2,1)S(1)} %pad_maximum_fusion.3), channel_id=1, source_target_pairs={{0,16},{16,0},{1,17},{17,1},{2,18},{18,2},{3,19},{19,3},{4,20},{20... | collective-permute-start | bytes 6291464 | tf_op jit(solution)/shard_map/ppermute | solution.py:92
  76.6 46.1 %collective-permute-done.10 = bf16[2,8,4,128,128]{4,3,2,1,0:T(8,128)(2,1)S(1)} collective-permute-done((bf16[2,8,4,128,128]{4,3,2,1,0:T(8,128)(2,1)S(1)}, bf16[2,8,4,128,128]{4,3,2,1,0:T(8,128)(2,1)S(1)}, u32[]{:S(2)}, u32[]{:S(2)}) %collective-permute-start.10) | collective-permute-done | bytes 2097184 | tf_op jit(solution)/shard_map/ppermute | solution.py:92
  122.7 1.1 add_convert_fusion
  123.8 1.5 %slice_bitcast_fusion = (bf16[8,4,128,128]{3,2,1,0:T(8,128)(2,1)}, bf16[8,4,128,128]{3,2,1,0:T(8,128)(2,1)}) fusion(bf16[2,8,4,128,128]{4,3,2,1,0:T(8,128)(2,1)S(1)} %add_convert_fusion), kind=kLoop, calls=%fused_computation.26 | loop fusion | bytes 4194304 | tf_op jit(solution)/shard_map/squeeze | solution.py:127
  125.2 1.9 %slice_reduce_fusion = (bf16[4,128,128]{2,1,0:T(8,128)(2,1)S(1)}, bf16[4,128,128]{2,1,0:T(8,128)(2,1)S(1)}) fusion(bf16[8,2,4,128,128]{4,3,2,1,0:T(8,128)(2,1)} %all-to-all-done), kind=kLoop, calls=%fused_computation.28 | loop fusion | flops 917504 | bytes 2359296 | tf_op jit(solution)/shard_map/reduce_sum | solution.py:108
  127.3 0.8 copy.81
  (52 shorter events, 9.6 us)
Async XLA Ops:
  0.6 51.1 %copy-start = (bf16[8,4,128,128]{3,2,1,0:T(8,128)(2,1)S(1)}, bf16[8,4,128,128]{3,2,1,0:T(8,128)(2,1)}, u32[]{:S(2)}) copy-start(bf16[8,4,128,128]{3,2,1,0:T(8,128)(2,1)} %param.10) | copy-start | bytes 3145732
  1.9 14.0 %collective-permute-start.5 = (bf16[1,4,128,128]{3,2,1,0:T(8,128)(2,1)S(1)}, bf16[1,4,128,128]{3,2,1,0:T(8,128)(2,1)S(1)}, u32[]{:S(2)}, u32[]{:S(2)}) collective-permute-start(bf16[1,4,128,128]{3,2,1,0:T(8,128)(2,1)S(1)} %bitcast.126), channel_id=1, source_target_pairs={{0,8},{2,10},{4,12},{6,14},{8,0},{10,2},{12,4},{14,6},{1,9},{3,11}... | collective-permute-start | bytes 393224 | tf_op jit(solution)/shard_map/ppermute | solution.py:42
  7.2 10.8 %collective-permute-start = (bf16[1,4,128,128]{3,2,1,0:T(8,128)(2,1)S(1)}, bf16[1,4,128,128]{3,2,1,0:T(8,128)(2,1)S(1)}, u32[]{:S(2)}, u32[]{:S(2)}) collective-permute-start(bf16[1,4,128,128]{3,2,1,0:T(8,128)(2,1)S(1)} %bitcast.124), channel_id=1, source_target_pairs={{0,8},{2,10},{4,12},{6,14},{8,0},{10,2},{12,4},{14,6},{1,9},{3,11}... | collective-permute-start | bytes 393224 | tf_op jit(solution)/shard_map/ppermute | solution.py:42
  16.0 7.6 %collective-permute-start.6 = (bf16[2,4,128,128]{3,2,1,0:T(8,128)(2,1)S(1)}, bf16[2,4,128,128]{3,2,1,0:T(8,128)(2,1)S(1)}, u32[]{:S(2)}, u32[]{:S(2)}) collective-permute-start(bf16[2,4,128,128]{3,2,1,0:T(8,128)(2,1)S(1)} %maximum_select_fusion.7), channel_id=1, source_target_pairs={{0,4},{2,6},{4,0},{6,2},{8,12},{10,14},{12,8},{14,10},{1,5},{3,7},... | collective-permute-start | bytes 786440 | tf_op jit(solution)/shard_map/ppermute | solution.py:42
  18.0 8.3 %collective-permute-start.1 = (bf16[2,4,128,128]{3,2,1,0:T(8,128)(2,1)S(1)}, bf16[2,4,128,128]{3,2,1,0:T(8,128)(2,1)S(1)}, u32[]{:S(2)}, u32[]{:S(2)}) collective-permute-start(bf16[2,4,128,128]{3,2,1,0:T(8,128)(2,1)S(1)} %maximum_select_fusion.6), channel_id=1, source_target_pairs={{0,2},{2,0},{4,6},{6,4},{8,10},{10,8},{12,14},{14,12},{1,3},{3,1},... | collective-permute-start | bytes 786440 | tf_op jit(solution)/shard_map/ppermute | solution.py:42
  23.6 13.1 %collective-permute-start.7 = (bf16[4,4,128,128]{3,2,1,0:T(8,128)(2,1)S(1)}, bf16[4,4,128,128]{3,2,1,0:T(8,128)(2,1)S(1)}, u32[]{:S(2)}, u32[]{:S(2)}) collective-permute-start(bf16[4,4,128,128]{3,2,1,0:T(8,128)(2,1)S(1)} %maximum_select_fusion.5), channel_id=1, source_target_pairs={{0,2},{2,0},{4,6},{6,4},{8,10},{10,8},{12,14},{14,12},{1,3},{3,1},... | collective-permute-start | bytes 1572872 | tf_op jit(solution)/shard_map/ppermute | solution.py:42
  26.4 13.2 %copy-start.4 = (s32[8,4]{0,1:T(4,128)S(1)}, s32[8,4]{0,1:T(4,128)}, u32[]{:S(2)}) copy-start(s32[8,4]{0,1:T(4,128)} %param.9) | copy-start | bytes 388
  26.4 13.4 %copy-start.5 = (s32[8,4]{0,1:T(4,128)S(1)}, s32[8,4]{0,1:T(4,128)}, u32[]{:S(2)}) copy-start(s32[8,4]{0,1:T(4,128)} %param.11) | copy-start | bytes 388
  26.4 12.0 %collective-permute-start.2 = (bf16[4,4,128,128]{3,2,1,0:T(8,128)(2,1)S(1)}, bf16[4,4,128,128]{3,2,1,0:T(8,128)(2,1)S(1)}, u32[]{:S(2)}, u32[]{:S(2)}) collective-permute-start(bf16[4,4,128,128]{3,2,1,0:T(8,128)(2,1)S(1)} %maximum_select_fusion.4), channel_id=1, source_target_pairs={{0,4},{2,6},{4,0},{6,2},{8,12},{10,14},{12,8},{14,10},{1,5},{3,7},... | collective-permute-start | bytes 1572872 | tf_op jit(solution)/shard_map/ppermute | solution.py:42
  37.9 3.6 %collective-permute-start.8 = (bf16[8,4,128,128]{3,2,1,0:T(8,128)(2,1)}, bf16[8,4,128,128]{3,2,1,0:T(8,128)(2,1)}, u32[]{:S(2)}, u32[]{:S(2)}) collective-permute-start(bf16[8,4,128,128]{3,2,1,0:T(8,128)(2,1)} %maximum_select_fusion.3), channel_id=1, source_target_pairs={{0,1},{1,0},{2,3},{3,2},{4,5},{5,4},{6,7},{7,6},{8,9},{9,8},{10,11... | collective-permute-start | bytes 3145736 | tf_op jit(solution)/shard_map/ppermute | solution.py:22
  39.5 5.0 %collective-permute-start.3 = (bf16[8,4,128,128]{3,2,1,0:T(8,128)(2,1)}, bf16[8,4,128,128]{3,2,1,0:T(8,128)(2,1)}, u32[]{:S(2)}, u32[]{:S(2)}) collective-permute-start(bf16[8,4,128,128]{3,2,1,0:T(8,128)(2,1)} %maximum_select_fusion.1), channel_id=1, source_target_pairs={{0,1},{1,0},{2,3},{3,2},{4,5},{5,4},{6,7},{7,6},{8,9},{9,8},{10,11... | collective-permute-start | bytes 3145736 | tf_op jit(solution)/shard_map/ppermute | solution.py:22
  50.0 2.2 %copy-start.2 = (bf16[32,128,128]{2,1,0:T(8,128)(2,1)S(1)}, bf16[32,128,128]{2,1,0:T(8,128)(2,1)}, u32[]{:S(2)}) copy-start(bf16[32,128,128]{2,1,0:T(8,128)(2,1)} %gather_fusion.1) | copy-start | bytes 3145732
  52.2 1.2 copy-start.1
  56.8 4.4 %collective-permute-start.4 = (f32[8,4,128,128]{3,2,1,0:T(8,128)S(1)}, f32[8,4,128,128]{3,2,1,0:T(8,128)S(1)}, u32[]{:S(2)}, u32[]{:S(2)}) collective-permute-start(f32[8,4,128,128]{3,2,1,0:T(8,128)S(1)} %bitcast.123), channel_id=1, source_target_pairs={{0,1},{1,0},{2,3},{3,2},{4,5},{5,4},{6,7},{7,6},{8,9},{9,8},{10,11... | collective-permute-start | bytes 6291464 | tf_op jit(solution)/shard_map/ppermute | solution.py:22
  57.7 6.4 %collective-permute-start.9 = (f32[8,4,128,128]{3,2,1,0:T(8,128)S(1)}, f32[8,4,128,128]{3,2,1,0:T(8,128)S(1)}, u32[]{:S(2)}, u32[]{:S(2)}) collective-permute-start(f32[8,4,128,128]{3,2,1,0:T(8,128)S(1)} %bitcast.122), channel_id=1, source_target_pairs={{0,1},{1,0},{2,3},{3,2},{4,5},{5,4},{6,7},{7,6},{8,9},{9,8},{10,11... | collective-permute-start | bytes 6291464 | tf_op jit(solution)/shard_map/ppermute | solution.py:22
  66.3 58.9 %all-to-all-start = ((bf16[8,2,4,128,128]{4,3,2,1,0:T(8,128)(2,1)}), bf16[8,2,4,128,128]{4,3,2,1,0:T(8,128)(2,1)}, u32[]{:S(2)}, u32[]{:S(2)}) async-start(bf16[8,2,4,128,128]{4,3,2,1,0:T(8,128)(2,1)} %copy.72), calls=%async_computation | async-start | bytes 4194304 | tf_op jit(solution)/shard_map/all_to_all | solution.py:122
  73.1 1.2 copy-start.3
  75.0 47.7 %collective-permute-start.10 = (bf16[2,8,4,128,128]{4,3,2,1,0:T(8,128)(2,1)S(1)}, bf16[2,8,4,128,128]{4,3,2,1,0:T(8,128)(2,1)S(1)}, u32[]{:S(2)}, u32[]{:S(2)}) collective-permute-start(bf16[2,8,4,128,128]{4,3,2,1,0:T(8,128)(2,1)S(1)} %pad_maximum_fusion.3), channel_id=1, source_target_pairs={{0,16},{16,0},{1,17},{17,1},{2,18},{18,2},{3,19},{19,3},{4,20},{20... | collective-permute-start | bytes 6291464 | tf_op jit(solution)/shard_map/ppermute | solution.py:92

commit v21 on v19

--- a/solution.py
+++ b/solution.py
@@ -93,16 +93,20 @@
             return (part.astype(jnp.float32) + got.astype(jnp.float32)).astype(jnp.bfloat16)
         return lax.psum(part, "dp")
 
-    columns = jnp.arange(col_count, dtype=jnp.int32)
+    chip_ids = jnp.arange(chips, dtype=jnp.int32)
+    sub_ids = jnp.arange(own_blocks, dtype=jnp.int32)
 
     def chip_sums(terms, flat):
         terms = terms.reshape(tok_rows, pair_count, block_size)
-        onehot = (flat[:, None] == columns[None, :]).astype(jnp.bfloat16)
-        local = jnp.einsum("tpo,pc->cto", terms.astype(jnp.bfloat16), onehot, preferred_element_type=jnp.float32)
-        local = local.reshape(chips, pair, own_blocks, tok_rows, block_size)
-        keep = lax.dynamic_index_in_dim(local, core, axis=1, keepdims=False)
-        give = lax.dynamic_index_in_dim(local, 1 - core, axis=1, keepdims=False)
-        return (keep + swap_core(give)).astype(jnp.bfloat16)
+        terms = terms.astype(jnp.bfloat16)
+
+        def half(side):
+            cols = (chip_ids[:, None] * pair + side) * own_blocks + sub_ids[None, :]
+            onehot = (flat[:, None] == cols.reshape(1, -1)).astype(jnp.bfloat16)
+            got = jnp.einsum("tpo,pc->cto", terms, onehot, preferred_element_type=jnp.float32)
+            return got.reshape(chips, own_blocks, tok_rows, block_size)
+
+        return (half(core) + swap_core(half(1 - core))).astype(jnp.bfloat16)
 
     def finish(got):
         total = got.astype(jnp.float32).sum(axis=0)

time: 129 us -> 132 us (1.023)
  waiting for transfers between devices: 73.8 us -> 76.8 us
  starting transfers between devices: 18.8 us -> 16.1 us
  matrix products: 6.99 us -> 8.4 us
    ppermute x6, waiting for transfers between devices: 24.7 us -> 28.9 us  [gather_chips(): got = lax.ppermute(held, 'chip', perm=[(i, i ^ step) for i in range(chips)])]
    all_to_all x1, starting transfers between devices: 6.79 us -> 4.35 us  [per_device(): lax.all_to_all(jnp.stack([out_send, in_send], axis=1), 'chip', split_axis...]
    dynamic_slice x3 -> x0, local copies, waits for them, and re-layouts: 1.59 us -> none  [the longest x2 0.81 us: chip_sums(): give = lax.dynamic_index_in_dim(local, 1 - core, axis=1, keepdims=False)]
    gather x2, local copies, waits for them, and re-layouts: 4.02 us -> 5.61 us  [select(): sel = sets[side, chip_slot(owner // pair, order), sub]]
    ppermute x4, waiting for transfers between devices: 5.78 us -> 4.31 us  [swap_core(): return lax.ppermute(x, 'core', perm=[(0, 1), (1, 0)])]
    dot_general x2 -> x4, matrix products: 1.68 us -> 3.09 us  [half(): jnp.einsum('tpo,pc->cto', terms, onehot, preferred_element_type=jnp.float32)]
    unnamed x17 -> x19, local copies, waits for them, and re-layouts: 5.89 us -> 5.99 us
  transfers between devices with their start and end apart: 13 -> 13, of which waited for: 10 -> 9; matrix products, arithmetic and copies ran while one was open for 12% -> 16% of each run, Pallas kernels for 0% -> 0%
where the time goes in v21:
time: 132 us; the launch traced here: 131 us
  waiting for transfers between devices  76.8 us (58%)
  starting transfers between devices  16.1 us (12%)
  other arithmetic  14.5 us (11%)
  local copies, waits for them, and re-layouts  14.3 us (11%)
  matrix products  8.4 us (6%)
    ppermute x2, waiting for transfers between devices, dp_total(): got = lax.ppermute(part, 'dp', perm=[(0, 1), (1, 0)])  43.7 us
    ppermute x6, waiting for transfers between devices, gather_chips(): got = lax.ppermute(held, 'chip', perm=[(i, i ^ step) for i in range(chips)])  28.9 us
    ppermute x6, starting transfers between devices, gather_chips(): got = lax.ppermute(held, 'chip', perm=[(i, i ^ step) for i in range(chips)])  8.52 us
    unnamed x19, local copies, waits for them, and re-layouts  5.99 us
    gather x2, local copies, waits for them, and re-layouts, select(): sel = sets[side, chip_slot(owner // pair, order), sub]  5.61 us
    another operation x2, other arithmetic, gather(): return jnp.stack([mine, swap_core(mine)], axis=0)  5.51 us
    all_to_all x1, starting transfers between devices, per_device(): lax.all_to_all(jnp.stack([out_send, in_send], axis=1), 'chip', split_axis...  4.35 us
    ppermute x4, waiting for transfers between devices, swap_core(): return lax.ppermute(x, 'core', perm=[(0, 1), (1, 0)])  4.31 us
  transfers between devices with their start and end apart: 13, of which 9 were waited for; matrix products, arithmetic and copies ran while one was open for 16% of the time, Pallas kernels for 0%

profile of v21, /device:TPU:0, one launch (start us, length us, event | category | flops | bytes accessed | tf_op | source)
XLA Modules:
  0.0 131.0 jit_solution(5600928839788868059)
XLA Ops:
  0.7 1.1 copy.68
  1.9 4.1 %collective-permute-start = (bf16[1,4,128,128]{3,2,1,0:T(8,128)(2,1)S(1)}, bf16[1,4,128,128]{3,2,1,0:T(8,128)(2,1)S(1)}, u32[]{:S(2)}, u32[]{:S(2)}) collective-permute-start(bf16[1,4,128,128]{3,2,1,0:T(8,128)(2,1)S(1)} %bitcast.116), channel_id=1, source_target_pairs={{0,8},{2,10},{4,12},{6,14},{8,0},{10,2},{12,4},{14,6},{1,9},{3,11}... | collective-permute-start | bytes 393224 | tf_op jit(solution)/shard_map/ppermute | solution.py:42
  6.0 6.3 %collective-permute-done = bf16[1,4,128,128]{3,2,1,0:T(8,128)(2,1)S(1)} collective-permute-done((bf16[1,4,128,128]{3,2,1,0:T(8,128)(2,1)S(1)}, bf16[1,4,128,128]{3,2,1,0:T(8,128)(2,1)S(1)}, u32[]{:S(2)}, u32[]{:S(2)}) %collective-permute-start) | collective-permute-done | bytes 131104 | tf_op jit(solution)/shard_map/ppermute | solution.py:42
  12.4 1.6 %collective-permute-start.1 = (bf16[2,4,128,128]{3,2,1,0:T(8,128)(2,1)S(1)}, bf16[2,4,128,128]{3,2,1,0:T(8,128)(2,1)S(1)}, u32[]{:S(2)}, u32[]{:S(2)}) collective-permute-start(bf16[2,4,128,128]{3,2,1,0:T(8,128)(2,1)S(1)} %maximum_select_fusion.6), channel_id=1, source_target_pairs={{0,2},{2,0},{4,6},{6,4},{8,10},{10,8},{12,14},{14,12},{1,3},{3,1},... | collective-permute-start | bytes 786440 | tf_op jit(solution)/shard_map/ppermute | solution.py:42
  14.0 1.0 copy.74
  15.2 8.3 %collective-permute-done.5 = bf16[1,4,128,128]{3,2,1,0:T(8,128)(2,1)S(1)} collective-permute-done((bf16[1,4,128,128]{3,2,1,0:T(8,128)(2,1)S(1)}, bf16[1,4,128,128]{3,2,1,0:T(8,128)(2,1)S(1)}, u32[]{:S(2)}, u32[]{:S(2)}) %collective-permute-start.5) | collective-permute-done | bytes 131104 | tf_op jit(solution)/shard_map/ppermute | solution.py:42
  23.8 2.1 %collective-permute-start.2 = (bf16[4,4,128,128]{3,2,1,0:T(8,128)(2,1)S(1)}, bf16[4,4,128,128]{3,2,1,0:T(8,128)(2,1)S(1)}, u32[]{:S(2)}, u32[]{:S(2)}) collective-permute-start(bf16[4,4,128,128]{3,2,1,0:T(8,128)(2,1)S(1)} %maximum_select_fusion.4), channel_id=1, source_target_pairs={{0,4},{2,6},{4,0},{6,2},{8,12},{10,14},{12,8},{14,10},{1,5},{3,7},... | collective-permute-start | bytes 1572872 | tf_op jit(solution)/shard_map/ppermute | solution.py:42
  25.9 7.1 %collective-permute-done.6 = bf16[2,4,128,128]{3,2,1,0:T(8,128)(2,1)S(1)} collective-permute-done((bf16[2,4,128,128]{3,2,1,0:T(8,128)(2,1)S(1)}, bf16[2,4,128,128]{3,2,1,0:T(8,128)(2,1)S(1)}, u32[]{:S(2)}, u32[]{:S(2)}) %collective-permute-start.6) | collective-permute-done | bytes 262176 | tf_op jit(solution)/shard_map/ppermute | solution.py:42
  33.8 6.6 %collective-permute-done.2 = bf16[4,4,128,128]{3,2,1,0:T(8,128)(2,1)S(1)} collective-permute-done((bf16[4,4,128,128]{3,2,1,0:T(8,128)(2,1)S(1)}, bf16[4,4,128,128]{3,2,1,0:T(8,128)(2,1)S(1)}, u32[]{:S(2)}, u32[]{:S(2)}) %collective-permute-start.2) | collective-permute-done | bytes 524320 | tf_op jit(solution)/shard_map/ppermute | solution.py:42
  40.4 1.1 maximum_select_fusion.1
  42.3 1.1 maximum_select_fusion.3
  43.8 1.1 maximum_select_fusion.2
  44.9 2.8 %pad_maximum_fusion = bf16[2,8,4,128,128]{4,3,2,1,0:T(8,128)(2,1)} fusion(bf16[1,8,4,128,128]{4,3,2,1,0:T(8,128)(2,1)} %bitcast.8, bf16[1,8,4,128,128]{4,3,2,1,0:T(8,128)(2,1)S(1)} %maximum_select_fusion), kind=kLoop, calls=%fused_computation.2 | loop fusion | flops 1048576 | bytes 4194304 | tf_op jit(solution)/shard_map/stack | solution.py:75
  47.7 2.4 %gather_fusion = bf16[32,128,128]{2,1,0:T(8,128)(2,1)S(1)} fusion(bf16[2,8,4,128,128]{4,3,2,1,0:T(8,128)(2,1)} %pad_maximum_fusion, s32[32]{0:T(128)S(1)} %fusion.66), kind=kCustom, calls=%fused_computation | custom fusion | bytes 2097536 | tf_op jit(solution)/shard_map/gather | solution.py:81
  50.1 1.7 %convolution_bitcast_fusion.1 = f32[128,8,128]{2,0,1:T(8,128)S(1)} fusion(bf16[8,4,128,128]{3,2,1,0:T(8,128)(2,1)S(1)} %bitcast.104, bf16[8,4,128,128]{3,2,1,0:T(8,128)(2,1)} %param.8), kind=kOutput, calls=%fused_computation.17 | convolution fusion | flops 134217728 | bytes 2621440 | tf_op jit(solution)/shard_map/rkti,rkio->tro/dot_general | solution.py:115
  51.8 2.8 %pad_maximum_fusion.1 = bf16[2,8,4,128,128]{4,3,2,1,0:T(8,128)(2,1)} fusion(bf16[1,8,4,128,128]{4,3,2,1,0:T(8,128)(2,1)} %bitcast.33, bf16[1,8,4,128,128]{4,3,2,1,0:T(8,128)(2,1)S(1)} %copy-done.3), kind=kLoop, calls=%fused_computation.3 | loop fusion | flops 1048576 | bytes 4194304 | tf_op jit(solution)/shard_map/stack | solution.py:75
  54.6 3.3 %gather_fusion.1 = bf16[32,128,128]{2,1,0:T(8,128)(2,1)} fusion(bf16[2,8,4,128,128]{4,3,2,1,0:T(8,128)(2,1)} %pad_maximum_fusion.1, s32[32]{0:T(128)S(1)} %fusion.65), kind=kCustom, calls=%fused_computation.1 | custom fusion | bytes 2097536 | tf_op jit(solution)/shard_map/gather | solution.py:81
  58.3 0.8 copy-done.2
  62.5 2.1 %collective-permute-done.4 = f32[8,4,128,128]{3,0,2,1:T(8,128)S(1)} collective-permute-done((f32[8,4,128,128]{3,0,2,1:T(8,128)S(1)}, f32[8,4,128,128]{3,0,2,1:T(8,128)S(1)}, u32[]{:S(2)}, u32[]{:S(2)}) %collective-permute-start.4) | collective-permute-done | bytes 2097184 | tf_op jit(solution)/shard_map/ppermute | solution.py:22
  64.7 0.8 fusion.1
  65.5 2.2 %collective-permute-done.9 = f32[8,4,128,128]{3,0,2,1:T(8,128)S(1)} collective-permute-done((f32[8,4,128,128]{3,0,2,1:T(8,128)S(1)}, f32[8,4,128,128]{3,0,2,1:T(8,128)S(1)}, u32[]{:S(2)}, u32[]{:S(2)}) %collective-permute-start.9) | collective-permute-done | bytes 2097184 | tf_op jit(solution)/shard_map/ppermute | solution.py:22
  67.7 0.8 fusion.2
  68.7 1.9 %copy.79 = bf16[8,2,4,128,128]{4,3,2,1,0:T(8,128)(2,1)} copy(bf16[8,2,4,128,128]{4,0,3,2,1:T(8,128)(2,1)S(1)} %pad_maximum_fusion.2) | data formatting | bytes 4194304 | tf_op jit(solution)/shard_map/stack | solution.py:127
  70.5 4.3 %all-to-all-start = ((bf16[8,2,4,128,128]{4,3,2,1,0:T(8,128)(2,1)}), bf16[8,2,4,128,128]{4,3,2,1,0:T(8,128)(2,1)}, u32[]{:S(2)}, u32[]{:S(2)}) async-start(bf16[8,2,4,128,128]{4,3,2,1,0:T(8,128)(2,1)} %copy.79), calls=%async_computation | async-start | bytes 4194304 | tf_op jit(solution)/shard_map/all_to_all | solution.py:127
  74.9 1.7 %fusion = bf16[8,4,128,128]{2,3,1,0:T(8,128)(2,1)S(1)} fusion(bf16[8,4,128,128]{3,2,1,0:T(8,128)(2,1)} %bitcast.112, f32[128,8,128]{2,0,1:T(8,128)S(1)} %convolution_bitcast_fusion.1), kind=kOutput, calls=%fused_computation.13 | convolution fusion | flops 135397376 | bytes 2621440 | tf_op jit(solution)/shard_map/tri,rkto->rkio/dot_general | solution.py:120
  76.6 1.6 %collective-permute-start.11 = (bf16[8,4,128,128]{2,3,1,0:T(8,128)(2,1)S(1)}, bf16[8,4,128,128]{2,3,1,0:T(8,128)(2,1)S(1)}, u32[]{:S(2)}, u32[]{:S(2)}) collective-permute-start(bf16[8,4,128,128]{2,3,1,0:T(8,128)(2,1)S(1)} %fusion), channel_id=1, source_target_pairs={{0,16},{16,0},{1,17},{17,1},{2,18},{18,2},{3,19},{19,3},{4,20},{20... | collective-permute-start | bytes 3145736 | tf_op jit(solution)/shard_map/ppermute | solution.py:92
  79.3 23.4 %collective-permute-done.11 = bf16[8,4,128,128]{2,3,1,0:T(8,128)(2,1)S(1)} collective-permute-done((bf16[8,4,128,128]{2,3,1,0:T(8,128)(2,1)S(1)}, bf16[8,4,128,128]{2,3,1,0:T(8,128)(2,1)S(1)}, u32[]{:S(2)}, u32[]{:S(2)}) %collective-permute-start.11) | collective-permute-done | bytes 1048608 | tf_op jit(solution)/shard_map/ppermute | solution.py:92
  103.1 1.3 %copy.88 = bf16[8,4,128,128]{3,2,1,0:T(8,128)(2,1)} copy(bf16[8,4,128,128]{2,3,1,0:T(8,128)(2,1)S(1)} %add_convert_fusion) | data formatting | bytes 2097152
  104.4 20.3 %collective-permute-done.10 = bf16[8,4,128,128]{3,2,1,0:T(8,128)(2,1)} collective-permute-done((bf16[8,4,128,128]{3,2,1,0:T(8,128)(2,1)S(1)}, bf16[8,4,128,128]{3,2,1,0:T(8,128)(2,1)}, u32[]{:S(2)}, u32[]{:S(2)}) %collective-permute-start.10) | collective-permute-done | bytes 1048608 | tf_op jit(solution)/shard_map/ppermute | solution.py:92
  124.7 2.6 %add_convert_fusion.1 = bf16[8,4,128,128]{3,2,1,0:T(8,128)(2,1)} fusion(bf16[8,4,128,128]{3,2,1,0:T(8,128)(2,1)} %collective-permute-done.10, bf16[8,4,128,128]{3,2,1,0:T(8,128)(2,1)S(1)} %convolution_convert_fusion.1), kind=kLoop, calls=%fused_computation.6 | loop fusion | flops 2097152 | bytes 3145728 | tf_op jit(solution)/shard_map/convert_element_type | solution.py:93
  127.3 1.9 %slice_reduce_fusion = (bf16[4,128,128]{2,1,0:T(8,128)(2,1)S(1)}, bf16[4,128,128]{2,1,0:T(8,128)(2,1)S(1)}) fusion(bf16[8,2,4,128,128]{4,3,2,1,0:T(8,128)(2,1)} %all-to-all-done), kind=kLoop, calls=%fused_computation.21 | loop fusion | flops 917504 | bytes 2359296 | tf_op jit(solution)/shard_map/reduce_sum | solution.py:112
  129.3 0.8 copy.86
  (54 shorter events, 9.2 us)
Async XLA Ops:
  0.6 57.2 %copy-start = (bf16[8,4,128,128]{3,2,1,0:T(8,128)(2,1)S(1)}, bf16[8,4,128,128]{3,2,1,0:T(8,128)(2,1)}, u32[]{:S(2)}) copy-start(bf16[8,4,128,128]{3,2,1,0:T(8,128)(2,1)} %param.10) | copy-start | bytes 3145732
  0.6 33.0 %copy-start.4 = (s32[8,4]{0,1:T(4,128)S(1)}, s32[8,4]{0,1:T(4,128)}, u32[]{:S(2)}) copy-start(s32[8,4]{0,1:T(4,128)} %param.9) | copy-start | bytes 388
  1.9 10.4 %collective-permute-start = (bf16[1,4,128,128]{3,2,1,0:T(8,128)(2,1)S(1)}, bf16[1,4,128,128]{3,2,1,0:T(8,128)(2,1)S(1)}, u32[]{:S(2)}, u32[]{:S(2)}) collective-permute-start(bf16[1,4,128,128]{3,2,1,0:T(8,128)(2,1)S(1)} %bitcast.116), channel_id=1, source_target_pairs={{0,8},{2,10},{4,12},{6,14},{8,0},{10,2},{12,4},{14,6},{1,9},{3,11}... | collective-permute-start | bytes 393224 | tf_op jit(solution)/shard_map/ppermute | solution.py:42
  12.4 11.4 %collective-permute-start.1 = (bf16[2,4,128,128]{3,2,1,0:T(8,128)(2,1)S(1)}, bf16[2,4,128,128]{3,2,1,0:T(8,128)(2,1)S(1)}, u32[]{:S(2)}, u32[]{:S(2)}) collective-permute-start(bf16[2,4,128,128]{3,2,1,0:T(8,128)(2,1)S(1)} %maximum_select_fusion.6), channel_id=1, source_target_pairs={{0,2},{2,0},{4,6},{6,4},{8,10},{10,8},{12,14},{14,12},{1,3},{3,1},... | collective-permute-start | bytes 786440 | tf_op jit(solution)/shard_map/ppermute | solution.py:42
  15.2 8.4 %collective-permute-start.5 = (bf16[1,4,128,128]{3,2,1,0:T(8,128)(2,1)S(1)}, bf16[1,4,128,128]{3,2,1,0:T(8,128)(2,1)S(1)}, u32[]{:S(2)}, u32[]{:S(2)}) collective-permute-start(bf16[1,4,128,128]{3,2,1,0:T(8,128)(2,1)S(1)} %bitcast.118), channel_id=1, source_target_pairs={{0,8},{2,10},{4,12},{6,14},{8,0},{10,2},{12,4},{14,6},{1,9},{3,11}... | collective-permute-start | bytes 393224 | tf_op jit(solution)/shard_map/ppermute | solution.py:42
  23.6 17.9 %copy-start.5 = (s32[8,4]{0,1:T(4,128)S(1)}, s32[8,4]{0,1:T(4,128)}, u32[]{:S(2)}) copy-start(s32[8,4]{0,1:T(4,128)} %param.11) | copy-start | bytes 388
  23.6 9.3 %collective-permute-start.6 = (bf16[2,4,128,128]{3,2,1,0:T(8,128)(2,1)S(1)}, bf16[2,4,128,128]{3,2,1,0:T(8,128)(2,1)S(1)}, u32[]{:S(2)}, u32[]{:S(2)}) collective-permute-start(bf16[2,4,128,128]{3,2,1,0:T(8,128)(2,1)S(1)} %maximum_select_fusion.7), channel_id=1, source_target_pairs={{0,4},{2,6},{4,0},{6,2},{8,12},{10,14},{12,8},{14,10},{1,5},{3,7},... | collective-permute-start | bytes 786440 | tf_op jit(solution)/shard_map/ppermute | solution.py:42
  23.8 16.6 %collective-permute-start.2 = (bf16[4,4,128,128]{3,2,1,0:T(8,128)(2,1)S(1)}, bf16[4,4,128,128]{3,2,1,0:T(8,128)(2,1)S(1)}, u32[]{:S(2)}, u32[]{:S(2)}) collective-permute-start(bf16[4,4,128,128]{3,2,1,0:T(8,128)(2,1)S(1)} %maximum_select_fusion.4), channel_id=1, source_target_pairs={{0,4},{2,6},{4,0},{6,2},{8,12},{10,14},{12,8},{14,10},{1,5},{3,7},... | collective-permute-start | bytes 1572872 | tf_op jit(solution)/shard_map/ppermute | solution.py:42
  33.0 9.2 %collective-permute-start.7 = (bf16[4,4,128,128]{3,2,1,0:T(8,128)(2,1)S(1)}, bf16[4,4,128,128]{3,2,1,0:T(8,128)(2,1)S(1)}, u32[]{:S(2)}, u32[]{:S(2)}) collective-permute-start(bf16[4,4,128,128]{3,2,1,0:T(8,128)(2,1)S(1)} %maximum_select_fusion.5), channel_id=1, source_target_pairs={{0,2},{2,0},{4,6},{6,4},{8,10},{10,8},{12,14},{14,12},{1,3},{3,1},... | collective-permute-start | bytes 1572872 | tf_op jit(solution)/shard_map/ppermute | solution.py:42
  41.5 3.4 %collective-permute-start.3 = (bf16[8,4,128,128]{3,2,1,0:T(8,128)(2,1)}, bf16[8,4,128,128]{3,2,1,0:T(8,128)(2,1)}, u32[]{:S(2)}, u32[]{:S(2)}) collective-permute-start(bf16[8,4,128,128]{3,2,1,0:T(8,128)(2,1)} %maximum_select_fusion.1), channel_id=1, source_target_pairs={{0,1},{1,0},{2,3},{3,2},{4,5},{5,4},{6,7},{7,6},{8,9},{9,8},{10,11... | collective-permute-start | bytes 3145736 | tf_op jit(solution)/shard_map/ppermute | solution.py:22
  43.4 8.4 %collective-permute-start.8 = (bf16[8,4,128,128]{3,2,1,0:T(8,128)(2,1)}, bf16[8,4,128,128]{3,2,1,0:T(8,128)(2,1)}, u32[]{:S(2)}, u32[]{:S(2)}) collective-permute-start(bf16[8,4,128,128]{3,2,1,0:T(8,128)(2,1)} %maximum_select_fusion.3), channel_id=1, source_target_pairs={{0,1},{1,0},{2,3},{3,2},{4,5},{5,4},{6,7},{7,6},{8,9},{9,8},{10,11... | collective-permute-start | bytes 3145736 | tf_op jit(solution)/shard_map/ppermute | solution.py:22
  50.1 1.8 %copy-start.3 = (bf16[1,8,4,128,128]{4,3,2,1,0:T(8,128)(2,1)S(1)}, bf16[1,8,4,128,128]{4,3,2,1,0:T(8,128)(2,1)}, u32[]{:S(2)}) copy-start(bf16[1,8,4,128,128]{4,3,2,1,0:T(8,128)(2,1)} %maximum_select_fusion.2) | copy-start | bytes 3145732
  57.8 1.2 copy-start.2
  59.6 1.3 %copy-start.1 = (bf16[8,4,128,128]{3,2,1,0:T(8,128)(2,1)S(1)}, bf16[8,4,128,128]{3,2,1,0:T(8,128)(2,1)}, u32[]{:S(2)}) copy-start(bf16[8,4,128,128]{3,2,1,0:T(8,128)(2,1)} %param.8) | copy-start | bytes 3145732
  60.3 4.4 %collective-permute-start.4 = (f32[8,4,128,128]{3,0,2,1:T(8,128)S(1)}, f32[8,4,128,128]{3,0,2,1:T(8,128)S(1)}, u32[]{:S(2)}, u32[]{:S(2)}) collective-permute-start(f32[8,4,128,128]{3,0,2,1:T(8,128)S(1)} %fusion.9), channel_id=1, source_target_pairs={{0,1},{1,0},{2,3},{3,2},{4,5},{5,4},{6,7},{7,6},{8,9},{9,8},{10,11... | collective-permute-start | bytes 6291464 | tf_op jit(solution)/shard_map/ppermute | solution.py:22
  62.1 5.6 %collective-permute-start.9 = (f32[8,4,128,128]{3,0,2,1:T(8,128)S(1)}, f32[8,4,128,128]{3,0,2,1:T(8,128)S(1)}, u32[]{:S(2)}, u32[]{:S(2)}) collective-permute-start(f32[8,4,128,128]{3,0,2,1:T(8,128)S(1)} %fusion.6), channel_id=1, source_target_pairs={{0,1},{1,0},{2,3},{3,2},{4,5},{5,4},{6,7},{7,6},{8,9},{9,8},{10,11... | collective-permute-start | bytes 6291464 | tf_op jit(solution)/shard_map/ppermute | solution.py:22
  70.5 56.7 %all-to-all-start = ((bf16[8,2,4,128,128]{4,3,2,1,0:T(8,128)(2,1)}), bf16[8,2,4,128,128]{4,3,2,1,0:T(8,128)(2,1)}, u32[]{:S(2)}, u32[]{:S(2)}) async-start(bf16[8,2,4,128,128]{4,3,2,1,0:T(8,128)(2,1)} %copy.79), calls=%async_computation | async-start | bytes 4194304 | tf_op jit(solution)/shard_map/all_to_all | solution.py:127
  76.6 26.1 %collective-permute-start.11 = (bf16[8,4,128,128]{2,3,1,0:T(8,128)(2,1)S(1)}, bf16[8,4,128,128]{2,3,1,0:T(8,128)(2,1)S(1)}, u32[]{:S(2)}, u32[]{:S(2)}) collective-permute-start(bf16[8,4,128,128]{2,3,1,0:T(8,128)(2,1)S(1)} %fusion), channel_id=1, source_target_pairs={{0,16},{16,0},{1,17},{17,1},{2,18},{18,2},{3,19},{19,3},{4,20},{20... | collective-permute-start | bytes 3145736 | tf_op jit(solution)/shard_map/ppermute | solution.py:92
  78.7 46.0 %collective-permute-start.10 = (bf16[8,4,128,128]{3,2,1,0:T(8,128)(2,1)S(1)}, bf16[8,4,128,128]{3,2,1,0:T(8,128)(2,1)}, u32[]{:S(2)}, u32[]{:S(2)}) collective-permute-start(bf16[8,4,128,128]{3,2,1,0:T(8,128)(2,1)S(1)} %convolution_convert_fusion.1), channel_id=1, source_target_pairs={{0,16},{16,0},{1,17},{17,1},{2,18},{18,2},{3,19},{19,3},{4,20},{20... | collective-permute-start | bytes 3145736 | tf_op jit(solution)/shard_map/ppermute | solution.py:92

commit v22 on v19

--- a/solution.py
+++ b/solution.py
@@ -98,15 +98,14 @@
     def chip_sums(terms, flat):
         terms = terms.reshape(tok_rows, pair_count, block_size)
         onehot = (flat[:, None] == columns[None, :]).astype(jnp.bfloat16)
-        local = jnp.einsum("tpo,pc->cto", terms.astype(jnp.bfloat16), onehot, preferred_element_type=jnp.float32)
-        local = local.reshape(chips, pair, own_blocks, tok_rows, block_size)
-        keep = lax.dynamic_index_in_dim(local, core, axis=1, keepdims=False)
-        give = lax.dynamic_index_in_dim(local, 1 - core, axis=1, keepdims=False)
+        local = jnp.einsum("tpo,pc->tco", terms.astype(jnp.bfloat16), onehot, preferred_element_type=jnp.float32)
+        local = local.reshape(tok_rows, chips, pair, own_blocks, block_size)
+        keep = lax.dynamic_index_in_dim(local, core, axis=2, keepdims=False)
+        give = lax.dynamic_index_in_dim(local, 1 - core, axis=2, keepdims=False)
         return (keep + swap_core(give)).astype(jnp.bfloat16)
 
     def finish(got):
-        total = got.astype(jnp.float32).sum(axis=0)
-        return total.transpose(1, 0, 2).reshape(tok_rows, own_cols).astype(jnp.bfloat16)
+        return got.astype(jnp.float32).sum(axis=1).reshape(tok_rows, own_cols).astype(jnp.bfloat16)
 
     preact = jnp.einsum("rkti,rkio->tro", in_sel, w_in, preferred_element_type=jnp.float32)
     hidden = gelu_value(preact).astype(jnp.bfloat16)
@@ -120,9 +119,9 @@
     pre_grad = (hid_grad * gelu_slope(preact)).astype(jnp.bfloat16)
     in_terms = jnp.einsum("tro,rkio->trki", pre_grad, w_in, preferred_element_type=jnp.float32)
     in_send = chip_sums(in_terms, in_flat)
-    got = lax.all_to_all(jnp.stack([out_send, in_send], axis=1), "chip", split_axis=0, concat_axis=0, tiled=True)
-    outputs = finish(got[:, 0])
-    in_grad = finish(got[:, 1])
+    got = lax.all_to_all(jnp.stack([out_send, in_send], axis=0), "chip", split_axis=2, concat_axis=2, tiled=True)
+    outputs = finish(got[0])
+    in_grad = finish(got[1])
     w_in_part = jnp.einsum("rkti,tro->rkio", in_sel, pre_grad, preferred_element_type=jnp.float32)
     w_in_grad = dp_total(w_in_part)
     return (outputs, in_grad, w_in_grad, w_out_grad)

time: 129 us -> 135 us (1.047)
  other arithmetic: 14.5 us -> 18 us
  local copies, waits for them, and re-layouts: 13.8 us -> 16 us
    dynamic_slice x3, local copies, waits for them, and re-layouts: 1.59 us -> 5.73 us  [the longest x1 3.38 us: chip_sums(): keep = lax.dynamic_index_in_dim(local, core, axis=2, keepdims=False)]
    another operation x3, other arithmetic: 1.22 us -> 4.04 us  [per_device(): jnp.stack([out_send, in_send], axis=0)]
    another operation x1 -> x0, local copies, waits for them, and re-layouts: 1.45 us -> none  [per_device(): jnp.stack([out_send, in_send], axis=1)]
where the time goes in v22:
time: 135 us
  waiting for transfers between devices  73.8 us (55%)
  starting transfers between devices  18.8 us (14%)
  other arithmetic  18 us (13%)
  local copies, waits for them, and re-layouts  16 us (12%)
  matrix products  7.11 us (5%)
    ppermute x2, waiting for transfers between devices, dp_total(): got = lax.ppermute(part, 'dp', perm=[(0, 1), (1, 0)])  43.4 us
    ppermute x6, waiting for transfers between devices, gather_chips(): got = lax.ppermute(held, 'chip', perm=[(i, i ^ step) for i in range(chips)])  24.7 us
    ppermute x6, starting transfers between devices, gather_chips(): got = lax.ppermute(held, 'chip', perm=[(i, i ^ step) for i in range(chips)])  9.22 us
    all_to_all x1, starting transfers between devices, per_device(): lax.all_to_all(jnp.stack([out_send, in_send], axis=0), 'chip', split_axis...  6.79 us
    ppermute x4, waiting for transfers between devices, swap_core(): return lax.ppermute(x, 'core', perm=[(0, 1), (1, 0)])  5.77 us
    unnamed x17, local copies, waits for them, and re-layouts  5.69 us
    another operation x2, other arithmetic, gather(): return jnp.stack([mine, swap_core(mine)], axis=0)  4.49 us
    another operation x3, other arithmetic, per_device(): jnp.stack([out_send, in_send], axis=0)  4.04 us
  transfers between devices with their start and end apart: 13, of which 10 were waited for; matrix products, arithmetic and copies ran while one was open for 12% of the time, Pallas kernels for 0%

profile of v22, /device:TPU:0, one launch (start us, length us, event | category | flops | bytes accessed | tf_op | source)
XLA Modules:
  0.0 134.7 jit_solution(3526128120701026643)
XLA Ops:
  0.6 1.1 copy.51
  1.9 4.1 %collective-permute-start.5 = (bf16[1,4,128,128]{3,2,1,0:T(8,128)(2,1)S(1)}, bf16[1,4,128,128]{3,2,1,0:T(8,128)(2,1)S(1)}, u32[]{:S(2)}, u32[]{:S(2)}) collective-permute-start(bf16[1,4,128,128]{3,2,1,0:T(8,128)(2,1)S(1)} %bitcast.122), channel_id=1, source_target_pairs={{0,8},{2,10},{4,12},{6,14},{8,0},{10,2},{12,4},{14,6},{1,9},{3,11}... | collective-permute-start | bytes 393224 | tf_op jit(solution)/shard_map/ppermute | solution.py:42
  6.0 1.0 copy.44
  7.3 8.7 %collective-permute-done.5 = bf16[1,4,128,128]{3,2,1,0:T(8,128)(2,1)S(1)} collective-permute-done((bf16[1,4,128,128]{3,2,1,0:T(8,128)(2,1)S(1)}, bf16[1,4,128,128]{3,2,1,0:T(8,128)(2,1)S(1)}, u32[]{:S(2)}, u32[]{:S(2)}) %collective-permute-start.5) | collective-permute-done | bytes 131104 | tf_op jit(solution)/shard_map/ppermute | solution.py:42
  16.1 2.0 %collective-permute-done = bf16[1,4,128,128]{3,2,1,0:T(8,128)(2,1)S(1)} collective-permute-done((bf16[1,4,128,128]{3,2,1,0:T(8,128)(2,1)S(1)}, bf16[1,4,128,128]{3,2,1,0:T(8,128)(2,1)S(1)}, u32[]{:S(2)}, u32[]{:S(2)}) %collective-permute-start) | collective-permute-done | bytes 131104 | tf_op jit(solution)/shard_map/ppermute | solution.py:42
  18.0 1.7 %collective-permute-start.1 = (bf16[2,4,128,128]{3,2,1,0:T(8,128)(2,1)S(1)}, bf16[2,4,128,128]{3,2,1,0:T(8,128)(2,1)S(1)}, u32[]{:S(2)}, u32[]{:S(2)}) collective-permute-start(bf16[2,4,128,128]{3,2,1,0:T(8,128)(2,1)S(1)} %maximum_select_fusion.6), channel_id=1, source_target_pairs={{0,2},{2,0},{4,6},{6,4},{8,10},{10,8},{12,14},{14,12},{1,3},{3,1},... | collective-permute-start | bytes 786440 | tf_op jit(solution)/shard_map/ppermute | solution.py:42
  19.7 3.8 %collective-permute-done.6 = bf16[2,4,128,128]{3,2,1,0:T(8,128)(2,1)S(1)} collective-permute-done((bf16[2,4,128,128]{3,2,1,0:T(8,128)(2,1)S(1)}, bf16[2,4,128,128]{3,2,1,0:T(8,128)(2,1)S(1)}, u32[]{:S(2)}, u32[]{:S(2)}) %collective-permute-start.6) | collective-permute-done | bytes 262176 | tf_op jit(solution)/shard_map/ppermute | solution.py:42
  23.6 1.6 %collective-permute-start.7 = (bf16[4,4,128,128]{3,2,1,0:T(8,128)(2,1)S(1)}, bf16[4,4,128,128]{3,2,1,0:T(8,128)(2,1)S(1)}, u32[]{:S(2)}, u32[]{:S(2)}) collective-permute-start(bf16[4,4,128,128]{3,2,1,0:T(8,128)(2,1)S(1)} %maximum_select_fusion.5), channel_id=1, source_target_pairs={{0,2},{2,0},{4,6},{6,4},{8,10},{10,8},{12,14},{14,12},{1,3},{3,1},... | collective-permute-start | bytes 1572872 | tf_op jit(solution)/shard_map/ppermute | solution.py:42
  25.3 1.0 collective-permute-done.1
  26.4 1.7 %collective-permute-start.2 = (bf16[4,4,128,128]{3,2,1,0:T(8,128)(2,1)S(1)}, bf16[4,4,128,128]{3,2,1,0:T(8,128)(2,1)S(1)}, u32[]{:S(2)}, u32[]{:S(2)}) collective-permute-start(bf16[4,4,128,128]{3,2,1,0:T(8,128)(2,1)S(1)} %maximum_select_fusion.4), channel_id=1, source_target_pairs={{0,4},{2,6},{4,0},{6,2},{8,12},{10,14},{12,8},{14,10},{1,5},{3,7},... | collective-permute-start | bytes 1572872 | tf_op jit(solution)/shard_map/ppermute | solution.py:42
  28.1 8.7 %collective-permute-done.7 = bf16[4,4,128,128]{3,2,1,0:T(8,128)(2,1)S(1)} collective-permute-done((bf16[4,4,128,128]{3,2,1,0:T(8,128)(2,1)S(1)}, bf16[4,4,128,128]{3,2,1,0:T(8,128)(2,1)S(1)}, u32[]{:S(2)}, u32[]{:S(2)}) %collective-permute-start.7) | collective-permute-done | bytes 524320 | tf_op jit(solution)/shard_map/ppermute | solution.py:42
  36.7 1.1 maximum_select_fusion.3
  38.4 1.1 maximum_select_fusion.1
  40.1 1.2 maximum_select_fusion
  41.5 1.4 %pad_maximum_fusion.1 = bf16[2,8,4,128,128]{4,3,2,1,0:T(8,128)(2,1)S(1)} fusion(bf16[1,8,4,128,128]{4,3,2,1,0:T(8,128)(2,1)} %bitcast.31, bf16[1,8,4,128,128]{4,3,2,1,0:T(8,128)(2,1)S(1)} %maximum_select_fusion.2), kind=kLoop, calls=%fused_computation.3 | loop fusion | flops 1048576 | bytes 4194304 | tf_op jit(solution)/shard_map/stack | solution.py:75
  42.9 1.7 %gather_fusion.1 = bf16[32,128,128]{2,1,0:T(8,128)(2,1)} fusion(bf16[2,8,4,128,128]{4,3,2,1,0:T(8,128)(2,1)S(1)} %pad_maximum_fusion.1, s32[32]{0:T(128)S(1)} %fusion.51), kind=kCustom, calls=%fused_computation.1 | custom fusion | bytes 2097536 | tf_op jit(solution)/shard_map/gather | solution.py:81
  44.6 3.1 %pad_maximum_fusion = bf16[2,8,4,128,128]{4,3,2,1,0:T(8,128)(2,1)} fusion(bf16[1,8,4,128,128]{4,3,2,1,0:T(8,128)(2,1)} %bitcast.7, bf16[1,8,4,128,128]{4,3,2,1,0:T(8,128)(2,1)} %maximum_select_fusion), kind=kLoop, calls=%fused_computation.2 | loop fusion | flops 1048576 | bytes 4194304 | tf_op jit(solution)/shard_map/stack | solution.py:75
  47.6 2.4 %gather_fusion = bf16[32,128,128]{2,1,0:T(8,128)(2,1)S(1)} fusion(bf16[2,8,4,128,128]{4,3,2,1,0:T(8,128)(2,1)} %pad_maximum_fusion, s32[32]{0:T(128)S(1)} %fusion.52), kind=kCustom, calls=%fused_computation | custom fusion | bytes 2097536 | tf_op jit(solution)/shard_map/gather | solution.py:81
  50.0 1.7 %convolution_bitcast_fusion.1 = f32[128,8,128]{2,0,1:T(8,128)S(1)} fusion(bf16[8,4,128,128]{3,2,1,0:T(8,128)(2,1)S(1)} %bitcast.108, bf16[8,4,128,128]{3,2,1,0:T(8,128)(2,1)} %param.8), kind=kOutput, calls=%fused_computation.19 | convolution fusion | flops 134217728 | bytes 2621440 | tf_op jit(solution)/shard_map/rkti,rkio->tro/dot_general | solution.py:110
  55.7 3.4 %constant_dynamic-slice_fusion.1 = (f32[128,8,1,4,128]{4,3,2,1,0:T(4,128)S(1)}, f32[128,8,1,4,128]{4,3,2,1,0:T(4,128)S(1)}, f32[128,8,1,4,128]{4,3,2,1,0:T(4,128)}, f32[128,8,1,4,128]{4,3,2,1,0:T(4,128)S(1)}) fusion(f32[128,8,2,4,128]{4,3,2,1,0:T(4,128)S(1)} %bitcast.106, s32[]{:T(128)S(6)} %select_n.412, s32[]{:T(128)S(6)} %select_n.413, ...), kind=kLoop, calls=%fused_computation.102 | loop fusion | bytes 16777224 | tf_op jit(solution)/shard_map/jit(dynamic_index_in_dim)/dynamic_slice | solution.py:103
  59.1 2.0 %copy.83 = f32[128,8,1,4,128]{4,3,0,1,2:T(4,128)S(1)} copy(f32[128,8,1,4,128]{4,3,2,1,0:T(4,128)} %get-tuple-element.26) | data formatting | bytes 4194304 | tf_op jit(solution)/shard_map/jit(dynamic_index_in_dim)/dynamic_slice | solution.py:104
  62.1 3.3 %collective-permute-done.4 = f32[128,8,4,128]{3,2,0,1:T(4,128)S(1)} collective-permute-done((f32[128,8,4,128]{3,2,0,1:T(4,128)S(1)}, f32[128,8,4,128]{3,2,0,1:T(4,128)S(1)}, u32[]{:S(2)}, u32[]{:S(2)}) %collective-permute-start.4) | collective-permute-done | bytes 2097184 | tf_op jit(solution)/shard_map/ppermute | solution.py:22
  65.9 2.4 %collective-permute-done.9 = f32[128,8,4,128]{3,2,0,1:T(4,128)S(1)} collective-permute-done((f32[128,8,4,128]{3,2,0,1:T(4,128)S(1)}, f32[128,8,4,128]{3,2,0,1:T(4,128)S(1)}, u32[]{:S(2)}, u32[]{:S(2)}) %collective-permute-start.9) | collective-permute-done | bytes 2097184 | tf_op jit(solution)/shard_map/ppermute | solution.py:22
  68.9 2.9 %pad_maximum_fusion.2 = bf16[2,128,8,4,128]{4,3,1,0,2:T(4,128)(2,1)} fusion(bf16[1,128,8,4,128]{4,3,1,0,2:T(4,128)(2,1)S(1)} %fusion.7, bf16[1,128,8,4,128]{4,3,1,0,2:T(4,128)(2,1)S(1)} %fusion.6), kind=kLoop, calls=%fused_computation.4 | loop fusion | flops 1048576 | bytes 4194304 | tf_op jit(solution)/shard_map/stack | solution.py:122
  71.9 6.8 %all-to-all-start = ((bf16[2,128,8,4,128]{4,3,1,0,2:T(4,128)(2,1)}), bf16[2,128,8,4,128]{4,3,1,0,2:T(4,128)(2,1)}, u32[]{:S(2)}, u32[]{:S(2)}) async-start(bf16[2,128,8,4,128]{4,3,1,0,2:T(4,128)(2,1)} %pad_maximum_fusion.2), calls=%async_computation | async-start | bytes 4194304 | tf_op jit(solution)/shard_map/all_to_all | solution.py:122
  78.7 1.7 %fusion.2 = bf16[8,4,128,128]{2,3,1,0:T(8,128)(2,1)S(1)} fusion(bf16[8,4,128,128]{3,2,1,0:T(8,128)(2,1)} %bitcast.112, f32[128,8,128]{2,0,1:T(8,128)S(1)} %convolution_bitcast_fusion.1), kind=kOutput, calls=%fused_computation.17 | convolution fusion | flops 135397376 | bytes 2621440 | tf_op jit(solution)/shard_map/tri,rkto->rkio/dot_general | solution.py:115
  80.4 1.6 %collective-permute-start.11 = (bf16[8,4,128,128]{2,3,1,0:T(8,128)(2,1)S(1)}, bf16[8,4,128,128]{2,3,1,0:T(8,128)(2,1)S(1)}, u32[]{:S(2)}, u32[]{:S(2)}) collective-permute-start(bf16[8,4,128,128]{2,3,1,0:T(8,128)(2,1)S(1)} %fusion.2), channel_id=1, source_target_pairs={{0,16},{16,0},{1,17},{17,1},{2,18},{18,2},{3,19},{19,3},{4,20},{20... | collective-permute-start | bytes 3145736 | tf_op jit(solution)/shard_map/ppermute | solution.py:92
  83.1 23.4 %collective-permute-done.11 = bf16[8,4,128,128]{2,3,1,0:T(8,128)(2,1)S(1)} collective-permute-done((bf16[8,4,128,128]{2,3,1,0:T(8,128)(2,1)S(1)}, bf16[8,4,128,128]{2,3,1,0:T(8,128)(2,1)S(1)}, u32[]{:S(2)}, u32[]{:S(2)}) %collective-permute-start.11) | collective-permute-done | bytes 1048608 | tf_op jit(solution)/shard_map/ppermute | solution.py:92
  106.9 1.3 copy.59
  108.2 20.0 %collective-permute-done.10 = bf16[8,4,128,128]{3,2,1,0:T(8,128)(2,1)} collective-permute-done((bf16[8,4,128,128]{3,2,1,0:T(8,128)(2,1)S(1)}, bf16[8,4,128,128]{3,2,1,0:T(8,128)(2,1)}, u32[]{:S(2)}, u32[]{:S(2)}) %collective-permute-start.10) | collective-permute-done | bytes 1048608 | tf_op jit(solution)/shard_map/ppermute | solution.py:92
  128.2 2.6 %add_convert_fusion.1 = bf16[8,4,128,128]{3,2,1,0:T(8,128)(2,1)} fusion(bf16[8,4,128,128]{3,2,1,0:T(8,128)(2,1)} %collective-permute-done.10, bf16[8,4,128,128]{3,2,1,0:T(8,128)(2,1)S(1)} %convolution_convert_fusion.1), kind=kLoop, calls=%fused_computation.12 | loop fusion | flops 2097152 | bytes 3145728 | tf_op jit(solution)/shard_map/convert_element_type | solution.py:93
  130.8 2.6 %slice_reduce_fusion = (bf16[128,4,128]{2,1,0:T(4,128)(2,1)S(1)}, bf16[128,4,128]{2,1,0:T(4,128)(2,1)S(1)}) fusion(bf16[2,128,8,4,128]{4,3,1,0,2:T(4,128)(2,1)} %all-to-all-done), kind=kLoop, calls=%fused_computation.25 | loop fusion | flops 917504 | bytes 2359296 | tf_op jit(solution)/shard_map/reduce_sum | solution.py:108
  (48 shorter events, 10.8 us)
Async XLA Ops:
  0.6 51.1 %copy-start = (bf16[8,4,128,128]{3,2,1,0:T(8,128)(2,1)S(1)}, bf16[8,4,128,128]{3,2,1,0:T(8,128)(2,1)}, u32[]{:S(2)}) copy-start(bf16[8,4,128,128]{3,2,1,0:T(8,128)(2,1)} %param.10) | copy-start | bytes 3145732
  1.9 14.0 %collective-permute-start.5 = (bf16[1,4,128,128]{3,2,1,0:T(8,128)(2,1)S(1)}, bf16[1,4,128,128]{3,2,1,0:T(8,128)(2,1)S(1)}, u32[]{:S(2)}, u32[]{:S(2)}) collective-permute-start(bf16[1,4,128,128]{3,2,1,0:T(8,128)(2,1)S(1)} %bitcast.122), channel_id=1, source_target_pairs={{0,8},{2,10},{4,12},{6,14},{8,0},{10,2},{12,4},{14,6},{1,9},{3,11}... | collective-permute-start | bytes 393224 | tf_op jit(solution)/shard_map/ppermute | solution.py:42
  7.2 10.8 %collective-permute-start = (bf16[1,4,128,128]{3,2,1,0:T(8,128)(2,1)S(1)}, bf16[1,4,128,128]{3,2,1,0:T(8,128)(2,1)S(1)}, u32[]{:S(2)}, u32[]{:S(2)}) collective-permute-start(bf16[1,4,128,128]{3,2,1,0:T(8,128)(2,1)S(1)} %bitcast.120), channel_id=1, source_target_pairs={{0,8},{2,10},{4,12},{6,14},{8,0},{10,2},{12,4},{14,6},{1,9},{3,11}... | collective-permute-start | bytes 393224 | tf_op jit(solution)/shard_map/ppermute | solution.py:42
  16.0 7.6 %collective-permute-start.6 = (bf16[2,4,128,128]{3,2,1,0:T(8,128)(2,1)S(1)}, bf16[2,4,128,128]{3,2,1,0:T(8,128)(2,1)S(1)}, u32[]{:S(2)}, u32[]{:S(2)}) collective-permute-start(bf16[2,4,128,128]{3,2,1,0:T(8,128)(2,1)S(1)} %maximum_select_fusion.7), channel_id=1, source_target_pairs={{0,4},{2,6},{4,0},{6,2},{8,12},{10,14},{12,8},{14,10},{1,5},{3,7},... | collective-permute-start | bytes 786440 | tf_op jit(solution)/shard_map/ppermute | solution.py:42
  18.0 8.3 %collective-permute-start.1 = (bf16[2,4,128,128]{3,2,1,0:T(8,128)(2,1)S(1)}, bf16[2,4,128,128]{3,2,1,0:T(8,128)(2,1)S(1)}, u32[]{:S(2)}, u32[]{:S(2)}) collective-permute-start(bf16[2,4,128,128]{3,2,1,0:T(8,128)(2,1)S(1)} %maximum_select_fusion.6), channel_id=1, source_target_pairs={{0,2},{2,0},{4,6},{6,4},{8,10},{10,8},{12,14},{14,12},{1,3},{3,1},... | collective-permute-start | bytes 786440 | tf_op jit(solution)/shard_map/ppermute | solution.py:42
  23.6 13.1 %collective-permute-start.7 = (bf16[4,4,128,128]{3,2,1,0:T(8,128)(2,1)S(1)}, bf16[4,4,128,128]{3,2,1,0:T(8,128)(2,1)S(1)}, u32[]{:S(2)}, u32[]{:S(2)}) collective-permute-start(bf16[4,4,128,128]{3,2,1,0:T(8,128)(2,1)S(1)} %maximum_select_fusion.5), channel_id=1, source_target_pairs={{0,2},{2,0},{4,6},{6,4},{8,10},{10,8},{12,14},{14,12},{1,3},{3,1},... | collective-permute-start | bytes 1572872 | tf_op jit(solution)/shard_map/ppermute | solution.py:42
  26.4 13.2 %copy-start.3 = (s32[8,4]{0,1:T(4,128)S(1)}, s32[8,4]{0,1:T(4,128)}, u32[]{:S(2)}) copy-start(s32[8,4]{0,1:T(4,128)} %param.9) | copy-start | bytes 388
  26.4 13.4 %copy-start.4 = (s32[8,4]{0,1:T(4,128)S(1)}, s32[8,4]{0,1:T(4,128)}, u32[]{:S(2)}) copy-start(s32[8,4]{0,1:T(4,128)} %param.11) | copy-start | bytes 388
  26.4 12.0 %collective-permute-start.2 = (bf16[4,4,128,128]{3,2,1,0:T(8,128)(2,1)S(1)}, bf16[4,4,128,128]{3,2,1,0:T(8,128)(2,1)S(1)}, u32[]{:S(2)}, u32[]{:S(2)}) collective-permute-start(bf16[4,4,128,128]{3,2,1,0:T(8,128)(2,1)S(1)} %maximum_select_fusion.4), channel_id=1, source_target_pairs={{0,4},{2,6},{4,0},{6,2},{8,12},{10,14},{12,8},{14,10},{1,5},{3,7},... | collective-permute-start | bytes 1572872 | tf_op jit(solution)/shard_map/ppermute | solution.py:42
  37.9 3.6 %collective-permute-start.8 = (bf16[8,4,128,128]{3,2,1,0:T(8,128)(2,1)}, bf16[8,4,128,128]{3,2,1,0:T(8,128)(2,1)}, u32[]{:S(2)}, u32[]{:S(2)}) collective-permute-start(bf16[8,4,128,128]{3,2,1,0:T(8,128)(2,1)} %maximum_select_fusion.3), channel_id=1, source_target_pairs={{0,1},{1,0},{2,3},{3,2},{4,5},{5,4},{6,7},{7,6},{8,9},{9,8},{10,11... | collective-permute-start | bytes 3145736 | tf_op jit(solution)/shard_map/ppermute | solution.py:22
  39.5 5.0 %collective-permute-start.3 = (bf16[8,4,128,128]{3,2,1,0:T(8,128)(2,1)}, bf16[8,4,128,128]{3,2,1,0:T(8,128)(2,1)}, u32[]{:S(2)}, u32[]{:S(2)}) collective-permute-start(bf16[8,4,128,128]{3,2,1,0:T(8,128)(2,1)} %maximum_select_fusion.1), channel_id=1, source_target_pairs={{0,1},{1,0},{2,3},{3,2},{4,5},{5,4},{6,7},{7,6},{8,9},{9,8},{10,11... | collective-permute-start | bytes 3145736 | tf_op jit(solution)/shard_map/ppermute | solution.py:22
  50.0 2.2 %copy-start.2 = (bf16[32,128,128]{2,1,0:T(8,128)(2,1)S(1)}, bf16[32,128,128]{2,1,0:T(8,128)(2,1)}, u32[]{:S(2)}) copy-start(bf16[32,128,128]{2,1,0:T(8,128)(2,1)} %gather_fusion.1) | copy-start | bytes 3145732
  52.2 1.2 copy-start.1
  61.0 4.4 %collective-permute-start.4 = (f32[128,8,4,128]{3,2,0,1:T(4,128)S(1)}, f32[128,8,4,128]{3,2,0,1:T(4,128)S(1)}, u32[]{:S(2)}, u32[]{:S(2)}) collective-permute-start(f32[128,8,4,128]{3,2,0,1:T(4,128)S(1)} %bitcast.119), channel_id=1, source_target_pairs={{0,1},{1,0},{2,3},{3,2},{4,5},{5,4},{6,7},{7,6},{8,9},{9,8},{10,11... | collective-permute-start | bytes 6291464 | tf_op jit(solution)/shard_map/ppermute | solution.py:22
  62.0 6.4 %collective-permute-start.9 = (f32[128,8,4,128]{3,2,0,1:T(4,128)S(1)}, f32[128,8,4,128]{3,2,0,1:T(4,128)S(1)}, u32[]{:S(2)}, u32[]{:S(2)}) collective-permute-start(f32[128,8,4,128]{3,2,0,1:T(4,128)S(1)} %bitcast.118), channel_id=1, source_target_pairs={{0,1},{1,0},{2,3},{3,2},{4,5},{5,4},{6,7},{7,6},{8,9},{9,8},{10,11... | collective-permute-start | bytes 6291464 | tf_op jit(solution)/shard_map/ppermute | solution.py:22
  71.9 58.9 %all-to-all-start = ((bf16[2,128,8,4,128]{4,3,1,0,2:T(4,128)(2,1)}), bf16[2,128,8,4,128]{4,3,1,0,2:T(4,128)(2,1)}, u32[]{:S(2)}, u32[]{:S(2)}) async-start(bf16[2,128,8,4,128]{4,3,1,0,2:T(4,128)(2,1)} %pad_maximum_fusion.2), calls=%async_computation | async-start | bytes 4194304 | tf_op jit(solution)/shard_map/all_to_all | solution.py:122
  80.4 26.1 %collective-permute-start.11 = (bf16[8,4,128,128]{2,3,1,0:T(8,128)(2,1)S(1)}, bf16[8,4,128,128]{2,3,1,0:T(8,128)(2,1)S(1)}, u32[]{:S(2)}, u32[]{:S(2)}) collective-permute-start(bf16[8,4,128,128]{2,3,1,0:T(8,128)(2,1)S(1)} %fusion.2), channel_id=1, source_target_pairs={{0,16},{16,0},{1,17},{17,1},{2,18},{18,2},{3,19},{19,3},{4,20},{20... | collective-permute-start | bytes 3145736 | tf_op jit(solution)/shard_map/ppermute | solution.py:92
  82.5 45.7 %collective-permute-start.10 = (bf16[8,4,128,128]{3,2,1,0:T(8,128)(2,1)S(1)}, bf16[8,4,128,128]{3,2,1,0:T(8,128)(2,1)}, u32[]{:S(2)}, u32[]{:S(2)}) collective-permute-start(bf16[8,4,128,128]{3,2,1,0:T(8,128)(2,1)S(1)} %convolution_convert_fusion.1), channel_id=1, source_target_pairs={{0,16},{16,0},{1,17},{17,1},{2,18},{18,2},{3,19},{19,3},{4,20},{20... | collective-permute-start | bytes 3145736 | tf_op jit(solution)/shard_map/ppermute | solution.py:92
